TPU v7x, 32 devices: a whole 2x2x4 slice. The times are simulated.
32 devices in a mesh: groups: 2 (over y), seq: 16 (over z, x, core).
Axes of the slice: x: 2, y: 2, z: 4, core: 2. Of those that a mesh axis runs over, the one named last changes fastest.
Arguments:
- query_rows: bfloat16 [4096, 768], P(('groups', 'seq')), parts along dimension 0, may hold values from -10 to 10
- key_rows: bfloat16 [4096, 768], P(('groups', 'seq')), parts along dimension 0, may hold values from -10 to 10
- value_rows: bfloat16 [4096, 768], P(('groups', 'seq')), parts along dimension 0, may hold values from -6 to 6
- output_grad: bfloat16 [4096, 768], P(('groups', 'seq')), parts along dimension 0, may hold values from -6 to 6
- head_offsets: int32 [3, 12], replicated, may hold values from 0 to 15, as said below
Outputs:
- attended: bfloat16 [4096, 768], P(('groups', 'seq')), parts along dimension 0
- query_grad: bfloat16 [4096, 768], P(('groups', 'seq')), parts along dimension 0
- key_grad: bfloat16 [4096, 768], P(('groups', 'seq')), parts along dimension 0
- value_grad: bfloat16 [4096, 768], P(('groups', 'seq')), parts along dimension 0
There are 2 independent parts, one for each index of `groups`. A program takes and returns all parts, laid end to end along the dimension named above; an argument that names none is the same for every part. Nothing has to cross between parts.
Inputs may be any that keep to these rules, and one draw needn't show every extreme that they name: `head_offsets`: row 0 is all zeros; the entries of row 1 lie below 4, those of row 2 below 16.
All inputs are finite; a program needn't handle non-finite values.
Results may differ from a plain program's by a relative error of at most 0.0084.
Values may be sent and summed in bfloat16 or wider, within the bound.
No kernel may reach another device: no remote copies, remote signals or barrier semaphores. Data moves between devices by JAX's collectives and lax.ppermute only.
A program may use at most 128 MiB of HBM per device.

v0:
```python
import math

import jax
import jax.numpy as jnp
from jax import lax
from jax.experimental import pallas as pl
from jax.experimental.pallas import tpu as pltpu
from jax.sharding import PartitionSpec as P

LEN_NEAR = 1024
LEN_MID = 4096
LEN_FAR = 16384
DILATION_FIRST = 1
DILATION_SECOND = 4
DILATION_THIRD = 16

NEG_FILL = -1e30
STRIDES = (DILATION_FIRST, DILATION_SECOND, DILATION_THIRD)


def exchange(block, bit):
    count = lax.axis_size("seq")
    route = [(index, index ^ (1 << bit)) for index in range(count)]
    return lax.ppermute(block, "seq", route)


def pick_rows(rows, stride, offsets_row):
    if stride == 1:
        return rows
    pair, count, width = rows.shape
    heads = offsets_row.shape[0]
    grouped = rows.reshape(pair, count // stride, stride, heads, width // heads)
    chosen = (jnp.arange(stride, dtype=jnp.int32)[:, None] == offsets_row[None, :])[
        None, None, :, :, None
    ]
    picked = jnp.sum(jnp.where(chosen, grouped, jnp.zeros((), rows.dtype)), axis=2)
    return picked.reshape(pair, count // stride, width)


def spread_rows(picked, stride, offsets_row):
    if stride == 1:
        return picked
    pair, count, width = picked.shape
    heads = offsets_row.shape[0]
    grouped = picked.reshape(pair, count, 1, heads, width // heads)
    chosen = (jnp.arange(stride, dtype=jnp.int32)[:, None] == offsets_row[None, :])[
        None, None, :, :, None
    ]
    widened = jnp.where(chosen, grouped, jnp.zeros((), picked.dtype))
    return widened.reshape(pair, count * stride, width)


def attention_kernel(head_dim, score_scale):
    def kernel(offsets_ref, query_ref, grad_ref, *refs):
        kv_refs = refs[:3]
        out_ref, qgrad_ref = refs[3:5]
        term_refs = refs[5:]
        pair = pl.program_id(0)
        rows = query_ref.shape[0]
        heads_per_block = query_ref.shape[1] // head_dim
        for sub in range(heads_per_block):
            head = pair * heads_per_block + sub
            cols = slice(sub * head_dim, (sub + 1) * head_dim)
            query = query_ref[:, cols]
            grad = grad_ref[:, cols]
            keys = [kv_ref[0, :, cols] for kv_ref in kv_refs]
            values = [kv_ref[1, :, cols] for kv_ref in kv_refs]
            members = []
            scores = []
            for branch in range(3):
                block = (
                    lax.dot_general(
                        query, keys[branch], (((1,), (1,)), ((), ())),
                        preferred_element_type=jnp.float32,
                    )
                    * score_scale
                )
                if STRIDES[branch] == 1:
                    member = None
                else:
                    row_index = lax.broadcasted_iota(jnp.int32, block.shape, 0)
                    member = (row_index % STRIDES[branch]) == offsets_ref[branch, head]
                    block = jnp.where(member, block, NEG_FILL)
                members.append(member)
                scores.append(block)
            peak = jnp.max(scores[0], axis=1, keepdims=True)
            for branch in range(1, 3):
                peak = jnp.maximum(peak, jnp.max(scores[branch], axis=1, keepdims=True))
            expos = []
            for branch in range(3):
                block = jnp.exp(scores[branch] - peak)
                if members[branch] is not None:
                    block = jnp.where(members[branch], block, 0.0)
                expos.append(block)
            total = jnp.sum(expos[0], axis=1, keepdims=True)
            for branch in range(1, 3):
                total = total + jnp.sum(expos[branch], axis=1, keepdims=True)
            probs = [block / total for block in expos]
            weights = [block.astype(jnp.bfloat16) for block in probs]
            mixed = jnp.dot(weights[0], values[0], preferred_element_type=jnp.float32)
            for branch in range(1, 3):
                mixed = mixed + jnp.dot(
                    weights[branch], values[branch], preferred_element_type=jnp.float32
                )
            out_ref[:, cols] = mixed.astype(out_ref.dtype)
            balance = jnp.sum(grad.astype(jnp.float32) * mixed, axis=1, keepdims=True)
            query_grad = None
            for branch in range(3):
                flow = lax.dot_general(
                    grad, values[branch], (((1,), (1,)), ((), ())),
                    preferred_element_type=jnp.float32,
                )
                score_grad = probs[branch] * (flow - balance)
                piece = jnp.dot(
                    score_grad.astype(jnp.bfloat16), keys[branch],
                    preferred_element_type=jnp.float32,
                )
                query_grad = piece if query_grad is None else query_grad + piece
                key_terms = (
                    jnp.dot(
                        jnp.transpose(score_grad).astype(jnp.bfloat16),
                        query,
                        preferred_element_type=jnp.float32,
                    )
                    * score_scale
                )
                value_terms = jnp.dot(
                    jnp.transpose(probs[branch]).astype(jnp.bfloat16),
                    grad,
                    preferred_element_type=jnp.float32,
                )
                term_refs[branch][0, :, cols] = key_terms
                term_refs[branch][1, :, cols] = value_terms
            qgrad_ref[:, cols] = (query_grad * score_scale).astype(qgrad_ref.dtype)

    return kernel


def make_per_device(branch_bits):
    top_bits = max(branch_bits)

    def per_device(query_rows, key_rows, value_rows, output_grad, head_offsets):
        local_rows, model_width = query_rows.shape
        head_count = head_offsets.shape[1]
        head_dim = model_width // head_count
        score_scale = 1.0 / math.sqrt(head_dim)
        kv_rows = jnp.stack([key_rows, value_rows])

        buffers = [
            pick_rows(kv_rows, STRIDES[branch], head_offsets[branch]) for branch in range(3)
        ]
        for bit in reversed(range(top_bits)):
            active = [branch for branch in range(3) if branch_bits[branch] > bit]
            outgoing = jnp.concatenate(
                [buffers[branch].reshape(-1, model_width) for branch in active]
            )
            incoming = exchange(outgoing, bit)
            cursor = 0
            for branch in active:
                count = buffers[branch].size // model_width
                arrived = incoming[cursor : cursor + count].reshape(buffers[branch].shape)
                cursor += count
                buffers[branch] = jnp.stack([buffers[branch], arrived], axis=1)
        gathered = [buffers[branch].reshape(2, -1, model_width) for branch in range(3)]

        block_width = 128 if (128 % head_dim == 0 and model_width % 128 == 0) else model_width
        pairs = model_width // block_width
        row_block = pl.BlockSpec((local_rows, block_width), lambda p, offs: (0, p))
        kv_blocks = [
            pl.BlockSpec((2, block.shape[1], block_width), lambda p, offs: (0, 0, p))
            for block in gathered
        ]
        outs = pl.pallas_call(
            attention_kernel(head_dim, score_scale),
            out_shape=(
                jax.ShapeDtypeStruct((local_rows, model_width), jnp.bfloat16),
                jax.ShapeDtypeStruct((local_rows, model_width), jnp.bfloat16),
            )
            + tuple(jax.ShapeDtypeStruct(block.shape, jnp.float32) for block in gathered),
            grid_spec=pltpu.PrefetchScalarGridSpec(
                num_scalar_prefetch=1,
                grid=(pairs,),
                in_specs=[row_block, row_block] + kv_blocks,
                out_specs=[row_block, row_block] + kv_blocks,
            ),
            compiler_params=pltpu.CompilerParams(vmem_limit_bytes=100 * 1024 * 1024),
        )(head_offsets, query_rows, output_grad, *gathered)
        attended, query_grad = outs[:2]
        terms = outs[2:]

        partial = [
            terms[branch].reshape((2,) + (2,) * branch_bits[branch] + (-1, model_width))
            for branch in range(3)
        ]
        for bit in range(top_bits):
            active = [branch for branch in range(3) if branch_bits[branch] > bit]
            outgoing = jnp.concatenate(
                [
                    partial[branch][:, 1].reshape(-1, model_width).astype(jnp.bfloat16)
                    for branch in active
                ]
            )
            incoming = exchange(outgoing, bit).astype(jnp.float32)
            cursor = 0
            for branch in active:
                kept = partial[branch][:, 0]
                count = kept.size // model_width
                partial[branch] = kept + incoming[cursor : cursor + count].reshape(kept.shape)
                cursor += count
        total_grad = None
        for branch in range(3):
            spread = spread_rows(partial[branch], STRIDES[branch], head_offsets[branch])
            total_grad = spread if total_grad is None else total_grad + spread

        return (
            attended,
            query_grad,
            total_grad[0].astype(jnp.bfloat16),
            total_grad[1].astype(jnp.bfloat16),
        )

    return per_device


def solution(mesh):
    group_count = mesh.shape["groups"]
    seq_devices = mesh.shape["seq"]

    def run(query_rows, key_rows, value_rows, output_grad, head_offsets):
        local_rows = query_rows.shape[0] // (group_count * seq_devices)
        tokens_all = seq_devices * local_rows
        seg_lengths = [min(LEN_NEAR, tokens_all), min(LEN_MID, tokens_all), min(LEN_FAR, tokens_all)]
        branch_bits = [(seg_length // local_rows).bit_length() - 1 for seg_length in seg_lengths]
        row_spec = P(("groups", "seq"), None)
        return jax.shard_map(
            make_per_device(branch_bits),
            mesh=mesh,
            in_specs=(row_spec, row_spec, row_spec, row_spec, P()),
            out_specs=(row_spec, row_spec, row_spec, row_spec),
            check_vma=False,
        )(query_rows, key_rows, value_rows, output_grad, head_offsets)

    return run
```

profile of v0, /device:TPU:0, one launch (start us, length us, event | category | flops | bytes accessed | tf_op | source)
XLA Modules:
  0.0 173.1 jit_solution(8001978236343833532)
XLA Ops:
  0.7 1.3 stack.89
  2.0 1.3 stack.86
  3.2 0.3 stack.88
  3.6 0.3 stack.85
  3.9 0.6 copy-done.7
  4.5 0.4 fusion.4
  4.9 0.1 reshape_reshape.7
  5.1 0.5 fusion.3
  5.5 0.2 reshape_reshape.6
  5.7 4.1 %collective-permute-start = (bf16[80,768]{1,0:T(8,128)(2,1)S(1)}, bf16[80,768]{1,0:T(8,128)(2,1)S(1)}, u32[]{:S(2)}, u32[]{:S(2)}) collective-permute-start(bf16[80,768]{1,0:T(8,128)(2,1)S(1)} %pad_maximum_fusion.16), channel_id=1, source_target_pairs={{0,8},{1,9},{2,10},{3,11},{4,12},{5,13},{6,14},{7,15},{8,0},{9,1},... | collective-permute-start | bytes 368648 | tf_op jit(solution)/shard_map/ppermute | solution.py:24
  9.8 0.1 stack_reshape.41
  9.9 0.2 stack_reshape.39
  10.2 5.6 %collective-permute-done = bf16[80,768]{1,0:T(8,128)(2,1)S(1)} collective-permute-done((bf16[80,768]{1,0:T(8,128)(2,1)S(1)}, bf16[80,768]{1,0:T(8,128)(2,1)S(1)}, u32[]{:S(2)}, u32[]{:S(2)}) %collective-permute-start) | collective-permute-done | bytes 122912 | tf_op jit(solution)/shard_map/ppermute | solution.py:24
  15.9 0.8 collective-permute-start.1
  16.7 14.8 %collective-permute-done.1 = bf16[416,768]{1,0:T(8,128)(2,1)S(1)} collective-permute-done((bf16[416,768]{1,0:T(8,128)(2,1)S(1)}, bf16[416,768]{1,0:T(8,128)(2,1)S(1)}, u32[]{:S(2)}, u32[]{:S(2)}) %collective-permute-start.1) | collective-permute-done | bytes 639008 | tf_op jit(solution)/shard_map/ppermute | solution.py:24
  31.8 0.1 fusion.22
  32.0 1.3 collective-permute-start.2
  33.3 27.1 %collective-permute-done.2 = bf16[832,768]{1,0:T(8,128)(2,1)S(1)} collective-permute-done((bf16[832,768]{1,0:T(8,128)(2,1)S(1)}, bf16[832,768]{1,0:T(8,128)(2,1)S(1)}, u32[]{:S(2)}, u32[]{:S(2)}) %collective-permute-start.2) | collective-permute-done | bytes 1277984 | tf_op jit(solution)/shard_map/ppermute | solution.py:24
  60.5 0.1 fusion.21
  60.7 0.2 fusion.23
  60.9 0.1 copy.31
  61.0 0.2 pad_maximum_fusion.1
  61.3 4.8 %collective-permute-done.3 = bf16[1664,768]{1,0:T(8,128)(2,1)S(1)} collective-permute-done((bf16[1664,768]{1,0:T(8,128)(2,1)S(1)}, bf16[1664,768]{1,0:T(8,128)(2,1)S(1)}, u32[]{:S(2)}, u32[]{:S(2)}) %collective-permute-start.3) | collective-permute-done | bytes 2555936 | tf_op jit(solution)/shard_map/ppermute | solution.py:24
  66.1 0.1 slice.215
  66.2 0.2 pad_maximum_fusion
  66.5 2.0 %copy.37 = bf16[2,2,2,2,128,768]{5,4,3,2,1,0:T(8,128)(2,1)} copy(bf16[2,2,2,2,128,768]{5,4,3,0,2,1:T(8,128)(2,1)S(1)} %pad_maximum_fusion) | data formatting | bytes 6291456 | tf_op jit(solution)/shard_map/stack | solution.py:163
  68.5 0.1 pad_maximum_fusion.4
  68.6 1.3 copy.39
  70.0 0.8 copy.41
  70.8 26.3 %shard_map.84 = (bf16[128,768]{1,0:T(8,128)(2,1)}, bf16[128,768]{1,0:T(8,128)(2,1)}, f32[2,1024,768]{2,1,0:T(8,128)}, f32[2,512,768]{2,1,0:T(8,128)}, f32[2,128,768]{2,1,0:T(8,128)}) custom-call(s32[3,12]{1,0:T(4,128)} %offsets_ref.1, bf16[128,768]{1,0:T(8,128)(2,1)} %query_ref.1, bf16[128,768]{1,0:T(8,128)(2,1)} %grad_ref.1, ...), custom_call_target="tpu_custom_call" | custom-call | tf_op jit(solution)/shard_map/pallas_call | solution.py:173
  97.1 1.0 slice.304
  98.1 1.5 slice.300
  99.6 2.1 %slice.298 = bf16[2,1,2,2,128,768]{5,4,3,2,1,0:T(8,128)(2,1)S(1)} slice(f32[2,2,2,2,128,768]{5,4,3,2,1,0:T(8,128)} %bitcast.132), slice={[0:2], [1:2], [0:2], [0:2], [0:128], [0:768]} | slice | bytes 3145728 | tf_op jit(solution)/shard_map/slice | solution.py:199
  101.7 0.2 pad_maximum_fusion.2
  101.9 0.2 collective-permute-start.4
  102.1 4.7 %collective-permute-done.4 = bf16[1664,768]{1,0:T(8,128)(2,1)S(1)} collective-permute-done((bf16[1664,768]{1,0:T(8,128)(2,1)S(1)}, bf16[1664,768]{1,0:T(8,128)(2,1)S(1)}, u32[]{:S(2)}, u32[]{:S(2)}) %collective-permute-start.4) | collective-permute-done | bytes 2555936 | tf_op jit(solution)/shard_map/ppermute | solution.py:24
  106.9 0.1 slice.226
  107.0 1.7 %copy-done.3 = f32[2,512,768]{2,1,0:T(8,128)S(1)} copy-done((f32[2,512,768]{2,1,0:T(8,128)S(1)}, f32[2,512,768]{2,1,0:T(8,128)}, u32[]{:S(2)}) %copy-start.3) | copy-done | bytes 3145752
  108.8 0.2 fusion.2
  109.1 0.2 slice.222
  109.3 0.7 slice-done
  110.0 0.8 slice-done.1
  110.8 0.4 fusion
  111.4 1.4 collective-permute-start.5
  112.8 28.8 %collective-permute-done.5 = bf16[832,768]{1,0:T(8,128)(2,1)S(1)} collective-permute-done((bf16[832,768]{1,0:T(8,128)(2,1)S(1)}, bf16[832,768]{1,0:T(8,128)(2,1)S(1)}, u32[]{:S(2)}, u32[]{:S(2)}) %collective-permute-start.5) | collective-permute-done | bytes 1277984 | tf_op jit(solution)/shard_map/ppermute | solution.py:24
  141.7 0.1 fusion.5
  141.9 0.1 slice.231
  142.0 0.2 fusion.1
  142.3 2.4 %collective-permute-start.6 = (bf16[416,768]{1,0:T(8,128)(2,1)S(1)}, bf16[416,768]{1,0:T(8,128)(2,1)S(1)}, u32[]{:S(2)}, u32[]{:S(2)}) collective-permute-start(bf16[416,768]{1,0:T(8,128)(2,1)S(1)} %pad_maximum_fusion.10), channel_id=1, source_target_pairs={{0,4},{1,5},{2,6},{3,7},{4,0},{5,1},{6,2},{7,3},{8,12},{9,13},{10,... | collective-permute-start | bytes 1916936 | tf_op jit(solution)/shard_map/ppermute | solution.py:24
  144.7 13.9 %collective-permute-done.6 = bf16[416,768]{1,0:T(8,128)(2,1)S(1)} collective-permute-done((bf16[416,768]{1,0:T(8,128)(2,1)S(1)}, bf16[416,768]{1,0:T(8,128)(2,1)S(1)}, u32[]{:S(2)}, u32[]{:S(2)}) %collective-permute-start.6) | collective-permute-done | bytes 639008 | tf_op jit(solution)/shard_map/ppermute | solution.py:24
  158.7 3.8 %collective-permute-start.7 = (bf16[80,768]{1,0:T(8,128)(2,1)S(1)}, bf16[80,768]{1,0:T(8,128)(2,1)S(1)}, u32[]{:S(2)}, u32[]{:S(2)}) collective-permute-start(bf16[80,768]{1,0:T(8,128)(2,1)S(1)} %pad_maximum_fusion.17), channel_id=1, source_target_pairs={{0,8},{1,9},{2,10},{3,11},{4,12},{5,13},{6,14},{7,15},{8,0},{9,1},... | collective-permute-start | bytes 368648 | tf_op jit(solution)/shard_map/ppermute | solution.py:24
  162.5 0.1 broadcast_in_dim.92
  162.6 1.0 broadcast_in_dim.93
  163.6 0.1 broadcast_in_dim.86
  163.8 1.0 broadcast_in_dim.87
  164.9 0.1 squeeze.43
  165.1 1.9 %collective-permute-done.7 = bf16[80,768]{1,0:T(8,128)(2,1)S(1)} collective-permute-done((bf16[80,768]{1,0:T(8,128)(2,1)S(1)}, bf16[80,768]{1,0:T(8,128)(2,1)S(1)}, u32[]{:S(2)}, u32[]{:S(2)}) %collective-permute-start.7) | collective-permute-done | bytes 122912 | tf_op jit(solution)/shard_map/ppermute | solution.py:24
  167.1 0.2 broadcast_in_dim.95
  167.3 1.4 broadcast_in_dim.96
  168.7 0.1 reshape.205
  168.9 0.2 broadcast_in_dim.89
  169.1 1.4 broadcast_in_dim.90
  170.5 1.8 %fusion.9 = bf16[2,128,768]{2,1,0:T(8,128)(2,1)S(1)} fusion(f32[2,128,768]{2,1,0:T(8,128)S(1)} %bitcast.136, f32[2,2,128,768]{3,2,1,0:T(8,128)} %copy-done, f32[2,128,768]{2,1,0:T(8,128)} %broadcast_in_dim.96, f32[2,128,768]{2,1,0:T(8,128)} %broadcast_in_dim.90, pred[128,768]{1,0:T(8,128)(4,1)S(1)} %copy-done.5, pred[128,768]{1,0:T(8,128)(4,1)S(1)} %copy-done.6), kind=kLoop, calls=%fused_computation.27 | loop fusion | flops 1179648 | bytes 3735552 | tf_op jit(solution)/shard_map/convert.3 | solution.py:235
  172.3 0.8 slice_bitcast_fusion.5
  (86 shorter events, 1.9 us)
Async XLA Ops:
  0.6 2.6 %copy-start.2 = (bf16[128,768]{1,0:T(8,128)(2,1)S(1)}, bf16[128,768]{1,0:T(8,128)(2,1)}, u32[]{:S(2)}) copy-start(bf16[128,768]{1,0:T(8,128)(2,1)} %param.6) | copy-start | bytes 589828
  0.6 3.3 %copy-start.9 = (s32[3,12]{1,0:T(4,128)S(1)}, s32[3,12]{1,0:T(4,128)}, u32[]{:S(2)}) copy-start(s32[3,12]{1,0:T(4,128)} %offsets_ref.1) | copy-start | bytes 436
  3.9 0.6 copy-start.7
  4.5 5.6 %copy-start.1 = (bf16[128,768]{1,0:T(8,128)(2,1)S(1)}, bf16[128,768]{1,0:T(8,128)(2,1)}, u32[]{:S(2)}) copy-start(bf16[128,768]{1,0:T(8,128)(2,1)} %param.7) | copy-start | bytes 589828
  5.1 5.1 %copy-start.10 = (pred[4,12]{1,0:T(4,128)(4,1)}, pred[4,12]{1,0:T(4,128)(4,1)S(1)}, u32[]{:S(2)}) copy-start(pred[4,12]{1,0:T(4,128)(4,1)S(1)} %iota_compare_fusion.1) | copy-start | bytes 148
  5.7 10.1 %collective-permute-start = (bf16[80,768]{1,0:T(8,128)(2,1)S(1)}, bf16[80,768]{1,0:T(8,128)(2,1)S(1)}, u32[]{:S(2)}, u32[]{:S(2)}) collective-permute-start(bf16[80,768]{1,0:T(8,128)(2,1)S(1)} %pad_maximum_fusion.16), channel_id=1, source_target_pairs={{0,8},{1,9},{2,10},{3,11},{4,12},{5,13},{6,14},{7,15},{8,0},{9,1},... | collective-permute-start | bytes 368648 | tf_op jit(solution)/shard_map/ppermute | solution.py:24
  15.9 15.6 %collective-permute-start.1 = (bf16[416,768]{1,0:T(8,128)(2,1)S(1)}, bf16[416,768]{1,0:T(8,128)(2,1)S(1)}, u32[]{:S(2)}, u32[]{:S(2)}) collective-permute-start(bf16[416,768]{1,0:T(8,128)(2,1)S(1)} %pad_maximum_fusion.9), channel_id=1, source_target_pairs={{0,4},{1,5},{2,6},{3,7},{4,0},{5,1},{6,2},{7,3},{8,12},{9,13},{10,... | collective-permute-start | bytes 1916936 | tf_op jit(solution)/shard_map/ppermute | solution.py:24
  32.0 28.4 %collective-permute-start.2 = (bf16[832,768]{1,0:T(8,128)(2,1)S(1)}, bf16[832,768]{1,0:T(8,128)(2,1)S(1)}, u32[]{:S(2)}, u32[]{:S(2)}) collective-permute-start(bf16[832,768]{1,0:T(8,128)(2,1)S(1)} %pad_maximum_fusion.5), channel_id=1, source_target_pairs={{0,2},{1,3},{2,0},{3,1},{4,6},{5,7},{6,4},{7,5},{8,10},{9,11},{10,... | collective-permute-start | bytes 3833864 | tf_op jit(solution)/shard_map/ppermute | solution.py:24
  61.2 4.9 %collective-permute-start.3 = (bf16[1664,768]{1,0:T(8,128)(2,1)S(1)}, bf16[1664,768]{1,0:T(8,128)(2,1)S(1)}, u32[]{:S(2)}, u32[]{:S(2)}) collective-permute-start(bf16[1664,768]{1,0:T(8,128)(2,1)S(1)} %pad_maximum_fusion.1), channel_id=1, source_target_pairs={{0,1},{1,0},{2,3},{3,2},{4,5},{5,4},{6,7},{7,6},{8,9},{9,8},{10,11... | collective-permute-start | bytes 7667720 | tf_op jit(solution)/shard_map/ppermute | solution.py:24
  101.7 5.1 %copy-start.4 = (f32[2,128,768]{2,1,0:T(8,128)S(1)}, f32[2,128,768]{2,1,0:T(8,128)}, u32[]{:S(2)}) copy-start(f32[2,128,768]{2,1,0:T(8,128)} %get-tuple-element.13) | copy-start | bytes 2359300
  101.9 4.9 %collective-permute-start.4 = (bf16[1664,768]{1,0:T(8,128)(2,1)S(1)}, bf16[1664,768]{1,0:T(8,128)(2,1)S(1)}, u32[]{:S(2)}, u32[]{:S(2)}) collective-permute-start(bf16[1664,768]{1,0:T(8,128)(2,1)S(1)} %pad_maximum_fusion.2), channel_id=1, source_target_pairs={{0,1},{1,0},{2,3},{3,2},{4,5},{5,4},{6,7},{7,6},{8,9},{9,8},{10,11... | collective-permute-start | bytes 7667720 | tf_op jit(solution)/shard_map/ppermute | solution.py:24
  106.9 1.9 %copy-start.3 = (f32[2,512,768]{2,1,0:T(8,128)S(1)}, f32[2,512,768]{2,1,0:T(8,128)}, u32[]{:S(2)}) copy-start(f32[2,512,768]{2,1,0:T(8,128)} %get-tuple-element.12) | copy-start | bytes 9437188
  106.9 3.1 %slice-start = ((s8[6291456]{0:T(1024)(128)(4,1)}), s8[4194304]{0:T(1024)(128)(4,1)S(1)}, s32[]{:S(2)}) async-start(s8[6291456]{0:T(1024)(128)(4,1)} %bitcast.133), calls=%async_computation | async-start | bytes 8388608
  109.0 1.9 %slice-start.1 = ((s8[6291456]{0:T(1024)(128)(4,1)}), s8[2097152]{0:T(1024)(128)(4,1)S(1)}, s32[]{:S(2)}) async-start(s8[6291456]{0:T(1024)(128)(4,1)} %bitcast.133), calls=%async_computation.1 | async-start | bytes 4194304
  111.4 30.2 %collective-permute-start.5 = (bf16[832,768]{1,0:T(8,128)(2,1)S(1)}, bf16[832,768]{1,0:T(8,128)(2,1)S(1)}, u32[]{:S(2)}, u32[]{:S(2)}) collective-permute-start(bf16[832,768]{1,0:T(8,128)(2,1)S(1)} %pad_maximum_fusion.6), channel_id=1, source_target_pairs={{0,2},{1,3},{2,0},{3,1},{4,6},{5,7},{6,4},{7,5},{8,10},{9,11},{10,... | collective-permute-start | bytes 3833864 | tf_op jit(solution)/shard_map/ppermute | solution.py:24
  142.2 16.4 %copy-start = (f32[2,2,128,768]{3,2,1,0:T(8,128)}, f32[2,2,128,768]{3,2,1,0:T(8,128)S(1)}, u32[]{:S(2)}) copy-start(f32[2,2,128,768]{3,2,1,0:T(8,128)S(1)} %fusion.1) | copy-start | bytes 4718596
  142.3 20.2 %copy-start.8 = (pred[16,12]{1,0:T(8,128)(4,1)S(1)}, pred[16,12]{1,0:T(8,128)(4,1)}, u32[]{:S(2)}) copy-start(pred[16,12]{1,0:T(8,128)(4,1)} %copy-done.7) | copy-start | bytes 580
  142.3 16.2 %collective-permute-start.6 = (bf16[416,768]{1,0:T(8,128)(2,1)S(1)}, bf16[416,768]{1,0:T(8,128)(2,1)S(1)}, u32[]{:S(2)}, u32[]{:S(2)}) collective-permute-start(bf16[416,768]{1,0:T(8,128)(2,1)S(1)} %pad_maximum_fusion.10), channel_id=1, source_target_pairs={{0,4},{1,5},{2,6},{3,7},{4,0},{5,1},{6,2},{7,3},{8,12},{9,13},{10,... | collective-permute-start | bytes 1916936 | tf_op jit(solution)/shard_map/ppermute | solution.py:24
  158.6 5.1 %copy-start.11 = (pred[4,12]{1,0:T(4,128)(4,1)S(1)}, pred[4,12]{1,0:T(4,128)(4,1)}, u32[]{:S(2)}) copy-start(pred[4,12]{1,0:T(4,128)(4,1)} %copy-done.10) | copy-start | bytes 148
  158.7 8.3 %collective-permute-start.7 = (bf16[80,768]{1,0:T(8,128)(2,1)S(1)}, bf16[80,768]{1,0:T(8,128)(2,1)S(1)}, u32[]{:S(2)}, u32[]{:S(2)}) collective-permute-start(bf16[80,768]{1,0:T(8,128)(2,1)S(1)} %pad_maximum_fusion.17), channel_id=1, source_target_pairs={{0,8},{1,9},{2,10},{3,11},{4,12},{5,13},{6,14},{7,15},{8,0},{9,1},... | collective-permute-start | bytes 368648 | tf_op jit(solution)/shard_map/ppermute | solution.py:24
  169.1 1.4 copy-start.5
  169.1 1.4 copy-start.6
where the time goes:
time: 173 us
  waiting for transfers between devices  102 us (59%)
  Pallas kernels  26.3 us (15%)
  local copies, waits for them, and re-layouts  24.4 us (14%)
  starting transfers between devices  14 us (8%)
  other arithmetic  5.49 us (3%)
    ppermute x8, waiting for transfers between devices, exchange(): return lax.ppermute(block, 'seq', route)  102 us
    pallas_call x1, Pallas kernels, per_device(): pl.pallas_call(attention_kernel(head_dim, score_scale), out_shape=(jax.Sh...  26.3 us
    ppermute x8, starting transfers between devices, exchange(): return lax.ppermute(block, 'seq', route)  14 us
    slice x12, local copies, waits for them, and re-layouts, per_device(): partial[branch][:, 1].reshape(-1, model_width).astype(jnp.bfloat16)  4.84 us
    another operation x13, local copies, waits for them, and re-layouts, per_device(): buffers[branch] = jnp.stack([buffers[branch], arrived], axis=1)  4.59 us
    unnamed x28, local copies, waits for them, and re-layouts  3.9 us
  transfers between devices with their start and end apart: 8, of which 8 were waited for; matrix products, arithmetic and copies ran while one was open for 2% of the time, Pallas kernels for 0%

commit v1 on v0

--- a/solution.py
+++ b/solution.py
@@ -50,7 +50,7 @@
     return widened.reshape(pair, count * stride, width)
 
 
-def attention_kernel(head_dim, score_scale):
+def attention_kernel(head_dim, score_scale, head_base):
     def kernel(offsets_ref, query_ref, grad_ref, *refs):
         kv_refs = refs[:3]
         out_ref, qgrad_ref = refs[3:5]
@@ -59,7 +59,7 @@
         rows = query_ref.shape[0]
         heads_per_block = query_ref.shape[1] // head_dim
         for sub in range(heads_per_block):
-            head = pair * heads_per_block + sub
+            head = head_base + pair * heads_per_block + sub
             cols = slice(sub * head_dim, (sub + 1) * head_dim)
             query = query_ref[:, cols]
             grad = grad_ref[:, cols]
@@ -136,6 +136,14 @@
     return kernel
 
 
+def gather_order(top_bits, swapped):
+    order = list(reversed(range(top_bits)))
+    if swapped and top_bits >= 3:
+        first, second = order.index(1), order.index(2)
+        order[first], order[second] = order[second], order[first]
+    return order
+
+
 def make_per_device(branch_bits):
     top_bits = max(branch_bits)
 
@@ -145,78 +153,98 @@
         head_dim = model_width // head_count
         score_scale = 1.0 / math.sqrt(head_dim)
         kv_rows = jnp.stack([key_rows, value_rows])
-
-        buffers = [
+        picked = [
             pick_rows(kv_rows, STRIDES[branch], head_offsets[branch]) for branch in range(3)
         ]
-        for bit in reversed(range(top_bits)):
-            active = [branch for branch in range(3) if branch_bits[branch] > bit]
-            outgoing = jnp.concatenate(
-                [buffers[branch].reshape(-1, model_width) for branch in active]
-            )
-            incoming = exchange(outgoing, bit)
-            cursor = 0
-            for branch in active:
-                count = buffers[branch].size // model_width
-                arrived = incoming[cursor : cursor + count].reshape(buffers[branch].shape)
-                cursor += count
-                buffers[branch] = jnp.stack([buffers[branch], arrived], axis=1)
-        gathered = [buffers[branch].reshape(2, -1, model_width) for branch in range(3)]
-
         block_width = 128 if (128 % head_dim == 0 and model_width % 128 == 0) else model_width
-        pairs = model_width // block_width
-        row_block = pl.BlockSpec((local_rows, block_width), lambda p, offs: (0, p))
-        kv_blocks = [
-            pl.BlockSpec((2, block.shape[1], block_width), lambda p, offs: (0, 0, p))
-            for block in gathered
-        ]
-        outs = pl.pallas_call(
-            attention_kernel(head_dim, score_scale),
-            out_shape=(
-                jax.ShapeDtypeStruct((local_rows, model_width), jnp.bfloat16),
-                jax.ShapeDtypeStruct((local_rows, model_width), jnp.bfloat16),
-            )
-            + tuple(jax.ShapeDtypeStruct(block.shape, jnp.float32) for block in gathered),
-            grid_spec=pltpu.PrefetchScalarGridSpec(
-                num_scalar_prefetch=1,
-                grid=(pairs,),
-                in_specs=[row_block, row_block] + kv_blocks,
-                out_specs=[row_block, row_block] + kv_blocks,
-            ),
-            compiler_params=pltpu.CompilerParams(vmem_limit_bytes=100 * 1024 * 1024),
-        )(head_offsets, query_rows, output_grad, *gathered)
-        attended, query_grad = outs[:2]
-        terms = outs[2:]
-
-        partial = [
-            terms[branch].reshape((2,) + (2,) * branch_bits[branch] + (-1, model_width))
-            for branch in range(3)
-        ]
-        for bit in range(top_bits):
-            active = [branch for branch in range(3) if branch_bits[branch] > bit]
-            outgoing = jnp.concatenate(
-                [
-                    partial[branch][:, 1].reshape(-1, model_width).astype(jnp.bfloat16)
-                    for branch in active
-                ]
-            )
-            incoming = exchange(outgoing, bit).astype(jnp.float32)
-            cursor = 0
-            for branch in active:
-                kept = partial[branch][:, 0]
-                count = kept.size // model_width
-                partial[branch] = kept + incoming[cursor : cursor + count].reshape(kept.shape)
-                cursor += count
-        total_grad = None
-        for branch in range(3):
-            spread = spread_rows(partial[branch], STRIDES[branch], head_offsets[branch])
-            total_grad = spread if total_grad is None else total_grad + spread
-
-        return (
-            attended,
-            query_grad,
-            total_grad[0].astype(jnp.bfloat16),
-            total_grad[1].astype(jnp.bfloat16),
+        halves = 2 if model_width % (2 * block_width) == 0 else 1
+        half_width = model_width // halves
+        heads_per_half = head_count // halves
+
+        gathered_halves = []
+        layouts = []
+        for half in range(halves):
+            cols = slice(half * half_width, (half + 1) * half_width)
+            buffers = [block[:, :, cols] for block in picked]
+            axis_bits = [[] for _ in range(3)]
+            for bit in gather_order(top_bits, half == 1):
+                active = [branch for branch in range(3) if branch_bits[branch] > bit]
+                outgoing = jnp.concatenate(
+                    [buffers[branch].reshape(-1, half_width) for branch in active]
+                )
+                incoming = exchange(outgoing, bit)
+                cursor = 0
+                for branch in active:
+                    count = buffers[branch].size // half_width
+                    arrived = incoming[cursor : cursor + count].reshape(buffers[branch].shape)
+                    cursor += count
+                    buffers[branch] = jnp.stack([buffers[branch], arrived], axis=1)
+                    axis_bits[branch].insert(0, bit)
+            gathered_halves.append([buffers[branch].reshape(2, -1, half_width) for branch in range(3)])
+            layouts.append(axis_bits)
+
+        results = []
+        for half in range(halves):
+            gathered = gathered_halves[half]
+            cols = slice(half * half_width, (half + 1) * half_width)
+            pairs = half_width // block_width
+            row_block = pl.BlockSpec((local_rows, block_width), lambda p, offs: (0, p))
+            kv_blocks = [
+                pl.BlockSpec((2, block.shape[1], block_width), lambda p, offs: (0, 0, p))
+                for block in gathered
+            ]
+            outs = pl.pallas_call(
+                attention_kernel(head_dim, score_scale, half * heads_per_half),
+                out_shape=(
+                    jax.ShapeDtypeStruct((local_rows, half_width), jnp.bfloat16),
+                    jax.ShapeDtypeStruct((local_rows, half_width), jnp.bfloat16),
+                )
+                + tuple(jax.ShapeDtypeStruct(block.shape, jnp.float32) for block in gathered),
+                grid_spec=pltpu.PrefetchScalarGridSpec(
+                    num_scalar_prefetch=1,
+                    grid=(pairs,),
+                    in_specs=[row_block, row_block] + kv_blocks,
+                    out_specs=[row_block, row_block] + kv_blocks,
+                ),
+                compiler_params=pltpu.CompilerParams(vmem_limit_bytes=100 * 1024 * 1024),
+            )(head_offsets, query_rows[:, cols], output_grad[:, cols], *gathered)
+            attended, query_grad = outs[:2]
+            terms = outs[2:]
+
+            axis_bits = [list(bits) for bits in layouts[half]]
+            partial = [
+                terms[branch].reshape((2,) + (2,) * branch_bits[branch] + (-1, half_width))
+                for branch in range(3)
+            ]
+            for bit in reversed(gather_order(top_bits, half == 1)):
+                active = [branch for branch in range(3) if branch_bits[branch] > bit]
+                places = {branch: 1 + axis_bits[branch].index(bit) for branch in active}
+                outgoing = jnp.concatenate(
+                    [
+                        lax.index_in_dim(partial[branch], 1, places[branch], keepdims=False)
+                        .reshape(-1, half_width)
+                        .astype(jnp.bfloat16)
+                        for branch in active
+                    ]
+                )
+                incoming = exchange(outgoing, bit).astype(jnp.float32)
+                cursor = 0
+                for branch in active:
+                    kept = lax.index_in_dim(partial[branch], 0, places[branch], keepdims=False)
+                    count = kept.size // half_width
+                    partial[branch] = kept + incoming[cursor : cursor + count].reshape(kept.shape)
+                    cursor += count
+                    axis_bits[branch].remove(bit)
+            offsets_half = head_offsets[:, half * heads_per_half : (half + 1) * heads_per_half]
+            total_grad = None
+            for branch in range(3):
+                spread = spread_rows(partial[branch], STRIDES[branch], offsets_half[branch])
+                total_grad = spread if total_grad is None else total_grad + spread
+            results.append((attended, query_grad, total_grad[0], total_grad[1]))
+
+        return tuple(
+            jnp.concatenate([result[index] for result in results], axis=1).astype(jnp.bfloat16)
+            for index in range(4)
         )
 
     return per_device

time: 173 us -> 149 us (0.86)
  waiting for transfers between devices: 102 us -> 40.3 us
  local copies, waits for them, and re-layouts: 24.4 us -> 40.1 us
  other arithmetic: 5.49 us -> 14.8 us
  starting transfers between devices: 14 us -> 22 us
  Pallas kernels: 26.3 us -> 29.2 us
    ppermute x8 -> x16, waiting for transfers between devices: 102 us -> 40.3 us  [exchange(): return lax.ppermute(block, 'seq', route)]
    ppermute x8 -> x16, starting transfers between devices: 14 us -> 22 us  [exchange(): return lax.ppermute(block, 'seq', route)]
    concatenate x8 -> x19, other arithmetic: 0.61 us -> 6.91 us  [the longest x8 2.61 us: per_device(): jnp.concatenate([buffers[branch].reshape(-1, half_width) for branch in ac...]
    slice x11 -> x22, local copies, waits for them, and re-layouts: 0.65 us -> 6.15 us  [per_device(): partial[branch] = kept + incoming[cursor:cursor + count].reshape(kept.shape)]
    broadcast_in_dim x4 -> x16, local copies, waits for them, and re-layouts: 3.12 us -> 6.49 us  [spread_rows(): widened = jnp.where(chosen, grouped, jnp.zeros((), picked.dtype))]
    slice x14 -> x31, local copies, waits for them, and re-layouts: 4.86 us -> 8.18 us  [the longest x25 6.79 us: per_device(): lax.index_in_dim(partial[branch], 1, places[branch], keepdims=False)]
    slice x10 -> x20, local copies, waits for them, and re-layouts: 0.31 us -> 3.5 us  [per_device(): arrived = incoming[cursor:cursor + count].reshape(buffers[branch].shape)]
    pallas_call x1 -> x2, Pallas kernels: 26.3 us -> 29.2 us  [per_device(): pl.pallas_call(attention_kernel(head_dim, score_scale, half * heads_per_h...]
  transfers between devices with their start and end apart: 8 -> 16, of which waited for: 8 -> 8; matrix products, arithmetic and copies ran while one was open for 2% -> 29% of each run, Pallas kernels for 0% -> 20%
where the time goes in v1:
time: 149 us; the launch traced here: 148 us
  waiting for transfers between devices  40.3 us (27%)
  local copies, waits for them, and re-layouts  40.1 us (27%)
  Pallas kernels  29.2 us (20%)
  starting transfers between devices  22 us (15%)
  other arithmetic  14.8 us (10%)
  between operations  1.99 us (1%)
    ppermute x16, waiting for transfers between devices, exchange(): return lax.ppermute(block, 'seq', route)  40.3 us
    pallas_call x2, Pallas kernels, per_device(): pl.pallas_call(attention_kernel(head_dim, score_scale, half * heads_per_h...  29.2 us
    ppermute x16, starting transfers between devices, exchange(): return lax.ppermute(block, 'seq', route)  22 us
    slice x25, local copies, waits for them, and re-layouts, per_device(): lax.index_in_dim(partial[branch], 1, places[branch], keepdims=False)  6.79 us
    another operation x25, local copies, waits for them, and re-layouts, per_device(): buffers[branch] = jnp.stack([buffers[branch], arrived], axis=1)  6.56 us
    broadcast_in_dim x16, local copies, waits for them, and re-layouts, spread_rows(): widened = jnp.where(chosen, grouped, jnp.zeros((), picked.dtype))  6.49 us
    slice x22, local copies, waits for them, and re-layouts, per_device(): partial[branch] = kept + incoming[cursor:cursor + count].reshape(kept.shape)  6.15 us
    another operation x22, other arithmetic, per_device(): buffers[branch] = jnp.stack([buffers[branch], arrived], axis=1)  3.83 us
  transfers between devices with their start and end apart: 16, of which 8 were waited for; matrix products, arithmetic and copies ran while one was open for 29% of the time, Pallas kernels for 20%

profile of v1, /device:TPU:0, one launch (start us, length us, event | category | flops | bytes accessed | tf_op | source)
XLA Modules:
  0.0 148.4 jit_solution(614915451672715450)
XLA Ops:
  0.7 1.3 stack.157
  2.0 1.3 stack.161
  5.2 4.1 %collective-permute-start = (bf16[80,384]{1,0:T(8,128)(2,1)S(1)}, bf16[80,384]{1,0:T(8,128)(2,1)S(1)}, u32[]{:S(2)}, u32[]{:S(2)}) collective-permute-start(bf16[80,384]{1,0:T(8,128)(2,1)S(1)} %pad_maximum_fusion.35), channel_id=1, source_target_pairs={{0,8},{1,9},{2,10},{3,11},{4,12},{5,13},{6,14},{7,15},{8,0},{9,1},... | collective-permute-start | bytes 184328 | tf_op jit(solution)/shard_map/ppermute | solution.py:24
  9.4 0.6 slice_bitcast_fusion.26
  10.0 0.7 fusion.45
  10.8 1.4 collective-permute-done
  12.3 2.7 %collective-permute-start.1 = (bf16[416,384]{1,0:T(8,128)(2,1)S(1)}, bf16[416,384]{1,0:T(8,128)(2,1)S(1)}, u32[]{:S(2)}, u32[]{:S(2)}) collective-permute-start(bf16[416,384]{1,0:T(8,128)(2,1)S(1)} %pad_maximum_fusion.18), channel_id=1, source_target_pairs={{0,4},{1,5},{2,6},{3,7},{4,0},{5,1},{6,2},{7,3},{8,12},{9,13},{10,... | collective-permute-start | bytes 958472 | tf_op jit(solution)/shard_map/ppermute | solution.py:24
  15.1 2.3 %collective-permute-start.5 = (bf16[416,384]{1,0:T(8,128)(2,1)S(1)}, bf16[416,384]{1,0:T(8,128)(2,1)S(1)}, u32[]{:S(2)}, u32[]{:S(2)}) collective-permute-start(bf16[416,384]{1,0:T(8,128)(2,1)S(1)} %pad_maximum_fusion.19), channel_id=1, source_target_pairs={{0,2},{1,3},{2,0},{3,1},{4,6},{5,7},{6,4},{7,5},{8,10},{9,11},{10,... | collective-permute-start | bytes 958472 | tf_op jit(solution)/shard_map/ppermute | solution.py:24
  17.3 5.2 %collective-permute-done.1 = bf16[416,384]{1,0:T(8,128)(2,1)S(1)} collective-permute-done((bf16[416,384]{1,0:T(8,128)(2,1)S(1)}, bf16[416,384]{1,0:T(8,128)(2,1)S(1)}, u32[]{:S(2)}, u32[]{:S(2)}) %collective-permute-start.1) | collective-permute-done | bytes 319520 | tf_op jit(solution)/shard_map/ppermute | solution.py:24
  22.9 1.6 %collective-permute-start.2 = (bf16[832,384]{1,0:T(8,128)(2,1)S(1)}, bf16[832,384]{1,0:T(8,128)(2,1)S(1)}, u32[]{:S(2)}, u32[]{:S(2)}) collective-permute-start(bf16[832,384]{1,0:T(8,128)(2,1)S(1)} %pad_maximum_fusion.10), channel_id=1, source_target_pairs={{0,2},{1,3},{2,0},{3,1},{4,6},{5,7},{6,4},{7,5},{8,10},{9,11},{10,... | collective-permute-start | bytes 1916936 | tf_op jit(solution)/shard_map/ppermute | solution.py:24
  24.8 1.8 %collective-permute-start.6 = (bf16[832,384]{1,0:T(8,128)(2,1)S(1)}, bf16[832,384]{1,0:T(8,128)(2,1)S(1)}, u32[]{:S(2)}, u32[]{:S(2)}) collective-permute-start(bf16[832,384]{1,0:T(8,128)(2,1)S(1)} %pad_maximum_fusion.11), channel_id=1, source_target_pairs={{0,4},{1,5},{2,6},{3,7},{4,0},{5,1},{6,2},{7,3},{8,12},{9,13},{10,... | collective-permute-start | bytes 1916936 | tf_op jit(solution)/shard_map/ppermute | solution.py:24
  26.6 12.0 %collective-permute-done.2 = bf16[832,384]{1,0:T(8,128)(2,1)S(1)} collective-permute-done((bf16[832,384]{1,0:T(8,128)(2,1)S(1)}, bf16[832,384]{1,0:T(8,128)(2,1)S(1)}, u32[]{:S(2)}, u32[]{:S(2)}) %collective-permute-start.2) | collective-permute-done | bytes 639008 | tf_op jit(solution)/shard_map/ppermute | solution.py:24
  39.1 1.2 pad_maximum_fusion.2
  40.3 0.8 fusion.39
  41.2 0.7 fusion.33
  42.0 1.1 fusion.43
  43.2 1.2 pad_maximum_fusion.3
  45.6 0.8 broadcast_in_dim.131
  46.4 0.7 fusion.46
  47.2 0.7 copy.76
  48.1 1.0 copy.74
  49.4 1.4 copy.72
  50.7 14.7 %shard_map.84 = (bf16[128,384]{1,0:T(8,128)(2,1)}, bf16[128,384]{1,0:T(8,128)(2,1)}, f32[2,1024,384]{2,1,0:T(8,128)}, f32[2,512,384]{2,1,0:T(8,128)}, f32[2,128,384]{2,1,0:T(8,128)}) custom-call(s32[3,12]{1,0:T(4,128)} %offsets_ref.3, bf16[128,384]{1,0:T(8,128)(2,1)} %get-tuple-element.46.query_ref, bf16[128,384]{1,0:T(8,128)(2,1)} %get-tuple-element.44.grad_ref, ...), custom_call_target="tpu_custom_call" | custom-call | tf_op jit(solution)/shard_map/pallas_call | solution.py:196
  65.4 1.5 %slice.664 = bf16[2,1,2,2,128,384]{5,4,3,2,1,0:T(8,128)(2,1)S(1)} slice(f32[2,2,2,2,128,384]{5,4,3,2,1,0:T(8,128)} %bitcast.280), slice={[0:2], [1:2], [0:2], [0:2], [0:128], [0:384]} | slice | bytes 1572864 | tf_op jit(solution)/shard_map/slice | solution.py:224
  66.9 1.2 slice.668
  68.1 1.0 slice.676
  69.1 1.2 pad_maximum_fusion.4
  70.3 0.9 slice.491
  71.3 0.7 copy.95
  72.0 1.0 slice.490
  73.1 1.0 copy.93
  74.2 1.2 slice.489
  75.6 1.3 copy.91
  76.9 14.5 %shard_map.85 = (bf16[128,384]{1,0:T(8,128)(2,1)}, bf16[128,384]{1,0:T(8,128)(2,1)}, f32[2,1024,384]{2,1,0:T(8,128)}, f32[2,512,384]{2,1,0:T(8,128)}, f32[2,128,384]{2,1,0:T(8,128)}) custom-call(s32[3,12]{1,0:T(4,128)} %offsets_ref.3, bf16[128,384]{1,0:T(8,128)(2,1)} %get-tuple-element.47.query_ref, bf16[128,384]{1,0:T(8,128)(2,1)} %get-tuple-element.45.grad_ref, ...), custom_call_target="tpu_custom_call" | custom-call | tf_op jit(solution)/shard_map/pallas_call | solution.py:196
  91.4 1.6 %slice.663 = bf16[2,1,2,2,128,384]{5,4,3,2,1,0:T(8,128)(2,1)S(1)} slice(f32[2,2,2,2,128,384]{5,4,3,2,1,0:T(8,128)} %bitcast.282), slice={[0:2], [1:2], [0:2], [0:2], [0:128], [0:384]} | slice | bytes 1572864 | tf_op jit(solution)/shard_map/slice | solution.py:224
  93.0 1.2 slice.666
  95.1 0.8 broadcast_in_dim.125
  96.1 0.8 broadcast_in_dim.141
  97.0 0.8 broadcast_in_dim.136
  97.9 0.8 pad_maximum_fusion.27
  98.6 1.4 slice.496
  100.0 0.7 copy-done.1
  101.0 1.2 slice.500
  102.6 0.9 slice.503
  103.7 1.0 collective-permute-start.9
  104.8 0.7 copy-done.2
  105.9 1.2 copy-done.8
  107.5 1.5 %collective-permute-start.13 = (bf16[832,384]{1,0:T(8,128)(2,1)S(1)}, bf16[832,384]{1,0:T(8,128)(2,1)S(1)}, u32[]{:S(2)}, u32[]{:S(2)}) collective-permute-start(bf16[832,384]{1,0:T(8,128)(2,1)S(1)} %pad_maximum_fusion.13), channel_id=1, source_target_pairs={{0,4},{1,5},{2,6},{3,7},{4,0},{5,1},{6,2},{7,3},{8,12},{9,13},{10,... | collective-permute-start | bytes 1916936 | tf_op jit(solution)/shard_map/ppermute | solution.py:24
  109.0 11.4 %collective-permute-done.9 = bf16[832,384]{1,0:T(8,128)(2,1)S(1)} collective-permute-done((bf16[832,384]{1,0:T(8,128)(2,1)S(1)}, bf16[832,384]{1,0:T(8,128)(2,1)S(1)}, u32[]{:S(2)}, u32[]{:S(2)}) %collective-permute-start.9) | collective-permute-done | bytes 639008 | tf_op jit(solution)/shard_map/ppermute | solution.py:24
  120.8 1.5 collective-permute-start.10
  122.3 2.5 %collective-permute-done.13 = bf16[832,384]{1,0:T(8,128)(2,1)S(1)} collective-permute-done((bf16[832,384]{1,0:T(8,128)(2,1)S(1)}, bf16[832,384]{1,0:T(8,128)(2,1)S(1)}, u32[]{:S(2)}, u32[]{:S(2)}) %collective-permute-start.13) | collective-permute-done | bytes 639008 | tf_op jit(solution)/shard_map/ppermute | solution.py:24
  125.2 1.0 collective-permute-start.14
  126.2 4.9 %collective-permute-done.10 = bf16[416,384]{1,0:T(8,128)(2,1)S(1)} collective-permute-done((bf16[416,384]{1,0:T(8,128)(2,1)S(1)}, bf16[416,384]{1,0:T(8,128)(2,1)S(1)}, u32[]{:S(2)}, u32[]{:S(2)}) %collective-permute-start.10) | collective-permute-done | bytes 319520 | tf_op jit(solution)/shard_map/ppermute | solution.py:24
  131.2 2.5 %collective-permute-done.14 = bf16[416,384]{1,0:T(8,128)(2,1)S(1)} collective-permute-done((bf16[416,384]{1,0:T(8,128)(2,1)S(1)}, bf16[416,384]{1,0:T(8,128)(2,1)S(1)}, u32[]{:S(2)}, u32[]{:S(2)}) %collective-permute-start.14) | collective-permute-done | bytes 319520 | tf_op jit(solution)/shard_map/ppermute | solution.py:24
  133.8 3.4 %collective-permute-start.11 = (bf16[80,384]{1,0:T(8,128)(2,1)S(1)}, bf16[80,384]{1,0:T(8,128)(2,1)S(1)}, u32[]{:S(2)}, u32[]{:S(2)}) collective-permute-start(bf16[80,384]{1,0:T(8,128)(2,1)S(1)} %pad_maximum_fusion.37), channel_id=1, source_target_pairs={{0,8},{1,9},{2,10},{3,11},{4,12},{5,13},{6,14},{7,15},{8,0},{9,1},... | collective-permute-start | bytes 184328 | tf_op jit(solution)/shard_map/ppermute | solution.py:24
  138.1 0.8 squeeze.102
  140.2 1.0 broadcast_in_dim.128
  141.2 0.7 slice.524
  142.1 1.0 broadcast_in_dim.134
  143.1 1.3 fusion.17
  144.4 0.8 slice.556
  145.7 0.7 slice.558
  147.0 0.7 pad_maximum_fusion.30
  147.7 0.7 pad_maximum_fusion.29
  (226 shorter events, 12.1 us)
Async XLA Ops:
  0.6 2.6 %copy-start.3 = (bf16[128,768]{1,0:T(8,128)(2,1)S(1)}, bf16[128,768]{1,0:T(8,128)(2,1)}, u32[]{:S(2)}) copy-start(bf16[128,768]{1,0:T(8,128)(2,1)} %param.7) | copy-start | bytes 589828
  0.6 3.3 %copy-start.22 = (s32[3,12]{1,0:T(4,128)S(1)}, s32[3,12]{1,0:T(4,128)}, u32[]{:S(2)}) copy-start(s32[3,12]{1,0:T(4,128)} %offsets_ref.3) | copy-start | bytes 436
  3.9 6.1 %copy-start.13 = (bf16[128,768]{1,0:T(8,128)(2,1)S(1)}, bf16[128,768]{1,0:T(8,128)(2,1)}, u32[]{:S(2)}) copy-start(bf16[128,768]{1,0:T(8,128)(2,1)} %param.8) | copy-start | bytes 589828
  4.4 6.3 %copy-start.4 = (bf16[128,768]{1,0:T(8,128)(2,1)S(1)}, bf16[128,768]{1,0:T(8,128)(2,1)}, u32[]{:S(2)}) copy-start(bf16[128,768]{1,0:T(8,128)(2,1)} %param.6) | copy-start | bytes 589828
  5.2 7.0 %collective-permute-start = (bf16[80,384]{1,0:T(8,128)(2,1)S(1)}, bf16[80,384]{1,0:T(8,128)(2,1)S(1)}, u32[]{:S(2)}, u32[]{:S(2)}) collective-permute-start(bf16[80,384]{1,0:T(8,128)(2,1)S(1)} %pad_maximum_fusion.35), channel_id=1, source_target_pairs={{0,8},{1,9},{2,10},{3,11},{4,12},{5,13},{6,14},{7,15},{8,0},{9,1},... | collective-permute-start | bytes 184328 | tf_op jit(solution)/shard_map/ppermute | solution.py:24
  9.3 5.6 %collective-permute-start.4 = (bf16[80,384]{1,0:T(8,128)(2,1)S(1)}, bf16[80,384]{1,0:T(8,128)(2,1)S(1)}, u32[]{:S(2)}, u32[]{:S(2)}) collective-permute-start(bf16[80,384]{1,0:T(8,128)(2,1)S(1)} %pad_maximum_fusion.36), channel_id=1, source_target_pairs={{0,8},{1,9},{2,10},{3,11},{4,12},{5,13},{6,14},{7,15},{8,0},{9,1},... | collective-permute-start | bytes 184328 | tf_op jit(solution)/shard_map/ppermute | solution.py:24
  12.3 10.3 %collective-permute-start.1 = (bf16[416,384]{1,0:T(8,128)(2,1)S(1)}, bf16[416,384]{1,0:T(8,128)(2,1)S(1)}, u32[]{:S(2)}, u32[]{:S(2)}) collective-permute-start(bf16[416,384]{1,0:T(8,128)(2,1)S(1)} %pad_maximum_fusion.18), channel_id=1, source_target_pairs={{0,4},{1,5},{2,6},{3,7},{4,0},{5,1},{6,2},{7,3},{8,12},{9,13},{10,... | collective-permute-start | bytes 958472 | tf_op jit(solution)/shard_map/ppermute | solution.py:24
  15.1 9.4 %collective-permute-start.5 = (bf16[416,384]{1,0:T(8,128)(2,1)S(1)}, bf16[416,384]{1,0:T(8,128)(2,1)S(1)}, u32[]{:S(2)}, u32[]{:S(2)}) collective-permute-start(bf16[416,384]{1,0:T(8,128)(2,1)S(1)} %pad_maximum_fusion.19), channel_id=1, source_target_pairs={{0,2},{1,3},{2,0},{3,1},{4,6},{5,7},{6,4},{7,5},{8,10},{9,11},{10,... | collective-permute-start | bytes 958472 | tf_op jit(solution)/shard_map/ppermute | solution.py:24
  22.9 15.7 %collective-permute-start.2 = (bf16[832,384]{1,0:T(8,128)(2,1)S(1)}, bf16[832,384]{1,0:T(8,128)(2,1)S(1)}, u32[]{:S(2)}, u32[]{:S(2)}) collective-permute-start(bf16[832,384]{1,0:T(8,128)(2,1)S(1)} %pad_maximum_fusion.10), channel_id=1, source_target_pairs={{0,2},{1,3},{2,0},{3,1},{4,6},{5,7},{6,4},{7,5},{8,10},{9,11},{10,... | collective-permute-start | bytes 1916936 | tf_op jit(solution)/shard_map/ppermute | solution.py:24
  24.8 15.5 %collective-permute-start.6 = (bf16[832,384]{1,0:T(8,128)(2,1)S(1)}, bf16[832,384]{1,0:T(8,128)(2,1)S(1)}, u32[]{:S(2)}, u32[]{:S(2)}) collective-permute-start(bf16[832,384]{1,0:T(8,128)(2,1)S(1)} %pad_maximum_fusion.11), channel_id=1, source_target_pairs={{0,4},{1,5},{2,6},{3,7},{4,0},{5,1},{6,2},{7,3},{8,12},{9,13},{10,... | collective-permute-start | bytes 1916936 | tf_op jit(solution)/shard_map/ppermute | solution.py:24
  40.3 6.8 %collective-permute-start.3 = (bf16[1664,384]{1,0:T(8,128)(2,1)}, bf16[1664,384]{1,0:T(8,128)(2,1)S(1)}, u32[]{:S(2)}, u32[]{:S(2)}) collective-permute-start(bf16[1664,384]{1,0:T(8,128)(2,1)} %pad_maximum_fusion.2), channel_id=1, source_target_pairs={{0,1},{1,0},{2,3},{3,2},{4,5},{5,4},{6,7},{7,6},{8,9},{9,8},{10,11... | collective-permute-start | bytes 3833864 | tf_op jit(solution)/shard_map/ppermute | solution.py:24
  43.2 3.3 %copy-start.14 = (bf16[128,768]{1,0:T(8,128)(2,1)S(1)}, bf16[128,768]{1,0:T(8,128)(2,1)}, u32[]{:S(2)}) copy-start(bf16[128,768]{1,0:T(8,128)(2,1)} %param.5) | copy-start | bytes 589828
  44.4 25.9 %collective-permute-start.7 = (bf16[1664,384]{1,0:T(8,128)(2,1)}, bf16[1664,384]{1,0:T(8,128)(2,1)}, u32[]{:S(2)}, u32[]{:S(2)}) collective-permute-start(bf16[1664,384]{1,0:T(8,128)(2,1)} %pad_maximum_fusion.3), channel_id=1, source_target_pairs={{0,1},{1,0},{2,3},{3,2},{4,5},{5,4},{6,7},{7,6},{8,9},{9,8},{10,11... | collective-permute-start | bytes 3833864 | tf_op jit(solution)/shard_map/ppermute | solution.py:24
  68.1 3.1 %copy-start.9 = (bf16[2,1,2,2,2,8,384]{6,5,0,4,3,2,1:T(8,128)(2,1)S(1)}, bf16[2,1,2,2,2,8,384]{6,5,0,4,3,2,1:T(8,128)(2,1)}, u32[]{:S(2)}) copy-start(bf16[2,1,2,2,2,8,384]{6,5,0,4,3,2,1:T(8,128)(2,1)} %get-tuple-element.58) | copy-start | bytes 294916
  69.1 3.9 %copy-start.5 = (bf16[2,1,2,2,2,32,384]{6,5,0,4,3,2,1:T(8,128)(2,1)S(1)}, bf16[2,1,2,2,2,32,384]{6,5,0,4,3,2,1:T(8,128)(2,1)}, u32[]{:S(2)}) copy-start(bf16[2,1,2,2,2,32,384]{6,5,0,4,3,2,1:T(8,128)(2,1)} %get-tuple-element.34) | copy-start | bytes 1179652
  70.3 28.3 %collective-permute-start.8 = (bf16[1664,384]{1,0:T(8,128)(2,1)}, bf16[1664,384]{1,0:T(8,128)(2,1)}, u32[]{:S(2)}, u32[]{:S(2)}) collective-permute-start(bf16[1664,384]{1,0:T(8,128)(2,1)} %pad_maximum_fusion.4), channel_id=1, source_target_pairs={{0,1},{1,0},{2,3},{3,2},{4,5},{5,4},{6,7},{7,6},{8,9},{9,8},{10,11... | collective-permute-start | bytes 3833864 | tf_op jit(solution)/shard_map/ppermute | solution.py:24
  73.1 2.2 %copy-start = (bf16[2,1,2,2,128,384]{5,4,0,3,2,1:T(8,128)(2,1)S(1)}, bf16[2,1,2,2,128,384]{5,4,0,3,2,1:T(8,128)(2,1)}, u32[]{:S(2)}) copy-start(bf16[2,1,2,2,128,384]{5,4,0,3,2,1:T(8,128)(2,1)} %get-tuple-element.26) | copy-start | bytes 2359300
  91.4 2.8 %copy-start.12 = (f32[2,128,384]{2,1,0:T(8,128)S(1)}, f32[2,128,384]{2,1,0:T(8,128)}, u32[]{:S(2)}) copy-start(f32[2,128,384]{2,1,0:T(8,128)} %get-tuple-element.23) | copy-start | bytes 1179652
  94.2 0.8 copy-start.24
  94.2 0.8 copy-start.25
  94.2 1.8 %copy-start.23 = (pred[16,6]{1,0:T(8,128)(4,1)S(1)}, pred[16,6]{1,0:T(8,128)(4,1)}, u32[]{:S(2)}) copy-start(pred[16,6]{1,0:T(8,128)(4,1)} %get-tuple-element.82) | copy-start | bytes 292
  94.2 3.6 %copy-start.18 = (bf16[128,384]{1,0:T(8,128)(2,1)S(1)}, bf16[128,384]{1,0:T(8,128)(2,1)}, u32[]{:S(2)}) copy-start(bf16[128,384]{1,0:T(8,128)(2,1)} %get-tuple-element.14) | copy-start | bytes 294916
  94.3 3.6 %copy-start.19 = (bf16[128,384]{1,0:T(8,128)(2,1)S(1)}, bf16[128,384]{1,0:T(8,128)(2,1)}, u32[]{:S(2)}) copy-start(bf16[128,384]{1,0:T(8,128)(2,1)} %get-tuple-element.16) | copy-start | bytes 294916
  94.3 3.6 %copy-start.20 = (bf16[128,384]{1,0:T(8,128)(2,1)S(1)}, bf16[128,384]{1,0:T(8,128)(2,1)}, u32[]{:S(2)}) copy-start(bf16[128,384]{1,0:T(8,128)(2,1)} %get-tuple-element.15) | copy-start | bytes 294916
  94.3 3.6 %copy-start.21 = (bf16[128,384]{1,0:T(8,128)(2,1)S(1)}, bf16[128,384]{1,0:T(8,128)(2,1)}, u32[]{:S(2)}) copy-start(bf16[128,384]{1,0:T(8,128)(2,1)} %get-tuple-element.17) | copy-start | bytes 294916
  94.4 10.3 %collective-permute-start.12 = (bf16[1664,384]{1,0:T(8,128)(2,1)S(1)}, bf16[1664,384]{1,0:T(8,128)(2,1)S(1)}, u32[]{:S(2)}, u32[]{:S(2)}) collective-permute-start(bf16[1664,384]{1,0:T(8,128)(2,1)S(1)} %pad_maximum_fusion.5), channel_id=1, source_target_pairs={{0,1},{1,0},{2,3},{3,2},{4,5},{5,4},{6,7},{7,6},{8,9},{9,8},{10,11... | collective-permute-start | bytes 3833864 | tf_op jit(solution)/shard_map/ppermute | solution.py:24
  98.6 2.1 %copy-start.1 = (f32[2,1024,384]{2,1,0:T(8,128)S(1)}, f32[2,1024,384]{2,1,0:T(8,128)}, u32[]{:S(2)}) copy-start(f32[2,1024,384]{2,1,0:T(8,128)} %get-tuple-element.18) | copy-start | bytes 9437188
  100.9 1.5 %copy-start.7 = (f32[2,512,384]{2,1,0:T(8,128)S(1)}, f32[2,512,384]{2,1,0:T(8,128)}, u32[]{:S(2)}) copy-start(f32[2,512,384]{2,1,0:T(8,128)} %get-tuple-element.19) | copy-start | bytes 4718596
  102.5 1.1 copy-start.11
  103.7 1.9 %copy-start.2 = (f32[2,1024,384]{2,1,0:T(8,128)S(1)}, f32[2,1024,384]{2,1,0:T(8,128)}, u32[]{:S(2)}) copy-start(f32[2,1024,384]{2,1,0:T(8,128)} %get-tuple-element.21) | copy-start | bytes 9437188
  103.7 16.7 %collective-permute-start.9 = (bf16[832,384]{1,0:T(8,128)(2,1)S(1)}, bf16[832,384]{1,0:T(8,128)(2,1)S(1)}, u32[]{:S(2)}, u32[]{:S(2)}) collective-permute-start(bf16[832,384]{1,0:T(8,128)(2,1)S(1)} %pad_maximum_fusion.12), channel_id=1, source_target_pairs={{0,2},{1,3},{2,0},{3,1},{4,6},{5,7},{6,4},{7,5},{8,10},{9,11},{10,... | collective-permute-start | bytes 1916936 | tf_op jit(solution)/shard_map/ppermute | solution.py:24
  105.7 1.4 copy-start.8
  107.5 17.3 %collective-permute-start.13 = (bf16[832,384]{1,0:T(8,128)(2,1)S(1)}, bf16[832,384]{1,0:T(8,128)(2,1)S(1)}, u32[]{:S(2)}, u32[]{:S(2)}) collective-permute-start(bf16[832,384]{1,0:T(8,128)(2,1)S(1)} %pad_maximum_fusion.13), channel_id=1, source_target_pairs={{0,4},{1,5},{2,6},{3,7},{4,0},{5,1},{6,2},{7,3},{8,12},{9,13},{10,... | collective-permute-start | bytes 1916936 | tf_op jit(solution)/shard_map/ppermute | solution.py:24
  120.8 10.2 %collective-permute-start.10 = (bf16[416,384]{1,0:T(8,128)(2,1)S(1)}, bf16[416,384]{1,0:T(8,128)(2,1)S(1)}, u32[]{:S(2)}, u32[]{:S(2)}) collective-permute-start(bf16[416,384]{1,0:T(8,128)(2,1)S(1)} %pad_maximum_fusion.20), channel_id=1, source_target_pairs={{0,4},{1,5},{2,6},{3,7},{4,0},{5,1},{6,2},{7,3},{8,12},{9,13},{10,... | collective-permute-start | bytes 958472 | tf_op jit(solution)/shard_map/ppermute | solution.py:24
  125.2 8.5 %collective-permute-start.14 = (bf16[416,384]{1,0:T(8,128)(2,1)S(1)}, bf16[416,384]{1,0:T(8,128)(2,1)S(1)}, u32[]{:S(2)}, u32[]{:S(2)}) collective-permute-start(bf16[416,384]{1,0:T(8,128)(2,1)S(1)} %pad_maximum_fusion.21), channel_id=1, source_target_pairs={{0,2},{1,3},{2,0},{3,1},{4,6},{5,7},{6,4},{7,5},{8,10},{9,11},{10,... | collective-permute-start | bytes 958472 | tf_op jit(solution)/shard_map/ppermute | solution.py:24
  133.8 5.6 %collective-permute-start.11 = (bf16[80,384]{1,0:T(8,128)(2,1)S(1)}, bf16[80,384]{1,0:T(8,128)(2,1)S(1)}, u32[]{:S(2)}, u32[]{:S(2)}) collective-permute-start(bf16[80,384]{1,0:T(8,128)(2,1)S(1)} %pad_maximum_fusion.37), channel_id=1, source_target_pairs={{0,8},{1,9},{2,10},{3,11},{4,12},{5,13},{6,14},{7,15},{8,0},{9,1},... | collective-permute-start | bytes 184328 | tf_op jit(solution)/shard_map/ppermute | solution.py:24
  138.1 6.3 %collective-permute-start.15 = (bf16[80,384]{1,0:T(8,128)(2,1)}, bf16[80,384]{1,0:T(8,128)(2,1)}, u32[]{:S(2)}, u32[]{:S(2)}) collective-permute-start(bf16[80,384]{1,0:T(8,128)(2,1)} %pad_maximum_fusion.38), channel_id=1, source_target_pairs={{0,8},{1,9},{2,10},{3,11},{4,12},{5,13},{6,14},{7,15},{8,0},{9,1},... | collective-permute-start | bytes 184328 | tf_op jit(solution)/shard_map/ppermute | solution.py:24
  139.4 0.6 copy-start.10
  142.0 1.1 copy-start.15
  143.1 2.2 %copy-start.6 = (f32[2,32,6,64]{3,2,1,0:T(8,128)S(1)}, f32[2,32,6,64]{3,2,1,0:T(8,128)}, u32[]{:S(2)}) copy-start(f32[2,32,6,64]{3,2,1,0:T(8,128)} %squeeze.102) | copy-start | bytes 294916
  145.7 1.1 copy-start.16
  145.7 1.1 copy-start.17

commit v2 on v1

--- a/solution.py
+++ b/solution.py
@@ -52,9 +52,9 @@
 
 def attention_kernel(head_dim, score_scale, head_base):
     def kernel(offsets_ref, query_ref, grad_ref, *refs):
-        kv_refs = refs[:3]
-        out_ref, qgrad_ref = refs[3:5]
-        term_refs = refs[5:]
+        kv_refs = refs[:6]
+        out_ref, qgrad_ref = refs[6:8]
+        term_refs = refs[8:]
         pair = pl.program_id(0)
         rows = query_ref.shape[0]
         heads_per_block = query_ref.shape[1] // head_dim
@@ -67,10 +67,11 @@
             values = [kv_ref[1, :, cols] for kv_ref in kv_refs]
             members = []
             scores = []
-            for branch in range(3):
+            for piece in range(6):
+                branch = piece // 2
                 block = (
                     lax.dot_general(
-                        query, keys[branch], (((1,), (1,)), ((), ())),
+                        query, keys[piece], (((1,), (1,)), ((), ())),
                         preferred_element_type=jnp.float32,
                     )
                     * score_scale
@@ -84,38 +85,38 @@
                 members.append(member)
                 scores.append(block)
             peak = jnp.max(scores[0], axis=1, keepdims=True)
-            for branch in range(1, 3):
-                peak = jnp.maximum(peak, jnp.max(scores[branch], axis=1, keepdims=True))
+            for piece in range(1, 6):
+                peak = jnp.maximum(peak, jnp.max(scores[piece], axis=1, keepdims=True))
             expos = []
-            for branch in range(3):
-                block = jnp.exp(scores[branch] - peak)
-                if members[branch] is not None:
-                    block = jnp.where(members[branch], block, 0.0)
+            for piece in range(6):
+                block = jnp.exp(scores[piece] - peak)
+                if members[piece] is not None:
+                    block = jnp.where(members[piece], block, 0.0)
                 expos.append(block)
             total = jnp.sum(expos[0], axis=1, keepdims=True)
-            for branch in range(1, 3):
-                total = total + jnp.sum(expos[branch], axis=1, keepdims=True)
+            for piece in range(1, 6):
+                total = total + jnp.sum(expos[piece], axis=1, keepdims=True)
             probs = [block / total for block in expos]
             weights = [block.astype(jnp.bfloat16) for block in probs]
             mixed = jnp.dot(weights[0], values[0], preferred_element_type=jnp.float32)
-            for branch in range(1, 3):
+            for piece in range(1, 6):
                 mixed = mixed + jnp.dot(
-                    weights[branch], values[branch], preferred_element_type=jnp.float32
+                    weights[piece], values[piece], preferred_element_type=jnp.float32
                 )
             out_ref[:, cols] = mixed.astype(out_ref.dtype)
             balance = jnp.sum(grad.astype(jnp.float32) * mixed, axis=1, keepdims=True)
             query_grad = None
-            for branch in range(3):
+            for piece in range(6):
                 flow = lax.dot_general(
-                    grad, values[branch], (((1,), (1,)), ((), ())),
+                    grad, values[piece], (((1,), (1,)), ((), ())),
                     preferred_element_type=jnp.float32,
                 )
-                score_grad = probs[branch] * (flow - balance)
-                piece = jnp.dot(
-                    score_grad.astype(jnp.bfloat16), keys[branch],
+                score_grad = probs[piece] * (flow - balance)
+                part = jnp.dot(
+                    score_grad.astype(jnp.bfloat16), keys[piece],
                     preferred_element_type=jnp.float32,
                 )
-                query_grad = piece if query_grad is None else query_grad + piece
+                query_grad = part if query_grad is None else query_grad + part
                 key_terms = (
                     jnp.dot(
                         jnp.transpose(score_grad).astype(jnp.bfloat16),
@@ -125,12 +126,12 @@
                     * score_scale
                 )
                 value_terms = jnp.dot(
-                    jnp.transpose(probs[branch]).astype(jnp.bfloat16),
+                    jnp.transpose(probs[piece]).astype(jnp.bfloat16),
                     grad,
                     preferred_element_type=jnp.float32,
                 )
-                term_refs[branch][0, :, cols] = key_terms
-                term_refs[branch][1, :, cols] = value_terms
+                term_refs[piece][0, :, cols] = key_terms
+                term_refs[piece][1, :, cols] = value_terms
             qgrad_ref[:, cols] = (query_grad * score_scale).astype(qgrad_ref.dtype)
 
     return kernel
@@ -167,7 +168,8 @@
             cols = slice(half * half_width, (half + 1) * half_width)
             buffers = [block[:, :, cols] for block in picked]
             axis_bits = [[] for _ in range(3)]
-            for bit in gather_order(top_bits, half == 1):
+            order = gather_order(top_bits, half == 1)
+            for bit in order[:-1]:
                 active = [branch for branch in range(3) if branch_bits[branch] > bit]
                 outgoing = jnp.concatenate(
                     [buffers[branch].reshape(-1, half_width) for branch in active]
@@ -180,13 +182,21 @@
                     cursor += count
                     buffers[branch] = jnp.stack([buffers[branch], arrived], axis=1)
                     axis_bits[branch].insert(0, bit)
-            gathered_halves.append([buffers[branch].reshape(2, -1, half_width) for branch in range(3)])
+            last = order[-1]
+            mine = [buffers[branch].reshape(2, -1, half_width) for branch in range(3)]
+            arrived = exchange(tuple(mine), last)
+            pieces = []
+            for branch in range(3):
+                pieces += [mine[branch], arrived[branch]]
+            gathered_halves.append(pieces)
             layouts.append(axis_bits)
 
         results = []
         for half in range(halves):
             gathered = gathered_halves[half]
             cols = slice(half * half_width, (half + 1) * half_width)
+            order = gather_order(top_bits, half == 1)
+            last = order[-1]
             pairs = half_width // block_width
             row_block = pl.BlockSpec((local_rows, block_width), lambda p, offs: (0, p))
             kv_blocks = [
@@ -212,11 +222,14 @@
             terms = outs[2:]
 
             axis_bits = [list(bits) for bits in layouts[half]]
+            returned = exchange(tuple(terms[2 * branch + 1] for branch in range(3)), last)
             partial = [
-                terms[branch].reshape((2,) + (2,) * branch_bits[branch] + (-1, half_width))
+                (terms[2 * branch] + returned[branch]).reshape(
+                    (2,) + (2,) * len(axis_bits[branch]) + (-1, half_width)
+                )
                 for branch in range(3)
             ]
-            for bit in reversed(gather_order(top_bits, half == 1)):
+            for bit in reversed(order[:-1]):
                 active = [branch for branch in range(3) if branch_bits[branch] > bit]
                 places = {branch: 1 + axis_bits[branch].index(bit) for branch in active}
                 outgoing = jnp.concatenate(

time: 149 us -> 153 us (1.027)
  local copies, waits for them, and re-layouts: 40.1 us -> 24.8 us
  Pallas kernels: 29.2 us -> 36.8 us
  waiting for transfers between devices: 40.3 us -> 45 us
  other arithmetic: 14.8 us -> 18.5 us
  starting transfers between devices: 22 us -> 24.8 us
    add x0 -> x6, other arithmetic: none -> 7.76 us  [per_device(): terms[2 * branch] + returned[branch]]
    pallas_call x2, Pallas kernels: 29.2 us -> 36.8 us  [per_device(): pl.pallas_call(attention_kernel(head_dim, score_scale, half * heads_per_h...]
    slice x25 -> x14, local copies, waits for them, and re-layouts: 6.79 us -> 0.27 us  [per_device(): lax.index_in_dim(partial[branch], 1, places[branch], keepdims=False)]
    another operation x25 -> x19, local copies, waits for them, and re-layouts: 6.56 us -> 1.36 us  [per_device(): buffers[branch] = jnp.stack([buffers[branch], arrived], axis=1)]
    ppermute x16 -> x24, waiting for transfers between devices: 40.3 us -> 45 us  [exchange(): return lax.ppermute(block, 'seq', route)]
    slice x22 -> x16, local copies, waits for them, and re-layouts: 6.15 us -> 2.52 us  [per_device(): partial[branch] = kept + incoming[cursor:cursor + count].reshape(kept.shape)]
    ppermute x16 -> x24, starting transfers between devices: 22 us -> 24.8 us  [exchange(): return lax.ppermute(block, 'seq', route)]
    concatenate x8 -> x6, other arithmetic: 2.61 us -> 0.22 us  [per_device(): jnp.concatenate([buffers[branch].reshape(-1, half_width) for branch in ac...]
  transfers between devices with their start and end apart: 16 -> 24, of which waited for: 8 -> 11; matrix products, arithmetic and copies ran while one was open for 29% -> 19% of each run, Pallas kernels for 20% -> 24%
where the time goes in v2:
time: 153 us; the launch traced here: 152 us
  waiting for transfers between devices  45 us (29%)
  Pallas kernels  36.8 us (24%)
  local copies, waits for them, and re-layouts  24.8 us (16%)
  starting transfers between devices  24.8 us (16%)
  other arithmetic  18.5 us (12%)
  between operations  1.82 us (1%)
    ppermute x24, waiting for transfers between devices, exchange(): return lax.ppermute(block, 'seq', route)  45 us
    pallas_call x2, Pallas kernels, per_device(): pl.pallas_call(attention_kernel(head_dim, score_scale, half * heads_per_h...  36.8 us
    ppermute x24, starting transfers between devices, exchange(): return lax.ppermute(block, 'seq', route)  24.8 us
    add x6, other arithmetic, per_device(): terms[2 * branch] + returned[branch]  7.76 us
    broadcast_in_dim x16, local copies, waits for them, and re-layouts, spread_rows(): widened = jnp.where(chosen, grouped, jnp.zeros((), picked.dtype))  6.49 us
    unnamed x56, local copies, waits for them, and re-layouts  5.72 us
    another operation x4, local copies, waits for them, and re-layouts, per_device(): kv_rows = jnp.stack([key_rows, value_rows])  3.2 us
    concatenate x3, other arithmetic, per_device(): jnp.concatenate([result[index] for result in results], axis=1)  3.2 us
  transfers between devices with their start and end apart: 24, of which 11 were waited for; matrix products, arithmetic and copies ran while one was open for 19% of the time, Pallas kernels for 24%

profile of v2, /device:TPU:0, one launch (start us, length us, event | category | flops | bytes accessed | tf_op | source)
XLA Modules:
  0.0 151.6 jit_solution(14584338962960749065)
XLA Ops:
  0.7 1.3 stack.121
  2.0 1.3 stack.125
  5.2 4.1 %collective-permute-start = (bf16[80,384]{1,0:T(8,128)(2,1)S(1)}, bf16[80,384]{1,0:T(8,128)(2,1)S(1)}, u32[]{:S(2)}, u32[]{:S(2)}) collective-permute-start(bf16[80,384]{1,0:T(8,128)(2,1)S(1)} %pad_maximum_fusion.25), channel_id=1, source_target_pairs={{0,8},{1,9},{2,10},{3,11},{4,12},{5,13},{6,14},{7,15},{8,0},{9,1},... | collective-permute-start | bytes 184328 | tf_op jit(solution)/shard_map/ppermute | solution.py:24
  9.4 2.7 %collective-permute-done = bf16[80,384]{1,0:T(8,128)(2,1)S(1)} collective-permute-done((bf16[80,384]{1,0:T(8,128)(2,1)S(1)}, bf16[80,384]{1,0:T(8,128)(2,1)S(1)}, u32[]{:S(2)}, u32[]{:S(2)}) %collective-permute-start) | collective-permute-done | bytes 61472 | tf_op jit(solution)/shard_map/ppermute | solution.py:24
  12.3 2.7 %collective-permute-start.1 = (bf16[416,384]{1,0:T(8,128)(2,1)S(1)}, bf16[416,384]{1,0:T(8,128)(2,1)S(1)}, u32[]{:S(2)}, u32[]{:S(2)}) collective-permute-start(bf16[416,384]{1,0:T(8,128)(2,1)S(1)} %pad_maximum_fusion.10), channel_id=1, source_target_pairs={{0,4},{1,5},{2,6},{3,7},{4,0},{5,1},{6,2},{7,3},{8,12},{9,13},{10,... | collective-permute-start | bytes 958472 | tf_op jit(solution)/shard_map/ppermute | solution.py:24
  15.1 2.3 %collective-permute-start.7 = (bf16[416,384]{1,0:T(8,128)(2,1)S(1)}, bf16[416,384]{1,0:T(8,128)(2,1)S(1)}, u32[]{:S(2)}, u32[]{:S(2)}) collective-permute-start(bf16[416,384]{1,0:T(8,128)(2,1)S(1)} %pad_maximum_fusion.11), channel_id=1, source_target_pairs={{0,2},{1,3},{2,0},{3,1},{4,6},{5,7},{6,4},{7,5},{8,10},{9,11},{10,... | collective-permute-start | bytes 958472 | tf_op jit(solution)/shard_map/ppermute | solution.py:24
  17.3 5.2 %collective-permute-done.1 = bf16[416,384]{1,0:T(8,128)(2,1)S(1)} collective-permute-done((bf16[416,384]{1,0:T(8,128)(2,1)S(1)}, bf16[416,384]{1,0:T(8,128)(2,1)S(1)}, u32[]{:S(2)}, u32[]{:S(2)}) %collective-permute-start.1) | collective-permute-done | bytes 319520 | tf_op jit(solution)/shard_map/ppermute | solution.py:24
  22.9 1.6 %collective-permute-start.2 = (bf16[832,384]{1,0:T(8,128)(2,1)S(1)}, bf16[832,384]{1,0:T(8,128)(2,1)S(1)}, u32[]{:S(2)}, u32[]{:S(2)}) collective-permute-start(bf16[832,384]{1,0:T(8,128)(2,1)S(1)} %pad_maximum_fusion.2), channel_id=1, source_target_pairs={{0,2},{1,3},{2,0},{3,1},{4,6},{5,7},{6,4},{7,5},{8,10},{9,11},{10,... | collective-permute-start | bytes 1916936 | tf_op jit(solution)/shard_map/ppermute | solution.py:24
  24.5 0.7 fusion.29
  25.2 0.6 fusion.25
  26.1 1.8 %collective-permute-start.8 = (bf16[832,384]{1,0:T(8,128)(2,1)S(1)}, bf16[832,384]{1,0:T(8,128)(2,1)S(1)}, u32[]{:S(2)}, u32[]{:S(2)}) collective-permute-start(bf16[832,384]{1,0:T(8,128)(2,1)S(1)} %pad_maximum_fusion.3), channel_id=1, source_target_pairs={{0,4},{1,5},{2,6},{3,7},{4,0},{5,1},{6,2},{7,3},{8,12},{9,13},{10,... | collective-permute-start | bytes 1916936 | tf_op jit(solution)/shard_map/ppermute | solution.py:24
  27.9 0.7 fusion.33
  28.6 10.0 %collective-permute-done.2 = bf16[832,384]{1,0:T(8,128)(2,1)S(1)} collective-permute-done((bf16[832,384]{1,0:T(8,128)(2,1)S(1)}, bf16[832,384]{1,0:T(8,128)(2,1)S(1)}, u32[]{:S(2)}, u32[]{:S(2)}) %collective-permute-start.2) | collective-permute-done | bytes 639008 | tf_op jit(solution)/shard_map/ppermute | solution.py:24
  39.0 0.5 collective-permute-start.5
  39.8 1.4 collective-permute-done.8
  41.4 1.0 copy.61
  42.4 0.7 fusion.34
  43.2 0.9 copy-done.11
  44.2 18.5 %shard_map.84 = (bf16[128,384]{1,0:T(8,128)(2,1)}, bf16[128,384]{1,0:T(8,128)(2,1)}, f32[2,512,384]{2,1,0:T(8,128)}, f32[2,512,384]{2,1,0:T(8,128)}, f32[2,256,3...) custom-call(s32[3,12]{1,0:T(4,128)} %offsets_ref.3, ...), custom_call_target="tpu_custom_call" | custom-call | tf_op jit(solution)/shard_map/pallas_call | solution.py:206
  62.7 0.5 collective-permute-start.12
  63.3 0.9 slice.382
  64.2 1.0 pad_maximum_fusion.9
  65.3 0.7 copy-done.6
  66.1 0.5 collective-permute-start.11
  66.6 1.2 collective-permute-done.11.refs_5_
  67.9 0.7 copy-done.16
  68.6 18.3 %shard_map.85 = (bf16[128,384]{1,0:T(8,128)(2,1)}, bf16[128,384]{1,0:T(8,128)(2,1)}, f32[2,512,384]{2,1,0:T(8,128)}, f32[2,512,384]{2,1,0:T(8,128)}, f32[2,256,3...) custom-call(s32[3,12]{1,0:T(4,128)} %offsets_ref.3, ...), custom_call_target="tpu_custom_call" | custom-call | tf_op jit(solution)/shard_map/pallas_call | solution.py:206
  88.0 0.9 slice_bitcast_fusion.20
  88.9 4.0 %collective-permute-done.14 = f32[2,64,384]{2,1,0:T(8,128)S(1)} collective-permute-done((f32[2,64,384]{2,1,0:T(8,128)}, f32[2,64,384]{2,1,0:T(8,128)S(1)}, u32[]{:S(2)}, u32[]{:S(2)}) %collective-permute-start.14) | collective-permute-done | bytes 196640 | tf_op jit(solution)/shard_map/ppermute | solution.py:24
  92.9 1.0 add.96
  93.9 1.3 add.95
  95.3 0.8 copy-done.1
  96.1 1.6 %add.94 = f32[2,512,384]{2,1,0:T(8,128)S(1)} add(f32[2,512,384]{2,1,0:T(8,128)S(1)} %copy-done.8, f32[2,512,384]{2,1,0:T(8,128)} %collective-permute-done.12) | non-fusion elementwise | flops 393216 | bytes 4718592 | tf_op jit(solution)/shard_map/add | solution.py:227
  97.8 0.9 pad_maximum_fusion.4
  98.6 1.2 collective-permute-start.15
  100.0 0.8 broadcast_in_dim.131
  101.0 0.8 broadcast_in_dim.125
  101.9 0.8 broadcast_in_dim.141
  102.9 0.8 broadcast_in_dim.136
  103.7 1.8 %pad_maximum_fusion.17 = (bf16[128,768]{1,0:T(8,128)(2,1)}, bf16[128,768]{1,0:T(8,128)(2,1)}) fusion(bf16[128,384]{1,0:T(8,128)(2,1)} %get-tuple-element.21, bf16[128,384]{1,0:T(8,128)(2,1)} %get-tuple-element.20, bf16[128,384]{1,0:T(8,128)(2,1)} %get-tuple-element.23, bf16[128,384]{1,0:T(8,128)(2,1)} %get-tuple-element.22), kind=kLoop, calls=%fused_computation.54 | loop fusion | flops 786432 | bytes 786432 | tf_op jit(solution)/shard_map/concatenate | solution.py:259
  105.5 0.9 add.109
  106.5 1.3 add.108
  108.2 1.6 %add.107 = f32[2,512,384]{2,1,0:T(8,128)S(1)} add(f32[2,512,384]{2,1,0:T(8,128)S(1)} %copy-done.7, f32[2,512,384]{2,1,0:T(8,128)} %collective-permute-done.18) | non-fusion elementwise | flops 393216 | bytes 4718592 | tf_op jit(solution)/shard_map/add | solution.py:227
  109.9 1.8 %collective-permute-start.21 = (bf16[832,384]{1,0:T(8,128)(2,1)S(1)}, bf16[832,384]{1,0:T(8,128)(2,1)S(1)}, u32[]{:S(2)}, u32[]{:S(2)}) collective-permute-start(bf16[832,384]{1,0:T(8,128)(2,1)S(1)} %pad_maximum_fusion.5), channel_id=1, source_target_pairs={{0,4},{1,5},{2,6},{3,7},{4,0},{5,1},{6,2},{7,3},{8,12},{9,13},{10,... | collective-permute-start | bytes 1916936 | tf_op jit(solution)/shard_map/ppermute | solution.py:24
  111.7 3.8 %collective-permute-done.15 = bf16[832,384]{1,0:T(8,128)(2,1)S(1)} collective-permute-done((bf16[832,384]{1,0:T(8,128)(2,1)}, bf16[832,384]{1,0:T(8,128)(2,1)S(1)}, u32[]{:S(2)}, u32[]{:S(2)}) %collective-permute-start.15) | collective-permute-done | bytes 639008 | tf_op jit(solution)/shard_map/ppermute | solution.py:24
  115.7 1.0 copy-done.2
  116.9 1.8 %collective-permute-start.16 = (bf16[416,384]{1,0:T(8,128)(2,1)S(1)}, bf16[416,384]{1,0:T(8,128)(2,1)S(1)}, u32[]{:S(2)}, u32[]{:S(2)}) collective-permute-start(bf16[416,384]{1,0:T(8,128)(2,1)S(1)} %pad_maximum_fusion.12), channel_id=1, source_target_pairs={{0,4},{1,5},{2,6},{3,7},{4,0},{5,1},{6,2},{7,3},{8,12},{9,13},{10,... | collective-permute-start | bytes 958472 | tf_op jit(solution)/shard_map/ppermute | solution.py:24
  118.7 8.4 %collective-permute-done.21 = bf16[832,384]{1,0:T(8,128)(2,1)S(1)} collective-permute-done((bf16[832,384]{1,0:T(8,128)(2,1)S(1)}, bf16[832,384]{1,0:T(8,128)(2,1)S(1)}, u32[]{:S(2)}, u32[]{:S(2)}) %collective-permute-start.21) | collective-permute-done | bytes 639008 | tf_op jit(solution)/shard_map/ppermute | solution.py:24
  127.5 0.9 collective-permute-start.22
  128.5 5.1 %collective-permute-done.16 = bf16[416,384]{1,0:T(8,128)(2,1)S(1)} collective-permute-done((bf16[416,384]{1,0:T(8,128)(2,1)S(1)}, bf16[416,384]{1,0:T(8,128)(2,1)S(1)}, u32[]{:S(2)}, u32[]{:S(2)}) %collective-permute-start.16) | collective-permute-done | bytes 319520 | tf_op jit(solution)/shard_map/ppermute | solution.py:24
  133.7 2.6 %collective-permute-done.22 = bf16[416,384]{1,0:T(8,128)(2,1)S(1)} collective-permute-done((bf16[416,384]{1,0:T(8,128)(2,1)S(1)}, bf16[416,384]{1,0:T(8,128)(2,1)S(1)}, u32[]{:S(2)}, u32[]{:S(2)}) %collective-permute-start.22) | collective-permute-done | bytes 319520 | tf_op jit(solution)/shard_map/ppermute | solution.py:24
  136.4 3.6 %collective-permute-start.17 = (bf16[80,384]{1,0:T(8,128)(2,1)S(1)}, bf16[80,384]{1,0:T(8,128)(2,1)S(1)}, u32[]{:S(2)}, u32[]{:S(2)}) collective-permute-start(bf16[80,384]{1,0:T(8,128)(2,1)S(1)} %pad_maximum_fusion.27), channel_id=1, source_target_pairs={{0,8},{1,9},{2,10},{3,11},{4,12},{5,13},{6,14},{7,15},{8,0},{9,1},... | collective-permute-start | bytes 184328 | tf_op jit(solution)/shard_map/ppermute | solution.py:24
  140.2 0.6 pad_maximum_fusion.28
  140.8 0.8 squeeze.78
  142.3 0.5 copy-done.17
  143.0 1.0 broadcast_in_dim.128
  143.9 0.7 slice.407
  144.8 1.0 broadcast_in_dim.134
  145.9 1.3 fusion.11
  147.2 0.8 slice.430
  148.4 0.7 slice.432
  149.6 0.5 copy-done.22
  150.2 0.7 pad_maximum_fusion.20
  150.9 0.7 pad_maximum_fusion.19
  (208 shorter events, 8.8 us)
Async XLA Ops:
  0.6 2.6 %copy-start.3 = (bf16[128,768]{1,0:T(8,128)(2,1)S(1)}, bf16[128,768]{1,0:T(8,128)(2,1)}, u32[]{:S(2)}) copy-start(bf16[128,768]{1,0:T(8,128)(2,1)} %param.7) | copy-start | bytes 589828
  0.6 3.3 %copy-start.27 = (s32[3,12]{1,0:T(4,128)S(1)}, s32[3,12]{1,0:T(4,128)}, u32[]{:S(2)}) copy-start(s32[3,12]{1,0:T(4,128)} %offsets_ref.3) | copy-start | bytes 436
  4.4 5.0 %copy-start.4 = (bf16[128,768]{1,0:T(8,128)(2,1)S(1)}, bf16[128,768]{1,0:T(8,128)(2,1)}, u32[]{:S(2)}) copy-start(bf16[128,768]{1,0:T(8,128)(2,1)} %param.6) | copy-start | bytes 589828
  5.2 7.0 %collective-permute-start = (bf16[80,384]{1,0:T(8,128)(2,1)S(1)}, bf16[80,384]{1,0:T(8,128)(2,1)S(1)}, u32[]{:S(2)}, u32[]{:S(2)}) collective-permute-start(bf16[80,384]{1,0:T(8,128)(2,1)S(1)} %pad_maximum_fusion.25), channel_id=1, source_target_pairs={{0,8},{1,9},{2,10},{3,11},{4,12},{5,13},{6,14},{7,15},{8,0},{9,1},... | collective-permute-start | bytes 184328 | tf_op jit(solution)/shard_map/ppermute | solution.py:24
  9.3 5.6 %collective-permute-start.6 = (bf16[80,384]{1,0:T(8,128)(2,1)S(1)}, bf16[80,384]{1,0:T(8,128)(2,1)S(1)}, u32[]{:S(2)}, u32[]{:S(2)}) collective-permute-start(bf16[80,384]{1,0:T(8,128)(2,1)S(1)} %pad_maximum_fusion.26), channel_id=1, source_target_pairs={{0,8},{1,9},{2,10},{3,11},{4,12},{5,13},{6,14},{7,15},{8,0},{9,1},... | collective-permute-start | bytes 184328 | tf_op jit(solution)/shard_map/ppermute | solution.py:24
  12.3 10.3 %collective-permute-start.1 = (bf16[416,384]{1,0:T(8,128)(2,1)S(1)}, bf16[416,384]{1,0:T(8,128)(2,1)S(1)}, u32[]{:S(2)}, u32[]{:S(2)}) collective-permute-start(bf16[416,384]{1,0:T(8,128)(2,1)S(1)} %pad_maximum_fusion.10), channel_id=1, source_target_pairs={{0,4},{1,5},{2,6},{3,7},{4,0},{5,1},{6,2},{7,3},{8,12},{9,13},{10,... | collective-permute-start | bytes 958472 | tf_op jit(solution)/shard_map/ppermute | solution.py:24
  15.1 9.4 %collective-permute-start.7 = (bf16[416,384]{1,0:T(8,128)(2,1)S(1)}, bf16[416,384]{1,0:T(8,128)(2,1)S(1)}, u32[]{:S(2)}, u32[]{:S(2)}) collective-permute-start(bf16[416,384]{1,0:T(8,128)(2,1)S(1)} %pad_maximum_fusion.11), channel_id=1, source_target_pairs={{0,2},{1,3},{2,0},{3,1},{4,6},{5,7},{6,4},{7,5},{8,10},{9,11},{10,... | collective-permute-start | bytes 958472 | tf_op jit(solution)/shard_map/ppermute | solution.py:24
  22.9 15.7 %collective-permute-start.2 = (bf16[832,384]{1,0:T(8,128)(2,1)S(1)}, bf16[832,384]{1,0:T(8,128)(2,1)S(1)}, u32[]{:S(2)}, u32[]{:S(2)}) collective-permute-start(bf16[832,384]{1,0:T(8,128)(2,1)S(1)} %pad_maximum_fusion.2), channel_id=1, source_target_pairs={{0,2},{1,3},{2,0},{3,1},{4,6},{5,7},{6,4},{7,5},{8,10},{9,11},{10,... | collective-permute-start | bytes 1916936 | tf_op jit(solution)/shard_map/ppermute | solution.py:24
  25.9 1.9 %copy-start.18 = (bf16[128,768]{1,0:T(8,128)(2,1)S(1)}, bf16[128,768]{1,0:T(8,128)(2,1)}, u32[]{:S(2)}) copy-start(bf16[128,768]{1,0:T(8,128)(2,1)} %param.8) | copy-start | bytes 589828
  26.1 15.1 %collective-permute-start.8 = (bf16[832,384]{1,0:T(8,128)(2,1)S(1)}, bf16[832,384]{1,0:T(8,128)(2,1)S(1)}, u32[]{:S(2)}, u32[]{:S(2)}) collective-permute-start(bf16[832,384]{1,0:T(8,128)(2,1)S(1)} %pad_maximum_fusion.3), channel_id=1, source_target_pairs={{0,4},{1,5},{2,6},{3,7},{4,0},{5,1},{6,2},{7,3},{8,12},{9,13},{10,... | collective-permute-start | bytes 1916936 | tf_op jit(solution)/shard_map/ppermute | solution.py:24
  38.8 2.4 %copy-start = (bf16[2,2,2,128,384]{4,3,2,1,0:T(8,128)(2,1)}, bf16[2,2,2,128,384]{4,3,2,1,0:T(8,128)(2,1)S(1)}, u32[]{:S(2)}) copy-start(bf16[2,2,2,128,384]{4,3,2,1,0:T(8,128)(2,1)S(1)} %copy.48) | copy-start | bytes 2359300
  38.9 4.3 %collective-permute-start.3 = (bf16[2,512,384]{2,1,0:T(8,128)(2,1)S(1)}, bf16[2,512,384]{2,1,0:T(8,128)(2,1)S(1)}, u32[]{:S(2)}, u32[]{:S(2)}) collective-permute-start(bf16[2,512,384]{2,1,0:T(8,128)(2,1)S(1)} %bitcast.204), channel_id=1, source_target_pairs={{0,1},{1,0},{2,3},{3,2},{4,5},{5,4},{6,7},{7,6},{8,9},{9,8},{10,11... | collective-permute-start | bytes 2359304 | tf_op jit(solution)/shard_map/ppermute | solution.py:24
  39.0 2.3 %copy-start.13 = (bf16[2,2,2,2,8,384]{5,4,3,2,1,0:T(8,128)(2,1)}, bf16[2,2,2,2,8,384]{5,4,3,2,1,0:T(8,128)(2,1)S(1)}, u32[]{:S(2)}) copy-start(bf16[2,2,2,2,8,384]{5,4,3,2,1,0:T(8,128)(2,1)S(1)} %copy.52) | copy-start | bytes 294916
  39.0 4.1 %collective-permute-start.5 = (bf16[2,64,384]{2,1,0:T(8,128)(2,1)S(1)}, bf16[2,64,384]{2,1,0:T(8,128)(2,1)S(1)}, u32[]{:S(2)}, u32[]{:S(2)}) collective-permute-start(bf16[2,64,384]{2,1,0:T(8,128)(2,1)S(1)} %bitcast.249), channel_id=1, source_target_pairs={{0,1},{1,0},{2,3},{3,2},{4,5},{5,4},{6,7},{7,6},{8,9},{9,8},{10,11... | collective-permute-start | bytes 294920 | tf_op jit(solution)/shard_map/ppermute | solution.py:24
  39.7 2.7 %copy-start.5 = (bf16[2,2,2,2,32,384]{5,4,3,2,1,0:T(8,128)(2,1)}, bf16[2,2,2,2,32,384]{5,4,3,2,1,0:T(8,128)(2,1)S(1)}, u32[]{:S(2)}) copy-start(bf16[2,2,2,2,32,384]{5,4,3,2,1,0:T(8,128)(2,1)S(1)} %copy.50) | copy-start | bytes 1179652
  39.7 3.5 %collective-permute-start.4 = (bf16[2,256,384]{2,1,0:T(8,128)(2,1)S(1)}, bf16[2,256,384]{2,1,0:T(8,128)(2,1)S(1)}, u32[]{:S(2)}, u32[]{:S(2)}) collective-permute-start(bf16[2,256,384]{2,1,0:T(8,128)(2,1)S(1)} %bitcast.219), channel_id=1, source_target_pairs={{0,1},{1,0},{2,3},{3,2},{4,5},{5,4},{6,7},{7,6},{8,9},{9,8},{10,11... | collective-permute-start | bytes 1179656 | tf_op jit(solution)/shard_map/ppermute | solution.py:24
  41.2 1.2 copy-start.12
  41.3 1.2 copy-start.19
  42.4 25.5 %collective-permute-start.9 = (bf16[2,512,384]{2,1,0:T(8,128)(2,1)}, bf16[2,512,384]{2,1,0:T(8,128)(2,1)}, u32[]{:S(2)}, u32[]{:S(2)}) collective-permute-start(bf16[2,512,384]{2,1,0:T(8,128)(2,1)} %bitcast.51.refs_0_), channel_id=1, source_target_pairs={{0,1},{1,0},{2,3},{3,2},{4,5},{5,4},{6,7},{7,6},{8,9},{9,8},{10,11... | collective-permute-start | bytes 2359304 | tf_op jit(solution)/shard_map/ppermute | solution.py:24
  43.1 1.0 copy-start.25
  43.2 1.1 copy-start.15
  43.2 0.9 copy-start.11
  62.7 3.3 %slice-start = ((bf16[832,384]{1,0:T(8,128)(2,1)}), bf16[64,384]{1,0:T(8,128)(2,1)S(1)}, s32[]{:S(2)}) async-start(bf16[832,384]{1,0:T(8,128)(2,1)} %copy-done.12), calls=%async_computation | async-start | bytes 98304 | tf_op jit(solution)/shard_map/slice | solution.py:181
  62.7 3.3 %copy-start.21 = (bf16[2,1,2,2,8,384]{5,4,0,3,2,1:T(8,128)(2,1)S(1)}, bf16[2,1,2,2,8,384]{5,4,0,3,2,1:T(8,128)(2,1)}, u32[]{:S(2)}) copy-start(bf16[2,1,2,2,8,384]{5,4,0,3,2,1:T(8,128)(2,1)} %get-tuple-element.64) | copy-start | bytes 147460
  62.7 32.5 %collective-permute-start.12 = (f32[2,512,384]{2,1,0:T(8,128)}, f32[2,512,384]{2,1,0:T(8,128)}, u32[]{:S(2)}, u32[]{:S(2)}) collective-permute-start(f32[2,512,384]{2,1,0:T(8,128)} %get-tuple-element.25), channel_id=1, source_target_pairs={{0,1},{1,0},{2,3},{3,2},{4,5},{5,4},{6,7},{7,6},{8,9},{9,8},{10,11... | collective-permute-start | bytes 4718600 | tf_op jit(solution)/shard_map/ppermute | solution.py:24
  65.2 0.7 copy-start.6
  66.0 1.9 %collective-permute-start.10 = (bf16[2,256,384]{2,1,0:T(8,128)(2,1)S(1)}, bf16[2,256,384]{2,1,0:T(8,128)(2,1)S(1)}, u32[]{:S(2)}, u32[]{:S(2)}) collective-permute-start(bf16[2,256,384]{2,1,0:T(8,128)(2,1)S(1)} %bitcast.221), channel_id=1, source_target_pairs={{0,1},{1,0},{2,3},{3,2},{4,5},{5,4},{6,7},{7,6},{8,9},{9,8},{10,11... | collective-permute-start | bytes 1179656 | tf_op jit(solution)/shard_map/ppermute | solution.py:24
  66.1 1.8 %copy-start.14 = (bf16[2,2,2,2,8,384]{5,4,3,2,1,0:T(8,128)(2,1)}, bf16[2,2,2,2,8,384]{5,4,3,2,1,0:T(8,128)(2,1)S(1)}, u32[]{:S(2)}) copy-start(bf16[2,2,2,2,8,384]{5,4,3,2,1,0:T(8,128)(2,1)S(1)} %copy.65) | copy-start | bytes 294916
  66.1 1.8 %collective-permute-start.11 = (bf16[2,64,384]{2,1,0:T(8,128)(2,1)S(1)}, bf16[2,64,384]{2,1,0:T(8,128)(2,1)S(1)}, u32[]{:S(2)}, u32[]{:S(2)}) collective-permute-start(bf16[2,64,384]{2,1,0:T(8,128)(2,1)S(1)} %bitcast.251), channel_id=1, source_target_pairs={{0,1},{1,0},{2,3},{3,2},{4,5},{5,4},{6,7},{7,6},{8,9},{9,8},{10,11... | collective-permute-start | bytes 294920 | tf_op jit(solution)/shard_map/ppermute | solution.py:24
  67.9 0.8 copy-start.26
  67.9 0.8 copy-start.16
  86.9 21.0 %collective-permute-start.18 = (f32[2,512,384]{2,1,0:T(8,128)}, f32[2,512,384]{2,1,0:T(8,128)}, u32[]{:S(2)}, u32[]{:S(2)}) collective-permute-start(f32[2,512,384]{2,1,0:T(8,128)} %get-tuple-element.31), channel_id=1, source_target_pairs={{0,1},{1,0},{2,3},{3,2},{4,5},{5,4},{6,7},{7,6},{8,9},{9,8},{10,11... | collective-permute-start | bytes 4718600 | tf_op jit(solution)/shard_map/ppermute | solution.py:24
  87.1 6.8 %collective-permute-start.13 = (f32[2,256,384]{2,1,0:T(8,128)}, f32[2,256,384]{2,1,0:T(8,128)S(1)}, u32[]{:S(2)}, u32[]{:S(2)}) collective-permute-start(f32[2,256,384]{2,1,0:T(8,128)} %get-tuple-element.27), channel_id=1, source_target_pairs={{0,1},{1,0},{2,3},{3,2},{4,5},{5,4},{6,7},{7,6},{8,9},{9,8},{10,11... | collective-permute-start | bytes 2359304 | tf_op jit(solution)/shard_map/ppermute | solution.py:24
  87.5 5.4 %collective-permute-start.14 = (f32[2,64,384]{2,1,0:T(8,128)}, f32[2,64,384]{2,1,0:T(8,128)S(1)}, u32[]{:S(2)}, u32[]{:S(2)}) collective-permute-start(f32[2,64,384]{2,1,0:T(8,128)} %get-tuple-element.29), channel_id=1, source_target_pairs={{0,1},{1,0},{2,3},{3,2},{4,5},{5,4},{6,7},{7,6},{8,9},{9,8},{10,11... | collective-permute-start | bytes 589832 | tf_op jit(solution)/shard_map/ppermute | solution.py:24
  87.6 18.9 %collective-permute-start.19 = (f32[2,256,384]{2,1,0:T(8,128)}, f32[2,256,384]{2,1,0:T(8,128)}, u32[]{:S(2)}, u32[]{:S(2)}) collective-permute-start(f32[2,256,384]{2,1,0:T(8,128)} %get-tuple-element.33), channel_id=1, source_target_pairs={{0,1},{1,0},{2,3},{3,2},{4,5},{5,4},{6,7},{7,6},{8,9},{9,8},{10,11... | collective-permute-start | bytes 2359304 | tf_op jit(solution)/shard_map/ppermute | solution.py:24
  93.9 2.2 %copy-start.8 = (f32[2,512,384]{2,1,0:T(8,128)S(1)}, f32[2,512,384]{2,1,0:T(8,128)}, u32[]{:S(2)}) copy-start(f32[2,512,384]{2,1,0:T(8,128)} %get-tuple-element.24) | copy-start | bytes 4718596
  95.2 0.9 copy-start.1
  98.6 6.9 %copy-start.20 = (f32[2,64,384]{2,1,0:T(8,128)S(1)}, f32[2,64,384]{2,1,0:T(8,128)}, u32[]{:S(2)}) copy-start(f32[2,64,384]{2,1,0:T(8,128)} %get-tuple-element.34) | copy-start | bytes 589828
  98.6 16.9 %collective-permute-start.15 = (bf16[832,384]{1,0:T(8,128)(2,1)}, bf16[832,384]{1,0:T(8,128)(2,1)S(1)}, u32[]{:S(2)}, u32[]{:S(2)}) collective-permute-start(bf16[832,384]{1,0:T(8,128)(2,1)} %pad_maximum_fusion.4), channel_id=1, source_target_pairs={{0,2},{1,3},{2,0},{3,1},{4,6},{5,7},{6,4},{7,5},{8,10},{9,11},{10,... | collective-permute-start | bytes 1916936 | tf_op jit(solution)/shard_map/ppermute | solution.py:24
  99.8 5.7 %collective-permute-start.20 = (f32[2,64,384]{2,1,0:T(8,128)}, f32[2,64,384]{2,1,0:T(8,128)}, u32[]{:S(2)}, u32[]{:S(2)}) collective-permute-start(f32[2,64,384]{2,1,0:T(8,128)} %get-tuple-element.35), channel_id=1, source_target_pairs={{0,1},{1,0},{2,3},{3,2},{4,5},{5,4},{6,7},{7,6},{8,9},{9,8},{10,11... | collective-permute-start | bytes 589832 | tf_op jit(solution)/shard_map/ppermute | solution.py:24
  100.0 6.5 %copy-start.10 = (f32[2,256,384]{2,1,0:T(8,128)S(1)}, f32[2,256,384]{2,1,0:T(8,128)}, u32[]{:S(2)}) copy-start(f32[2,256,384]{2,1,0:T(8,128)} %get-tuple-element.32) | copy-start | bytes 2359300
  106.5 1.6 %copy-start.7 = (f32[2,512,384]{2,1,0:T(8,128)S(1)}, f32[2,512,384]{2,1,0:T(8,128)}, u32[]{:S(2)}) copy-start(f32[2,512,384]{2,1,0:T(8,128)} %get-tuple-element.30) | copy-start | bytes 4718596
  109.9 17.2 %collective-permute-start.21 = (bf16[832,384]{1,0:T(8,128)(2,1)S(1)}, bf16[832,384]{1,0:T(8,128)(2,1)S(1)}, u32[]{:S(2)}, u32[]{:S(2)}) collective-permute-start(bf16[832,384]{1,0:T(8,128)(2,1)S(1)} %pad_maximum_fusion.5), channel_id=1, source_target_pairs={{0,4},{1,5},{2,6},{3,7},{4,0},{5,1},{6,2},{7,3},{8,12},{9,13},{10,... | collective-permute-start | bytes 1916936 | tf_op jit(solution)/shard_map/ppermute | solution.py:24
  115.6 1.1 copy-start.2
  116.9 16.7 %collective-permute-start.16 = (bf16[416,384]{1,0:T(8,128)(2,1)S(1)}, bf16[416,384]{1,0:T(8,128)(2,1)S(1)}, u32[]{:S(2)}, u32[]{:S(2)}) collective-permute-start(bf16[416,384]{1,0:T(8,128)(2,1)S(1)} %pad_maximum_fusion.12), channel_id=1, source_target_pairs={{0,4},{1,5},{2,6},{3,7},{4,0},{5,1},{6,2},{7,3},{8,12},{9,13},{10,... | collective-permute-start | bytes 958472 | tf_op jit(solution)/shard_map/ppermute | solution.py:24
  127.5 8.7 %collective-permute-start.22 = (bf16[416,384]{1,0:T(8,128)(2,1)S(1)}, bf16[416,384]{1,0:T(8,128)(2,1)S(1)}, u32[]{:S(2)}, u32[]{:S(2)}) collective-permute-start(bf16[416,384]{1,0:T(8,128)(2,1)S(1)} %pad_maximum_fusion.13), channel_id=1, source_target_pairs={{0,2},{1,3},{2,0},{3,1},{4,6},{5,7},{6,4},{7,5},{8,10},{9,11},{10,... | collective-permute-start | bytes 958472 | tf_op jit(solution)/shard_map/ppermute | solution.py:24
  136.4 5.8 %collective-permute-start.17 = (bf16[80,384]{1,0:T(8,128)(2,1)S(1)}, bf16[80,384]{1,0:T(8,128)(2,1)S(1)}, u32[]{:S(2)}, u32[]{:S(2)}) collective-permute-start(bf16[80,384]{1,0:T(8,128)(2,1)S(1)} %pad_maximum_fusion.27), channel_id=1, source_target_pairs={{0,8},{1,9},{2,10},{3,11},{4,12},{5,13},{6,14},{7,15},{8,0},{9,1},... | collective-permute-start | bytes 184328 | tf_op jit(solution)/shard_map/ppermute | solution.py:24
  140.8 6.3 %collective-permute-start.23 = (bf16[80,384]{1,0:T(8,128)(2,1)}, bf16[80,384]{1,0:T(8,128)(2,1)}, u32[]{:S(2)}, u32[]{:S(2)}) collective-permute-start(bf16[80,384]{1,0:T(8,128)(2,1)} %pad_maximum_fusion.28), channel_id=1, source_target_pairs={{0,8},{1,9},{2,10},{3,11},{4,12},{5,13},{6,14},{7,15},{8,0},{9,1},... | collective-permute-start | bytes 184328 | tf_op jit(solution)/shard_map/ppermute | solution.py:24
  142.2 0.6 copy-start.17
  144.7 1.1 copy-start.24
  145.9 2.2 %copy-start.9 = (f32[2,32,6,64]{3,2,1,0:T(8,128)S(1)}, f32[2,32,6,64]{3,2,1,0:T(8,128)}, u32[]{:S(2)}) copy-start(f32[2,32,6,64]{3,2,1,0:T(8,128)} %squeeze.78) | copy-start | bytes 294916
  149.2 0.8 copy-start.22
  149.2 0.8 copy-start.23

commit v3 on v1

--- a/solution.py
+++ b/solution.py
@@ -117,16 +117,14 @@
                 )
                 query_grad = piece if query_grad is None else query_grad + piece
                 key_terms = (
-                    jnp.dot(
-                        jnp.transpose(score_grad).astype(jnp.bfloat16),
-                        query,
+                    lax.dot_general(
+                        score_grad.astype(jnp.bfloat16), query, (((0,), (0,)), ((), ())),
                         preferred_element_type=jnp.float32,
                     )
                     * score_scale
                 )
-                value_terms = jnp.dot(
-                    jnp.transpose(probs[branch]).astype(jnp.bfloat16),
-                    grad,
+                value_terms = lax.dot_general(
+                    weights[branch], grad, (((0,), (0,)), ((), ())),
                     preferred_element_type=jnp.float32,
                 )
                 term_refs[branch][0, :, cols] = key_terms

time: 149 us -> 149 us (level)
  no operation moved by 1% of the time
where the time goes in v3:
time: 149 us; the launch traced here: 148 us
  waiting for transfers between devices  40.3 us (27%)
  local copies, waits for them, and re-layouts  40 us (27%)
  Pallas kernels  29 us (19%)
  starting transfers between devices  22.1 us (15%)
  other arithmetic  14.8 us (10%)
  between operations  1.99 us (1%)
    ppermute x16, waiting for transfers between devices, exchange(): return lax.ppermute(block, 'seq', route)  40.3 us
    pallas_call x2, Pallas kernels, per_device(): pl.pallas_call(attention_kernel(head_dim, score_scale, half * heads_per_h...  29 us
    ppermute x16, starting transfers between devices, exchange(): return lax.ppermute(block, 'seq', route)  22.1 us
    slice x25, local copies, waits for them, and re-layouts, per_device(): lax.index_in_dim(partial[branch], 1, places[branch], keepdims=False)  6.79 us
    another operation x25, local copies, waits for them, and re-layouts, per_device(): buffers[branch] = jnp.stack([buffers[branch], arrived], axis=1)  6.56 us
    broadcast_in_dim x16, local copies, waits for them, and re-layouts, spread_rows(): widened = jnp.where(chosen, grouped, jnp.zeros((), picked.dtype))  6.49 us
    slice x22, local copies, waits for them, and re-layouts, per_device(): partial[branch] = kept + incoming[cursor:cursor + count].reshape(kept.shape)  6.15 us
    another operation x22, other arithmetic, per_device(): buffers[branch] = jnp.stack([buffers[branch], arrived], axis=1)  3.83 us
  transfers between devices with their start and end apart: 16, of which 8 were waited for; matrix products, arithmetic and copies ran while one was open for 29% of the time, Pallas kernels for 20%

profile of v3, /device:TPU:0, one launch (start us, length us, event | category | flops | bytes accessed | tf_op | source)
XLA Modules:
  0.0 148.2 jit_solution(11750407693628961937)
XLA Ops:
  0.7 1.3 stack.157
  2.0 1.3 stack.161
  5.2 4.1 %collective-permute-start = (bf16[80,384]{1,0:T(8,128)(2,1)S(1)}, bf16[80,384]{1,0:T(8,128)(2,1)S(1)}, u32[]{:S(2)}, u32[]{:S(2)}) collective-permute-start(bf16[80,384]{1,0:T(8,128)(2,1)S(1)} %pad_maximum_fusion.35), channel_id=1, source_target_pairs={{0,8},{1,9},{2,10},{3,11},{4,12},{5,13},{6,14},{7,15},{8,0},{9,1},... | collective-permute-start | bytes 184328 | tf_op jit(solution)/shard_map/ppermute | solution.py:24
  9.4 0.6 slice_bitcast_fusion.26
  10.0 0.7 fusion.45
  10.8 1.4 collective-permute-done
  12.3 2.7 %collective-permute-start.1 = (bf16[416,384]{1,0:T(8,128)(2,1)S(1)}, bf16[416,384]{1,0:T(8,128)(2,1)S(1)}, u32[]{:S(2)}, u32[]{:S(2)}) collective-permute-start(bf16[416,384]{1,0:T(8,128)(2,1)S(1)} %pad_maximum_fusion.18), channel_id=1, source_target_pairs={{0,4},{1,5},{2,6},{3,7},{4,0},{5,1},{6,2},{7,3},{8,12},{9,13},{10,... | collective-permute-start | bytes 958472 | tf_op jit(solution)/shard_map/ppermute | solution.py:24
  15.1 2.3 %collective-permute-start.5 = (bf16[416,384]{1,0:T(8,128)(2,1)S(1)}, bf16[416,384]{1,0:T(8,128)(2,1)S(1)}, u32[]{:S(2)}, u32[]{:S(2)}) collective-permute-start(bf16[416,384]{1,0:T(8,128)(2,1)S(1)} %pad_maximum_fusion.19), channel_id=1, source_target_pairs={{0,2},{1,3},{2,0},{3,1},{4,6},{5,7},{6,4},{7,5},{8,10},{9,11},{10,... | collective-permute-start | bytes 958472 | tf_op jit(solution)/shard_map/ppermute | solution.py:24
  17.3 5.2 %collective-permute-done.1 = bf16[416,384]{1,0:T(8,128)(2,1)S(1)} collective-permute-done((bf16[416,384]{1,0:T(8,128)(2,1)S(1)}, bf16[416,384]{1,0:T(8,128)(2,1)S(1)}, u32[]{:S(2)}, u32[]{:S(2)}) %collective-permute-start.1) | collective-permute-done | bytes 319520 | tf_op jit(solution)/shard_map/ppermute | solution.py:24
  22.9 1.6 %collective-permute-start.2 = (bf16[832,384]{1,0:T(8,128)(2,1)S(1)}, bf16[832,384]{1,0:T(8,128)(2,1)S(1)}, u32[]{:S(2)}, u32[]{:S(2)}) collective-permute-start(bf16[832,384]{1,0:T(8,128)(2,1)S(1)} %pad_maximum_fusion.10), channel_id=1, source_target_pairs={{0,2},{1,3},{2,0},{3,1},{4,6},{5,7},{6,4},{7,5},{8,10},{9,11},{10,... | collective-permute-start | bytes 1916936 | tf_op jit(solution)/shard_map/ppermute | solution.py:24
  24.8 1.8 %collective-permute-start.6 = (bf16[832,384]{1,0:T(8,128)(2,1)S(1)}, bf16[832,384]{1,0:T(8,128)(2,1)S(1)}, u32[]{:S(2)}, u32[]{:S(2)}) collective-permute-start(bf16[832,384]{1,0:T(8,128)(2,1)S(1)} %pad_maximum_fusion.11), channel_id=1, source_target_pairs={{0,4},{1,5},{2,6},{3,7},{4,0},{5,1},{6,2},{7,3},{8,12},{9,13},{10,... | collective-permute-start | bytes 1916936 | tf_op jit(solution)/shard_map/ppermute | solution.py:24
  26.6 12.0 %collective-permute-done.2 = bf16[832,384]{1,0:T(8,128)(2,1)S(1)} collective-permute-done((bf16[832,384]{1,0:T(8,128)(2,1)S(1)}, bf16[832,384]{1,0:T(8,128)(2,1)S(1)}, u32[]{:S(2)}, u32[]{:S(2)}) %collective-permute-start.2) | collective-permute-done | bytes 639008 | tf_op jit(solution)/shard_map/ppermute | solution.py:24
  39.1 1.2 pad_maximum_fusion.2
  40.3 0.8 fusion.39
  41.2 0.7 fusion.33
  42.0 1.1 fusion.43
  43.2 1.2 pad_maximum_fusion.3
  45.6 0.8 broadcast_in_dim.131
  46.4 0.7 fusion.46
  47.2 0.7 copy.76
  48.1 1.0 copy.74
  49.4 1.4 copy.72
  50.7 14.6 %shard_map.84 = (bf16[128,384]{1,0:T(8,128)(2,1)}, bf16[128,384]{1,0:T(8,128)(2,1)}, f32[2,1024,384]{2,1,0:T(8,128)}, f32[2,512,384]{2,1,0:T(8,128)}, f32[2,128,384]{2,1,0:T(8,128)}) custom-call(s32[3,12]{1,0:T(4,128)} %offsets_ref.3, bf16[128,384]{1,0:T(8,128)(2,1)} %get-tuple-element.46.query_ref, bf16[128,384]{1,0:T(8,128)(2,1)} %get-tuple-element.44.grad_ref, ...), custom_call_target="tpu_custom_call" | custom-call | tf_op jit(solution)/shard_map/pallas_call | solution.py:194
  65.3 1.5 %slice.664 = bf16[2,1,2,2,128,384]{5,4,3,2,1,0:T(8,128)(2,1)S(1)} slice(f32[2,2,2,2,128,384]{5,4,3,2,1,0:T(8,128)} %bitcast.280), slice={[0:2], [1:2], [0:2], [0:2], [0:128], [0:384]} | slice | bytes 1572864 | tf_op jit(solution)/shard_map/slice | solution.py:222
  66.8 1.2 slice.668
  68.0 1.0 slice.676
  69.0 1.2 pad_maximum_fusion.4
  70.2 0.9 slice.491
  71.2 0.7 copy.95
  71.9 1.0 slice.490
  73.0 1.0 copy.93
  74.1 1.2 slice.489
  75.5 1.3 copy.91
  76.8 14.4 %shard_map.85 = (bf16[128,384]{1,0:T(8,128)(2,1)}, bf16[128,384]{1,0:T(8,128)(2,1)}, f32[2,1024,384]{2,1,0:T(8,128)}, f32[2,512,384]{2,1,0:T(8,128)}, f32[2,128,384]{2,1,0:T(8,128)}) custom-call(s32[3,12]{1,0:T(4,128)} %offsets_ref.3, bf16[128,384]{1,0:T(8,128)(2,1)} %get-tuple-element.47.query_ref, bf16[128,384]{1,0:T(8,128)(2,1)} %get-tuple-element.45.grad_ref, ...), custom_call_target="tpu_custom_call" | custom-call | tf_op jit(solution)/shard_map/pallas_call | solution.py:194
  91.2 1.6 %slice.663 = bf16[2,1,2,2,128,384]{5,4,3,2,1,0:T(8,128)(2,1)S(1)} slice(f32[2,2,2,2,128,384]{5,4,3,2,1,0:T(8,128)} %bitcast.282), slice={[0:2], [1:2], [0:2], [0:2], [0:128], [0:384]} | slice | bytes 1572864 | tf_op jit(solution)/shard_map/slice | solution.py:222
  92.8 1.2 slice.666
  94.9 0.8 broadcast_in_dim.125
  95.9 0.8 broadcast_in_dim.141
  96.8 0.8 broadcast_in_dim.136
  97.7 0.8 pad_maximum_fusion.27
  98.4 1.4 slice.496
  99.8 0.7 copy-done.1
  100.8 1.2 slice.500
  102.4 0.9 slice.503
  103.5 1.1 collective-permute-start.9
  104.7 0.7 copy-done.2
  105.7 1.2 copy-done.8
  107.3 1.5 %collective-permute-start.13 = (bf16[832,384]{1,0:T(8,128)(2,1)S(1)}, bf16[832,384]{1,0:T(8,128)(2,1)S(1)}, u32[]{:S(2)}, u32[]{:S(2)}) collective-permute-start(bf16[832,384]{1,0:T(8,128)(2,1)S(1)} %pad_maximum_fusion.13), channel_id=1, source_target_pairs={{0,4},{1,5},{2,6},{3,7},{4,0},{5,1},{6,2},{7,3},{8,12},{9,13},{10,... | collective-permute-start | bytes 1916936 | tf_op jit(solution)/shard_map/ppermute | solution.py:24
  108.8 11.4 %collective-permute-done.9 = bf16[832,384]{1,0:T(8,128)(2,1)S(1)} collective-permute-done((bf16[832,384]{1,0:T(8,128)(2,1)S(1)}, bf16[832,384]{1,0:T(8,128)(2,1)S(1)}, u32[]{:S(2)}, u32[]{:S(2)}) %collective-permute-start.9) | collective-permute-done | bytes 639008 | tf_op jit(solution)/shard_map/ppermute | solution.py:24
  120.6 1.5 %collective-permute-start.10 = (bf16[416,384]{1,0:T(8,128)(2,1)S(1)}, bf16[416,384]{1,0:T(8,128)(2,1)S(1)}, u32[]{:S(2)}, u32[]{:S(2)}) collective-permute-start(bf16[416,384]{1,0:T(8,128)(2,1)S(1)} %pad_maximum_fusion.20), channel_id=1, source_target_pairs={{0,4},{1,5},{2,6},{3,7},{4,0},{5,1},{6,2},{7,3},{8,12},{9,13},{10,... | collective-permute-start | bytes 958472 | tf_op jit(solution)/shard_map/ppermute | solution.py:24
  122.1 2.4 %collective-permute-done.13 = bf16[832,384]{1,0:T(8,128)(2,1)S(1)} collective-permute-done((bf16[832,384]{1,0:T(8,128)(2,1)S(1)}, bf16[832,384]{1,0:T(8,128)(2,1)S(1)}, u32[]{:S(2)}, u32[]{:S(2)}) %collective-permute-start.13) | collective-permute-done | bytes 639008 | tf_op jit(solution)/shard_map/ppermute | solution.py:24
  125.0 1.0 collective-permute-start.14
  126.0 4.8 %collective-permute-done.10 = bf16[416,384]{1,0:T(8,128)(2,1)S(1)} collective-permute-done((bf16[416,384]{1,0:T(8,128)(2,1)S(1)}, bf16[416,384]{1,0:T(8,128)(2,1)S(1)}, u32[]{:S(2)}, u32[]{:S(2)}) %collective-permute-start.10) | collective-permute-done | bytes 319520 | tf_op jit(solution)/shard_map/ppermute | solution.py:24
  131.0 2.5 %collective-permute-done.14 = bf16[416,384]{1,0:T(8,128)(2,1)S(1)} collective-permute-done((bf16[416,384]{1,0:T(8,128)(2,1)S(1)}, bf16[416,384]{1,0:T(8,128)(2,1)S(1)}, u32[]{:S(2)}, u32[]{:S(2)}) %collective-permute-start.14) | collective-permute-done | bytes 319520 | tf_op jit(solution)/shard_map/ppermute | solution.py:24
  133.6 3.4 %collective-permute-start.11 = (bf16[80,384]{1,0:T(8,128)(2,1)S(1)}, bf16[80,384]{1,0:T(8,128)(2,1)S(1)}, u32[]{:S(2)}, u32[]{:S(2)}) collective-permute-start(bf16[80,384]{1,0:T(8,128)(2,1)S(1)} %pad_maximum_fusion.37), channel_id=1, source_target_pairs={{0,8},{1,9},{2,10},{3,11},{4,12},{5,13},{6,14},{7,15},{8,0},{9,1},... | collective-permute-start | bytes 184328 | tf_op jit(solution)/shard_map/ppermute | solution.py:24
  137.9 0.8 squeeze.102
  140.0 1.0 broadcast_in_dim.128
  141.0 0.7 slice.524
  141.9 1.0 broadcast_in_dim.134
  142.9 1.3 fusion.17
  144.2 0.8 slice.556
  145.5 0.7 slice.558
  146.8 0.7 pad_maximum_fusion.30
  147.5 0.7 pad_maximum_fusion.29
  (226 shorter events, 12.1 us)
Async XLA Ops:
  0.6 2.6 %copy-start.3 = (bf16[128,768]{1,0:T(8,128)(2,1)S(1)}, bf16[128,768]{1,0:T(8,128)(2,1)}, u32[]{:S(2)}) copy-start(bf16[128,768]{1,0:T(8,128)(2,1)} %param.7) | copy-start | bytes 589828
  0.6 3.3 %copy-start.22 = (s32[3,12]{1,0:T(4,128)S(1)}, s32[3,12]{1,0:T(4,128)}, u32[]{:S(2)}) copy-start(s32[3,12]{1,0:T(4,128)} %offsets_ref.3) | copy-start | bytes 436
  3.9 6.1 %copy-start.13 = (bf16[128,768]{1,0:T(8,128)(2,1)S(1)}, bf16[128,768]{1,0:T(8,128)(2,1)}, u32[]{:S(2)}) copy-start(bf16[128,768]{1,0:T(8,128)(2,1)} %param.8) | copy-start | bytes 589828
  4.4 6.3 %copy-start.4 = (bf16[128,768]{1,0:T(8,128)(2,1)S(1)}, bf16[128,768]{1,0:T(8,128)(2,1)}, u32[]{:S(2)}) copy-start(bf16[128,768]{1,0:T(8,128)(2,1)} %param.6) | copy-start | bytes 589828
  5.2 7.0 %collective-permute-start = (bf16[80,384]{1,0:T(8,128)(2,1)S(1)}, bf16[80,384]{1,0:T(8,128)(2,1)S(1)}, u32[]{:S(2)}, u32[]{:S(2)}) collective-permute-start(bf16[80,384]{1,0:T(8,128)(2,1)S(1)} %pad_maximum_fusion.35), channel_id=1, source_target_pairs={{0,8},{1,9},{2,10},{3,11},{4,12},{5,13},{6,14},{7,15},{8,0},{9,1},... | collective-permute-start | bytes 184328 | tf_op jit(solution)/shard_map/ppermute | solution.py:24
  9.3 5.6 %collective-permute-start.4 = (bf16[80,384]{1,0:T(8,128)(2,1)S(1)}, bf16[80,384]{1,0:T(8,128)(2,1)S(1)}, u32[]{:S(2)}, u32[]{:S(2)}) collective-permute-start(bf16[80,384]{1,0:T(8,128)(2,1)S(1)} %pad_maximum_fusion.36), channel_id=1, source_target_pairs={{0,8},{1,9},{2,10},{3,11},{4,12},{5,13},{6,14},{7,15},{8,0},{9,1},... | collective-permute-start | bytes 184328 | tf_op jit(solution)/shard_map/ppermute | solution.py:24
  12.3 10.3 %collective-permute-start.1 = (bf16[416,384]{1,0:T(8,128)(2,1)S(1)}, bf16[416,384]{1,0:T(8,128)(2,1)S(1)}, u32[]{:S(2)}, u32[]{:S(2)}) collective-permute-start(bf16[416,384]{1,0:T(8,128)(2,1)S(1)} %pad_maximum_fusion.18), channel_id=1, source_target_pairs={{0,4},{1,5},{2,6},{3,7},{4,0},{5,1},{6,2},{7,3},{8,12},{9,13},{10,... | collective-permute-start | bytes 958472 | tf_op jit(solution)/shard_map/ppermute | solution.py:24
  15.1 9.4 %collective-permute-start.5 = (bf16[416,384]{1,0:T(8,128)(2,1)S(1)}, bf16[416,384]{1,0:T(8,128)(2,1)S(1)}, u32[]{:S(2)}, u32[]{:S(2)}) collective-permute-start(bf16[416,384]{1,0:T(8,128)(2,1)S(1)} %pad_maximum_fusion.19), channel_id=1, source_target_pairs={{0,2},{1,3},{2,0},{3,1},{4,6},{5,7},{6,4},{7,5},{8,10},{9,11},{10,... | collective-permute-start | bytes 958472 | tf_op jit(solution)/shard_map/ppermute | solution.py:24
  22.9 15.7 %collective-permute-start.2 = (bf16[832,384]{1,0:T(8,128)(2,1)S(1)}, bf16[832,384]{1,0:T(8,128)(2,1)S(1)}, u32[]{:S(2)}, u32[]{:S(2)}) collective-permute-start(bf16[832,384]{1,0:T(8,128)(2,1)S(1)} %pad_maximum_fusion.10), channel_id=1, source_target_pairs={{0,2},{1,3},{2,0},{3,1},{4,6},{5,7},{6,4},{7,5},{8,10},{9,11},{10,... | collective-permute-start | bytes 1916936 | tf_op jit(solution)/shard_map/ppermute | solution.py:24
  24.8 15.5 %collective-permute-start.6 = (bf16[832,384]{1,0:T(8,128)(2,1)S(1)}, bf16[832,384]{1,0:T(8,128)(2,1)S(1)}, u32[]{:S(2)}, u32[]{:S(2)}) collective-permute-start(bf16[832,384]{1,0:T(8,128)(2,1)S(1)} %pad_maximum_fusion.11), channel_id=1, source_target_pairs={{0,4},{1,5},{2,6},{3,7},{4,0},{5,1},{6,2},{7,3},{8,12},{9,13},{10,... | collective-permute-start | bytes 1916936 | tf_op jit(solution)/shard_map/ppermute | solution.py:24
  40.3 6.8 %collective-permute-start.3 = (bf16[1664,384]{1,0:T(8,128)(2,1)}, bf16[1664,384]{1,0:T(8,128)(2,1)S(1)}, u32[]{:S(2)}, u32[]{:S(2)}) collective-permute-start(bf16[1664,384]{1,0:T(8,128)(2,1)} %pad_maximum_fusion.2), channel_id=1, source_target_pairs={{0,1},{1,0},{2,3},{3,2},{4,5},{5,4},{6,7},{7,6},{8,9},{9,8},{10,11... | collective-permute-start | bytes 3833864 | tf_op jit(solution)/shard_map/ppermute | solution.py:24
  43.2 3.3 %copy-start.14 = (bf16[128,768]{1,0:T(8,128)(2,1)S(1)}, bf16[128,768]{1,0:T(8,128)(2,1)}, u32[]{:S(2)}) copy-start(bf16[128,768]{1,0:T(8,128)(2,1)} %param.5) | copy-start | bytes 589828
  44.4 25.8 %collective-permute-start.7 = (bf16[1664,384]{1,0:T(8,128)(2,1)}, bf16[1664,384]{1,0:T(8,128)(2,1)}, u32[]{:S(2)}, u32[]{:S(2)}) collective-permute-start(bf16[1664,384]{1,0:T(8,128)(2,1)} %pad_maximum_fusion.3), channel_id=1, source_target_pairs={{0,1},{1,0},{2,3},{3,2},{4,5},{5,4},{6,7},{7,6},{8,9},{9,8},{10,11... | collective-permute-start | bytes 3833864 | tf_op jit(solution)/shard_map/ppermute | solution.py:24
  68.0 3.1 %copy-start.9 = (bf16[2,1,2,2,2,8,384]{6,5,0,4,3,2,1:T(8,128)(2,1)S(1)}, bf16[2,1,2,2,2,8,384]{6,5,0,4,3,2,1:T(8,128)(2,1)}, u32[]{:S(2)}) copy-start(bf16[2,1,2,2,2,8,384]{6,5,0,4,3,2,1:T(8,128)(2,1)} %get-tuple-element.58) | copy-start | bytes 294916
  69.0 3.9 %copy-start.5 = (bf16[2,1,2,2,2,32,384]{6,5,0,4,3,2,1:T(8,128)(2,1)S(1)}, bf16[2,1,2,2,2,32,384]{6,5,0,4,3,2,1:T(8,128)(2,1)}, u32[]{:S(2)}) copy-start(bf16[2,1,2,2,2,32,384]{6,5,0,4,3,2,1:T(8,128)(2,1)} %get-tuple-element.34) | copy-start | bytes 1179652
  70.2 28.2 %collective-permute-start.8 = (bf16[1664,384]{1,0:T(8,128)(2,1)}, bf16[1664,384]{1,0:T(8,128)(2,1)}, u32[]{:S(2)}, u32[]{:S(2)}) collective-permute-start(bf16[1664,384]{1,0:T(8,128)(2,1)} %pad_maximum_fusion.4), channel_id=1, source_target_pairs={{0,1},{1,0},{2,3},{3,2},{4,5},{5,4},{6,7},{7,6},{8,9},{9,8},{10,11... | collective-permute-start | bytes 3833864 | tf_op jit(solution)/shard_map/ppermute | solution.py:24
  73.0 2.2 %copy-start = (bf16[2,1,2,2,128,384]{5,4,0,3,2,1:T(8,128)(2,1)S(1)}, bf16[2,1,2,2,128,384]{5,4,0,3,2,1:T(8,128)(2,1)}, u32[]{:S(2)}) copy-start(bf16[2,1,2,2,128,384]{5,4,0,3,2,1:T(8,128)(2,1)} %get-tuple-element.26) | copy-start | bytes 2359300
  91.2 2.8 %copy-start.12 = (f32[2,128,384]{2,1,0:T(8,128)S(1)}, f32[2,128,384]{2,1,0:T(8,128)}, u32[]{:S(2)}) copy-start(f32[2,128,384]{2,1,0:T(8,128)} %get-tuple-element.23) | copy-start | bytes 1179652
  94.0 0.8 copy-start.24
  94.0 0.8 copy-start.25
  94.0 1.8 %copy-start.23 = (pred[16,6]{1,0:T(8,128)(4,1)S(1)}, pred[16,6]{1,0:T(8,128)(4,1)}, u32[]{:S(2)}) copy-start(pred[16,6]{1,0:T(8,128)(4,1)} %get-tuple-element.82) | copy-start | bytes 292
  94.0 3.6 %copy-start.18 = (bf16[128,384]{1,0:T(8,128)(2,1)S(1)}, bf16[128,384]{1,0:T(8,128)(2,1)}, u32[]{:S(2)}) copy-start(bf16[128,384]{1,0:T(8,128)(2,1)} %get-tuple-element.14) | copy-start | bytes 294916
  94.1 3.6 %copy-start.19 = (bf16[128,384]{1,0:T(8,128)(2,1)S(1)}, bf16[128,384]{1,0:T(8,128)(2,1)}, u32[]{:S(2)}) copy-start(bf16[128,384]{1,0:T(8,128)(2,1)} %get-tuple-element.16) | copy-start | bytes 294916
  94.1 3.6 %copy-start.20 = (bf16[128,384]{1,0:T(8,128)(2,1)S(1)}, bf16[128,384]{1,0:T(8,128)(2,1)}, u32[]{:S(2)}) copy-start(bf16[128,384]{1,0:T(8,128)(2,1)} %get-tuple-element.15) | copy-start | bytes 294916
  94.1 3.6 %copy-start.21 = (bf16[128,384]{1,0:T(8,128)(2,1)S(1)}, bf16[128,384]{1,0:T(8,128)(2,1)}, u32[]{:S(2)}) copy-start(bf16[128,384]{1,0:T(8,128)(2,1)} %get-tuple-element.17) | copy-start | bytes 294916
  94.2 10.3 %collective-permute-start.12 = (bf16[1664,384]{1,0:T(8,128)(2,1)S(1)}, bf16[1664,384]{1,0:T(8,128)(2,1)S(1)}, u32[]{:S(2)}, u32[]{:S(2)}) collective-permute-start(bf16[1664,384]{1,0:T(8,128)(2,1)S(1)} %pad_maximum_fusion.5), channel_id=1, source_target_pairs={{0,1},{1,0},{2,3},{3,2},{4,5},{5,4},{6,7},{7,6},{8,9},{9,8},{10,11... | collective-permute-start | bytes 3833864 | tf_op jit(solution)/shard_map/ppermute | solution.py:24
  98.4 2.1 %copy-start.1 = (f32[2,1024,384]{2,1,0:T(8,128)S(1)}, f32[2,1024,384]{2,1,0:T(8,128)}, u32[]{:S(2)}) copy-start(f32[2,1024,384]{2,1,0:T(8,128)} %get-tuple-element.18) | copy-start | bytes 9437188
  100.7 1.5 %copy-start.7 = (f32[2,512,384]{2,1,0:T(8,128)S(1)}, f32[2,512,384]{2,1,0:T(8,128)}, u32[]{:S(2)}) copy-start(f32[2,512,384]{2,1,0:T(8,128)} %get-tuple-element.19) | copy-start | bytes 4718596
  102.2 1.1 copy-start.11
  103.5 1.9 %copy-start.2 = (f32[2,1024,384]{2,1,0:T(8,128)S(1)}, f32[2,1024,384]{2,1,0:T(8,128)}, u32[]{:S(2)}) copy-start(f32[2,1024,384]{2,1,0:T(8,128)} %get-tuple-element.21) | copy-start | bytes 9437188
  103.5 16.7 %collective-permute-start.9 = (bf16[832,384]{1,0:T(8,128)(2,1)S(1)}, bf16[832,384]{1,0:T(8,128)(2,1)S(1)}, u32[]{:S(2)}, u32[]{:S(2)}) collective-permute-start(bf16[832,384]{1,0:T(8,128)(2,1)S(1)} %pad_maximum_fusion.12), channel_id=1, source_target_pairs={{0,2},{1,3},{2,0},{3,1},{4,6},{5,7},{6,4},{7,5},{8,10},{9,11},{10,... | collective-permute-start | bytes 1916936 | tf_op jit(solution)/shard_map/ppermute | solution.py:24
  105.5 1.4 copy-start.8
  107.3 17.3 %collective-permute-start.13 = (bf16[832,384]{1,0:T(8,128)(2,1)S(1)}, bf16[832,384]{1,0:T(8,128)(2,1)S(1)}, u32[]{:S(2)}, u32[]{:S(2)}) collective-permute-start(bf16[832,384]{1,0:T(8,128)(2,1)S(1)} %pad_maximum_fusion.13), channel_id=1, source_target_pairs={{0,4},{1,5},{2,6},{3,7},{4,0},{5,1},{6,2},{7,3},{8,12},{9,13},{10,... | collective-permute-start | bytes 1916936 | tf_op jit(solution)/shard_map/ppermute | solution.py:24
  120.6 10.2 %collective-permute-start.10 = (bf16[416,384]{1,0:T(8,128)(2,1)S(1)}, bf16[416,384]{1,0:T(8,128)(2,1)S(1)}, u32[]{:S(2)}, u32[]{:S(2)}) collective-permute-start(bf16[416,384]{1,0:T(8,128)(2,1)S(1)} %pad_maximum_fusion.20), channel_id=1, source_target_pairs={{0,4},{1,5},{2,6},{3,7},{4,0},{5,1},{6,2},{7,3},{8,12},{9,13},{10,... | collective-permute-start | bytes 958472 | tf_op jit(solution)/shard_map/ppermute | solution.py:24
  125.0 8.5 %collective-permute-start.14 = (bf16[416,384]{1,0:T(8,128)(2,1)S(1)}, bf16[416,384]{1,0:T(8,128)(2,1)S(1)}, u32[]{:S(2)}, u32[]{:S(2)}) collective-permute-start(bf16[416,384]{1,0:T(8,128)(2,1)S(1)} %pad_maximum_fusion.21), channel_id=1, source_target_pairs={{0,2},{1,3},{2,0},{3,1},{4,6},{5,7},{6,4},{7,5},{8,10},{9,11},{10,... | collective-permute-start | bytes 958472 | tf_op jit(solution)/shard_map/ppermute | solution.py:24
  133.6 5.6 %collective-permute-start.11 = (bf16[80,384]{1,0:T(8,128)(2,1)S(1)}, bf16[80,384]{1,0:T(8,128)(2,1)S(1)}, u32[]{:S(2)}, u32[]{:S(2)}) collective-permute-start(bf16[80,384]{1,0:T(8,128)(2,1)S(1)} %pad_maximum_fusion.37), channel_id=1, source_target_pairs={{0,8},{1,9},{2,10},{3,11},{4,12},{5,13},{6,14},{7,15},{8,0},{9,1},... | collective-permute-start | bytes 184328 | tf_op jit(solution)/shard_map/ppermute | solution.py:24
  137.9 6.3 %collective-permute-start.15 = (bf16[80,384]{1,0:T(8,128)(2,1)}, bf16[80,384]{1,0:T(8,128)(2,1)}, u32[]{:S(2)}, u32[]{:S(2)}) collective-permute-start(bf16[80,384]{1,0:T(8,128)(2,1)} %pad_maximum_fusion.38), channel_id=1, source_target_pairs={{0,8},{1,9},{2,10},{3,11},{4,12},{5,13},{6,14},{7,15},{8,0},{9,1},... | collective-permute-start | bytes 184328 | tf_op jit(solution)/shard_map/ppermute | solution.py:24
  139.3 0.6 copy-start.10
  141.8 1.1 copy-start.15
  142.9 2.2 %copy-start.6 = (f32[2,32,6,64]{3,2,1,0:T(8,128)S(1)}, f32[2,32,6,64]{3,2,1,0:T(8,128)}, u32[]{:S(2)}) copy-start(f32[2,32,6,64]{3,2,1,0:T(8,128)} %squeeze.102) | copy-start | bytes 294916
  145.5 1.1 copy-start.16
  145.5 1.1 copy-start.17

commit v4 on v3

--- a/solution.py
+++ b/solution.py
@@ -221,11 +221,10 @@
                     [
                         lax.index_in_dim(partial[branch], 1, places[branch], keepdims=False)
                         .reshape(-1, half_width)
-                        .astype(jnp.bfloat16)
                         for branch in active
                     ]
                 )
-                incoming = exchange(outgoing, bit).astype(jnp.float32)
+                incoming = exchange(outgoing, bit)
                 cursor = 0
                 for branch in active:
                     kept = lax.index_in_dim(partial[branch], 0, places[branch], keepdims=False)

time: 149 us -> 171 us (1.15)
  local copies, waits for them, and re-layouts: 40 us -> 51.6 us
  waiting for transfers between devices: 40.3 us -> 45.5 us
  starting transfers between devices: 22.1 us -> 25.9 us
    slice x22 -> x24, local copies, waits for them, and re-layouts: 6.15 us -> 14.2 us  [per_device(): partial[branch] = kept + incoming[cursor:cursor + count].reshape(kept.shape)]
    ppermute x16, waiting for transfers between devices: 40.3 us -> 45.5 us  [exchange(): return lax.ppermute(block, 'seq', route)]
    ppermute x16, starting transfers between devices: 22.1 us -> 25.9 us  [exchange(): return lax.ppermute(block, 'seq', route)]
    broadcast_in_dim x16, local copies, waits for them, and re-layouts: 6.49 us -> 9.75 us  [spread_rows(): widened = jnp.where(chosen, grouped, jnp.zeros((), picked.dtype))]
    slice x4 -> x5, local copies, waits for them, and re-layouts: 0.02 us -> 2.98 us  [per_device(): kept = lax.index_in_dim(partial[branch], 0, places[branch], keepdims=False)]
    slice x25 -> x21, local copies, waits for them, and re-layouts: 6.79 us -> 3.93 us  [per_device(): lax.index_in_dim(partial[branch], 1, places[branch], keepdims=False)]
    concatenate x8, other arithmetic: 2.14 us -> 4.86 us  [per_device(): jnp.concatenate([lax.index_in_dim(partial[branch], 1, places[branch], kee...]
    unnamed x52 -> x62, local copies, waits for them, and re-layouts: 3.59 us -> 4.96 us
  transfers between devices with their start and end apart: 16 -> 16, of which waited for: 8 -> 7; matrix products, arithmetic and copies ran while one was open for 29% -> 32% of each run, Pallas kernels for 20% -> 17%
where the time goes in v4:
time: 171 us
  local copies, waits for them, and re-layouts  51.6 us (30%)
  waiting for transfers between devices  45.5 us (27%)
  Pallas kernels  29 us (17%)
  starting transfers between devices  25.9 us (15%)
  other arithmetic  16.5 us (10%)
  between operations  1.99 us (1%)
    ppermute x16, waiting for transfers between devices, exchange(): return lax.ppermute(block, 'seq', route)  45.5 us
    pallas_call x2, Pallas kernels, per_device(): pl.pallas_call(attention_kernel(head_dim, score_scale, half * heads_per_h...  29 us
    ppermute x16, starting transfers between devices, exchange(): return lax.ppermute(block, 'seq', route)  25.9 us
    slice x24, local copies, waits for them, and re-layouts, per_device(): partial[branch] = kept + incoming[cursor:cursor + count].reshape(kept.shape)  14.2 us
    broadcast_in_dim x16, local copies, waits for them, and re-layouts, spread_rows(): widened = jnp.where(chosen, grouped, jnp.zeros((), picked.dtype))  9.75 us
    another operation x25, local copies, waits for them, and re-layouts, per_device(): buffers[branch] = jnp.stack([buffers[branch], arrived], axis=1)  6.6 us
    unnamed x62, local copies, waits for them, and re-layouts  4.96 us
    concatenate x8, other arithmetic, per_device(): jnp.concatenate([lax.index_in_dim(partial[branch], 1, places[branch], kee...  4.86 us
  transfers between devices with their start and end apart: 16, of which 7 were waited for; matrix products, arithmetic and copies ran while one was open for 32% of the time, Pallas kernels for 17%

profile of v4, /device:TPU:0, one launch (start us, length us, event | category | flops | bytes accessed | tf_op | source)
XLA Modules:
  0.0 170.5 jit_solution(17591091943991411186)
XLA Ops:
  0.7 1.3 stack.157
  2.0 1.3 stack.161
  5.2 4.1 %collective-permute-start = (bf16[80,384]{1,0:T(8,128)(2,1)S(1)}, bf16[80,384]{1,0:T(8,128)(2,1)S(1)}, u32[]{:S(2)}, u32[]{:S(2)}) collective-permute-start(bf16[80,384]{1,0:T(8,128)(2,1)S(1)} %pad_maximum_fusion.37), channel_id=1, source_target_pairs={{0,8},{1,9},{2,10},{3,11},{4,12},{5,13},{6,14},{7,15},{8,0},{9,1},... | collective-permute-start | bytes 184328 | tf_op jit(solution)/shard_map/ppermute | solution.py:24
  9.4 2.7 %collective-permute-done = bf16[80,384]{1,0:T(8,128)(2,1)S(1)} collective-permute-done((bf16[80,384]{1,0:T(8,128)(2,1)S(1)}, bf16[80,384]{1,0:T(8,128)(2,1)S(1)}, u32[]{:S(2)}, u32[]{:S(2)}) %collective-permute-start) | collective-permute-done | bytes 61472 | tf_op jit(solution)/shard_map/ppermute | solution.py:24
  12.3 2.7 %collective-permute-start.1 = (bf16[416,384]{1,0:T(8,128)(2,1)S(1)}, bf16[416,384]{1,0:T(8,128)(2,1)S(1)}, u32[]{:S(2)}, u32[]{:S(2)}) collective-permute-start(bf16[416,384]{1,0:T(8,128)(2,1)S(1)} %pad_maximum_fusion.20), channel_id=1, source_target_pairs={{0,4},{1,5},{2,6},{3,7},{4,0},{5,1},{6,2},{7,3},{8,12},{9,13},{10,... | collective-permute-start | bytes 958472 | tf_op jit(solution)/shard_map/ppermute | solution.py:24
  15.1 2.3 %collective-permute-start.5 = (bf16[416,384]{1,0:T(8,128)(2,1)S(1)}, bf16[416,384]{1,0:T(8,128)(2,1)S(1)}, u32[]{:S(2)}, u32[]{:S(2)}) collective-permute-start(bf16[416,384]{1,0:T(8,128)(2,1)S(1)} %pad_maximum_fusion.21), channel_id=1, source_target_pairs={{0,2},{1,3},{2,0},{3,1},{4,6},{5,7},{6,4},{7,5},{8,10},{9,11},{10,... | collective-permute-start | bytes 958472 | tf_op jit(solution)/shard_map/ppermute | solution.py:24
  17.3 5.2 %collective-permute-done.1 = bf16[416,384]{1,0:T(8,128)(2,1)S(1)} collective-permute-done((bf16[416,384]{1,0:T(8,128)(2,1)S(1)}, bf16[416,384]{1,0:T(8,128)(2,1)S(1)}, u32[]{:S(2)}, u32[]{:S(2)}) %collective-permute-start.1) | collective-permute-done | bytes 319520 | tf_op jit(solution)/shard_map/ppermute | solution.py:24
  22.9 1.6 collective-permute-start.2
  24.8 1.8 %collective-permute-start.6 = (bf16[832,384]{1,0:T(8,128)(2,1)S(1)}, bf16[832,384]{1,0:T(8,128)(2,1)S(1)}, u32[]{:S(2)}, u32[]{:S(2)}) collective-permute-start(bf16[832,384]{1,0:T(8,128)(2,1)S(1)} %pad_maximum_fusion.13), channel_id=1, source_target_pairs={{0,4},{1,5},{2,6},{3,7},{4,0},{5,1},{6,2},{7,3},{8,12},{9,13},{10,... | collective-permute-start | bytes 1916936 | tf_op jit(solution)/shard_map/ppermute | solution.py:24
  26.6 12.0 %collective-permute-done.2 = bf16[832,384]{1,0:T(8,128)(2,1)S(1)} collective-permute-done((bf16[832,384]{1,0:T(8,128)(2,1)S(1)}, bf16[832,384]{1,0:T(8,128)(2,1)S(1)}, u32[]{:S(2)}, u32[]{:S(2)}) %collective-permute-start.2) | collective-permute-done | bytes 639008 | tf_op jit(solution)/shard_map/ppermute | solution.py:24
  40.0 0.7 fusion.50
  41.5 0.8 fusion.37
  43.1 1.1 fusion.41
  44.3 1.2 pad_maximum_fusion.5
  46.4 1.0 copy.74
  47.7 1.4 copy.72
  49.1 14.6 %shard_map.84 = (bf16[128,384]{1,0:T(8,128)(2,1)}, bf16[128,384]{1,0:T(8,128)(2,1)}, f32[2,1024,384]{2,1,0:T(8,128)}, f32[2,512,384]{2,1,0:T(8,128)}, f32[2,128,384]{2,1,0:T(8,128)}) custom-call(s32[3,12]{1,0:T(4,128)} %offsets_ref.3, bf16[128,384]{1,0:T(8,128)(2,1)} %get-tuple-element.60.query_ref, bf16[128,384]{1,0:T(8,128)(2,1)} %get-tuple-element.58.grad_ref, ...), custom_call_target="tpu_custom_call" | custom-call | tf_op jit(solution)/shard_map/pallas_call | solution.py:194
  63.7 1.7 slice.471
  65.4 0.7 fusion.46
  66.1 1.1 fusion.44
  67.2 1.6 pad_maximum_fusion
  69.3 0.9 slice.469
  71.0 1.0 slice.468
  72.1 1.0 copy.93
  73.2 1.2 slice.467
  74.6 1.3 copy.91
  75.9 14.4 %shard_map.85 = (bf16[128,384]{1,0:T(8,128)(2,1)}, bf16[128,384]{1,0:T(8,128)(2,1)}, f32[2,1024,384]{2,1,0:T(8,128)}, f32[2,512,384]{2,1,0:T(8,128)}, f32[2,128,384]{2,1,0:T(8,128)}) custom-call(s32[3,12]{1,0:T(4,128)} %offsets_ref.3, bf16[128,384]{1,0:T(8,128)(2,1)} %get-tuple-element.61.query_ref, bf16[128,384]{1,0:T(8,128)(2,1)} %get-tuple-element.59.grad_ref, ...), custom_call_target="tpu_custom_call" | custom-call | tf_op jit(solution)/shard_map/pallas_call | solution.py:194
  90.4 1.0 fusion.47
  91.4 1.7 fusion.45
  94.8 1.7 slice.474
  97.3 1.8 %slice.478 = f32[512,384]{1,0:T(8,128)S(1)} slice(f32[1664,384]{1,0:T(8,128)} %collective-permute-done.8), slice={[1024:1536], [0:384]} | slice | bytes 1572864 | tf_op jit(solution)/shard_map/slice | solution.py:232
  99.3 0.9 copy-done.8
  100.3 1.0 slice.481
  101.6 1.1 pad_maximum_fusion.6
  102.7 1.0 collective-permute-start.9
  104.3 1.0 copy-done.10
  105.4 1.2 pad_maximum_fusion.7
  106.6 1.9 %collective-permute-start.13 = (f32[832,384]{1,0:T(8,128)}, f32[832,384]{1,0:T(8,128)}, u32[]{:S(2)}, u32[]{:S(2)}) collective-permute-start(f32[832,384]{1,0:T(8,128)} %pad_maximum_fusion.7), channel_id=1, source_target_pairs={{0,4},{1,5},{2,6},{3,7},{4,0},{5,1},{6,2},{7,3},{8,12},{9,13},{10,... | collective-permute-start | bytes 3833864 | tf_op jit(solution)/shard_map/ppermute | solution.py:24
  108.7 0.8 broadcast_in_dim.131
  109.5 0.8 broadcast_in_dim.124
  110.3 1.9 %broadcast_in_dim.125 = pred[128,384]{1,0:T(8,128)(4,1)} reshape(pred[32,4,6,64]{3,2,1,0:T(8,128)(4,1)} %broadcast_in_dim.124) | data formatting | bytes 98304 | tf_op jit(solution)/shard_map/jit(_where)/broadcast_in_dim | solution.py:49
  112.1 0.8 broadcast_in_dim.140
  112.9 1.7 %broadcast_in_dim.141 = pred[128,384]{1,0:T(8,128)(4,1)} reshape(pred[8,16,6,64]{3,2,1,0:T(8,128)(4,1)} %broadcast_in_dim.140) | data formatting | bytes 98304 | tf_op jit(solution)/shard_map/jit(_where)/broadcast_in_dim | solution.py:49
  114.6 0.8 broadcast_in_dim.135
  115.4 1.7 %broadcast_in_dim.136 = pred[128,384]{1,0:T(8,128)(4,1)} reshape(pred[32,4,6,64]{3,2,1,0:T(8,128)(4,1)} %broadcast_in_dim.135) | data formatting | bytes 98304 | tf_op jit(solution)/shard_map/jit(_where)/broadcast_in_dim | solution.py:49
  117.1 1.8 %pad_maximum_fusion.27 = (bf16[128,768]{1,0:T(8,128)(2,1)}, bf16[128,768]{1,0:T(8,128)(2,1)}) fusion(bf16[128,384]{1,0:T(8,128)(2,1)} %get-tuple-element.15, bf16[128,384]{1,0:T(8,128)(2,1)} %get-tuple-element.14, bf16[128,384]{1,0:T(8,128)(2,1)} %get-tuple-element.17, bf16[128,384]{1,0:T(8,128)(2,1)} %get-tuple-element.16), kind=kLoop, calls=%fused_computation.64 | loop fusion | flops 786432 | bytes 786432 | tf_op jit(solution)/shard_map/concatenate | solution.py:243
  118.9 14.2 %collective-permute-done.9 = f32[832,384]{1,0:T(8,128)} collective-permute-done((f32[832,384]{1,0:T(8,128)}, f32[832,384]{1,0:T(8,128)}, u32[]{:S(2)}, u32[]{:S(2)}) %collective-permute-start.9) | collective-permute-done | bytes 1277984 | tf_op jit(solution)/shard_map/ppermute | solution.py:24
  133.1 1.2 slice.483
  134.4 1.4 slice.487
  135.9 0.9 slice.490
  136.9 1.5 collective-permute-start.10
  138.4 1.2 slice.517
  139.7 1.4 slice.521
  141.2 0.9 slice.524
  142.2 1.6 collective-permute-start.14
  143.7 8.7 %collective-permute-done.10 = f32[416,384]{1,0:T(8,128)S(1)} collective-permute-done((f32[416,384]{1,0:T(8,128)S(1)}, f32[416,384]{1,0:T(8,128)S(1)}, u32[]{:S(2)}, u32[]{:S(2)}) %collective-permute-start.10) | collective-permute-done | bytes 639008 | tf_op jit(solution)/shard_map/ppermute | solution.py:24
  152.6 3.4 %collective-permute-start.11 = (f32[80,384]{1,0:T(8,128)S(1)}, f32[80,384]{1,0:T(8,128)S(1)}, u32[]{:S(2)}, u32[]{:S(2)}) collective-permute-start(f32[80,384]{1,0:T(8,128)S(1)} %pad_maximum_fusion.31), channel_id=1, source_target_pairs={{0,8},{1,9},{2,10},{3,11},{4,12},{5,13},{6,14},{7,15},{8,0},{9,1},... | collective-permute-start | bytes 368648 | tf_op jit(solution)/shard_map/ppermute | solution.py:24
  156.1 1.4 collective-permute-done.14
  158.4 3.4 %collective-permute-start.15 = (f32[80,384]{1,0:T(8,128)}, f32[80,384]{1,0:T(8,128)}, u32[]{:S(2)}, u32[]{:S(2)}) collective-permute-start(f32[80,384]{1,0:T(8,128)} %pad_maximum_fusion.32), channel_id=1, source_target_pairs={{0,8},{1,9},{2,10},{3,11},{4,12},{5,13},{6,14},{7,15},{8,0},{9,1},... | collective-permute-start | bytes 368648 | tf_op jit(solution)/shard_map/ppermute | solution.py:24
  162.9 0.8 slice.502
  164.2 0.9 fusion.17
  165.1 1.2 collective-permute-done.15
  166.3 0.9 slice.534
  167.7 0.8 slice.536
  (235 shorter events, 17.5 us)
Async XLA Ops:
  0.6 2.6 %copy-start.14 = (bf16[128,768]{1,0:T(8,128)(2,1)S(1)}, bf16[128,768]{1,0:T(8,128)(2,1)}, u32[]{:S(2)}) copy-start(bf16[128,768]{1,0:T(8,128)(2,1)} %param.7) | copy-start | bytes 589828
  0.6 3.3 %copy-start.29 = (s32[3,12]{1,0:T(4,128)S(1)}, s32[3,12]{1,0:T(4,128)}, u32[]{:S(2)}) copy-start(s32[3,12]{1,0:T(4,128)} %offsets_ref.3) | copy-start | bytes 436
  3.9 5.5 %copy-start.15 = (bf16[128,768]{1,0:T(8,128)(2,1)S(1)}, bf16[128,768]{1,0:T(8,128)(2,1)}, u32[]{:S(2)}) copy-start(bf16[128,768]{1,0:T(8,128)(2,1)} %param.6) | copy-start | bytes 589828
  5.2 7.0 %collective-permute-start = (bf16[80,384]{1,0:T(8,128)(2,1)S(1)}, bf16[80,384]{1,0:T(8,128)(2,1)S(1)}, u32[]{:S(2)}, u32[]{:S(2)}) collective-permute-start(bf16[80,384]{1,0:T(8,128)(2,1)S(1)} %pad_maximum_fusion.37), channel_id=1, source_target_pairs={{0,8},{1,9},{2,10},{3,11},{4,12},{5,13},{6,14},{7,15},{8,0},{9,1},... | collective-permute-start | bytes 184328 | tf_op jit(solution)/shard_map/ppermute | solution.py:24
  9.3 5.6 %collective-permute-start.4 = (bf16[80,384]{1,0:T(8,128)(2,1)S(1)}, bf16[80,384]{1,0:T(8,128)(2,1)S(1)}, u32[]{:S(2)}, u32[]{:S(2)}) collective-permute-start(bf16[80,384]{1,0:T(8,128)(2,1)S(1)} %pad_maximum_fusion.38), channel_id=1, source_target_pairs={{0,8},{1,9},{2,10},{3,11},{4,12},{5,13},{6,14},{7,15},{8,0},{9,1},... | collective-permute-start | bytes 184328 | tf_op jit(solution)/shard_map/ppermute | solution.py:24
  12.3 10.3 %collective-permute-start.1 = (bf16[416,384]{1,0:T(8,128)(2,1)S(1)}, bf16[416,384]{1,0:T(8,128)(2,1)S(1)}, u32[]{:S(2)}, u32[]{:S(2)}) collective-permute-start(bf16[416,384]{1,0:T(8,128)(2,1)S(1)} %pad_maximum_fusion.20), channel_id=1, source_target_pairs={{0,4},{1,5},{2,6},{3,7},{4,0},{5,1},{6,2},{7,3},{8,12},{9,13},{10,... | collective-permute-start | bytes 958472 | tf_op jit(solution)/shard_map/ppermute | solution.py:24
  15.1 9.4 %collective-permute-start.5 = (bf16[416,384]{1,0:T(8,128)(2,1)S(1)}, bf16[416,384]{1,0:T(8,128)(2,1)S(1)}, u32[]{:S(2)}, u32[]{:S(2)}) collective-permute-start(bf16[416,384]{1,0:T(8,128)(2,1)S(1)} %pad_maximum_fusion.21), channel_id=1, source_target_pairs={{0,2},{1,3},{2,0},{3,1},{4,6},{5,7},{6,4},{7,5},{8,10},{9,11},{10,... | collective-permute-start | bytes 958472 | tf_op jit(solution)/shard_map/ppermute | solution.py:24
  22.9 15.7 %collective-permute-start.2 = (bf16[832,384]{1,0:T(8,128)(2,1)S(1)}, bf16[832,384]{1,0:T(8,128)(2,1)S(1)}, u32[]{:S(2)}, u32[]{:S(2)}) collective-permute-start(bf16[832,384]{1,0:T(8,128)(2,1)S(1)} %pad_maximum_fusion.12), channel_id=1, source_target_pairs={{0,2},{1,3},{2,0},{3,1},{4,6},{5,7},{6,4},{7,5},{8,10},{9,11},{10,... | collective-permute-start | bytes 1916936 | tf_op jit(solution)/shard_map/ppermute | solution.py:24
  24.8 16.6 %collective-permute-start.6 = (bf16[832,384]{1,0:T(8,128)(2,1)S(1)}, bf16[832,384]{1,0:T(8,128)(2,1)S(1)}, u32[]{:S(2)}, u32[]{:S(2)}) collective-permute-start(bf16[832,384]{1,0:T(8,128)(2,1)S(1)} %pad_maximum_fusion.13), channel_id=1, source_target_pairs={{0,4},{1,5},{2,6},{3,7},{4,0},{5,1},{6,2},{7,3},{8,12},{9,13},{10,... | collective-permute-start | bytes 1916936 | tf_op jit(solution)/shard_map/ppermute | solution.py:24
  39.1 0.9 copy-start.23
  39.1 1.6 copy-start.24
  39.3 6.2 %collective-permute-start.3 = (bf16[1664,384]{1,0:T(8,128)(2,1)S(1)}, bf16[1664,384]{1,0:T(8,128)(2,1)S(1)}, u32[]{:S(2)}, u32[]{:S(2)}) collective-permute-start(bf16[1664,384]{1,0:T(8,128)(2,1)S(1)} %pad_maximum_fusion.4), channel_id=1, source_target_pairs={{0,1},{1,0},{2,3},{3,2},{4,5},{5,4},{6,7},{7,6},{8,9},{9,8},{10,11... | collective-permute-start | bytes 3833864 | tf_op jit(solution)/shard_map/ppermute | solution.py:24
  45.5 23.8 %collective-permute-start.7 = (bf16[1664,384]{1,0:T(8,128)(2,1)}, bf16[1664,384]{1,0:T(8,128)(2,1)}, u32[]{:S(2)}, u32[]{:S(2)}) collective-permute-start(bf16[1664,384]{1,0:T(8,128)(2,1)} %pad_maximum_fusion.5), channel_id=1, source_target_pairs={{0,1},{1,0},{2,3},{3,2},{4,5},{5,4},{6,7},{7,6},{8,9},{9,8},{10,11... | collective-permute-start | bytes 3833864 | tf_op jit(solution)/shard_map/ppermute | solution.py:24
  63.7 1.7 copy-start.21
  63.7 2.4 %copy-start.16 = (f32[2,512,384]{2,1,0:T(8,128)S(1)}, f32[2,512,384]{2,1,0:T(8,128)}, u32[]{:S(2)}) copy-start(f32[2,512,384]{2,1,0:T(8,128)} %get-tuple-element.19) | copy-start | bytes 4718596
  67.2 3.1 %copy-start.22 = (bf16[2,1,2,2,2,8,384]{6,5,0,4,3,2,1:T(8,128)(2,1)S(1)}, bf16[2,1,2,2,2,8,384]{6,5,0,4,3,2,1:T(8,128)(2,1)}, u32[]{:S(2)}) copy-start(bf16[2,1,2,2,2,8,384]{6,5,0,4,3,2,1:T(8,128)(2,1)} %get-tuple-element.72) | copy-start | bytes 294916
  68.8 3.2 %copy-start.19 = (bf16[2,1,2,2,2,32,384]{6,5,0,4,3,2,1:T(8,128)(2,1)S(1)}, bf16[2,1,2,2,2,32,384]{6,5,0,4,3,2,1:T(8,128)(2,1)}, u32[]{:S(2)}) copy-start(bf16[2,1,2,2,2,32,384]{6,5,0,4,3,2,1:T(8,128)(2,1)} %get-tuple-element.44) | copy-start | bytes 1179652
  68.8 26.0 %collective-permute-start.8 = (f32[1664,384]{1,0:T(8,128)}, f32[1664,384]{1,0:T(8,128)}, u32[]{:S(2)}, u32[]{:S(2)}) collective-permute-start(f32[1664,384]{1,0:T(8,128)} %pad_maximum_fusion), channel_id=1, source_target_pairs={{0,1},{1,0},{2,3},{3,2},{4,5},{5,4},{6,7},{7,6},{8,9},{9,8},{10,11... | collective-permute-start | bytes 7667720 | tf_op jit(solution)/shard_map/ppermute | solution.py:24
  72.1 2.3 %copy-start.12 = (bf16[2,1,2,2,128,384]{5,4,0,3,2,1:T(8,128)(2,1)S(1)}, bf16[2,1,2,2,128,384]{5,4,0,3,2,1:T(8,128)(2,1)}, u32[]{:S(2)}) copy-start(bf16[2,1,2,2,128,384]{5,4,0,3,2,1:T(8,128)(2,1)} %get-tuple-element.32) | copy-start | bytes 2359300
  91.4 2.4 %copy-start.2 = (f32[2,1024,384]{2,1,0:T(8,128)S(1)}, f32[2,1024,384]{2,1,0:T(8,128)}, u32[]{:S(2)}) copy-start(f32[2,1024,384]{2,1,0:T(8,128)} %get-tuple-element.21) | copy-start | bytes 9437188
  94.0 0.7 copy-start.30
  94.2 9.5 %collective-permute-start.12 = (f32[1664,384]{1,0:T(8,128)S(1)}, f32[1664,384]{1,0:T(8,128)S(1)}, u32[]{:S(2)}, u32[]{:S(2)}) collective-permute-start(f32[1664,384]{1,0:T(8,128)S(1)} %pad_maximum_fusion.1), channel_id=1, source_target_pairs={{0,1},{1,0},{2,3},{3,2},{4,5},{5,4},{6,7},{7,6},{8,9},{9,8},{10,11... | collective-permute-start | bytes 7667720 | tf_op jit(solution)/shard_map/ppermute | solution.py:24
  94.8 2.4 %copy-start.7 = (f32[2,1024,384]{2,1,0:T(8,128)S(1)}, f32[2,1024,384]{2,1,0:T(8,128)}, u32[]{:S(2)}) copy-start(f32[2,1024,384]{2,1,0:T(8,128)} %get-tuple-element.18) | copy-start | bytes 9437188
  97.3 1.8 %copy-start = (f32[2,2,2,128,384]{4,3,2,1,0:T(8,128)}, f32[2,2,2,128,384]{4,3,2,1,0:T(8,128)S(1)}, u32[]{:S(2)}) copy-start(f32[2,2,2,128,384]{4,3,2,1,0:T(8,128)S(1)} %fusion) | copy-start | bytes 4718596
  97.3 1.9 %copy-start.13 = (f32[2,1,2,2,2,32,384]{6,5,4,3,2,1,0:T(8,128)S(1)}, f32[2,1,2,2,2,32,384]{6,5,4,3,2,1,0:T(8,128)}, u32[]{:S(2)}) copy-start(f32[2,1,2,2,2,32,384]{6,5,4,3,2,1,0:T(8,128)} %get-tuple-element.26) | copy-start | bytes 2359300
  99.3 0.9 copy-start.8
  100.2 1.1 copy-start.20
  100.2 1.3 slice-start
  102.7 30.4 %collective-permute-start.9 = (f32[832,384]{1,0:T(8,128)}, f32[832,384]{1,0:T(8,128)}, u32[]{:S(2)}, u32[]{:S(2)}) collective-permute-start(f32[832,384]{1,0:T(8,128)} %pad_maximum_fusion.6), channel_id=1, source_target_pairs={{0,2},{1,3},{2,0},{3,1},{4,6},{5,7},{6,4},{7,5},{8,10},{9,11},{10,... | collective-permute-start | bytes 3833864 | tf_op jit(solution)/shard_map/ppermute | solution.py:24
  104.3 1.0 copy-start.10
  106.6 31.8 %collective-permute-start.13 = (f32[832,384]{1,0:T(8,128)}, f32[832,384]{1,0:T(8,128)}, u32[]{:S(2)}, u32[]{:S(2)}) collective-permute-start(f32[832,384]{1,0:T(8,128)} %pad_maximum_fusion.7), channel_id=1, source_target_pairs={{0,4},{1,5},{2,6},{3,7},{4,0},{5,1},{6,2},{7,3},{8,12},{9,13},{10,... | collective-permute-start | bytes 3833864 | tf_op jit(solution)/shard_map/ppermute | solution.py:24
  110.3 24.0 %copy-start.1 = (f32[2,2,2,128,384]{4,3,2,1,0:T(8,128)S(1)}, f32[2,2,2,128,384]{4,3,2,1,0:T(8,128)}, u32[]{:S(2)}) copy-start(f32[2,2,2,128,384]{4,3,2,1,0:T(8,128)} %copy-done) | copy-start | bytes 4718596
  134.3 1.5 copy-start.9
  134.4 1.5 copy-start.5
  136.9 15.6 %collective-permute-start.10 = (f32[416,384]{1,0:T(8,128)S(1)}, f32[416,384]{1,0:T(8,128)S(1)}, u32[]{:S(2)}, u32[]{:S(2)}) collective-permute-start(f32[416,384]{1,0:T(8,128)S(1)} %pad_maximum_fusion.14), channel_id=1, source_target_pairs={{0,4},{1,5},{2,6},{3,7},{4,0},{5,1},{6,2},{7,3},{8,12},{9,13},{10,... | collective-permute-start | bytes 1916936 | tf_op jit(solution)/shard_map/ppermute | solution.py:24
  139.6 1.5 copy-start.11
  139.7 1.5 copy-start.3
  142.2 15.3 %collective-permute-start.14 = (f32[416,384]{1,0:T(8,128)S(1)}, f32[416,384]{1,0:T(8,128)S(1)}, u32[]{:S(2)}, u32[]{:S(2)}) collective-permute-start(f32[416,384]{1,0:T(8,128)S(1)} %pad_maximum_fusion.15), channel_id=1, source_target_pairs={{0,2},{1,3},{2,0},{3,1},{4,6},{5,7},{6,4},{7,5},{8,10},{9,11},{10,... | collective-permute-start | bytes 1916936 | tf_op jit(solution)/shard_map/ppermute | solution.py:24
  152.5 9.5 %copy-start.18 = (f32[416,384]{1,0:T(8,128)}, f32[416,384]{1,0:T(8,128)S(1)}, u32[]{:S(2)}) copy-start(f32[416,384]{1,0:T(8,128)S(1)} %collective-permute-done.10) | copy-start | bytes 1916932
  152.6 9.4 %collective-permute-start.11 = (f32[80,384]{1,0:T(8,128)S(1)}, f32[80,384]{1,0:T(8,128)S(1)}, u32[]{:S(2)}, u32[]{:S(2)}) collective-permute-start(f32[80,384]{1,0:T(8,128)S(1)} %pad_maximum_fusion.31), channel_id=1, source_target_pairs={{0,8},{1,9},{2,10},{3,11},{4,12},{5,13},{6,14},{7,15},{8,0},{9,1},... | collective-permute-start | bytes 368648 | tf_op jit(solution)/shard_map/ppermute | solution.py:24
  157.5 4.5 %copy-start.17 = (f32[416,384]{1,0:T(8,128)}, f32[416,384]{1,0:T(8,128)S(1)}, u32[]{:S(2)}) copy-start(f32[416,384]{1,0:T(8,128)S(1)} %collective-permute-done.14) | copy-start | bytes 1916932
  158.4 7.9 %collective-permute-start.15 = (f32[80,384]{1,0:T(8,128)}, f32[80,384]{1,0:T(8,128)}, u32[]{:S(2)}, u32[]{:S(2)}) collective-permute-start(f32[80,384]{1,0:T(8,128)} %pad_maximum_fusion.32), channel_id=1, source_target_pairs={{0,8},{1,9},{2,10},{3,11},{4,12},{5,13},{6,14},{7,15},{8,0},{9,1},... | collective-permute-start | bytes 368648 | tf_op jit(solution)/shard_map/ppermute | solution.py:24
  162.0 0.7 copy-start.28
  162.9 1.3 copy-start.6
  162.9 1.3 slice-start.2
  162.9 1.3 copy-start.27
  167.7 1.3 copy-start.4
  167.7 1.3 slice-start.1
  167.7 1.3 copy-start.25
  167.7 1.3 copy-start.26

commit v5 on v3

--- a/solution.py
+++ b/solution.py
@@ -181,9 +181,7 @@
             gathered_halves.append([buffers[branch].reshape(2, -1, half_width) for branch in range(3)])
             layouts.append(axis_bits)
 
-        results = []
-        for half in range(halves):
-            gathered = gathered_halves[half]
+        def run_kernel(half, gathered):
             cols = slice(half * half_width, (half + 1) * half_width)
             pairs = half_width // block_width
             row_block = pl.BlockSpec((local_rows, block_width), lambda p, offs: (0, p))
@@ -191,7 +189,7 @@
                 pl.BlockSpec((2, block.shape[1], block_width), lambda p, offs: (0, 0, p))
                 for block in gathered
             ]
-            outs = pl.pallas_call(
+            return pl.pallas_call(
                 attention_kernel(head_dim, score_scale, half * heads_per_half),
                 out_shape=(
                     jax.ShapeDtypeStruct((local_rows, half_width), jnp.bfloat16),
@@ -206,15 +204,9 @@
                 ),
                 compiler_params=pltpu.CompilerParams(vmem_limit_bytes=100 * 1024 * 1024),
             )(head_offsets, query_rows[:, cols], output_grad[:, cols], *gathered)
-            attended, query_grad = outs[:2]
-            terms = outs[2:]
-
-            axis_bits = [list(bits) for bits in layouts[half]]
-            partial = [
-                terms[branch].reshape((2,) + (2,) * branch_bits[branch] + (-1, half_width))
-                for branch in range(3)
-            ]
-            for bit in reversed(gather_order(top_bits, half == 1)):
+
+        def reduce_steps(partial, axis_bits, bits):
+            for bit in bits:
                 active = [branch for branch in range(3) if branch_bits[branch] > bit]
                 places = {branch: 1 + axis_bits[branch].index(bit) for branch in active}
                 outgoing = jnp.concatenate(
@@ -233,11 +225,37 @@
                     partial[branch] = kept + incoming[cursor : cursor + count].reshape(kept.shape)
                     cursor += count
                     axis_bits[branch].remove(bit)
+            return partial
+
+        kernel_outs = [None] * halves
+        partials = [None] * halves
+        axis_states = [None] * halves
+        reduce_orders = [list(reversed(gather_order(top_bits, half == 1))) for half in range(halves)]
+        for half in range(halves):
+            gathered = gathered_halves[half]
+            if half > 0:
+                partials[half - 1], gathered = lax.optimization_barrier(
+                    (partials[half - 1], gathered)
+                )
+            kernel_outs[half] = run_kernel(half, gathered)
+            terms = kernel_outs[half][2:]
+            axis_states[half] = [list(bits) for bits in layouts[half]]
+            partials[half] = [
+                terms[branch].reshape((2,) + (2,) * branch_bits[branch] + (-1, half_width))
+                for branch in range(3)
+            ]
+            partials[half] = reduce_steps(
+                partials[half], axis_states[half], reduce_orders[half][:1]
+            )
+        results = []
+        for half in range(halves):
+            partial = reduce_steps(partials[half], axis_states[half], reduce_orders[half][1:])
             offsets_half = head_offsets[:, half * heads_per_half : (half + 1) * heads_per_half]
             total_grad = None
             for branch in range(3):
                 spread = spread_rows(partial[branch], STRIDES[branch], offsets_half[branch])
                 total_grad = spread if total_grad is None else total_grad + spread
+            attended, query_grad = kernel_outs[half][:2]
             results.append((attended, query_grad, total_grad[0], total_grad[1]))
 
         return tuple(

time: 149 us -> 159 us (1.067)
  local copies, waits for them, and re-layouts: 40 us -> 47.8 us
    unnamed x52 -> x74, local copies, waits for them, and re-layouts: 3.59 us -> 10.7 us
    slice x53, local copies, waits for them, and re-layouts: 14.3 us -> 16.5 us  [the longest x22 9.4 us: reduce_steps(): partial[branch] = kept + incoming[cursor:cursor + count].reshape(kept.shape)]
  transfers between devices with their start and end apart: 16 -> 16, of which waited for: 8 -> 7; matrix products, arithmetic and copies ran while one was open for 29% -> 26% of each run, Pallas kernels for 20% -> 18%
where the time goes in v5:
time: 159 us; the launch traced here: 158 us
  local copies, waits for them, and re-layouts  47.8 us (30%)
  waiting for transfers between devices  40.9 us (26%)
  Pallas kernels  29 us (18%)
  starting transfers between devices  23.2 us (15%)
  other arithmetic  14.5 us (9%)
  between operations  2.09 us (1%)
    ppermute x16, waiting for transfers between devices, exchange(): return lax.ppermute(block, 'seq', route)  40.9 us
    pallas_call x2, Pallas kernels, run_kernel(): pl.pallas_call(attention_kernel(head_dim, score_scale, half * heads_per_h...  29 us
    ppermute x16, starting transfers between devices, exchange(): return lax.ppermute(block, 'seq', route)  23.2 us
    unnamed x74, local copies, waits for them, and re-layouts  10.7 us
    slice x22, local copies, waits for them, and re-layouts, reduce_steps(): partial[branch] = kept + incoming[cursor:cursor + count].reshape(kept.shape)  9.4 us
    another operation x25, local copies, waits for them, and re-layouts, per_device(): buffers[branch] = jnp.stack([buffers[branch], arrived], axis=1)  6.58 us
    slice x25, local copies, waits for them, and re-layouts, reduce_steps(): lax.index_in_dim(partial[branch], 1, places[branch], keepdims=False)  5.71 us
    broadcast_in_dim x16, local copies, waits for them, and re-layouts, spread_rows(): widened = jnp.where(chosen, grouped, jnp.zeros((), picked.dtype))  5.09 us
  transfers between devices with their start and end apart: 16, of which 7 were waited for; matrix products, arithmetic and copies ran while one was open for 26% of the time, Pallas kernels for 18%

profile of v5, /device:TPU:0, one launch (start us, length us, event | category | flops | bytes accessed | tf_op | source)
XLA Modules:
  0.0 157.5 jit_solution(10737327104639557478)
XLA Ops:
  0.7 1.3 stack.157
  2.0 1.3 stack.161
  5.2 4.1 %collective-permute-start.5 = (bf16[80,384]{1,0:T(8,128)(2,1)S(1)}, bf16[80,384]{1,0:T(8,128)(2,1)S(1)}, u32[]{:S(2)}, u32[]{:S(2)}) collective-permute-start(bf16[80,384]{1,0:T(8,128)(2,1)S(1)} %pad_maximum_fusion.36), channel_id=1, source_target_pairs={{0,8},{1,9},{2,10},{3,11},{4,12},{5,13},{6,14},{7,15},{8,0},{9,1},... | collective-permute-start | bytes 184328 | tf_op jit(solution)/shard_map/ppermute | solution.py:24
  9.4 5.4 %collective-permute-done = bf16[80,384]{1,0:T(8,128)(2,1)S(1)} collective-permute-done((bf16[80,384]{1,0:T(8,128)(2,1)S(1)}, bf16[80,384]{1,0:T(8,128)(2,1)S(1)}, u32[]{:S(2)}, u32[]{:S(2)}) %collective-permute-start) | collective-permute-done | bytes 61472 | tf_op jit(solution)/shard_map/ppermute | solution.py:24
  15.0 1.3 collective-permute-start.1
  16.4 1.6 %collective-permute-start.6 = (bf16[416,384]{1,0:T(8,128)(2,1)S(1)}, bf16[416,384]{1,0:T(8,128)(2,1)S(1)}, u32[]{:S(2)}, u32[]{:S(2)}) collective-permute-start(bf16[416,384]{1,0:T(8,128)(2,1)S(1)} %pad_maximum_fusion.19), channel_id=1, source_target_pairs={{0,2},{1,3},{2,0},{3,1},{4,6},{5,7},{6,4},{7,5},{8,10},{9,11},{10,... | collective-permute-start | bytes 958472 | tf_op jit(solution)/shard_map/ppermute | solution.py:24
  18.0 5.9 %collective-permute-done.1 = bf16[416,384]{1,0:T(8,128)(2,1)S(1)} collective-permute-done((bf16[416,384]{1,0:T(8,128)(2,1)S(1)}, bf16[416,384]{1,0:T(8,128)(2,1)S(1)}, u32[]{:S(2)}, u32[]{:S(2)}) %collective-permute-start.1) | collective-permute-done | bytes 319520 | tf_op jit(solution)/shard_map/ppermute | solution.py:24
  24.2 1.9 %collective-permute-start.2 = (bf16[832,384]{1,0:T(8,128)(2,1)S(1)}, bf16[832,384]{1,0:T(8,128)(2,1)S(1)}, u32[]{:S(2)}, u32[]{:S(2)}) collective-permute-start(bf16[832,384]{1,0:T(8,128)(2,1)S(1)} %pad_maximum_fusion.10), channel_id=1, source_target_pairs={{0,2},{1,3},{2,0},{3,1},{4,6},{5,7},{6,4},{7,5},{8,10},{9,11},{10,... | collective-permute-start | bytes 1916936 | tf_op jit(solution)/shard_map/ppermute | solution.py:24
  26.5 1.4 collective-permute-start.7
  27.9 11.3 %collective-permute-done.2 = bf16[832,384]{1,0:T(8,128)(2,1)S(1)} collective-permute-done((bf16[832,384]{1,0:T(8,128)(2,1)S(1)}, bf16[832,384]{1,0:T(8,128)(2,1)S(1)}, u32[]{:S(2)}, u32[]{:S(2)}) %collective-permute-start.2) | collective-permute-done | bytes 639008 | tf_op jit(solution)/shard_map/ppermute | solution.py:24
  42.1 0.8 fusion.36
  43.7 1.1 fusion.40
  44.9 1.2 pad_maximum_fusion.4
  46.2 0.7 copy.76
  47.1 1.0 copy.74
  48.4 1.3 copy.72
  49.7 14.7 %shard_map.84 = (bf16[128,384]{1,0:T(8,128)(2,1)}, bf16[128,384]{1,0:T(8,128)(2,1)}, f32[2,1024,384]{2,1,0:T(8,128)}, f32[2,512,384]{2,1,0:T(8,128)}, f32[2,128,384]{2,1,0:T(8,128)}) custom-call(s32[3,12]{1,0:T(4,128)} %offsets_ref.3, bf16[128,384]{1,0:T(8,128)(2,1)} %get-tuple-element.60.query_ref, bf16[128,384]{1,0:T(8,128)(2,1)} %get-tuple-element.58.grad_ref, ...), custom_call_target="tpu_custom_call" | custom-call | tf_op jit(solution)/shard_map/pallas_call | solution.py:192
  64.4 1.6 %slice.655 = bf16[2,1,2,2,128,384]{5,4,3,2,1,0:T(8,128)(2,1)S(1)} slice(f32[2,2,2,2,128,384]{5,4,3,2,1,0:T(8,128)} %bitcast.276), slice={[0:2], [1:2], [0:2], [0:2], [0:128], [0:384]} | slice | bytes 1572864 | tf_op jit(solution)/shard_map/slice | solution.py:214
  67.1 0.9 slice.500
  68.0 0.7 copy.100
  68.7 1.0 slice.499
  69.9 1.0 copy.98
  70.9 1.2 slice.498
  72.3 1.3 copy.96
  74.0 2.1 %copy-done.6 = f32[2,1024,384]{2,1,0:T(8,128)S(1)} copy-done((f32[2,1024,384]{2,1,0:T(8,128)S(1)}, f32[2,1024,384]{2,1,0:T(8,128)}, u32[]{:S(2)}) %copy-start.6) | copy-done | bytes 3145752
  76.3 1.2 copy-done
  77.7 0.9 pad_maximum_fusion.12
  78.5 1.5 collective-permute-start.9
  80.7 14.4 %shard_map.85 = (bf16[128,384]{1,0:T(8,128)(2,1)}, bf16[128,384]{1,0:T(8,128)(2,1)}, f32[2,1024,384]{2,1,0:T(8,128)}, f32[2,512,384]{2,1,0:T(8,128)}, f32[2,128,384]{2,1,0:T(8,128)}) custom-call(s32[3,12]{1,0:T(4,128)} %offsets_ref.3, bf16[128,384]{1,0:T(8,128)(2,1)} %get-tuple-element.61.query_ref, bf16[128,384]{1,0:T(8,128)(2,1)} %get-tuple-element.59.grad_ref, ...), custom_call_target="tpu_custom_call" | custom-call | tf_op jit(solution)/shard_map/pallas_call | solution.py:192
  95.0 1.5 slice.654
  96.5 1.2 slice.657
  97.7 0.9 slice.665
  98.9 1.2 slice.504
  100.4 1.0 slice.507
  101.5 0.7 copy-done.10
  102.3 0.8 slice.509
  103.2 0.8 pad_maximum_fusion.20
  103.9 2.1 %collective-permute-start.10 = (bf16[416,384]{1,0:T(8,128)(2,1)}, bf16[416,384]{1,0:T(8,128)(2,1)}, u32[]{:S(2)}, u32[]{:S(2)}) collective-permute-start(bf16[416,384]{1,0:T(8,128)(2,1)} %pad_maximum_fusion.20), channel_id=1, source_target_pairs={{0,4},{1,5},{2,6},{3,7},{4,0},{5,1},{6,2},{7,3},{8,12},{9,13},{10,... | collective-permute-start | bytes 958472 | tf_op jit(solution)/shard_map/ppermute | solution.py:24
  106.1 0.8 broadcast_in_dim.131
  107.1 0.8 broadcast_in_dim.125
  108.4 0.8 broadcast_in_dim.136
  109.2 5.1 %collective-permute-done.10 = bf16[416,384]{1,0:T(8,128)(2,1)} collective-permute-done((bf16[416,384]{1,0:T(8,128)(2,1)}, bf16[416,384]{1,0:T(8,128)(2,1)}, u32[]{:S(2)}, u32[]{:S(2)}) %collective-permute-start.10) | collective-permute-done | bytes 319520 | tf_op jit(solution)/shard_map/ppermute | solution.py:24
  114.3 0.9 slice.513
  115.3 1.8 %copy-done.5 = f32[2,1024,384]{2,1,0:T(8,128)S(1)} copy-done((f32[2,1024,384]{2,1,0:T(8,128)S(1)}, f32[2,1024,384]{2,1,0:T(8,128)}, u32[]{:S(2)}) %copy-start.5) | copy-done | bytes 3145752
  117.4 1.2 copy-done.14
  118.9 0.8 copy-done.22
  119.8 1.8 %collective-permute-start.13 = (bf16[832,384]{1,0:T(8,128)(2,1)S(1)}, bf16[832,384]{1,0:T(8,128)(2,1)S(1)}, u32[]{:S(2)}, u32[]{:S(2)}) collective-permute-start(bf16[832,384]{1,0:T(8,128)(2,1)S(1)} %pad_maximum_fusion.13), channel_id=1, source_target_pairs={{0,4},{1,5},{2,6},{3,7},{4,0},{5,1},{6,2},{7,3},{8,12},{9,13},{10,... | collective-permute-start | bytes 1916936 | tf_op jit(solution)/shard_map/ppermute | solution.py:24
  121.7 0.7 slice.517
  122.4 3.6 %collective-permute-start.11 = (bf16[80,384]{1,0:T(8,128)(2,1)S(1)}, bf16[80,384]{1,0:T(8,128)(2,1)S(1)}, u32[]{:S(2)}, u32[]{:S(2)}) collective-permute-start(bf16[80,384]{1,0:T(8,128)(2,1)S(1)} %pad_maximum_fusion.37), channel_id=1, source_target_pairs={{0,8},{1,9},{2,10},{3,11},{4,12},{5,13},{6,14},{7,15},{8,0},{9,1},... | collective-permute-start | bytes 184328 | tf_op jit(solution)/shard_map/ppermute | solution.py:24
  126.0 11.2 %collective-permute-done.13 = bf16[832,384]{1,0:T(8,128)(2,1)S(1)} collective-permute-done((bf16[832,384]{1,0:T(8,128)(2,1)S(1)}, bf16[832,384]{1,0:T(8,128)(2,1)S(1)}, u32[]{:S(2)}, u32[]{:S(2)}) %collective-permute-start.13) | collective-permute-done | bytes 639008 | tf_op jit(solution)/shard_map/ppermute | solution.py:24
  137.6 0.7 copy-done.12
  138.4 0.8 pad_maximum_fusion.21
  139.8 0.8 pad_maximum_fusion.27
  140.7 0.7 squeeze.92
  141.4 1.0 slice.511
  143.4 0.7 slice.521
  144.2 0.8 add.105
  145.2 1.0 broadcast_in_dim.134
  146.2 1.2 fusion.15
  147.8 0.9 slice.547
  148.8 0.7 slice.551
  149.5 2.4 %collective-permute-start.15 = (bf16[80,384]{1,0:T(8,128)(2,1)S(1)}, bf16[80,384]{1,0:T(8,128)(2,1)S(1)}, u32[]{:S(2)}, u32[]{:S(2)}) collective-permute-start(bf16[80,384]{1,0:T(8,128)(2,1)S(1)} %pad_maximum_fusion.38), channel_id=1, source_target_pairs={{0,8},{1,9},{2,10},{3,11},{4,12},{5,13},{6,14},{7,15},{8,0},{9,1},... | collective-permute-start | bytes 184328 | tf_op jit(solution)/shard_map/ppermute | solution.py:24
  152.2 1.0 slice.545
  153.2 1.6 %collective-permute-done.15 = bf16[80,384]{1,0:T(8,128)(2,1)S(1)} collective-permute-done((bf16[80,384]{1,0:T(8,128)(2,1)S(1)}, bf16[80,384]{1,0:T(8,128)(2,1)S(1)}, u32[]{:S(2)}, u32[]{:S(2)}) %collective-permute-start.15) | collective-permute-done | bytes 61472 | tf_op jit(solution)/shard_map/ppermute | solution.py:24
  (248 shorter events, 17.1 us)
Async XLA Ops:
  0.6 2.6 %copy-start.7 = (bf16[128,768]{1,0:T(8,128)(2,1)S(1)}, bf16[128,768]{1,0:T(8,128)(2,1)}, u32[]{:S(2)}) copy-start(bf16[128,768]{1,0:T(8,128)(2,1)} %param.7) | copy-start | bytes 589828
  0.6 3.3 %copy-start.31 = (s32[3,12]{1,0:T(4,128)S(1)}, s32[3,12]{1,0:T(4,128)}, u32[]{:S(2)}) copy-start(s32[3,12]{1,0:T(4,128)} %offsets_ref.3) | copy-start | bytes 436
  3.9 5.5 %copy-start.8 = (bf16[128,768]{1,0:T(8,128)(2,1)S(1)}, bf16[128,768]{1,0:T(8,128)(2,1)}, u32[]{:S(2)}) copy-start(bf16[128,768]{1,0:T(8,128)(2,1)} %param.6) | copy-start | bytes 589828
  5.2 11.0 %collective-permute-start.5 = (bf16[80,384]{1,0:T(8,128)(2,1)S(1)}, bf16[80,384]{1,0:T(8,128)(2,1)S(1)}, u32[]{:S(2)}, u32[]{:S(2)}) collective-permute-start(bf16[80,384]{1,0:T(8,128)(2,1)S(1)} %pad_maximum_fusion.36), channel_id=1, source_target_pairs={{0,8},{1,9},{2,10},{3,11},{4,12},{5,13},{6,14},{7,15},{8,0},{9,1},... | collective-permute-start | bytes 184328 | tf_op jit(solution)/shard_map/ppermute | solution.py:24
  9.3 5.5 %collective-permute-start = (bf16[80,384]{1,0:T(8,128)(2,1)S(1)}, bf16[80,384]{1,0:T(8,128)(2,1)S(1)}, u32[]{:S(2)}, u32[]{:S(2)}) collective-permute-start(bf16[80,384]{1,0:T(8,128)(2,1)S(1)} %pad_maximum_fusion.35), channel_id=1, source_target_pairs={{0,8},{1,9},{2,10},{3,11},{4,12},{5,13},{6,14},{7,15},{8,0},{9,1},... | collective-permute-start | bytes 184328 | tf_op jit(solution)/shard_map/ppermute | solution.py:24
  15.0 8.9 %collective-permute-start.1 = (bf16[416,384]{1,0:T(8,128)(2,1)S(1)}, bf16[416,384]{1,0:T(8,128)(2,1)S(1)}, u32[]{:S(2)}, u32[]{:S(2)}) collective-permute-start(bf16[416,384]{1,0:T(8,128)(2,1)S(1)} %pad_maximum_fusion.18), channel_id=1, source_target_pairs={{0,4},{1,5},{2,6},{3,7},{4,0},{5,1},{6,2},{7,3},{8,12},{9,13},{10,... | collective-permute-start | bytes 958472 | tf_op jit(solution)/shard_map/ppermute | solution.py:24
  16.4 9.8 %collective-permute-start.6 = (bf16[416,384]{1,0:T(8,128)(2,1)S(1)}, bf16[416,384]{1,0:T(8,128)(2,1)S(1)}, u32[]{:S(2)}, u32[]{:S(2)}) collective-permute-start(bf16[416,384]{1,0:T(8,128)(2,1)S(1)} %pad_maximum_fusion.19), channel_id=1, source_target_pairs={{0,2},{1,3},{2,0},{3,1},{4,6},{5,7},{6,4},{7,5},{8,10},{9,11},{10,... | collective-permute-start | bytes 958472 | tf_op jit(solution)/shard_map/ppermute | solution.py:24
  24.2 15.0 %collective-permute-start.2 = (bf16[832,384]{1,0:T(8,128)(2,1)S(1)}, bf16[832,384]{1,0:T(8,128)(2,1)S(1)}, u32[]{:S(2)}, u32[]{:S(2)}) collective-permute-start(bf16[832,384]{1,0:T(8,128)(2,1)S(1)} %pad_maximum_fusion.10), channel_id=1, source_target_pairs={{0,2},{1,3},{2,0},{3,1},{4,6},{5,7},{6,4},{7,5},{8,10},{9,11},{10,... | collective-permute-start | bytes 1916936 | tf_op jit(solution)/shard_map/ppermute | solution.py:24
  26.5 15.6 %collective-permute-start.7 = (bf16[832,384]{1,0:T(8,128)(2,1)S(1)}, bf16[832,384]{1,0:T(8,128)(2,1)S(1)}, u32[]{:S(2)}, u32[]{:S(2)}) collective-permute-start(bf16[832,384]{1,0:T(8,128)(2,1)S(1)} %pad_maximum_fusion.11), channel_id=1, source_target_pairs={{0,4},{1,5},{2,6},{3,7},{4,0},{5,1},{6,2},{7,3},{8,12},{9,13},{10,... | collective-permute-start | bytes 1916936 | tf_op jit(solution)/shard_map/ppermute | solution.py:24
  39.8 0.9 copy-start.24
  39.8 1.6 %copy-start.25 = (bf16[128,768]{1,0:T(8,128)(2,1)S(1)}, bf16[128,768]{1,0:T(8,128)(2,1)}, u32[]{:S(2)}) copy-start(bf16[128,768]{1,0:T(8,128)(2,1)} %param.5) | copy-start | bytes 589828
  39.9 6.2 %collective-permute-start.3 = (bf16[1664,384]{1,0:T(8,128)(2,1)S(1)}, bf16[1664,384]{1,0:T(8,128)(2,1)S(1)}, u32[]{:S(2)}, u32[]{:S(2)}) collective-permute-start(bf16[1664,384]{1,0:T(8,128)(2,1)S(1)} %pad_maximum_fusion.2), channel_id=1, source_target_pairs={{0,1},{1,0},{2,3},{3,2},{4,5},{5,4},{6,7},{7,6},{8,9},{9,8},{10,11... | collective-permute-start | bytes 3833864 | tf_op jit(solution)/shard_map/ppermute | solution.py:24
  46.1 20.9 %collective-permute-start.8 = (bf16[1664,384]{1,0:T(8,128)(2,1)}, bf16[1664,384]{1,0:T(8,128)(2,1)}, u32[]{:S(2)}, u32[]{:S(2)}) collective-permute-start(bf16[1664,384]{1,0:T(8,128)(2,1)} %pad_maximum_fusion.4), channel_id=1, source_target_pairs={{0,1},{1,0},{2,3},{3,2},{4,5},{5,4},{6,7},{7,6},{8,9},{9,8},{10,11... | collective-permute-start | bytes 3833864 | tf_op jit(solution)/shard_map/ppermute | solution.py:24
  64.4 1.9 %copy-start.15 = (f32[2,512,384]{2,1,0:T(8,128)S(1)}, f32[2,512,384]{2,1,0:T(8,128)}, u32[]{:S(2)}) copy-start(f32[2,512,384]{2,1,0:T(8,128)} %get-tuple-element.22) | copy-start | bytes 4718596
  64.4 2.0 %copy-start.23 = (f32[2,128,384]{2,1,0:T(8,128)S(1)}, f32[2,128,384]{2,1,0:T(8,128)}, u32[]{:S(2)}) copy-start(f32[2,128,384]{2,1,0:T(8,128)} %get-tuple-element.23) | copy-start | bytes 1179652
  66.3 1.7 %copy-start.18 = (bf16[2,1,2,2,2,8,384]{6,5,0,4,3,2,1:T(8,128)(2,1)S(1)}, bf16[2,1,2,2,2,8,384]{6,5,0,4,3,2,1:T(8,128)(2,1)}, u32[]{:S(2)}) copy-start(bf16[2,1,2,2,2,8,384]{6,5,0,4,3,2,1:T(8,128)(2,1)} %get-tuple-element.62) | copy-start | bytes 294916
  66.4 3.4 %copy-start.9 = (bf16[2,1,2,2,2,32,384]{6,5,0,4,3,2,1:T(8,128)(2,1)S(1)}, bf16[2,1,2,2,2,32,384]{6,5,0,4,3,2,1:T(8,128)(2,1)}, u32[]{:S(2)}) copy-start(bf16[2,1,2,2,2,32,384]{6,5,0,4,3,2,1:T(8,128)(2,1)} %get-tuple-element.40) | copy-start | bytes 1179652
  66.5 7.2 %collective-permute-start.4 = (bf16[1664,384]{1,0:T(8,128)(2,1)S(1)}, bf16[1664,384]{1,0:T(8,128)(2,1)S(1)}, u32[]{:S(2)}, u32[]{:S(2)}) collective-permute-start(bf16[1664,384]{1,0:T(8,128)(2,1)S(1)} %pad_maximum_fusion.3), channel_id=1, source_target_pairs={{0,1},{1,0},{2,3},{3,2},{4,5},{5,4},{6,7},{7,6},{8,9},{9,8},{10,11... | collective-permute-start | bytes 3833864 | tf_op jit(solution)/shard_map/ppermute | solution.py:24
  69.9 2.3 %copy-start.2 = (bf16[2,1,2,2,128,384]{5,4,0,3,2,1:T(8,128)(2,1)S(1)}, bf16[2,1,2,2,128,384]{5,4,0,3,2,1:T(8,128)(2,1)}, u32[]{:S(2)}) copy-start(bf16[2,1,2,2,128,384]{5,4,0,3,2,1:T(8,128)(2,1)} %get-tuple-element.36) | copy-start | bytes 2359300
  73.7 3.9 %copy-start.16 = (f32[2,2,2,2,8,384]{5,4,3,0,2,1:T(8,128)}, f32[2,2,2,2,8,384]{5,4,3,0,2,1:T(8,128)S(1)}, u32[]{:S(2)}) copy-start(f32[2,2,2,2,8,384]{5,4,3,0,2,1:T(8,128)S(1)} %fusion.20) | copy-start | bytes 589828
  73.9 3.6 %copy-start.3 = (f32[2,2,2,2,32,384]{5,4,3,0,2,1:T(8,128)}, f32[2,2,2,2,32,384]{5,4,3,0,2,1:T(8,128)S(1)}, u32[]{:S(2)}) copy-start(f32[2,2,2,2,32,384]{5,4,3,0,2,1:T(8,128)S(1)} %fusion.6) | copy-start | bytes 2359300
  73.9 2.2 %copy-start.6 = (f32[2,1024,384]{2,1,0:T(8,128)S(1)}, f32[2,1024,384]{2,1,0:T(8,128)}, u32[]{:S(2)}) copy-start(f32[2,1024,384]{2,1,0:T(8,128)} %get-tuple-element.21) | copy-start | bytes 9437188
  76.3 1.2 copy-start
  76.3 3.8 %copy-start.32 = (s32[3,12]{1,0:T(4,128)S(1)}, s32[3,12]{1,0:T(4,128)}, u32[]{:S(2)}) copy-start(s32[3,12]{1,0:T(4,128)} %offsets_ref.3) | copy-start | bytes 436
  78.5 20.4 %collective-permute-start.9 = (bf16[832,384]{1,0:T(8,128)(2,1)}, bf16[832,384]{1,0:T(8,128)(2,1)}, u32[]{:S(2)}, u32[]{:S(2)}) collective-permute-start(bf16[832,384]{1,0:T(8,128)(2,1)} %pad_maximum_fusion.12), channel_id=1, source_target_pairs={{0,2},{1,3},{2,0},{3,1},{4,6},{5,7},{6,4},{7,5},{8,10},{9,11},{10,... | collective-permute-start | bytes 1916936 | tf_op jit(solution)/shard_map/ppermute | solution.py:24
  98.7 1.5 copy-start.1
  98.8 16.4 %collective-permute-start.12 = (bf16[1664,384]{1,0:T(8,128)(2,1)S(1)}, bf16[1664,384]{1,0:T(8,128)(2,1)S(1)}, u32[]{:S(2)}, u32[]{:S(2)}) collective-permute-start(bf16[1664,384]{1,0:T(8,128)(2,1)S(1)} %pad_maximum_fusion.5), channel_id=1, source_target_pairs={{0,1},{1,0},{2,3},{3,2},{4,5},{5,4},{6,7},{7,6},{8,9},{9,8},{10,11... | collective-permute-start | bytes 3833864 | tf_op jit(solution)/shard_map/ppermute | solution.py:24
  100.2 1.2 copy-start.4
  100.3 2.8 %copy-start.17 = (f32[2,2,2,2,8,384]{5,4,3,0,2,1:T(8,128)S(1)}, f32[2,2,2,2,8,384]{5,4,3,0,2,1:T(8,128)}, u32[]{:S(2)}) copy-start(f32[2,2,2,2,8,384]{5,4,3,0,2,1:T(8,128)} %copy-done.16) | copy-start | bytes 589828
  100.4 5.6 %copy-start.33 = (s32[6]{0:T(128)S(1)}, s32[6]{0:T(128)}, u32[]{:S(2)}) copy-start(s32[6]{0:T(128)} %get-tuple-element.87) | copy-start | bytes 76
  100.4 5.6 %copy-start.34 = (s32[6]{0:T(128)S(1)}, s32[6]{0:T(128)}, u32[]{:S(2)}) copy-start(s32[6]{0:T(128)} %get-tuple-element.88) | copy-start | bytes 76
  101.4 5.5 %copy-start.35 = (s32[6]{0:T(128)S(1)}, s32[6]{0:T(128)}, u32[]{:S(2)}) copy-start(s32[6]{0:T(128)} %get-tuple-element.86) | copy-start | bytes 76
  101.4 5.5 %copy-start.36 = (s32[6]{0:T(128)S(1)}, s32[6]{0:T(128)}, u32[]{:S(2)}) copy-start(s32[6]{0:T(128)} %get-tuple-element.89) | copy-start | bytes 76
  101.5 0.7 copy-start.10
  103.1 2.9 %copy-start.19 = (f32[2,2,2,8,384]{4,3,2,0,1:T(8,128)}, f32[2,2,2,8,384]{4,3,2,0,1:T(8,128)S(1)}, u32[]{:S(2)}) copy-start(f32[2,2,2,8,384]{4,3,2,0,1:T(8,128)S(1)} %bitcast_add_fusion.2) | copy-start | bytes 294916
  103.9 10.4 %collective-permute-start.10 = (bf16[416,384]{1,0:T(8,128)(2,1)}, bf16[416,384]{1,0:T(8,128)(2,1)}, u32[]{:S(2)}, u32[]{:S(2)}) collective-permute-start(bf16[416,384]{1,0:T(8,128)(2,1)} %pad_maximum_fusion.20), channel_id=1, source_target_pairs={{0,4},{1,5},{2,6},{3,7},{4,0},{5,1},{6,2},{7,3},{8,12},{9,13},{10,... | collective-permute-start | bytes 958472 | tf_op jit(solution)/shard_map/ppermute | solution.py:24
  115.2 1.9 %copy-start.5 = (f32[2,1024,384]{2,1,0:T(8,128)S(1)}, f32[2,1024,384]{2,1,0:T(8,128)}, u32[]{:S(2)}) copy-start(f32[2,1024,384]{2,1,0:T(8,128)} %get-tuple-element.33) | copy-start | bytes 9437188
  117.3 1.4 copy-start.14
  118.7 1.0 copy-start.22
  118.8 2.8 %copy-start.11 = (f32[2,2,2,32,384]{4,3,2,0,1:T(8,128)S(1)}, f32[2,2,2,32,384]{4,3,2,0,1:T(8,128)}, u32[]{:S(2)}) copy-start(f32[2,2,2,32,384]{4,3,2,0,1:T(8,128)} %copy-done.10) | copy-start | bytes 1179652
  118.8 3.6 %copy-start.20 = (f32[2,2,2,8,384]{4,3,2,0,1:T(8,128)S(1)}, f32[2,2,2,8,384]{4,3,2,0,1:T(8,128)}, u32[]{:S(2)}) copy-start(f32[2,2,2,8,384]{4,3,2,0,1:T(8,128)} %copy-done.19) | copy-start | bytes 294916
  119.8 17.4 %collective-permute-start.13 = (bf16[832,384]{1,0:T(8,128)(2,1)S(1)}, bf16[832,384]{1,0:T(8,128)(2,1)S(1)}, u32[]{:S(2)}, u32[]{:S(2)}) collective-permute-start(bf16[832,384]{1,0:T(8,128)(2,1)S(1)} %pad_maximum_fusion.13), channel_id=1, source_target_pairs={{0,4},{1,5},{2,6},{3,7},{4,0},{5,1},{6,2},{7,3},{8,12},{9,13},{10,... | collective-permute-start | bytes 1916936 | tf_op jit(solution)/shard_map/ppermute | solution.py:24
  122.4 19.9 %collective-permute-start.11 = (bf16[80,384]{1,0:T(8,128)(2,1)S(1)}, bf16[80,384]{1,0:T(8,128)(2,1)S(1)}, u32[]{:S(2)}, u32[]{:S(2)}) collective-permute-start(bf16[80,384]{1,0:T(8,128)(2,1)S(1)} %pad_maximum_fusion.37), channel_id=1, source_target_pairs={{0,8},{1,9},{2,10},{3,11},{4,12},{5,13},{6,14},{7,15},{8,0},{9,1},... | collective-permute-start | bytes 184328 | tf_op jit(solution)/shard_map/ppermute | solution.py:24
  137.4 2.3 %copy-start.27 = (bf16[128,384]{1,0:T(8,128)(2,1)S(1)}, bf16[128,384]{1,0:T(8,128)(2,1)}, u32[]{:S(2)}) copy-start(bf16[128,384]{1,0:T(8,128)(2,1)} %get-tuple-element.20) | copy-start | bytes 294916
  137.5 2.3 %copy-start.28 = (bf16[128,384]{1,0:T(8,128)(2,1)S(1)}, bf16[128,384]{1,0:T(8,128)(2,1)}, u32[]{:S(2)}) copy-start(bf16[128,384]{1,0:T(8,128)(2,1)} %get-tuple-element.28) | copy-start | bytes 294916
  137.5 2.3 %copy-start.29 = (bf16[128,384]{1,0:T(8,128)(2,1)S(1)}, bf16[128,384]{1,0:T(8,128)(2,1)}, u32[]{:S(2)}) copy-start(bf16[128,384]{1,0:T(8,128)(2,1)} %get-tuple-element.27) | copy-start | bytes 294916
  137.5 2.3 %copy-start.30 = (bf16[128,384]{1,0:T(8,128)(2,1)S(1)}, bf16[128,384]{1,0:T(8,128)(2,1)}, u32[]{:S(2)}) copy-start(bf16[128,384]{1,0:T(8,128)(2,1)} %get-tuple-element.29) | copy-start | bytes 294916
  137.6 0.8 copy-start.12
  139.1 8.7 %collective-permute-start.14 = (bf16[416,384]{1,0:T(8,128)(2,1)}, bf16[416,384]{1,0:T(8,128)(2,1)}, u32[]{:S(2)}, u32[]{:S(2)}) collective-permute-start(bf16[416,384]{1,0:T(8,128)(2,1)} %pad_maximum_fusion.21), channel_id=1, source_target_pairs={{0,2},{1,3},{2,0},{3,1},{4,6},{5,7},{6,4},{7,5},{8,10},{9,11},{10,... | collective-permute-start | bytes 958472 | tf_op jit(solution)/shard_map/ppermute | solution.py:24
  142.3 0.6 copy-start.21
  146.1 2.6 %copy-start.13 = (f32[2,2,2,32,384]{4,3,2,0,1:T(8,128)S(1)}, f32[2,2,2,32,384]{4,3,2,0,1:T(8,128)}, u32[]{:S(2)}) copy-start(f32[2,2,2,32,384]{4,3,2,0,1:T(8,128)} %copy-done.12) | copy-start | bytes 1179652
  149.5 5.2 %collective-permute-start.15 = (bf16[80,384]{1,0:T(8,128)(2,1)S(1)}, bf16[80,384]{1,0:T(8,128)(2,1)S(1)}, u32[]{:S(2)}, u32[]{:S(2)}) collective-permute-start(bf16[80,384]{1,0:T(8,128)(2,1)S(1)} %pad_maximum_fusion.38), channel_id=1, source_target_pairs={{0,8},{1,9},{2,10},{3,11},{4,12},{5,13},{6,14},{7,15},{8,0},{9,1},... | collective-permute-start | bytes 184328 | tf_op jit(solution)/shard_map/ppermute | solution.py:24
  155.2 0.8 copy-start.26

commit v6 on v3

--- a/solution.py
+++ b/solution.py
@@ -54,7 +54,8 @@
     def kernel(offsets_ref, query_ref, grad_ref, *refs):
         kv_refs = refs[:3]
         out_ref, qgrad_ref = refs[3:5]
-        term_refs = refs[5:]
+        keep_refs = refs[5:8]
+        message_ref = refs[8]
         pair = pl.program_id(0)
         rows = query_ref.shape[0]
         heads_per_block = query_ref.shape[1] // head_dim
@@ -127,8 +128,16 @@
                     weights[branch], grad, (((0,), (0,)), ((), ())),
                     preferred_element_type=jnp.float32,
                 )
-                term_refs[branch][0, :, cols] = key_terms
-                term_refs[branch][1, :, cols] = value_terms
+                half_keys = key_terms.shape[0] // 2
+                start = sum(kv_ref.shape[1] for kv_ref in kv_refs[:branch])
+                keep_refs[branch][0, :, cols] = key_terms[:half_keys]
+                keep_refs[branch][1, :, cols] = value_terms[:half_keys]
+                message_ref[start : start + half_keys, cols] = key_terms[half_keys:].astype(
+                    message_ref.dtype
+                )
+                message_ref[start + half_keys : start + 2 * half_keys, cols] = value_terms[
+                    half_keys:
+                ].astype(message_ref.dtype)
             qgrad_ref[:, cols] = (query_grad * score_scale).astype(qgrad_ref.dtype)
 
     return kernel
@@ -186,6 +195,7 @@
             gathered = gathered_halves[half]
             cols = slice(half * half_width, (half + 1) * half_width)
             pairs = half_width // block_width
+            key_rows_total = sum(block.shape[1] for block in gathered)
             row_block = pl.BlockSpec((local_rows, block_width), lambda p, offs: (0, p))
             kv_blocks = [
                 pl.BlockSpec((2, block.shape[1], block_width), lambda p, offs: (0, 0, p))
@@ -197,24 +207,43 @@
                     jax.ShapeDtypeStruct((local_rows, half_width), jnp.bfloat16),
                     jax.ShapeDtypeStruct((local_rows, half_width), jnp.bfloat16),
                 )
-                + tuple(jax.ShapeDtypeStruct(block.shape, jnp.float32) for block in gathered),
+                + tuple(
+                    jax.ShapeDtypeStruct((2, block.shape[1] // 2, half_width), jnp.float32)
+                    for block in gathered
+                )
+                + (jax.ShapeDtypeStruct((key_rows_total, half_width), jnp.bfloat16),),
                 grid_spec=pltpu.PrefetchScalarGridSpec(
                     num_scalar_prefetch=1,
                     grid=(pairs,),
                     in_specs=[row_block, row_block] + kv_blocks,
-                    out_specs=[row_block, row_block] + kv_blocks,
+                    out_specs=[row_block, row_block]
+                    + [
+                        pl.BlockSpec((2, block.shape[1] // 2, block_width), lambda p, offs: (0, 0, p))
+                        for block in gathered
+                    ]
+                    + [pl.BlockSpec((key_rows_total, block_width), lambda p, offs: (0, p))],
                 ),
                 compiler_params=pltpu.CompilerParams(vmem_limit_bytes=100 * 1024 * 1024),
             )(head_offsets, query_rows[:, cols], output_grad[:, cols], *gathered)
             attended, query_grad = outs[:2]
-            terms = outs[2:]
+            kept_terms = outs[2:5]
+            message = outs[5]
 
             axis_bits = [list(bits) for bits in layouts[half]]
-            partial = [
-                terms[branch].reshape((2,) + (2,) * branch_bits[branch] + (-1, half_width))
-                for branch in range(3)
-            ]
-            for bit in reversed(gather_order(top_bits, half == 1)):
+            order = list(reversed(gather_order(top_bits, half == 1)))
+            first = order[0]
+            incoming = exchange(message, first).astype(jnp.float32)
+            partial = []
+            cursor = 0
+            for branch in range(3):
+                axis_bits[branch].remove(first)
+                kept = kept_terms[branch].reshape(
+                    (2,) + (2,) * len(axis_bits[branch]) + (-1, half_width)
+                )
+                count = kept.size // half_width
+                partial.append(kept + incoming[cursor : cursor + count].reshape(kept.shape))
+                cursor += count
+            for bit in order[1:]:
                 active = [branch for branch in range(3) if branch_bits[branch] > bit]
                 places = {branch: 1 + axis_bits[branch].index(bit) for branch in active}
                 outgoing = jnp.concatenate(

time: 149 us -> 144 us (0.966)
  local copies, waits for them, and re-layouts: 40 us -> 33.3 us
    slice x25 -> x19, local copies, waits for them, and re-layouts: 6.79 us -> 0.37 us  [per_device(): lax.index_in_dim(partial[branch], 1, places[branch], keepdims=False)]
    slice x22 -> x16, local copies, waits for them, and re-layouts: 6.15 us -> 2.53 us  [per_device(): partial[branch] = kept + incoming[cursor:cursor + count].reshape(kept.shape)]
    slice x0 -> x6, local copies, waits for them, and re-layouts: none -> 3.55 us  [per_device(): partial.append(kept + incoming[cursor:cursor + count].reshape(kept.shape))]
    unnamed x52 -> x36, local copies, waits for them, and re-layouts: 3.59 us -> 2.68 us
  transfers between devices with their start and end apart: 16 -> 16, of which waited for: 8 -> 9; matrix products, arithmetic and copies ran while one was open for 29% -> 27% of each run, Pallas kernels for 20% -> 20%
where the time goes in v6:
time: 144 us; the launch traced here: 143 us
  waiting for transfers between devices  40.9 us (28%)
  local copies, waits for them, and re-layouts  33.3 us (23%)
  Pallas kernels  28.1 us (20%)
  starting transfers between devices  23 us (16%)
  other arithmetic  15.7 us (11%)
  between operations  1.86 us (1%)
    ppermute x16, waiting for transfers between devices, exchange(): return lax.ppermute(block, 'seq', route)  40.9 us
    pallas_call x2, Pallas kernels, per_device(): pl.pallas_call(attention_kernel(head_dim, score_scale, half * heads_per_h...  28.1 us
    ppermute x16, starting transfers between devices, exchange(): return lax.ppermute(block, 'seq', route)  23 us
    broadcast_in_dim x16, local copies, waits for them, and re-layouts, spread_rows(): widened = jnp.where(chosen, grouped, jnp.zeros((), picked.dtype))  7.21 us
    another operation x25, local copies, waits for them, and re-layouts, per_device(): buffers[branch] = jnp.stack([buffers[branch], arrived], axis=1)  6.51 us
    another operation x22, other arithmetic, per_device(): buffers[branch] = jnp.stack([buffers[branch], arrived], axis=1)  4.71 us
    slice x6, local copies, waits for them, and re-layouts, per_device(): partial.append(kept + incoming[cursor:cursor + count].reshape(kept.shape))  3.55 us
    slice x20, local copies, waits for them, and re-layouts, per_device(): arrived = incoming[cursor:cursor + count].reshape(buffers[branch].shape)  3.5 us
  transfers between devices with their start and end apart: 16, of which 9 were waited for; matrix products, arithmetic and copies ran while one was open for 27% of the time, Pallas kernels for 20%

profile of v6, /device:TPU:0, one launch (start us, length us, event | category | flops | bytes accessed | tf_op | source)
XLA Modules:
  0.0 142.9 jit_solution(4446232091161007827)
XLA Ops:
  0.7 1.3 stack.157
  2.0 1.3 stack.161
  5.2 4.1 %collective-permute-start = (bf16[80,384]{1,0:T(8,128)(2,1)S(1)}, bf16[80,384]{1,0:T(8,128)(2,1)S(1)}, u32[]{:S(2)}, u32[]{:S(2)}) collective-permute-start(bf16[80,384]{1,0:T(8,128)(2,1)S(1)} %pad_maximum_fusion.33), channel_id=1, source_target_pairs={{0,8},{1,9},{2,10},{3,11},{4,12},{5,13},{6,14},{7,15},{8,0},{9,1},... | collective-permute-start | bytes 184328 | tf_op jit(solution)/shard_map/ppermute | solution.py:24
  9.4 0.7 fusion.39
  10.1 2.0 %collective-permute-done = bf16[80,384]{1,0:T(8,128)(2,1)S(1)} collective-permute-done((bf16[80,384]{1,0:T(8,128)(2,1)S(1)}, bf16[80,384]{1,0:T(8,128)(2,1)S(1)}, u32[]{:S(2)}, u32[]{:S(2)}) %collective-permute-start) | collective-permute-done | bytes 61472 | tf_op jit(solution)/shard_map/ppermute | solution.py:24
  12.3 2.7 %collective-permute-start.1 = (bf16[416,384]{1,0:T(8,128)(2,1)S(1)}, bf16[416,384]{1,0:T(8,128)(2,1)S(1)}, u32[]{:S(2)}, u32[]{:S(2)}) collective-permute-start(bf16[416,384]{1,0:T(8,128)(2,1)S(1)} %pad_maximum_fusion.16), channel_id=1, source_target_pairs={{0,4},{1,5},{2,6},{3,7},{4,0},{5,1},{6,2},{7,3},{8,12},{9,13},{10,... | collective-permute-start | bytes 958472 | tf_op jit(solution)/shard_map/ppermute | solution.py:24
  15.1 2.3 %collective-permute-start.5 = (bf16[416,384]{1,0:T(8,128)(2,1)S(1)}, bf16[416,384]{1,0:T(8,128)(2,1)S(1)}, u32[]{:S(2)}, u32[]{:S(2)}) collective-permute-start(bf16[416,384]{1,0:T(8,128)(2,1)S(1)} %pad_maximum_fusion.17), channel_id=1, source_target_pairs={{0,2},{1,3},{2,0},{3,1},{4,6},{5,7},{6,4},{7,5},{8,10},{9,11},{10,... | collective-permute-start | bytes 958472 | tf_op jit(solution)/shard_map/ppermute | solution.py:24
  17.3 5.2 %collective-permute-done.1 = bf16[416,384]{1,0:T(8,128)(2,1)S(1)} collective-permute-done((bf16[416,384]{1,0:T(8,128)(2,1)S(1)}, bf16[416,384]{1,0:T(8,128)(2,1)S(1)}, u32[]{:S(2)}, u32[]{:S(2)}) %collective-permute-start.1) | collective-permute-done | bytes 319520 | tf_op jit(solution)/shard_map/ppermute | solution.py:24
  22.9 1.6 %collective-permute-start.2 = (bf16[832,384]{1,0:T(8,128)(2,1)S(1)}, bf16[832,384]{1,0:T(8,128)(2,1)S(1)}, u32[]{:S(2)}, u32[]{:S(2)}) collective-permute-start(bf16[832,384]{1,0:T(8,128)(2,1)S(1)} %pad_maximum_fusion.8), channel_id=1, source_target_pairs={{0,2},{1,3},{2,0},{3,1},{4,6},{5,7},{6,4},{7,5},{8,10},{9,11},{10,... | collective-permute-start | bytes 1916936 | tf_op jit(solution)/shard_map/ppermute | solution.py:24
  24.8 1.8 %collective-permute-start.6 = (bf16[832,384]{1,0:T(8,128)(2,1)S(1)}, bf16[832,384]{1,0:T(8,128)(2,1)S(1)}, u32[]{:S(2)}, u32[]{:S(2)}) collective-permute-start(bf16[832,384]{1,0:T(8,128)(2,1)S(1)} %pad_maximum_fusion.9), channel_id=1, source_target_pairs={{0,4},{1,5},{2,6},{3,7},{4,0},{5,1},{6,2},{7,3},{8,12},{9,13},{10,... | collective-permute-start | bytes 1916936 | tf_op jit(solution)/shard_map/ppermute | solution.py:24
  26.6 12.0 %collective-permute-done.2 = bf16[832,384]{1,0:T(8,128)(2,1)S(1)} collective-permute-done((bf16[832,384]{1,0:T(8,128)(2,1)S(1)}, bf16[832,384]{1,0:T(8,128)(2,1)S(1)}, u32[]{:S(2)}, u32[]{:S(2)}) %collective-permute-start.2) | collective-permute-done | bytes 639008 | tf_op jit(solution)/shard_map/ppermute | solution.py:24
  39.3 0.6 collective-permute-done.6
  40.0 0.8 fusion.33
  40.9 0.7 fusion.27
  41.6 1.1 fusion.37
  42.8 1.3 pad_maximum_fusion.3
  44.1 0.7 slice_bitcast_fusion.25
  44.7 0.7 fusion.40
  45.5 0.7 copy.79
  46.4 1.0 copy.77
  47.7 1.3 copy.75
  49.0 14.1 %shard_map.84 = (bf16[128,384]{1,0:T(8,128)(2,1)}, bf16[128,384]{1,0:T(8,128)(2,1)}, f32[2,512,384]{2,1,0:T(8,128)}, f32[2,256,384]{2,1,0:T(8,128)}, f32[2,64,384]{2,1,0:T(8,128)}, /*index=5*/bf16[1664,384]{1,0:T(8,128)(2,1)}) custom-call(s32[3,12]{1,0:T(4,128)} %offsets_ref.3, bf16[128,384]{1,0:T(8,128)(2,1)} %get-tuple-element.50.query_ref, ...), custom_call_target="tpu_custom_call" | custom-call | tf_op jit(solution)/shard_map/pallas_call | solution.py:204
  63.1 0.6 collective-permute-start.8
  63.7 1.2 iota_compare_fusion
  65.0 0.8 broadcast_in_dim.131
  65.8 0.9 slice.437
  66.7 0.9 pad_maximum_fusion.24
  67.7 0.7 copy.98
  68.4 1.0 slice.436
  69.5 1.0 copy.96
  70.6 1.2 slice.435
  72.0 1.3 copy.94
  73.3 14.0 %shard_map.85 = (bf16[128,384]{1,0:T(8,128)(2,1)}, bf16[128,384]{1,0:T(8,128)(2,1)}, f32[2,512,384]{2,1,0:T(8,128)}, f32[2,256,384]{2,1,0:T(8,128)}, f32[2,64,384]{2,1,0:T(8,128)}, /*index=5*/bf16[1664,384]{1,0:T(8,128)(2,1)}) custom-call(s32[3,12]{1,0:T(4,128)} %offsets_ref.3, bf16[128,384]{1,0:T(8,128)(2,1)} %get-tuple-element.51.query_ref, ...), custom_call_target="tpu_custom_call" | custom-call | tf_op jit(solution)/shard_map/pallas_call | solution.py:204
  87.4 0.7 iota_compare_fusion.3
  88.2 0.8 broadcast_in_dim.125
  89.0 0.8 broadcast_in_dim.140
  89.8 0.8 broadcast_in_dim.141
  90.8 0.8 broadcast_in_dim.136
  91.6 1.8 %pad_maximum_fusion.25 = (bf16[128,768]{1,0:T(8,128)(2,1)}, bf16[128,768]{1,0:T(8,128)(2,1)}) fusion(bf16[128,384]{1,0:T(8,128)(2,1)} %get-tuple-element.17, bf16[128,384]{1,0:T(8,128)(2,1)} %get-tuple-element.16, bf16[128,384]{1,0:T(8,128)(2,1)} %get-tuple-element.19, bf16[128,384]{1,0:T(8,128)(2,1)} %get-tuple-element.18), kind=kLoop, calls=%fused_computation.66 | loop fusion | flops 786432 | bytes 786432 | tf_op jit(solution)/shard_map/concatenate | solution.py:273
  93.4 1.4 slice.438
  95.3 1.1 slice.441
  96.6 0.9 slice.443
  97.7 1.2 collective-permute-start.9
  99.5 1.0 copy-done.8
  100.6 0.7 copy-done.13
  101.5 1.8 %collective-permute-start.13 = (bf16[832,384]{1,0:T(8,128)(2,1)S(1)}, bf16[832,384]{1,0:T(8,128)(2,1)S(1)}, u32[]{:S(2)}, u32[]{:S(2)}) collective-permute-start(bf16[832,384]{1,0:T(8,128)(2,1)S(1)} %pad_maximum_fusion.11), channel_id=1, source_target_pairs={{0,4},{1,5},{2,6},{3,7},{4,0},{5,1},{6,2},{7,3},{8,12},{9,13},{10,... | collective-permute-start | bytes 1916936 | tf_op jit(solution)/shard_map/ppermute | solution.py:24
  103.3 11.2 %collective-permute-done.9 = bf16[832,384]{1,0:T(8,128)(2,1)S(1)} collective-permute-done((bf16[832,384]{1,0:T(8,128)(2,1)S(1)}, bf16[832,384]{1,0:T(8,128)(2,1)S(1)}, u32[]{:S(2)}, u32[]{:S(2)}) %collective-permute-start.9) | collective-permute-done | bytes 639008 | tf_op jit(solution)/shard_map/ppermute | solution.py:24
  114.9 1.8 %collective-permute-start.10 = (bf16[416,384]{1,0:T(8,128)(2,1)S(1)}, bf16[416,384]{1,0:T(8,128)(2,1)S(1)}, u32[]{:S(2)}, u32[]{:S(2)}) collective-permute-start(bf16[416,384]{1,0:T(8,128)(2,1)S(1)} %pad_maximum_fusion.18), channel_id=1, source_target_pairs={{0,4},{1,5},{2,6},{3,7},{4,0},{5,1},{6,2},{7,3},{8,12},{9,13},{10,... | collective-permute-start | bytes 958472 | tf_op jit(solution)/shard_map/ppermute | solution.py:24
  116.7 2.0 %collective-permute-done.13 = bf16[832,384]{1,0:T(8,128)(2,1)S(1)} collective-permute-done((bf16[832,384]{1,0:T(8,128)(2,1)S(1)}, bf16[832,384]{1,0:T(8,128)(2,1)S(1)}, u32[]{:S(2)}, u32[]{:S(2)}) %collective-permute-start.13) | collective-permute-done | bytes 639008 | tf_op jit(solution)/shard_map/ppermute | solution.py:24
  119.1 1.2 collective-permute-start.14
  120.4 4.8 %collective-permute-done.10 = bf16[416,384]{1,0:T(8,128)(2,1)S(1)} collective-permute-done((bf16[416,384]{1,0:T(8,128)(2,1)S(1)}, bf16[416,384]{1,0:T(8,128)(2,1)S(1)}, u32[]{:S(2)}, u32[]{:S(2)}) %collective-permute-start.10) | collective-permute-done | bytes 319520 | tf_op jit(solution)/shard_map/ppermute | solution.py:24
  125.3 2.6 %collective-permute-done.14 = bf16[416,384]{1,0:T(8,128)(2,1)S(1)} collective-permute-done((bf16[416,384]{1,0:T(8,128)(2,1)S(1)}, bf16[416,384]{1,0:T(8,128)(2,1)S(1)}, u32[]{:S(2)}, u32[]{:S(2)}) %collective-permute-start.14) | collective-permute-done | bytes 319520 | tf_op jit(solution)/shard_map/ppermute | solution.py:24
  128.0 3.8 %collective-permute-start.11 = (bf16[80,384]{1,0:T(8,128)(2,1)S(1)}, bf16[80,384]{1,0:T(8,128)(2,1)S(1)}, u32[]{:S(2)}, u32[]{:S(2)}) collective-permute-start(bf16[80,384]{1,0:T(8,128)(2,1)S(1)} %pad_maximum_fusion.35), channel_id=1, source_target_pairs={{0,8},{1,9},{2,10},{3,11},{4,12},{5,13},{6,14},{7,15},{8,0},{9,1},... | collective-permute-start | bytes 184328 | tf_op jit(solution)/shard_map/ppermute | solution.py:24
  132.0 0.6 pad_maximum_fusion.36
  132.6 0.8 squeeze.78
  134.1 0.5 copy-done.9
  134.7 1.0 broadcast_in_dim.128
  135.8 0.7 slice.464
  136.6 1.0 broadcast_in_dim.134
  137.7 1.3 fusion.13
  139.0 0.8 slice.490
  140.3 0.7 slice.492
  141.5 0.7 pad_maximum_fusion.28
  142.2 0.7 pad_maximum_fusion.27
  (202 shorter events, 9.3 us)
Async XLA Ops:
  0.6 2.6 %copy-start.1 = (bf16[128,768]{1,0:T(8,128)(2,1)S(1)}, bf16[128,768]{1,0:T(8,128)(2,1)}, u32[]{:S(2)}) copy-start(bf16[128,768]{1,0:T(8,128)(2,1)} %param.7) | copy-start | bytes 589828
  0.6 3.3 %copy-start.17 = (s32[3,12]{1,0:T(4,128)S(1)}, s32[3,12]{1,0:T(4,128)}, u32[]{:S(2)}) copy-start(s32[3,12]{1,0:T(4,128)} %offsets_ref.3) | copy-start | bytes 436
  3.9 5.5 %copy-start.10 = (bf16[128,768]{1,0:T(8,128)(2,1)S(1)}, bf16[128,768]{1,0:T(8,128)(2,1)}, u32[]{:S(2)}) copy-start(bf16[128,768]{1,0:T(8,128)(2,1)} %param.8) | copy-start | bytes 589828
  4.4 5.7 %copy-start.2 = (bf16[128,768]{1,0:T(8,128)(2,1)S(1)}, bf16[128,768]{1,0:T(8,128)(2,1)}, u32[]{:S(2)}) copy-start(bf16[128,768]{1,0:T(8,128)(2,1)} %param.6) | copy-start | bytes 589828
  5.2 7.0 %collective-permute-start = (bf16[80,384]{1,0:T(8,128)(2,1)S(1)}, bf16[80,384]{1,0:T(8,128)(2,1)S(1)}, u32[]{:S(2)}, u32[]{:S(2)}) collective-permute-start(bf16[80,384]{1,0:T(8,128)(2,1)S(1)} %pad_maximum_fusion.33), channel_id=1, source_target_pairs={{0,8},{1,9},{2,10},{3,11},{4,12},{5,13},{6,14},{7,15},{8,0},{9,1},... | collective-permute-start | bytes 184328 | tf_op jit(solution)/shard_map/ppermute | solution.py:24
  9.3 5.6 %collective-permute-start.4 = (bf16[80,384]{1,0:T(8,128)(2,1)S(1)}, bf16[80,384]{1,0:T(8,128)(2,1)S(1)}, u32[]{:S(2)}, u32[]{:S(2)}) collective-permute-start(bf16[80,384]{1,0:T(8,128)(2,1)S(1)} %pad_maximum_fusion.34), channel_id=1, source_target_pairs={{0,8},{1,9},{2,10},{3,11},{4,12},{5,13},{6,14},{7,15},{8,0},{9,1},... | collective-permute-start | bytes 184328 | tf_op jit(solution)/shard_map/ppermute | solution.py:24
  12.3 10.3 %collective-permute-start.1 = (bf16[416,384]{1,0:T(8,128)(2,1)S(1)}, bf16[416,384]{1,0:T(8,128)(2,1)S(1)}, u32[]{:S(2)}, u32[]{:S(2)}) collective-permute-start(bf16[416,384]{1,0:T(8,128)(2,1)S(1)} %pad_maximum_fusion.16), channel_id=1, source_target_pairs={{0,4},{1,5},{2,6},{3,7},{4,0},{5,1},{6,2},{7,3},{8,12},{9,13},{10,... | collective-permute-start | bytes 958472 | tf_op jit(solution)/shard_map/ppermute | solution.py:24
  15.1 9.4 %collective-permute-start.5 = (bf16[416,384]{1,0:T(8,128)(2,1)S(1)}, bf16[416,384]{1,0:T(8,128)(2,1)S(1)}, u32[]{:S(2)}, u32[]{:S(2)}) collective-permute-start(bf16[416,384]{1,0:T(8,128)(2,1)S(1)} %pad_maximum_fusion.17), channel_id=1, source_target_pairs={{0,2},{1,3},{2,0},{3,1},{4,6},{5,7},{6,4},{7,5},{8,10},{9,11},{10,... | collective-permute-start | bytes 958472 | tf_op jit(solution)/shard_map/ppermute | solution.py:24
  22.9 15.7 %collective-permute-start.2 = (bf16[832,384]{1,0:T(8,128)(2,1)S(1)}, bf16[832,384]{1,0:T(8,128)(2,1)S(1)}, u32[]{:S(2)}, u32[]{:S(2)}) collective-permute-start(bf16[832,384]{1,0:T(8,128)(2,1)S(1)} %pad_maximum_fusion.8), channel_id=1, source_target_pairs={{0,2},{1,3},{2,0},{3,1},{4,6},{5,7},{6,4},{7,5},{8,10},{9,11},{10,... | collective-permute-start | bytes 1916936 | tf_op jit(solution)/shard_map/ppermute | solution.py:24
  24.8 15.1 %collective-permute-start.6 = (bf16[832,384]{1,0:T(8,128)(2,1)S(1)}, bf16[832,384]{1,0:T(8,128)(2,1)S(1)}, u32[]{:S(2)}, u32[]{:S(2)}) collective-permute-start(bf16[832,384]{1,0:T(8,128)(2,1)S(1)} %pad_maximum_fusion.9), channel_id=1, source_target_pairs={{0,4},{1,5},{2,6},{3,7},{4,0},{5,1},{6,2},{7,3},{8,12},{9,13},{10,... | collective-permute-start | bytes 1916936 | tf_op jit(solution)/shard_map/ppermute | solution.py:24
  39.3 6.2 %collective-permute-start.3 = (bf16[1664,384]{1,0:T(8,128)(2,1)S(1)}, bf16[1664,384]{1,0:T(8,128)(2,1)S(1)}, u32[]{:S(2)}, u32[]{:S(2)}) collective-permute-start(bf16[1664,384]{1,0:T(8,128)(2,1)S(1)} %pad_maximum_fusion.2), channel_id=1, source_target_pairs={{0,1},{1,0},{2,3},{3,2},{4,5},{5,4},{6,7},{7,6},{8,9},{9,8},{10,11... | collective-permute-start | bytes 3833864 | tf_op jit(solution)/shard_map/ppermute | solution.py:24
  42.8 1.9 %copy-start.11 = (bf16[128,768]{1,0:T(8,128)(2,1)S(1)}, bf16[128,768]{1,0:T(8,128)(2,1)}, u32[]{:S(2)}) copy-start(bf16[128,768]{1,0:T(8,128)(2,1)} %param.5) | copy-start | bytes 589828
  44.1 21.7 %collective-permute-start.7 = (bf16[1664,384]{1,0:T(8,128)(2,1)}, bf16[1664,384]{1,0:T(8,128)(2,1)}, u32[]{:S(2)}, u32[]{:S(2)}) collective-permute-start(bf16[1664,384]{1,0:T(8,128)(2,1)} %pad_maximum_fusion.3), channel_id=1, source_target_pairs={{0,1},{1,0},{2,3},{3,2},{4,5},{5,4},{6,7},{7,6},{8,9},{9,8},{10,11... | collective-permute-start | bytes 3833864 | tf_op jit(solution)/shard_map/ppermute | solution.py:24
  63.1 6.3 %copy-start.5 = (bf16[2,1,2,2,2,32,384]{6,5,0,4,3,2,1:T(8,128)(2,1)S(1)}, bf16[2,1,2,2,2,32,384]{6,5,0,4,3,2,1:T(8,128)(2,1)}, u32[]{:S(2)}) copy-start(bf16[2,1,2,2,2,32,384]{6,5,0,4,3,2,1:T(8,128)(2,1)} %get-tuple-element.38) | copy-start | bytes 1179652
  63.1 30.3 %collective-permute-start.8 = (bf16[1664,384]{1,0:T(8,128)(2,1)}, bf16[1664,384]{1,0:T(8,128)(2,1)}, u32[]{:S(2)}, u32[]{:S(2)}) collective-permute-start(bf16[1664,384]{1,0:T(8,128)(2,1)} %get-tuple-element.21), channel_id=1, source_target_pairs={{0,1},{1,0},{2,3},{3,2},{4,5},{5,4},{6,7},{7,6},{8,9},{9,8},{10,11... | collective-permute-start | bytes 3833864 | tf_op jit(solution)/shard_map/ppermute | solution.py:24
  69.5 2.3 %copy-start = (bf16[2,1,2,2,128,384]{5,4,0,3,2,1:T(8,128)(2,1)S(1)}, bf16[2,1,2,2,128,384]{5,4,0,3,2,1:T(8,128)(2,1)}, u32[]{:S(2)}) copy-start(bf16[2,1,2,2,128,384]{5,4,0,3,2,1:T(8,128)(2,1)} %get-tuple-element.30) | copy-start | bytes 2359300
  87.3 11.6 %collective-permute-start.12 = (bf16[1664,384]{1,0:T(8,128)(2,1)}, bf16[1664,384]{1,0:T(8,128)(2,1)S(1)}, u32[]{:S(2)}, u32[]{:S(2)}) collective-permute-start(bf16[1664,384]{1,0:T(8,128)(2,1)} %get-tuple-element.25), channel_id=1, source_target_pairs={{0,1},{1,0},{2,3},{3,2},{4,5},{5,4},{6,7},{7,6},{8,9},{9,8},{10,11... | collective-permute-start | bytes 3833864 | tf_op jit(solution)/shard_map/ppermute | solution.py:24
  93.4 1.6 %copy-start.3 = (f32[2,512,384]{2,1,0:T(8,128)S(1)}, f32[2,512,384]{2,1,0:T(8,128)}, u32[]{:S(2)}) copy-start(f32[2,512,384]{2,1,0:T(8,128)} %get-tuple-element.20) | copy-start | bytes 4718596
  95.2 1.3 copy-start.7
  96.5 1.1 copy-start.12
  97.7 1.4 copy-start.4
  97.7 16.8 %collective-permute-start.9 = (bf16[832,384]{1,0:T(8,128)(2,1)S(1)}, bf16[832,384]{1,0:T(8,128)(2,1)S(1)}, u32[]{:S(2)}, u32[]{:S(2)}) collective-permute-start(bf16[832,384]{1,0:T(8,128)(2,1)S(1)} %pad_maximum_fusion.10), channel_id=1, source_target_pairs={{0,2},{1,3},{2,0},{3,1},{4,6},{5,7},{6,4},{7,5},{8,10},{9,11},{10,... | collective-permute-start | bytes 1916936 | tf_op jit(solution)/shard_map/ppermute | solution.py:24
  99.3 1.1 copy-start.8
  100.4 0.9 copy-start.13
  101.5 17.2 %collective-permute-start.13 = (bf16[832,384]{1,0:T(8,128)(2,1)S(1)}, bf16[832,384]{1,0:T(8,128)(2,1)S(1)}, u32[]{:S(2)}, u32[]{:S(2)}) collective-permute-start(bf16[832,384]{1,0:T(8,128)(2,1)S(1)} %pad_maximum_fusion.11), channel_id=1, source_target_pairs={{0,4},{1,5},{2,6},{3,7},{4,0},{5,1},{6,2},{7,3},{8,12},{9,13},{10,... | collective-permute-start | bytes 1916936 | tf_op jit(solution)/shard_map/ppermute | solution.py:24
  114.9 10.2 %collective-permute-start.10 = (bf16[416,384]{1,0:T(8,128)(2,1)S(1)}, bf16[416,384]{1,0:T(8,128)(2,1)S(1)}, u32[]{:S(2)}, u32[]{:S(2)}) collective-permute-start(bf16[416,384]{1,0:T(8,128)(2,1)S(1)} %pad_maximum_fusion.18), channel_id=1, source_target_pairs={{0,4},{1,5},{2,6},{3,7},{4,0},{5,1},{6,2},{7,3},{8,12},{9,13},{10,... | collective-permute-start | bytes 958472 | tf_op jit(solution)/shard_map/ppermute | solution.py:24
  119.1 8.7 %collective-permute-start.14 = (bf16[416,384]{1,0:T(8,128)(2,1)S(1)}, bf16[416,384]{1,0:T(8,128)(2,1)S(1)}, u32[]{:S(2)}, u32[]{:S(2)}) collective-permute-start(bf16[416,384]{1,0:T(8,128)(2,1)S(1)} %pad_maximum_fusion.19), channel_id=1, source_target_pairs={{0,2},{1,3},{2,0},{3,1},{4,6},{5,7},{6,4},{7,5},{8,10},{9,11},{10,... | collective-permute-start | bytes 958472 | tf_op jit(solution)/shard_map/ppermute | solution.py:24
  128.0 6.0 %collective-permute-start.11 = (bf16[80,384]{1,0:T(8,128)(2,1)S(1)}, bf16[80,384]{1,0:T(8,128)(2,1)S(1)}, u32[]{:S(2)}, u32[]{:S(2)}) collective-permute-start(bf16[80,384]{1,0:T(8,128)(2,1)S(1)} %pad_maximum_fusion.35), channel_id=1, source_target_pairs={{0,8},{1,9},{2,10},{3,11},{4,12},{5,13},{6,14},{7,15},{8,0},{9,1},... | collective-permute-start | bytes 184328 | tf_op jit(solution)/shard_map/ppermute | solution.py:24
  132.6 6.4 %collective-permute-start.15 = (bf16[80,384]{1,0:T(8,128)(2,1)}, bf16[80,384]{1,0:T(8,128)(2,1)}, u32[]{:S(2)}, u32[]{:S(2)}) collective-permute-start(bf16[80,384]{1,0:T(8,128)(2,1)} %pad_maximum_fusion.36), channel_id=1, source_target_pairs={{0,8},{1,9},{2,10},{3,11},{4,12},{5,13},{6,14},{7,15},{8,0},{9,1},... | collective-permute-start | bytes 184328 | tf_op jit(solution)/shard_map/ppermute | solution.py:24
  134.0 0.6 copy-start.9
  136.6 1.1 copy-start.14
  137.7 2.2 %copy-start.6 = (f32[2,32,6,64]{3,2,1,0:T(8,128)S(1)}, f32[2,32,6,64]{3,2,1,0:T(8,128)}, u32[]{:S(2)}) copy-start(f32[2,32,6,64]{3,2,1,0:T(8,128)} %squeeze.78) | copy-start | bytes 294916
  140.2 1.1 copy-start.15
  140.2 1.1 copy-start.16

commit v7 on v6

--- a/solution.py
+++ b/solution.py
@@ -50,12 +50,11 @@
     return widened.reshape(pair, count * stride, width)
 
 
-def attention_kernel(head_dim, score_scale, head_base):
-    def kernel(offsets_ref, query_ref, grad_ref, *refs):
-        kv_refs = refs[:3]
-        out_ref, qgrad_ref = refs[3:5]
-        keep_refs = refs[5:8]
-        message_ref = refs[8]
+def attention_kernel(head_dim, score_scale, head_base, half_counts):
+    def kernel(offsets_ref, query_ref, grad_ref, mine_ref, arrived_ref, *refs):
+        out_ref, qgrad_ref = refs[0:2]
+        keep_refs = refs[2:5]
+        message_ref = refs[5]
         pair = pl.program_id(0)
         rows = query_ref.shape[0]
         heads_per_block = query_ref.shape[1] // head_dim
@@ -64,8 +63,24 @@
             cols = slice(sub * head_dim, (sub + 1) * head_dim)
             query = query_ref[:, cols]
             grad = grad_ref[:, cols]
-            keys = [kv_ref[0, :, cols] for kv_ref in kv_refs]
-            values = [kv_ref[1, :, cols] for kv_ref in kv_refs]
+            keys = []
+            values = []
+            start = 0
+            for count in half_counts:
+                keys.append(
+                    jnp.concatenate(
+                        [mine_ref[start : start + count, cols], arrived_ref[start : start + count, cols]]
+                    )
+                )
+                values.append(
+                    jnp.concatenate(
+                        [
+                            mine_ref[start + count : start + 2 * count, cols],
+                            arrived_ref[start + count : start + 2 * count, cols],
+                        ]
+                    )
+                )
+                start += 2 * count
             members = []
             scores = []
             for branch in range(3):
@@ -129,7 +144,7 @@
                     preferred_element_type=jnp.float32,
                 )
                 half_keys = key_terms.shape[0] // 2
-                start = sum(kv_ref.shape[1] for kv_ref in kv_refs[:branch])
+                start = 2 * sum(half_counts[:branch])
                 keep_refs[branch][0, :, cols] = key_terms[:half_keys]
                 keep_refs[branch][1, :, cols] = value_terms[:half_keys]
                 message_ref[start : start + half_keys, cols] = key_terms[half_keys:].astype(
@@ -174,7 +189,8 @@
             cols = slice(half * half_width, (half + 1) * half_width)
             buffers = [block[:, :, cols] for block in picked]
             axis_bits = [[] for _ in range(3)]
-            for bit in gather_order(top_bits, half == 1):
+            order = gather_order(top_bits, half == 1)
+            for bit in order[:-1]:
                 active = [branch for branch in range(3) if branch_bits[branch] > bit]
                 outgoing = jnp.concatenate(
                     [buffers[branch].reshape(-1, half_width) for branch in active]
@@ -187,44 +203,45 @@
                     cursor += count
                     buffers[branch] = jnp.stack([buffers[branch], arrived], axis=1)
                     axis_bits[branch].insert(0, bit)
-            gathered_halves.append([buffers[branch].reshape(2, -1, half_width) for branch in range(3)])
+            for branch in range(3):
+                axis_bits[branch].insert(0, order[-1])
+            mine = jnp.concatenate([buffers[branch].reshape(-1, half_width) for branch in range(3)])
+            half_counts = [buffers[branch].size // (2 * half_width) for branch in range(3)]
+            gathered_halves.append((mine, exchange(mine, order[-1]), half_counts))
             layouts.append(axis_bits)
 
         results = []
         for half in range(halves):
-            gathered = gathered_halves[half]
+            mine, arrived, half_counts = gathered_halves[half]
             cols = slice(half * half_width, (half + 1) * half_width)
             pairs = half_width // block_width
-            key_rows_total = sum(block.shape[1] for block in gathered)
+            key_rows_total = 2 * sum(half_counts)
             row_block = pl.BlockSpec((local_rows, block_width), lambda p, offs: (0, p))
-            kv_blocks = [
-                pl.BlockSpec((2, block.shape[1], block_width), lambda p, offs: (0, 0, p))
-                for block in gathered
-            ]
+            message_block = pl.BlockSpec((key_rows_total, block_width), lambda p, offs: (0, p))
             outs = pl.pallas_call(
-                attention_kernel(head_dim, score_scale, half * heads_per_half),
+                attention_kernel(head_dim, score_scale, half * heads_per_half, half_counts),
                 out_shape=(
                     jax.ShapeDtypeStruct((local_rows, half_width), jnp.bfloat16),
                     jax.ShapeDtypeStruct((local_rows, half_width), jnp.bfloat16),
                 )
                 + tuple(
-                    jax.ShapeDtypeStruct((2, block.shape[1] // 2, half_width), jnp.float32)
-                    for block in gathered
+                    jax.ShapeDtypeStruct((2, count, half_width), jnp.float32)
+                    for count in half_counts
                 )
                 + (jax.ShapeDtypeStruct((key_rows_total, half_width), jnp.bfloat16),),
                 grid_spec=pltpu.PrefetchScalarGridSpec(
                     num_scalar_prefetch=1,
                     grid=(pairs,),
-                    in_specs=[row_block, row_block] + kv_blocks,
+                    in_specs=[row_block, row_block, message_block, message_block],
                     out_specs=[row_block, row_block]
                     + [
-                        pl.BlockSpec((2, block.shape[1] // 2, block_width), lambda p, offs: (0, 0, p))
-                        for block in gathered
+                        pl.BlockSpec((2, count, block_width), lambda p, offs: (0, 0, p))
+                        for count in half_counts
                     ]
-                    + [pl.BlockSpec((key_rows_total, block_width), lambda p, offs: (0, p))],
+                    + [message_block],
                 ),
                 compiler_params=pltpu.CompilerParams(vmem_limit_bytes=100 * 1024 * 1024),
-            )(head_offsets, query_rows[:, cols], output_grad[:, cols], *gathered)
+            )(head_offsets, query_rows[:, cols], output_grad[:, cols], mine, arrived)
             attended, query_grad = outs[:2]
             kept_terms = outs[2:5]
             message = outs[5]

time: 144 us -> 132 us (0.917)
  local copies, waits for them, and re-layouts: 33.3 us -> 26.5 us
  other arithmetic: 15.7 us -> 10.8 us
    another operation x25 -> x19, local copies, waits for them, and re-layouts: 6.51 us -> 0.44 us  [per_device(): buffers[branch] = jnp.stack([buffers[branch], arrived], axis=1)]
    another operation x22 -> x16, other arithmetic: 4.71 us -> 0.62 us  [per_device(): buffers[branch] = jnp.stack([buffers[branch], arrived], axis=1)]
    slice x20 -> x14, local copies, waits for them, and re-layouts: 3.5 us -> 0.22 us  [per_device(): arrived = incoming[cursor:cursor + count].reshape(buffers[branch].shape)]
    unnamed x36, local copies, waits for them, and re-layouts: 2.68 us -> 4.47 us
  transfers between devices with their start and end apart: 16 -> 16, of which waited for: 9 -> 9; matrix products, arithmetic and copies ran while one was open for 27% -> 19% of each run, Pallas kernels for 20% -> 21%
where the time goes in v7:
time: 132 us; the launch traced here: 131 us
  waiting for transfers between devices  42 us (32%)
  Pallas kernels  27.9 us (21%)
  local copies, waits for them, and re-layouts  26.5 us (20%)
  starting transfers between devices  22.4 us (17%)
  other arithmetic  10.8 us (8%)
  between operations  1.79 us (1%)
    ppermute x16, waiting for transfers between devices, exchange(): return lax.ppermute(block, 'seq', route)  42 us
    pallas_call x2, Pallas kernels, per_device(): pl.pallas_call(attention_kernel(head_dim, score_scale, half * heads_per_h...  27.9 us
    ppermute x16, starting transfers between devices, exchange(): return lax.ppermute(block, 'seq', route)  22.4 us
    broadcast_in_dim x16, local copies, waits for them, and re-layouts, spread_rows(): widened = jnp.where(chosen, grouped, jnp.zeros((), picked.dtype))  7.2 us
    unnamed x36, local copies, waits for them, and re-layouts  4.47 us
    slice x6, local copies, waits for them, and re-layouts, per_device(): partial.append(kept + incoming[cursor:cursor + count].reshape(kept.shape))  3.55 us
    another operation x4, local copies, waits for them, and re-layouts, per_device(): kv_rows = jnp.stack([key_rows, value_rows])  3.2 us
    concatenate x3, other arithmetic, per_device(): jnp.concatenate([result[index] for result in results], axis=1)  3.2 us
  transfers between devices with their start and end apart: 16, of which 9 were waited for; matrix products, arithmetic and copies ran while one was open for 19% of the time, Pallas kernels for 21%

profile of v7, /device:TPU:0, one launch (start us, length us, event | category | flops | bytes accessed | tf_op | source)
XLA Modules:
  0.0 131.5 jit_solution(12413779573832058861)
XLA Ops:
  0.7 1.3 stack.121
  2.0 1.3 stack.125
  3.2 0.3 stack.122
  3.6 0.3 stack.126
  3.9 0.5 fusion
  4.4 0.2 reshape.381
  4.6 0.4 fusion.1
  5.2 4.1 %collective-permute-start = (bf16[80,384]{1,0:T(8,128)(2,1)S(1)}, bf16[80,384]{1,0:T(8,128)(2,1)S(1)}, u32[]{:S(2)}, u32[]{:S(2)}) collective-permute-start(bf16[80,384]{1,0:T(8,128)(2,1)S(1)} %pad_maximum_fusion.27), channel_id=1, source_target_pairs={{0,8},{1,9},{2,10},{3,11},{4,12},{5,13},{6,14},{7,15},{8,0},{9,1},... | collective-permute-start | bytes 184328 | tf_op jit(solution)/shard_map/ppermute | solution.py:24
  9.4 2.7 %collective-permute-done = bf16[80,384]{1,0:T(8,128)(2,1)S(1)} collective-permute-done((bf16[80,384]{1,0:T(8,128)(2,1)S(1)}, bf16[80,384]{1,0:T(8,128)(2,1)S(1)}, u32[]{:S(2)}, u32[]{:S(2)}) %collective-permute-start) | collective-permute-done | bytes 61472 | tf_op jit(solution)/shard_map/ppermute | solution.py:24
  12.3 2.7 %collective-permute-start.1 = (bf16[416,384]{1,0:T(8,128)(2,1)S(1)}, bf16[416,384]{1,0:T(8,128)(2,1)S(1)}, u32[]{:S(2)}, u32[]{:S(2)}) collective-permute-start(bf16[416,384]{1,0:T(8,128)(2,1)S(1)} %pad_maximum_fusion.12), channel_id=1, source_target_pairs={{0,4},{1,5},{2,6},{3,7},{4,0},{5,1},{6,2},{7,3},{8,12},{9,13},{10,... | collective-permute-start | bytes 958472 | tf_op jit(solution)/shard_map/ppermute | solution.py:24
  15.1 2.3 %collective-permute-start.5 = (bf16[416,384]{1,0:T(8,128)(2,1)S(1)}, bf16[416,384]{1,0:T(8,128)(2,1)S(1)}, u32[]{:S(2)}, u32[]{:S(2)}) collective-permute-start(bf16[416,384]{1,0:T(8,128)(2,1)S(1)} %pad_maximum_fusion.13), channel_id=1, source_target_pairs={{0,2},{1,3},{2,0},{3,1},{4,6},{5,7},{6,4},{7,5},{8,10},{9,11},{10,... | collective-permute-start | bytes 958472 | tf_op jit(solution)/shard_map/ppermute | solution.py:24
  17.3 5.2 %collective-permute-done.1 = bf16[416,384]{1,0:T(8,128)(2,1)S(1)} collective-permute-done((bf16[416,384]{1,0:T(8,128)(2,1)S(1)}, bf16[416,384]{1,0:T(8,128)(2,1)S(1)}, u32[]{:S(2)}, u32[]{:S(2)}) %collective-permute-start.1) | collective-permute-done | bytes 319520 | tf_op jit(solution)/shard_map/ppermute | solution.py:24
  22.9 1.6 %collective-permute-start.2 = (bf16[832,384]{1,0:T(8,128)(2,1)S(1)}, bf16[832,384]{1,0:T(8,128)(2,1)S(1)}, u32[]{:S(2)}, u32[]{:S(2)}) collective-permute-start(bf16[832,384]{1,0:T(8,128)(2,1)S(1)} %pad_maximum_fusion.4), channel_id=1, source_target_pairs={{0,2},{1,3},{2,0},{3,1},{4,6},{5,7},{6,4},{7,5},{8,10},{9,11},{10,... | collective-permute-start | bytes 1916936 | tf_op jit(solution)/shard_map/ppermute | solution.py:24
  24.8 1.8 %collective-permute-start.6 = (bf16[832,384]{1,0:T(8,128)(2,1)S(1)}, bf16[832,384]{1,0:T(8,128)(2,1)S(1)}, u32[]{:S(2)}, u32[]{:S(2)}) collective-permute-start(bf16[832,384]{1,0:T(8,128)(2,1)S(1)} %pad_maximum_fusion.5), channel_id=1, source_target_pairs={{0,4},{1,5},{2,6},{3,7},{4,0},{5,1},{6,2},{7,3},{8,12},{9,13},{10,... | collective-permute-start | bytes 1916936 | tf_op jit(solution)/shard_map/ppermute | solution.py:24
  26.6 12.0 %collective-permute-done.2 = bf16[832,384]{1,0:T(8,128)(2,1)S(1)} collective-permute-done((bf16[832,384]{1,0:T(8,128)(2,1)S(1)}, bf16[832,384]{1,0:T(8,128)(2,1)S(1)}, u32[]{:S(2)}, u32[]{:S(2)}) %collective-permute-start.2) | collective-permute-done | bytes 639008 | tf_op jit(solution)/shard_map/ppermute | solution.py:24
  39.3 0.7 collective-permute-done.6
  40.5 1.2 pad_maximum_fusion.1.mine_ref
  41.7 0.7 fusion.33
  42.4 0.7 fusion.34
  43.1 1.1 copy-done.5
  44.2 14.0 %shard_map.84 = (bf16[128,384]{1,0:T(8,128)(2,1)}, bf16[128,384]{1,0:T(8,128)(2,1)}, f32[2,512,384]{2,1,0:T(8,128)}, f32[2,256,384]{2,1,0:T(8,128)}, f32[2,64,384]{2,1,0:T(8,128)}, /*index=5*/bf16[1664,384]{1,0:T(8,128)(2,1)}) custom-call(s32[3,12]{1,0:T(4,128)} %offsets_ref.3, bf16[128,384]{1,0:T(8,128)(2,1)} %get-tuple-element.42.query_ref, ...), custom_call_target="tpu_custom_call" | custom-call | tf_op jit(solution)/shard_map/pallas_call | solution.py:221
  58.1 0.5 collective-permute-start.8
  58.6 1.4 %slice_bitcast_fusion.25 = (s32[6]{0:T(128)}, s32[6]{0:T(128)S(1)}, s32[6]{0:T(128)S(1)}, s32[6]{0:T(128)}) fusion(s32[3,12]{1,0:T(4,128)} %offsets_ref.3), kind=kLoop, calls=%fused_computation.115 | loop fusion | bytes 192 | tf_op jit(solution)/shard_map/eq | solution.py:46
  60.0 0.6 iota_compare_fusion
  60.7 0.8 broadcast_in_dim.131
  61.6 14.0 %shard_map.85 = (bf16[128,384]{1,0:T(8,128)(2,1)}, bf16[128,384]{1,0:T(8,128)(2,1)}, f32[2,512,384]{2,1,0:T(8,128)}, f32[2,256,384]{2,1,0:T(8,128)}, f32[2,64,384]{2,1,0:T(8,128)}, /*index=5*/bf16[1664,384]{1,0:T(8,128)(2,1)}) custom-call(s32[3,12]{1,0:T(4,128)} %offsets_ref.3, bf16[128,384]{1,0:T(8,128)(2,1)} %get-tuple-element.43.query_ref, ...), custom_call_target="tpu_custom_call" | custom-call | tf_op jit(solution)/shard_map/pallas_call | solution.py:221
  75.6 0.6 iota_compare_fusion.3
  76.3 0.8 broadcast_in_dim.125
  77.1 0.8 broadcast_in_dim.140
  77.9 0.8 broadcast_in_dim.141
  78.8 0.8 broadcast_in_dim.136
  79.7 1.8 %pad_maximum_fusion.19 = (bf16[128,768]{1,0:T(8,128)(2,1)}, bf16[128,768]{1,0:T(8,128)(2,1)}) fusion(bf16[128,384]{1,0:T(8,128)(2,1)} %get-tuple-element.17, bf16[128,384]{1,0:T(8,128)(2,1)} %get-tuple-element.16, bf16[128,384]{1,0:T(8,128)(2,1)} %get-tuple-element.19, bf16[128,384]{1,0:T(8,128)(2,1)} %get-tuple-element.18), kind=kLoop, calls=%fused_computation.60 | loop fusion | flops 786432 | bytes 786432 | tf_op jit(solution)/shard_map/concatenate | solution.py:290
  81.5 1.4 %slice.408 = f32[1024,384]{1,0:T(8,128)S(1)} slice(bf16[1664,384]{1,0:T(8,128)(2,1)} %collective-permute-done.8), slice={[0:1024], [0:384]} | slice | bytes 3145728 | tf_op jit(solution)/shard_map/slice | solution.py:261
  82.9 0.3 copy-done.3
  83.1 0.2 copy_add_fusion.1
  83.4 1.1 slice.411
  84.7 0.9 slice.413
  85.8 1.1 collective-permute-start.9
  87.2 0.2 copy_add_fusion
  87.5 1.0 copy-done.7
  88.8 0.7 copy-done.12
  89.6 1.8 %collective-permute-start.13 = (bf16[832,384]{1,0:T(8,128)(2,1)S(1)}, bf16[832,384]{1,0:T(8,128)(2,1)S(1)}, u32[]{:S(2)}, u32[]{:S(2)}) collective-permute-start(bf16[832,384]{1,0:T(8,128)(2,1)S(1)} %pad_maximum_fusion.7), channel_id=1, source_target_pairs={{0,4},{1,5},{2,6},{3,7},{4,0},{5,1},{6,2},{7,3},{8,12},{9,13},{10,... | collective-permute-start | bytes 1916936 | tf_op jit(solution)/shard_map/ppermute | solution.py:24
  91.4 11.3 %collective-permute-done.9 = bf16[832,384]{1,0:T(8,128)(2,1)S(1)} collective-permute-done((bf16[832,384]{1,0:T(8,128)(2,1)S(1)}, bf16[832,384]{1,0:T(8,128)(2,1)S(1)}, u32[]{:S(2)}, u32[]{:S(2)}) %collective-permute-start.9) | collective-permute-done | bytes 639008 | tf_op jit(solution)/shard_map/ppermute | solution.py:24
  103.1 1.7 %collective-permute-start.10 = (bf16[416,384]{1,0:T(8,128)(2,1)S(1)}, bf16[416,384]{1,0:T(8,128)(2,1)S(1)}, u32[]{:S(2)}, u32[]{:S(2)}) collective-permute-start(bf16[416,384]{1,0:T(8,128)(2,1)S(1)} %pad_maximum_fusion.14), channel_id=1, source_target_pairs={{0,4},{1,5},{2,6},{3,7},{4,0},{5,1},{6,2},{7,3},{8,12},{9,13},{10,... | collective-permute-start | bytes 958472 | tf_op jit(solution)/shard_map/ppermute | solution.py:24
  104.8 2.1 %collective-permute-done.13 = bf16[832,384]{1,0:T(8,128)(2,1)S(1)} collective-permute-done((bf16[832,384]{1,0:T(8,128)(2,1)S(1)}, bf16[832,384]{1,0:T(8,128)(2,1)S(1)}, u32[]{:S(2)}, u32[]{:S(2)}) %collective-permute-start.13) | collective-permute-done | bytes 639008 | tf_op jit(solution)/shard_map/ppermute | solution.py:24
  107.3 1.1 collective-permute-start.14
  108.4 4.9 %collective-permute-done.10 = bf16[416,384]{1,0:T(8,128)(2,1)S(1)} collective-permute-done((bf16[416,384]{1,0:T(8,128)(2,1)S(1)}, bf16[416,384]{1,0:T(8,128)(2,1)S(1)}, u32[]{:S(2)}, u32[]{:S(2)}) %collective-permute-start.10) | collective-permute-done | bytes 319520 | tf_op jit(solution)/shard_map/ppermute | solution.py:24
  113.4 2.6 %collective-permute-done.14 = bf16[416,384]{1,0:T(8,128)(2,1)S(1)} collective-permute-done((bf16[416,384]{1,0:T(8,128)(2,1)S(1)}, bf16[416,384]{1,0:T(8,128)(2,1)S(1)}, u32[]{:S(2)}, u32[]{:S(2)}) %collective-permute-start.14) | collective-permute-done | bytes 319520 | tf_op jit(solution)/shard_map/ppermute | solution.py:24
  116.3 3.6 %collective-permute-start.11 = (bf16[80,384]{1,0:T(8,128)(2,1)S(1)}, bf16[80,384]{1,0:T(8,128)(2,1)S(1)}, u32[]{:S(2)}, u32[]{:S(2)}) collective-permute-start(bf16[80,384]{1,0:T(8,128)(2,1)S(1)} %pad_maximum_fusion.29), channel_id=1, source_target_pairs={{0,8},{1,9},{2,10},{3,11},{4,12},{5,13},{6,14},{7,15},{8,0},{9,1},... | collective-permute-start | bytes 184328 | tf_op jit(solution)/shard_map/ppermute | solution.py:24
  120.0 0.6 pad_maximum_fusion.30
  120.7 0.8 squeeze.78
  121.6 0.4 collective-permute-done.11
  122.2 0.5 copy-done.9
  122.8 1.0 broadcast_in_dim.128
  123.8 0.7 slice.434
  124.7 1.0 broadcast_in_dim.134
  125.7 1.3 fusion.13
  127.0 0.8 slice.460
  128.1 0.2 broadcast_in_dim.139
  128.3 0.7 slice.462
  129.2 0.2 broadcast_in_dim.144
  129.4 0.5 copy-done.14
  130.1 0.7 pad_maximum_fusion.22
  130.8 0.7 pad_maximum_fusion.21
  (184 shorter events, 5.6 us)
Async XLA Ops:
  0.6 2.6 %copy-start.1 = (bf16[128,768]{1,0:T(8,128)(2,1)S(1)}, bf16[128,768]{1,0:T(8,128)(2,1)}, u32[]{:S(2)}) copy-start(bf16[128,768]{1,0:T(8,128)(2,1)} %param.7) | copy-start | bytes 589828
  0.6 3.3 %copy-start.17 = (s32[3,12]{1,0:T(4,128)S(1)}, s32[3,12]{1,0:T(4,128)}, u32[]{:S(2)}) copy-start(s32[3,12]{1,0:T(4,128)} %offsets_ref.3) | copy-start | bytes 436
  4.4 5.0 %copy-start.2 = (bf16[128,768]{1,0:T(8,128)(2,1)S(1)}, bf16[128,768]{1,0:T(8,128)(2,1)}, u32[]{:S(2)}) copy-start(bf16[128,768]{1,0:T(8,128)(2,1)} %param.6) | copy-start | bytes 589828
  5.2 7.0 %collective-permute-start = (bf16[80,384]{1,0:T(8,128)(2,1)S(1)}, bf16[80,384]{1,0:T(8,128)(2,1)S(1)}, u32[]{:S(2)}, u32[]{:S(2)}) collective-permute-start(bf16[80,384]{1,0:T(8,128)(2,1)S(1)} %pad_maximum_fusion.27), channel_id=1, source_target_pairs={{0,8},{1,9},{2,10},{3,11},{4,12},{5,13},{6,14},{7,15},{8,0},{9,1},... | collective-permute-start | bytes 184328 | tf_op jit(solution)/shard_map/ppermute | solution.py:24
  9.3 5.6 %collective-permute-start.4 = (bf16[80,384]{1,0:T(8,128)(2,1)S(1)}, bf16[80,384]{1,0:T(8,128)(2,1)S(1)}, u32[]{:S(2)}, u32[]{:S(2)}) collective-permute-start(bf16[80,384]{1,0:T(8,128)(2,1)S(1)} %pad_maximum_fusion.28), channel_id=1, source_target_pairs={{0,8},{1,9},{2,10},{3,11},{4,12},{5,13},{6,14},{7,15},{8,0},{9,1},... | collective-permute-start | bytes 184328 | tf_op jit(solution)/shard_map/ppermute | solution.py:24
  12.3 10.3 %collective-permute-start.1 = (bf16[416,384]{1,0:T(8,128)(2,1)S(1)}, bf16[416,384]{1,0:T(8,128)(2,1)S(1)}, u32[]{:S(2)}, u32[]{:S(2)}) collective-permute-start(bf16[416,384]{1,0:T(8,128)(2,1)S(1)} %pad_maximum_fusion.12), channel_id=1, source_target_pairs={{0,4},{1,5},{2,6},{3,7},{4,0},{5,1},{6,2},{7,3},{8,12},{9,13},{10,... | collective-permute-start | bytes 958472 | tf_op jit(solution)/shard_map/ppermute | solution.py:24
  15.1 9.4 %collective-permute-start.5 = (bf16[416,384]{1,0:T(8,128)(2,1)S(1)}, bf16[416,384]{1,0:T(8,128)(2,1)S(1)}, u32[]{:S(2)}, u32[]{:S(2)}) collective-permute-start(bf16[416,384]{1,0:T(8,128)(2,1)S(1)} %pad_maximum_fusion.13), channel_id=1, source_target_pairs={{0,2},{1,3},{2,0},{3,1},{4,6},{5,7},{6,4},{7,5},{8,10},{9,11},{10,... | collective-permute-start | bytes 958472 | tf_op jit(solution)/shard_map/ppermute | solution.py:24
  22.9 15.7 %collective-permute-start.2 = (bf16[832,384]{1,0:T(8,128)(2,1)S(1)}, bf16[832,384]{1,0:T(8,128)(2,1)S(1)}, u32[]{:S(2)}, u32[]{:S(2)}) collective-permute-start(bf16[832,384]{1,0:T(8,128)(2,1)S(1)} %pad_maximum_fusion.4), channel_id=1, source_target_pairs={{0,2},{1,3},{2,0},{3,1},{4,6},{5,7},{6,4},{7,5},{8,10},{9,11},{10,... | collective-permute-start | bytes 1916936 | tf_op jit(solution)/shard_map/ppermute | solution.py:24
  24.8 15.1 %collective-permute-start.6 = (bf16[832,384]{1,0:T(8,128)(2,1)S(1)}, bf16[832,384]{1,0:T(8,128)(2,1)S(1)}, u32[]{:S(2)}, u32[]{:S(2)}) collective-permute-start(bf16[832,384]{1,0:T(8,128)(2,1)S(1)} %pad_maximum_fusion.5), channel_id=1, source_target_pairs={{0,4},{1,5},{2,6},{3,7},{4,0},{5,1},{6,2},{7,3},{8,12},{9,13},{10,... | collective-permute-start | bytes 1916936 | tf_op jit(solution)/shard_map/ppermute | solution.py:24
  39.2 1.1 copy-start
  39.2 3.9 %collective-permute-start.3 = (bf16[1664,384]{1,0:T(8,128)(2,1)S(1)}, bf16[1664,384]{1,0:T(8,128)(2,1)S(1)}, u32[]{:S(2)}, u32[]{:S(2)}) collective-permute-start(bf16[1664,384]{1,0:T(8,128)(2,1)S(1)} %pad_maximum_fusion.mine_ref), channel_id=1, source_target_pairs={{0,1},{1,0},{2,3},{3,2},{4,5},{5,4},{6,7},{7,6},{8,9},{9,8},{10,11... | collective-permute-start | bytes 3833864 | tf_op jit(solution)/shard_map/ppermute | solution.py:24
  40.5 1.2 copy-start.10
  40.5 1.9 %copy-start.11 = (bf16[128,768]{1,0:T(8,128)(2,1)S(1)}, bf16[128,768]{1,0:T(8,128)(2,1)}, u32[]{:S(2)}) copy-start(bf16[128,768]{1,0:T(8,128)(2,1)} %param.5) | copy-start | bytes 589828
  41.7 19.9 %collective-permute-start.7 = (bf16[1664,384]{1,0:T(8,128)(2,1)}, bf16[1664,384]{1,0:T(8,128)(2,1)}, u32[]{:S(2)}, u32[]{:S(2)}) collective-permute-start(bf16[1664,384]{1,0:T(8,128)(2,1)} %pad_maximum_fusion.1.mine_ref), channel_id=1, source_target_pairs={{0,1},{1,0},{2,3},{3,2},{4,5},{5,4},{6,7},{7,6},{8,9},{9,8},{10,11... | collective-permute-start | bytes 3833864 | tf_op jit(solution)/shard_map/ppermute | solution.py:24
  43.1 1.1 copy-start.5
  58.1 23.4 %collective-permute-start.8 = (bf16[1664,384]{1,0:T(8,128)(2,1)}, bf16[1664,384]{1,0:T(8,128)(2,1)}, u32[]{:S(2)}, u32[]{:S(2)}) collective-permute-start(bf16[1664,384]{1,0:T(8,128)(2,1)} %get-tuple-element.21), channel_id=1, source_target_pairs={{0,1},{1,0},{2,3},{3,2},{4,5},{5,4},{6,7},{7,6},{8,9},{9,8},{10,11... | collective-permute-start | bytes 3833864 | tf_op jit(solution)/shard_map/ppermute | solution.py:24
  75.5 11.4 %collective-permute-start.12 = (bf16[1664,384]{1,0:T(8,128)(2,1)}, bf16[1664,384]{1,0:T(8,128)(2,1)S(1)}, u32[]{:S(2)}, u32[]{:S(2)}) collective-permute-start(bf16[1664,384]{1,0:T(8,128)(2,1)} %get-tuple-element.25), channel_id=1, source_target_pairs={{0,1},{1,0},{2,3},{3,2},{4,5},{5,4},{6,7},{7,6},{8,9},{9,8},{10,11... | collective-permute-start | bytes 3833864 | tf_op jit(solution)/shard_map/ppermute | solution.py:24
  81.5 1.6 %copy-start.3 = (f32[2,512,384]{2,1,0:T(8,128)S(1)}, f32[2,512,384]{2,1,0:T(8,128)}, u32[]{:S(2)}) copy-start(f32[2,512,384]{2,1,0:T(8,128)} %get-tuple-element.20) | copy-start | bytes 4718596
  83.3 1.3 copy-start.8
  84.6 1.1 copy-start.13
  85.8 1.4 %copy-start.4 = (f32[2,512,384]{2,1,0:T(8,128)S(1)}, f32[2,512,384]{2,1,0:T(8,128)}, u32[]{:S(2)}) copy-start(f32[2,512,384]{2,1,0:T(8,128)} %get-tuple-element.24) | copy-start | bytes 4718596
  85.8 16.8 %collective-permute-start.9 = (bf16[832,384]{1,0:T(8,128)(2,1)S(1)}, bf16[832,384]{1,0:T(8,128)(2,1)S(1)}, u32[]{:S(2)}, u32[]{:S(2)}) collective-permute-start(bf16[832,384]{1,0:T(8,128)(2,1)S(1)} %pad_maximum_fusion.6), channel_id=1, source_target_pairs={{0,2},{1,3},{2,0},{3,1},{4,6},{5,7},{6,4},{7,5},{8,10},{9,11},{10,... | collective-permute-start | bytes 1916936 | tf_op jit(solution)/shard_map/ppermute | solution.py:24
  87.4 1.1 copy-start.7
  88.6 0.9 copy-start.12
  89.6 17.2 %collective-permute-start.13 = (bf16[832,384]{1,0:T(8,128)(2,1)S(1)}, bf16[832,384]{1,0:T(8,128)(2,1)S(1)}, u32[]{:S(2)}, u32[]{:S(2)}) collective-permute-start(bf16[832,384]{1,0:T(8,128)(2,1)S(1)} %pad_maximum_fusion.7), channel_id=1, source_target_pairs={{0,4},{1,5},{2,6},{3,7},{4,0},{5,1},{6,2},{7,3},{8,12},{9,13},{10,... | collective-permute-start | bytes 1916936 | tf_op jit(solution)/shard_map/ppermute | solution.py:24
  103.1 10.2 %collective-permute-start.10 = (bf16[416,384]{1,0:T(8,128)(2,1)S(1)}, bf16[416,384]{1,0:T(8,128)(2,1)S(1)}, u32[]{:S(2)}, u32[]{:S(2)}) collective-permute-start(bf16[416,384]{1,0:T(8,128)(2,1)S(1)} %pad_maximum_fusion.14), channel_id=1, source_target_pairs={{0,4},{1,5},{2,6},{3,7},{4,0},{5,1},{6,2},{7,3},{8,12},{9,13},{10,... | collective-permute-start | bytes 958472 | tf_op jit(solution)/shard_map/ppermute | solution.py:24
  107.3 8.8 %collective-permute-start.14 = (bf16[416,384]{1,0:T(8,128)(2,1)S(1)}, bf16[416,384]{1,0:T(8,128)(2,1)S(1)}, u32[]{:S(2)}, u32[]{:S(2)}) collective-permute-start(bf16[416,384]{1,0:T(8,128)(2,1)S(1)} %pad_maximum_fusion.15), channel_id=1, source_target_pairs={{0,2},{1,3},{2,0},{3,1},{4,6},{5,7},{6,4},{7,5},{8,10},{9,11},{10,... | collective-permute-start | bytes 958472 | tf_op jit(solution)/shard_map/ppermute | solution.py:24
  116.3 5.8 %collective-permute-start.11 = (bf16[80,384]{1,0:T(8,128)(2,1)S(1)}, bf16[80,384]{1,0:T(8,128)(2,1)S(1)}, u32[]{:S(2)}, u32[]{:S(2)}) collective-permute-start(bf16[80,384]{1,0:T(8,128)(2,1)S(1)} %pad_maximum_fusion.29), channel_id=1, source_target_pairs={{0,8},{1,9},{2,10},{3,11},{4,12},{5,13},{6,14},{7,15},{8,0},{9,1},... | collective-permute-start | bytes 184328 | tf_op jit(solution)/shard_map/ppermute | solution.py:24
  120.7 6.4 %collective-permute-start.15 = (bf16[80,384]{1,0:T(8,128)(2,1)}, bf16[80,384]{1,0:T(8,128)(2,1)}, u32[]{:S(2)}, u32[]{:S(2)}) collective-permute-start(bf16[80,384]{1,0:T(8,128)(2,1)} %pad_maximum_fusion.30), channel_id=1, source_target_pairs={{0,8},{1,9},{2,10},{3,11},{4,12},{5,13},{6,14},{7,15},{8,0},{9,1},... | collective-permute-start | bytes 184328 | tf_op jit(solution)/shard_map/ppermute | solution.py:24
  122.1 0.6 copy-start.9
  124.6 1.1 copy-start.15
  125.7 2.2 %copy-start.6 = (f32[2,32,6,64]{3,2,1,0:T(8,128)S(1)}, f32[2,32,6,64]{3,2,1,0:T(8,128)}, u32[]{:S(2)}) copy-start(f32[2,32,6,64]{3,2,1,0:T(8,128)} %squeeze.78) | copy-start | bytes 294916
  129.1 0.8 copy-start.14
  129.1 0.8 copy-start.16

commit v8 on v7

--- a/solution.py
+++ b/solution.py
@@ -43,11 +43,10 @@
     pair, count, width = picked.shape
     heads = offsets_row.shape[0]
     grouped = picked.reshape(pair, count, 1, heads, width // heads)
-    chosen = (jnp.arange(stride, dtype=jnp.int32)[:, None] == offsets_row[None, :])[
-        None, None, :, :, None
-    ]
-    widened = jnp.where(chosen, grouped, jnp.zeros((), picked.dtype))
-    return widened.reshape(pair, count * stride, width)
+    chosen = (jnp.arange(stride, dtype=jnp.int32)[:, None] == offsets_row[None, :]).astype(
+        picked.dtype
+    )[None, None, :, :, None]
+    return (grouped * chosen).reshape(pair, count * stride, width)
 
 
 def attention_kernel(head_dim, score_scale, head_base, half_counts):

time: 132 us -> 132 us (level)
    mul x0 -> x16, local copies, waits for them, and re-layouts: none -> 7.24 us  [spread_rows(): return (grouped * chosen).reshape(pair, count * stride, width)]
    broadcast_in_dim x16 -> x0, local copies, waits for them, and re-layouts: 7.2 us -> none  [spread_rows(): widened = jnp.where(chosen, grouped, jnp.zeros((), picked.dtype))]
    unnamed x36 -> x44, local copies, waits for them, and re-layouts: 4.47 us -> 4.92 us
  transfers between devices with their start and end apart: 16 -> 16, of which waited for: 9 -> 8; matrix products, arithmetic and copies ran while one was open for 19% -> 18% of each run, Pallas kernels for 21% -> 21%
where the time goes in v8:
time: 132 us; the launch traced here: 131 us
  waiting for transfers between devices  41.5 us (31%)
  Pallas kernels  27.9 us (21%)
  local copies, waits for them, and re-layouts  27.6 us (21%)
  starting transfers between devices  22.5 us (17%)
  other arithmetic  9.89 us (7%)
  between operations  1.81 us (1%)
    ppermute x16, waiting for transfers between devices, exchange(): return lax.ppermute(block, 'seq', route)  41.5 us
    pallas_call x2, Pallas kernels, per_device(): pl.pallas_call(attention_kernel(head_dim, score_scale, half * heads_per_h...  27.9 us
    ppermute x16, starting transfers between devices, exchange(): return lax.ppermute(block, 'seq', route)  22.5 us
    mul x16, local copies, waits for them, and re-layouts, spread_rows(): return (grouped * chosen).reshape(pair, count * stride, width)  7.24 us
    unnamed x44, local copies, waits for them, and re-layouts  4.92 us
    slice x6, local copies, waits for them, and re-layouts, per_device(): partial.append(kept + incoming[cursor:cursor + count].reshape(kept.shape))  3.55 us
    another operation x4, local copies, waits for them, and re-layouts, per_device(): kv_rows = jnp.stack([key_rows, value_rows])  3.2 us
  transfers between devices with their start and end apart: 16, of which 8 were waited for; matrix products, arithmetic and copies ran while one was open for 18% of the time, Pallas kernels for 21%

profile of v8, /device:TPU:0, one launch (start us, length us, event | category | flops | bytes accessed | tf_op | source)
XLA Modules:
  0.0 131.3 jit_solution(5585366474526546088)
XLA Ops:
  0.7 1.3 stack.121
  2.0 1.3 stack.125
  3.2 0.3 stack.122
  3.6 0.3 stack.126
  3.9 0.5 fusion
  4.4 0.2 reshape.385
  4.6 0.4 fusion.1
  5.2 4.1 %collective-permute-start = (bf16[80,384]{1,0:T(8,128)(2,1)S(1)}, bf16[80,384]{1,0:T(8,128)(2,1)S(1)}, u32[]{:S(2)}, u32[]{:S(2)}) collective-permute-start(bf16[80,384]{1,0:T(8,128)(2,1)S(1)} %pad_maximum_fusion.27), channel_id=1, source_target_pairs={{0,8},{1,9},{2,10},{3,11},{4,12},{5,13},{6,14},{7,15},{8,0},{9,1},... | collective-permute-start | bytes 184328 | tf_op jit(solution)/shard_map/ppermute | solution.py:24
  9.4 2.7 %collective-permute-done = bf16[80,384]{1,0:T(8,128)(2,1)S(1)} collective-permute-done((bf16[80,384]{1,0:T(8,128)(2,1)S(1)}, bf16[80,384]{1,0:T(8,128)(2,1)S(1)}, u32[]{:S(2)}, u32[]{:S(2)}) %collective-permute-start) | collective-permute-done | bytes 61472 | tf_op jit(solution)/shard_map/ppermute | solution.py:24
  12.3 2.7 %collective-permute-start.1 = (bf16[416,384]{1,0:T(8,128)(2,1)S(1)}, bf16[416,384]{1,0:T(8,128)(2,1)S(1)}, u32[]{:S(2)}, u32[]{:S(2)}) collective-permute-start(bf16[416,384]{1,0:T(8,128)(2,1)S(1)} %pad_maximum_fusion.12), channel_id=1, source_target_pairs={{0,4},{1,5},{2,6},{3,7},{4,0},{5,1},{6,2},{7,3},{8,12},{9,13},{10,... | collective-permute-start | bytes 958472 | tf_op jit(solution)/shard_map/ppermute | solution.py:24
  15.1 2.3 %collective-permute-start.5 = (bf16[416,384]{1,0:T(8,128)(2,1)S(1)}, bf16[416,384]{1,0:T(8,128)(2,1)S(1)}, u32[]{:S(2)}, u32[]{:S(2)}) collective-permute-start(bf16[416,384]{1,0:T(8,128)(2,1)S(1)} %pad_maximum_fusion.13), channel_id=1, source_target_pairs={{0,2},{1,3},{2,0},{3,1},{4,6},{5,7},{6,4},{7,5},{8,10},{9,11},{10,... | collective-permute-start | bytes 958472 | tf_op jit(solution)/shard_map/ppermute | solution.py:24
  17.3 5.2 %collective-permute-done.1 = bf16[416,384]{1,0:T(8,128)(2,1)S(1)} collective-permute-done((bf16[416,384]{1,0:T(8,128)(2,1)S(1)}, bf16[416,384]{1,0:T(8,128)(2,1)S(1)}, u32[]{:S(2)}, u32[]{:S(2)}) %collective-permute-start.1) | collective-permute-done | bytes 319520 | tf_op jit(solution)/shard_map/ppermute | solution.py:24
  22.9 1.6 %collective-permute-start.2 = (bf16[832,384]{1,0:T(8,128)(2,1)S(1)}, bf16[832,384]{1,0:T(8,128)(2,1)S(1)}, u32[]{:S(2)}, u32[]{:S(2)}) collective-permute-start(bf16[832,384]{1,0:T(8,128)(2,1)S(1)} %pad_maximum_fusion.4), channel_id=1, source_target_pairs={{0,2},{1,3},{2,0},{3,1},{4,6},{5,7},{6,4},{7,5},{8,10},{9,11},{10,... | collective-permute-start | bytes 1916936 | tf_op jit(solution)/shard_map/ppermute | solution.py:24
  24.8 1.8 %collective-permute-start.6 = (bf16[832,384]{1,0:T(8,128)(2,1)S(1)}, bf16[832,384]{1,0:T(8,128)(2,1)S(1)}, u32[]{:S(2)}, u32[]{:S(2)}) collective-permute-start(bf16[832,384]{1,0:T(8,128)(2,1)S(1)} %pad_maximum_fusion.5), channel_id=1, source_target_pairs={{0,4},{1,5},{2,6},{3,7},{4,0},{5,1},{6,2},{7,3},{8,12},{9,13},{10,... | collective-permute-start | bytes 1916936 | tf_op jit(solution)/shard_map/ppermute | solution.py:24
  26.6 12.0 %collective-permute-done.2 = bf16[832,384]{1,0:T(8,128)(2,1)S(1)} collective-permute-done((bf16[832,384]{1,0:T(8,128)(2,1)S(1)}, bf16[832,384]{1,0:T(8,128)(2,1)S(1)}, u32[]{:S(2)}, u32[]{:S(2)}) %collective-permute-start.2) | collective-permute-done | bytes 639008 | tf_op jit(solution)/shard_map/ppermute | solution.py:24
  39.3 0.7 collective-permute-done.6
  40.5 1.2 pad_maximum_fusion.1.mine_ref
  41.7 0.7 fusion.37
  42.4 0.7 fusion.38
  43.1 1.1 copy-done.5
  44.2 13.9 %shard_map.84 = (bf16[128,384]{1,0:T(8,128)(2,1)}, bf16[128,384]{1,0:T(8,128)(2,1)}, f32[2,512,384]{2,1,0:T(8,128)}, f32[2,256,384]{2,1,0:T(8,128)}, f32[2,64,384]{2,1,0:T(8,128)}, /*index=5*/bf16[1664,384]{1,0:T(8,128)(2,1)}) custom-call(s32[3,12]{1,0:T(4,128)} %offsets_ref.3, bf16[128,384]{1,0:T(8,128)(2,1)} %get-tuple-element.42.query_ref, ...), custom_call_target="tpu_custom_call" | custom-call | tf_op jit(solution)/shard_map/pallas_call | solution.py:220
  58.1 0.5 collective-permute-start.8
  58.6 1.4 %slice_bitcast_fusion.25 = (s32[6]{0:T(128)}, s32[6]{0:T(128)S(1)}, s32[6]{0:T(128)S(1)}, s32[6]{0:T(128)}) fusion(s32[3,12]{1,0:T(4,128)} %offsets_ref.3), kind=kLoop, calls=%fused_computation.119 | loop fusion | bytes 192 | tf_op jit(solution)/shard_map/eq | solution.py:46
  60.0 0.6 fusion.23
  60.7 0.8 mul.89
  61.6 14.0 %shard_map.85 = (bf16[128,384]{1,0:T(8,128)(2,1)}, bf16[128,384]{1,0:T(8,128)(2,1)}, f32[2,512,384]{2,1,0:T(8,128)}, f32[2,256,384]{2,1,0:T(8,128)}, f32[2,64,384]{2,1,0:T(8,128)}, /*index=5*/bf16[1664,384]{1,0:T(8,128)(2,1)}) custom-call(s32[3,12]{1,0:T(4,128)} %offsets_ref.3, bf16[128,384]{1,0:T(8,128)(2,1)} %get-tuple-element.43.query_ref, ...), custom_call_target="tpu_custom_call" | custom-call | tf_op jit(solution)/shard_map/pallas_call | solution.py:220
  75.6 0.6 fusion.25
  76.3 0.8 mul.83
  77.2 0.8 mul.100
  78.0 0.8 mul.101
  79.0 0.8 mul.95
  79.8 0.8 pad_maximum_fusion.19
  80.6 1.4 %slice.408 = f32[1024,384]{1,0:T(8,128)S(1)} slice(bf16[1664,384]{1,0:T(8,128)(2,1)} %collective-permute-done.8), slice={[0:1024], [0:384]} | slice | bytes 3145728 | tf_op jit(solution)/shard_map/slice | solution.py:260
  82.0 0.3 copy-done.3
  82.2 0.2 copy_add_fusion.1
  82.5 1.1 slice.411
  83.8 0.9 slice.413
  84.9 1.1 collective-permute-start.9
  86.3 0.2 copy_add_fusion
  86.6 1.0 copy-done.9
  87.9 0.7 copy-done.15
  88.7 1.8 %collective-permute-start.13 = (bf16[832,384]{1,0:T(8,128)(2,1)S(1)}, bf16[832,384]{1,0:T(8,128)(2,1)S(1)}, u32[]{:S(2)}, u32[]{:S(2)}) collective-permute-start(bf16[832,384]{1,0:T(8,128)(2,1)S(1)} %pad_maximum_fusion.7), channel_id=1, source_target_pairs={{0,4},{1,5},{2,6},{3,7},{4,0},{5,1},{6,2},{7,3},{8,12},{9,13},{10,... | collective-permute-start | bytes 1916936 | tf_op jit(solution)/shard_map/ppermute | solution.py:24
  90.5 11.2 %collective-permute-done.9 = bf16[832,384]{1,0:T(8,128)(2,1)S(1)} collective-permute-done((bf16[832,384]{1,0:T(8,128)(2,1)S(1)}, bf16[832,384]{1,0:T(8,128)(2,1)S(1)}, u32[]{:S(2)}, u32[]{:S(2)}) %collective-permute-start.9) | collective-permute-done | bytes 639008 | tf_op jit(solution)/shard_map/ppermute | solution.py:24
  102.2 1.7 %collective-permute-start.10 = (bf16[416,384]{1,0:T(8,128)(2,1)S(1)}, bf16[416,384]{1,0:T(8,128)(2,1)S(1)}, u32[]{:S(2)}, u32[]{:S(2)}) collective-permute-start(bf16[416,384]{1,0:T(8,128)(2,1)S(1)} %pad_maximum_fusion.14), channel_id=1, source_target_pairs={{0,4},{1,5},{2,6},{3,7},{4,0},{5,1},{6,2},{7,3},{8,12},{9,13},{10,... | collective-permute-start | bytes 958472 | tf_op jit(solution)/shard_map/ppermute | solution.py:24
  103.9 2.1 %collective-permute-done.13 = bf16[832,384]{1,0:T(8,128)(2,1)S(1)} collective-permute-done((bf16[832,384]{1,0:T(8,128)(2,1)S(1)}, bf16[832,384]{1,0:T(8,128)(2,1)S(1)}, u32[]{:S(2)}, u32[]{:S(2)}) %collective-permute-start.13) | collective-permute-done | bytes 639008 | tf_op jit(solution)/shard_map/ppermute | solution.py:24
  106.4 1.1 collective-permute-start.14
  107.5 4.9 %collective-permute-done.10 = bf16[416,384]{1,0:T(8,128)(2,1)S(1)} collective-permute-done((bf16[416,384]{1,0:T(8,128)(2,1)S(1)}, bf16[416,384]{1,0:T(8,128)(2,1)S(1)}, u32[]{:S(2)}, u32[]{:S(2)}) %collective-permute-start.10) | collective-permute-done | bytes 319520 | tf_op jit(solution)/shard_map/ppermute | solution.py:24
  112.5 2.6 %collective-permute-done.14 = bf16[416,384]{1,0:T(8,128)(2,1)S(1)} collective-permute-done((bf16[416,384]{1,0:T(8,128)(2,1)S(1)}, bf16[416,384]{1,0:T(8,128)(2,1)S(1)}, u32[]{:S(2)}, u32[]{:S(2)}) %collective-permute-start.14) | collective-permute-done | bytes 319520 | tf_op jit(solution)/shard_map/ppermute | solution.py:24
  115.3 3.7 %collective-permute-start.11 = (bf16[80,384]{1,0:T(8,128)(2,1)S(1)}, bf16[80,384]{1,0:T(8,128)(2,1)S(1)}, u32[]{:S(2)}, u32[]{:S(2)}) collective-permute-start(bf16[80,384]{1,0:T(8,128)(2,1)S(1)} %pad_maximum_fusion.29), channel_id=1, source_target_pairs={{0,8},{1,9},{2,10},{3,11},{4,12},{5,13},{6,14},{7,15},{8,0},{9,1},... | collective-permute-start | bytes 184328 | tf_op jit(solution)/shard_map/ppermute | solution.py:24
  119.2 0.6 pad_maximum_fusion.30
  119.8 0.8 squeeze.78
  120.6 0.7 squeeze.80
  121.6 1.0 mul.81
  122.8 1.0 mul.87
  123.8 1.4 %fusion.13 = bf16[2,128,384]{2,1,0:T(8,128)(2,1)S(1)} fusion(f32[2,128,384]{2,1,0:T(8,128)S(1)} %bitcast.231, f32[2,2,128,384]{3,2,1,0:T(8,128)S(1)} %fusion.3, f32[2,128,384]{2,1,0:T(8,128)} %mul.87, f32[2,128,384]{2,1,0:T(8,128)} %mul.81, f32[128,384]{1,0:T(8,128)} %mul.89, f32[128,384]{1,0:T(8,128)} %mul.83), kind=kLoop, calls=%fused_computation.38 | loop fusion | flops 589824 | bytes 2162688 | tf_op jit(solution)/shard_map/convert.13 | solution.py:306
  125.2 0.7 slice_bitcast_fusion.9
  125.9 0.8 slice.460
  126.9 0.2 mul.93
  127.1 0.7 slice.462
  128.0 0.2 mul.99
  128.3 0.6 copy-done.7
  129.1 0.8 copy-done.11
  129.9 0.7 pad_maximum_fusion.22
  130.6 0.7 pad_maximum_fusion.21
  (192 shorter events, 5.6 us)
Async XLA Ops:
  0.6 2.6 %copy-start.1 = (bf16[128,768]{1,0:T(8,128)(2,1)S(1)}, bf16[128,768]{1,0:T(8,128)(2,1)}, u32[]{:S(2)}) copy-start(bf16[128,768]{1,0:T(8,128)(2,1)} %param.7) | copy-start | bytes 589828
  0.6 3.3 %copy-start.21 = (s32[3,12]{1,0:T(4,128)S(1)}, s32[3,12]{1,0:T(4,128)}, u32[]{:S(2)}) copy-start(s32[3,12]{1,0:T(4,128)} %offsets_ref.3) | copy-start | bytes 436
  4.4 5.0 %copy-start.2 = (bf16[128,768]{1,0:T(8,128)(2,1)S(1)}, bf16[128,768]{1,0:T(8,128)(2,1)}, u32[]{:S(2)}) copy-start(bf16[128,768]{1,0:T(8,128)(2,1)} %param.6) | copy-start | bytes 589828
  5.2 7.0 %collective-permute-start = (bf16[80,384]{1,0:T(8,128)(2,1)S(1)}, bf16[80,384]{1,0:T(8,128)(2,1)S(1)}, u32[]{:S(2)}, u32[]{:S(2)}) collective-permute-start(bf16[80,384]{1,0:T(8,128)(2,1)S(1)} %pad_maximum_fusion.27), channel_id=1, source_target_pairs={{0,8},{1,9},{2,10},{3,11},{4,12},{5,13},{6,14},{7,15},{8,0},{9,1},... | collective-permute-start | bytes 184328 | tf_op jit(solution)/shard_map/ppermute | solution.py:24
  9.3 5.6 %collective-permute-start.4 = (bf16[80,384]{1,0:T(8,128)(2,1)S(1)}, bf16[80,384]{1,0:T(8,128)(2,1)S(1)}, u32[]{:S(2)}, u32[]{:S(2)}) collective-permute-start(bf16[80,384]{1,0:T(8,128)(2,1)S(1)} %pad_maximum_fusion.28), channel_id=1, source_target_pairs={{0,8},{1,9},{2,10},{3,11},{4,12},{5,13},{6,14},{7,15},{8,0},{9,1},... | collective-permute-start | bytes 184328 | tf_op jit(solution)/shard_map/ppermute | solution.py:24
  12.3 10.3 %collective-permute-start.1 = (bf16[416,384]{1,0:T(8,128)(2,1)S(1)}, bf16[416,384]{1,0:T(8,128)(2,1)S(1)}, u32[]{:S(2)}, u32[]{:S(2)}) collective-permute-start(bf16[416,384]{1,0:T(8,128)(2,1)S(1)} %pad_maximum_fusion.12), channel_id=1, source_target_pairs={{0,4},{1,5},{2,6},{3,7},{4,0},{5,1},{6,2},{7,3},{8,12},{9,13},{10,... | collective-permute-start | bytes 958472 | tf_op jit(solution)/shard_map/ppermute | solution.py:24
  15.1 9.4 %collective-permute-start.5 = (bf16[416,384]{1,0:T(8,128)(2,1)S(1)}, bf16[416,384]{1,0:T(8,128)(2,1)S(1)}, u32[]{:S(2)}, u32[]{:S(2)}) collective-permute-start(bf16[416,384]{1,0:T(8,128)(2,1)S(1)} %pad_maximum_fusion.13), channel_id=1, source_target_pairs={{0,2},{1,3},{2,0},{3,1},{4,6},{5,7},{6,4},{7,5},{8,10},{9,11},{10,... | collective-permute-start | bytes 958472 | tf_op jit(solution)/shard_map/ppermute | solution.py:24
  22.9 15.7 %collective-permute-start.2 = (bf16[832,384]{1,0:T(8,128)(2,1)S(1)}, bf16[832,384]{1,0:T(8,128)(2,1)S(1)}, u32[]{:S(2)}, u32[]{:S(2)}) collective-permute-start(bf16[832,384]{1,0:T(8,128)(2,1)S(1)} %pad_maximum_fusion.4), channel_id=1, source_target_pairs={{0,2},{1,3},{2,0},{3,1},{4,6},{5,7},{6,4},{7,5},{8,10},{9,11},{10,... | collective-permute-start | bytes 1916936 | tf_op jit(solution)/shard_map/ppermute | solution.py:24
  24.8 15.1 %collective-permute-start.6 = (bf16[832,384]{1,0:T(8,128)(2,1)S(1)}, bf16[832,384]{1,0:T(8,128)(2,1)S(1)}, u32[]{:S(2)}, u32[]{:S(2)}) collective-permute-start(bf16[832,384]{1,0:T(8,128)(2,1)S(1)} %pad_maximum_fusion.5), channel_id=1, source_target_pairs={{0,4},{1,5},{2,6},{3,7},{4,0},{5,1},{6,2},{7,3},{8,12},{9,13},{10,... | collective-permute-start | bytes 1916936 | tf_op jit(solution)/shard_map/ppermute | solution.py:24
  39.2 1.1 copy-start
  39.2 3.9 %collective-permute-start.3 = (bf16[1664,384]{1,0:T(8,128)(2,1)S(1)}, bf16[1664,384]{1,0:T(8,128)(2,1)S(1)}, u32[]{:S(2)}, u32[]{:S(2)}) collective-permute-start(bf16[1664,384]{1,0:T(8,128)(2,1)S(1)} %pad_maximum_fusion.mine_ref), channel_id=1, source_target_pairs={{0,1},{1,0},{2,3},{3,2},{4,5},{5,4},{6,7},{7,6},{8,9},{9,8},{10,11... | collective-permute-start | bytes 3833864 | tf_op jit(solution)/shard_map/ppermute | solution.py:24
  40.5 1.2 copy-start.13
  40.5 1.9 %copy-start.14 = (bf16[128,768]{1,0:T(8,128)(2,1)S(1)}, bf16[128,768]{1,0:T(8,128)(2,1)}, u32[]{:S(2)}) copy-start(bf16[128,768]{1,0:T(8,128)(2,1)} %param.5) | copy-start | bytes 589828
  41.7 19.9 %collective-permute-start.7 = (bf16[1664,384]{1,0:T(8,128)(2,1)}, bf16[1664,384]{1,0:T(8,128)(2,1)}, u32[]{:S(2)}, u32[]{:S(2)}) collective-permute-start(bf16[1664,384]{1,0:T(8,128)(2,1)} %pad_maximum_fusion.1.mine_ref), channel_id=1, source_target_pairs={{0,1},{1,0},{2,3},{3,2},{4,5},{5,4},{6,7},{7,6},{8,9},{9,8},{10,11... | collective-permute-start | bytes 3833864 | tf_op jit(solution)/shard_map/ppermute | solution.py:24
  43.1 1.1 copy-start.5
  58.1 22.5 %collective-permute-start.8 = (bf16[1664,384]{1,0:T(8,128)(2,1)}, bf16[1664,384]{1,0:T(8,128)(2,1)}, u32[]{:S(2)}, u32[]{:S(2)}) collective-permute-start(bf16[1664,384]{1,0:T(8,128)(2,1)} %get-tuple-element.21), channel_id=1, source_target_pairs={{0,1},{1,0},{2,3},{3,2},{4,5},{5,4},{6,7},{7,6},{8,9},{9,8},{10,11... | collective-permute-start | bytes 3833864 | tf_op jit(solution)/shard_map/ppermute | solution.py:24
  75.5 10.5 %collective-permute-start.12 = (bf16[1664,384]{1,0:T(8,128)(2,1)}, bf16[1664,384]{1,0:T(8,128)(2,1)S(1)}, u32[]{:S(2)}, u32[]{:S(2)}) collective-permute-start(bf16[1664,384]{1,0:T(8,128)(2,1)} %get-tuple-element.25), channel_id=1, source_target_pairs={{0,1},{1,0},{2,3},{3,2},{4,5},{5,4},{6,7},{7,6},{8,9},{9,8},{10,11... | collective-permute-start | bytes 3833864 | tf_op jit(solution)/shard_map/ppermute | solution.py:24
  77.2 2.6 %copy-start.17 = (bf16[128,384]{1,0:T(8,128)(2,1)S(1)}, bf16[128,384]{1,0:T(8,128)(2,1)}, u32[]{:S(2)}) copy-start(bf16[128,384]{1,0:T(8,128)(2,1)} %get-tuple-element.16) | copy-start | bytes 294916
  77.2 2.6 %copy-start.18 = (bf16[128,384]{1,0:T(8,128)(2,1)S(1)}, bf16[128,384]{1,0:T(8,128)(2,1)}, u32[]{:S(2)}) copy-start(bf16[128,384]{1,0:T(8,128)(2,1)} %get-tuple-element.18) | copy-start | bytes 294916
  77.2 2.6 %copy-start.19 = (bf16[128,384]{1,0:T(8,128)(2,1)S(1)}, bf16[128,384]{1,0:T(8,128)(2,1)}, u32[]{:S(2)}) copy-start(bf16[128,384]{1,0:T(8,128)(2,1)} %get-tuple-element.17) | copy-start | bytes 294916
  77.2 2.6 %copy-start.20 = (bf16[128,384]{1,0:T(8,128)(2,1)S(1)}, bf16[128,384]{1,0:T(8,128)(2,1)}, u32[]{:S(2)}) copy-start(bf16[128,384]{1,0:T(8,128)(2,1)} %get-tuple-element.19) | copy-start | bytes 294916
  80.6 1.6 %copy-start.3 = (f32[2,512,384]{2,1,0:T(8,128)S(1)}, f32[2,512,384]{2,1,0:T(8,128)}, u32[]{:S(2)}) copy-start(f32[2,512,384]{2,1,0:T(8,128)} %get-tuple-element.20) | copy-start | bytes 4718596
  82.4 1.3 copy-start.10
  83.7 1.1 copy-start.16
  84.9 1.4 %copy-start.4 = (f32[2,512,384]{2,1,0:T(8,128)S(1)}, f32[2,512,384]{2,1,0:T(8,128)}, u32[]{:S(2)}) copy-start(f32[2,512,384]{2,1,0:T(8,128)} %get-tuple-element.24) | copy-start | bytes 4718596
  84.9 16.8 %collective-permute-start.9 = (bf16[832,384]{1,0:T(8,128)(2,1)S(1)}, bf16[832,384]{1,0:T(8,128)(2,1)S(1)}, u32[]{:S(2)}, u32[]{:S(2)}) collective-permute-start(bf16[832,384]{1,0:T(8,128)(2,1)S(1)} %pad_maximum_fusion.6), channel_id=1, source_target_pairs={{0,2},{1,3},{2,0},{3,1},{4,6},{5,7},{6,4},{7,5},{8,10},{9,11},{10,... | collective-permute-start | bytes 1916936 | tf_op jit(solution)/shard_map/ppermute | solution.py:24
  86.5 1.1 copy-start.9
  87.7 0.9 copy-start.15
  88.7 17.2 %collective-permute-start.13 = (bf16[832,384]{1,0:T(8,128)(2,1)S(1)}, bf16[832,384]{1,0:T(8,128)(2,1)S(1)}, u32[]{:S(2)}, u32[]{:S(2)}) collective-permute-start(bf16[832,384]{1,0:T(8,128)(2,1)S(1)} %pad_maximum_fusion.7), channel_id=1, source_target_pairs={{0,4},{1,5},{2,6},{3,7},{4,0},{5,1},{6,2},{7,3},{8,12},{9,13},{10,... | collective-permute-start | bytes 1916936 | tf_op jit(solution)/shard_map/ppermute | solution.py:24
  102.2 10.2 %collective-permute-start.10 = (bf16[416,384]{1,0:T(8,128)(2,1)S(1)}, bf16[416,384]{1,0:T(8,128)(2,1)S(1)}, u32[]{:S(2)}, u32[]{:S(2)}) collective-permute-start(bf16[416,384]{1,0:T(8,128)(2,1)S(1)} %pad_maximum_fusion.14), channel_id=1, source_target_pairs={{0,4},{1,5},{2,6},{3,7},{4,0},{5,1},{6,2},{7,3},{8,12},{9,13},{10,... | collective-permute-start | bytes 958472 | tf_op jit(solution)/shard_map/ppermute | solution.py:24
  106.4 8.8 %collective-permute-start.14 = (bf16[416,384]{1,0:T(8,128)(2,1)S(1)}, bf16[416,384]{1,0:T(8,128)(2,1)S(1)}, u32[]{:S(2)}, u32[]{:S(2)}) collective-permute-start(bf16[416,384]{1,0:T(8,128)(2,1)S(1)} %pad_maximum_fusion.15), channel_id=1, source_target_pairs={{0,2},{1,3},{2,0},{3,1},{4,6},{5,7},{6,4},{7,5},{8,10},{9,11},{10,... | collective-permute-start | bytes 958472 | tf_op jit(solution)/shard_map/ppermute | solution.py:24
  115.3 6.0 %collective-permute-start.11 = (bf16[80,384]{1,0:T(8,128)(2,1)S(1)}, bf16[80,384]{1,0:T(8,128)(2,1)S(1)}, u32[]{:S(2)}, u32[]{:S(2)}) collective-permute-start(bf16[80,384]{1,0:T(8,128)(2,1)S(1)} %pad_maximum_fusion.29), channel_id=1, source_target_pairs={{0,8},{1,9},{2,10},{3,11},{4,12},{5,13},{6,14},{7,15},{8,0},{9,1},... | collective-permute-start | bytes 184328 | tf_op jit(solution)/shard_map/ppermute | solution.py:24
  119.8 6.1 %collective-permute-start.15 = (bf16[80,384]{1,0:T(8,128)(2,1)}, bf16[80,384]{1,0:T(8,128)(2,1)}, u32[]{:S(2)}, u32[]{:S(2)}) collective-permute-start(bf16[80,384]{1,0:T(8,128)(2,1)} %pad_maximum_fusion.30), channel_id=1, source_target_pairs={{0,8},{1,9},{2,10},{3,11},{4,12},{5,13},{6,14},{7,15},{8,0},{9,1},... | collective-permute-start | bytes 184328 | tf_op jit(solution)/shard_map/ppermute | solution.py:24
  123.8 2.9 %copy-start.6 = (f32[2,32,6,64]{3,2,1,0:T(8,128)S(1)}, f32[2,32,6,64]{3,2,1,0:T(8,128)}, u32[]{:S(2)}) copy-start(f32[2,32,6,64]{3,2,1,0:T(8,128)} %squeeze.78) | copy-start | bytes 294916
  126.8 1.1 copy-start.12
  127.9 0.9 copy-start.7
  128.0 1.0 copy-start.8
  129.0 0.9 copy-start.11

commit v9 on v8

--- a/solution.py
+++ b/solution.py
@@ -49,8 +49,9 @@
     return (grouped * chosen).reshape(pair, count * stride, width)
 
 
-def attention_kernel(head_dim, score_scale, head_base, half_counts):
+def attention_kernel(head_dim, score_scale, head_base, half_counts, aliased):
     def kernel(offsets_ref, query_ref, grad_ref, mine_ref, arrived_ref, *refs):
+        refs = refs[aliased:]
         out_ref, qgrad_ref = refs[0:2]
         keep_refs = refs[2:5]
         message_ref = refs[5]
@@ -210,18 +211,24 @@
             layouts.append(axis_bits)
 
         results = []
+        full_outs = ()
         for half in range(halves):
             mine, arrived, half_counts = gathered_halves[half]
             cols = slice(half * half_width, (half + 1) * half_width)
             pairs = half_width // block_width
             key_rows_total = 2 * sum(half_counts)
             row_block = pl.BlockSpec((local_rows, block_width), lambda p, offs: (0, p))
+            wide_block = pl.BlockSpec(
+                (local_rows, block_width), lambda p, offs, base=half * pairs: (0, p + base)
+            )
             message_block = pl.BlockSpec((key_rows_total, block_width), lambda p, offs: (0, p))
             outs = pl.pallas_call(
-                attention_kernel(head_dim, score_scale, half * heads_per_half, half_counts),
+                attention_kernel(
+                    head_dim, score_scale, half * heads_per_half, half_counts, len(full_outs)
+                ),
                 out_shape=(
-                    jax.ShapeDtypeStruct((local_rows, half_width), jnp.bfloat16),
-                    jax.ShapeDtypeStruct((local_rows, half_width), jnp.bfloat16),
+                    jax.ShapeDtypeStruct((local_rows, model_width), jnp.bfloat16),
+                    jax.ShapeDtypeStruct((local_rows, model_width), jnp.bfloat16),
                 )
                 + tuple(
                     jax.ShapeDtypeStruct((2, count, half_width), jnp.float32)
@@ -231,17 +238,19 @@
                 grid_spec=pltpu.PrefetchScalarGridSpec(
                     num_scalar_prefetch=1,
                     grid=(pairs,),
-                    in_specs=[row_block, row_block, message_block, message_block],
-                    out_specs=[row_block, row_block]
+                    in_specs=[row_block, row_block, message_block, message_block]
+                    + [pl.BlockSpec(memory_space=pl.ANY) for _ in full_outs],
+                    out_specs=[wide_block, wide_block]
                     + [
                         pl.BlockSpec((2, count, block_width), lambda p, offs: (0, 0, p))
                         for count in half_counts
                     ]
                     + [message_block],
                 ),
+                input_output_aliases={5 + index: index for index in range(len(full_outs))},
                 compiler_params=pltpu.CompilerParams(vmem_limit_bytes=100 * 1024 * 1024),
-            )(head_offsets, query_rows[:, cols], output_grad[:, cols], mine, arrived)
-            attended, query_grad = outs[:2]
+            )(head_offsets, query_rows[:, cols], output_grad[:, cols], mine, arrived, *full_outs)
+            full_outs = tuple(outs[:2])
             kept_terms = outs[2:5]
             message = outs[5]
 
@@ -283,11 +292,11 @@
             for branch in range(3):
                 spread = spread_rows(partial[branch], STRIDES[branch], offsets_half[branch])
                 total_grad = spread if total_grad is None else total_grad + spread
-            results.append((attended, query_grad, total_grad[0], total_grad[1]))
-
-        return tuple(
+            results.append((total_grad[0], total_grad[1]))
+
+        return full_outs + tuple(
             jnp.concatenate([result[index] for result in results], axis=1).astype(jnp.bfloat16)
-            for index in range(4)
+            for index in range(2)
         )
 
     return per_device

time: 132 us -> 129 us (0.977)
  other arithmetic: 9.89 us -> 8.57 us
    unnamed x44 -> x40, local copies, waits for them, and re-layouts: 4.92 us -> 5.08 us
  transfers between devices with their start and end apart: 16 -> 16, of which waited for: 8 -> 8; matrix products, arithmetic and copies ran while one was open for 18% -> 17% of each run, Pallas kernels for 21% -> 22%
where the time goes in v9:
time: 129 us
  waiting for transfers between devices  41.5 us (32%)
  Pallas kernels  28 us (22%)
  local copies, waits for them, and re-layouts  26.4 us (20%)
  starting transfers between devices  22.2 us (17%)
  other arithmetic  8.57 us (7%)
  between operations  1.81 us (1%)
    ppermute x16, waiting for transfers between devices, exchange(): return lax.ppermute(block, 'seq', route)  41.5 us
    pallas_call x2, Pallas kernels, per_device(): pl.pallas_call(attention_kernel(head_dim, score_scale, half * heads_per_h...  28 us
    ppermute x16, starting transfers between devices, exchange(): return lax.ppermute(block, 'seq', route)  22.2 us
    mul x16, local copies, waits for them, and re-layouts, spread_rows(): return (grouped * chosen).reshape(pair, count * stride, width)  6.5 us
    unnamed x40, local copies, waits for them, and re-layouts  5.08 us
    slice x6, local copies, waits for them, and re-layouts, per_device(): partial.append(kept + incoming[cursor:cursor + count].reshape(kept.shape))  3.55 us
    another operation x4, local copies, waits for them, and re-layouts, per_device(): kv_rows = jnp.stack([key_rows, value_rows])  3.2 us
  transfers between devices with their start and end apart: 16, of which 8 were waited for; matrix products, arithmetic and copies ran while one was open for 17% of the time, Pallas kernels for 22%

profile of v9, /device:TPU:0, one launch (start us, length us, event | category | flops | bytes accessed | tf_op | source)
XLA Modules:
  0.0 128.5 jit_solution(6587014117797990583)
XLA Ops:
  0.7 1.3 %stack.121 = bf16[1,32,4,12,64]{4,3,2,1,0:T(8,128)(2,1)S(1)} reshape(bf16[128,768]{1,0:T(8,128)(2,1)} %param.6) | data formatting | bytes 393216 | tf_op jit(solution)/shard_map/stack | solution.py:177
  2.0 1.3 stack.125
  3.2 0.3 stack.122
  3.6 0.3 stack.126
  3.9 0.5 fusion
  4.4 0.2 reshape.385
  4.6 0.4 fusion.1
  5.2 4.1 %collective-permute-start.4 = (bf16[80,384]{1,0:T(8,128)(2,1)S(1)}, bf16[80,384]{1,0:T(8,128)(2,1)S(1)}, u32[]{:S(2)}, u32[]{:S(2)}) collective-permute-start(bf16[80,384]{1,0:T(8,128)(2,1)S(1)} %pad_maximum_fusion.26), channel_id=1, source_target_pairs={{0,8},{1,9},{2,10},{3,11},{4,12},{5,13},{6,14},{7,15},{8,0},{9,1},... | collective-permute-start | bytes 184328 | tf_op jit(solution)/shard_map/ppermute | solution.py:24
  9.4 2.7 %collective-permute-done.4 = bf16[80,384]{1,0:T(8,128)(2,1)S(1)} collective-permute-done((bf16[80,384]{1,0:T(8,128)(2,1)S(1)}, bf16[80,384]{1,0:T(8,128)(2,1)S(1)}, u32[]{:S(2)}, u32[]{:S(2)}) %collective-permute-start.4) | collective-permute-done | bytes 61472 | tf_op jit(solution)/shard_map/ppermute | solution.py:24
  12.3 2.7 %collective-permute-start.5 = (bf16[416,384]{1,0:T(8,128)(2,1)S(1)}, bf16[416,384]{1,0:T(8,128)(2,1)S(1)}, u32[]{:S(2)}, u32[]{:S(2)}) collective-permute-start(bf16[416,384]{1,0:T(8,128)(2,1)S(1)} %pad_maximum_fusion.13), channel_id=1, source_target_pairs={{0,4},{1,5},{2,6},{3,7},{4,0},{5,1},{6,2},{7,3},{8,12},{9,13},{10,... | collective-permute-start | bytes 958472 | tf_op jit(solution)/shard_map/ppermute | solution.py:24
  15.1 2.3 %collective-permute-start.1 = (bf16[416,384]{1,0:T(8,128)(2,1)S(1)}, bf16[416,384]{1,0:T(8,128)(2,1)S(1)}, u32[]{:S(2)}, u32[]{:S(2)}) collective-permute-start(bf16[416,384]{1,0:T(8,128)(2,1)S(1)} %pad_maximum_fusion.12), channel_id=1, source_target_pairs={{0,2},{1,3},{2,0},{3,1},{4,6},{5,7},{6,4},{7,5},{8,10},{9,11},{10,... | collective-permute-start | bytes 958472 | tf_op jit(solution)/shard_map/ppermute | solution.py:24
  17.3 5.2 %collective-permute-done.5 = bf16[416,384]{1,0:T(8,128)(2,1)S(1)} collective-permute-done((bf16[416,384]{1,0:T(8,128)(2,1)S(1)}, bf16[416,384]{1,0:T(8,128)(2,1)S(1)}, u32[]{:S(2)}, u32[]{:S(2)}) %collective-permute-start.5) | collective-permute-done | bytes 319520 | tf_op jit(solution)/shard_map/ppermute | solution.py:24
  22.9 1.6 %collective-permute-start.6 = (bf16[832,384]{1,0:T(8,128)(2,1)S(1)}, bf16[832,384]{1,0:T(8,128)(2,1)S(1)}, u32[]{:S(2)}, u32[]{:S(2)}) collective-permute-start(bf16[832,384]{1,0:T(8,128)(2,1)S(1)} %pad_maximum_fusion.5), channel_id=1, source_target_pairs={{0,2},{1,3},{2,0},{3,1},{4,6},{5,7},{6,4},{7,5},{8,10},{9,11},{10,... | collective-permute-start | bytes 1916936 | tf_op jit(solution)/shard_map/ppermute | solution.py:24
  24.8 1.8 %collective-permute-start.2 = (bf16[832,384]{1,0:T(8,128)(2,1)S(1)}, bf16[832,384]{1,0:T(8,128)(2,1)S(1)}, u32[]{:S(2)}, u32[]{:S(2)}) collective-permute-start(bf16[832,384]{1,0:T(8,128)(2,1)S(1)} %pad_maximum_fusion.4), channel_id=1, source_target_pairs={{0,4},{1,5},{2,6},{3,7},{4,0},{5,1},{6,2},{7,3},{8,12},{9,13},{10,... | collective-permute-start | bytes 1916936 | tf_op jit(solution)/shard_map/ppermute | solution.py:24
  26.6 12.0 %collective-permute-done.6 = bf16[832,384]{1,0:T(8,128)(2,1)S(1)} collective-permute-done((bf16[832,384]{1,0:T(8,128)(2,1)S(1)}, bf16[832,384]{1,0:T(8,128)(2,1)S(1)}, u32[]{:S(2)}, u32[]{:S(2)}) %collective-permute-start.6) | collective-permute-done | bytes 639008 | tf_op jit(solution)/shard_map/ppermute | solution.py:24
  39.1 0.1 pad_maximum_fusion.1.mine_ref
  39.3 0.6 collective-permute-done.2
  40.2 0.2 copy-done
  40.6 1.2 pad_maximum_fusion.mine_ref
  41.7 0.7 fusion.37
  42.5 1.1 copy-done.5
  43.6 14.0 %shard_map.84 = (bf16[128,768]{1,0:T(8,128)(2,1)}, bf16[128,768]{1,0:T(8,128)(2,1)}, f32[2,512,384]{2,1,0:T(8,128)}, f32[2,256,384]{2,1,0:T(8,128)}, f32[2,64,384]{2,1,0:T(8,128)}, /*index=5*/bf16[1664,384]{1,0:T(8,128)(2,1)}) custom-call(s32[3,12]{1,0:T(4,128)} %offsets_ref.3, bf16[128,384]{1,0:T(8,128)(2,1)} %get-tuple-element.73.query_ref, ...), custom_call_target="tpu_custom_call" | custom-call | tf_op jit(solution)/shard_map/pallas_call | solution.py:225
  57.5 0.5 collective-permute-start.8
  58.0 1.5 %slice_bitcast_fusion.25 = (s32[6]{0:T(128)}, s32[6]{0:T(128)}, s32[6]{0:T(128)}, s32[6]{0:T(128)}) fusion(s32[3,12]{1,0:T(4,128)} %offsets_ref.3), kind=kLoop, calls=%fused_computation.117 | loop fusion | bytes 192 | tf_op jit(solution)/shard_map/eq | solution.py:46
  59.5 14.0 %shard_map.85 = (bf16[128,768]{1,0:T(8,128)(2,1)}, bf16[128,768]{1,0:T(8,128)(2,1)}, f32[2,512,384]{2,1,0:T(8,128)}, f32[2,256,384]{2,1,0:T(8,128)}, f32[2,64,384]{2,1,0:T(8,128)}, /*index=5*/bf16[1664,384]{1,0:T(8,128)(2,1)}) custom-call(s32[3,12]{1,0:T(4,128)} %offsets_ref.3, ...), custom_call_target="tpu_custom_call", output_to_operand_aliasing={{0}: (5, {}), {1}: (6, {})} | custom-call | tf_op jit(solution)/shard_map/pallas_call | solution.py:225
  73.6 0.7 fusion.23
  74.4 0.8 mul.89
  75.2 0.1 mul.82
  75.3 0.8 mul.83
  76.3 0.8 mul.101
  77.2 0.8 mul.95
  78.1 1.4 %slice.408 = f32[1024,384]{1,0:T(8,128)S(1)} slice(bf16[1664,384]{1,0:T(8,128)(2,1)} %collective-permute-done.8), slice={[0:1024], [0:384]} | slice | bytes 3145728 | tf_op jit(solution)/shard_map/slice | solution.py:269
  79.4 0.3 copy-done.4
  79.7 0.2 copy_add_fusion.1
  79.9 1.1 slice.411
  81.3 0.9 slice.413
  82.4 1.1 collective-permute-start.9
  83.5 0.2 copy-done.3
  83.8 0.2 copy_add_fusion
  84.1 1.0 copy-done.9
  85.3 0.7 copy-done.15
  86.2 1.8 %collective-permute-start.13 = (bf16[832,384]{1,0:T(8,128)(2,1)S(1)}, bf16[832,384]{1,0:T(8,128)(2,1)S(1)}, u32[]{:S(2)}, u32[]{:S(2)}) collective-permute-start(bf16[832,384]{1,0:T(8,128)(2,1)S(1)} %pad_maximum_fusion.7), channel_id=1, source_target_pairs={{0,4},{1,5},{2,6},{3,7},{4,0},{5,1},{6,2},{7,3},{8,12},{9,13},{10,... | collective-permute-start | bytes 1916936 | tf_op jit(solution)/shard_map/ppermute | solution.py:24
  88.0 11.2 %collective-permute-done.9 = bf16[832,384]{1,0:T(8,128)(2,1)S(1)} collective-permute-done((bf16[832,384]{1,0:T(8,128)(2,1)S(1)}, bf16[832,384]{1,0:T(8,128)(2,1)S(1)}, u32[]{:S(2)}, u32[]{:S(2)}) %collective-permute-start.9) | collective-permute-done | bytes 639008 | tf_op jit(solution)/shard_map/ppermute | solution.py:24
  99.6 1.7 %collective-permute-start.10 = (bf16[416,384]{1,0:T(8,128)(2,1)S(1)}, bf16[416,384]{1,0:T(8,128)(2,1)S(1)}, u32[]{:S(2)}, u32[]{:S(2)}) collective-permute-start(bf16[416,384]{1,0:T(8,128)(2,1)S(1)} %pad_maximum_fusion.14), channel_id=1, source_target_pairs={{0,4},{1,5},{2,6},{3,7},{4,0},{5,1},{6,2},{7,3},{8,12},{9,13},{10,... | collective-permute-start | bytes 958472 | tf_op jit(solution)/shard_map/ppermute | solution.py:24
  101.3 2.1 %collective-permute-done.13 = bf16[832,384]{1,0:T(8,128)(2,1)S(1)} collective-permute-done((bf16[832,384]{1,0:T(8,128)(2,1)S(1)}, bf16[832,384]{1,0:T(8,128)(2,1)S(1)}, u32[]{:S(2)}, u32[]{:S(2)}) %collective-permute-start.13) | collective-permute-done | bytes 639008 | tf_op jit(solution)/shard_map/ppermute | solution.py:24
  103.8 1.1 collective-permute-start.14
  105.0 4.9 %collective-permute-done.10 = bf16[416,384]{1,0:T(8,128)(2,1)S(1)} collective-permute-done((bf16[416,384]{1,0:T(8,128)(2,1)S(1)}, bf16[416,384]{1,0:T(8,128)(2,1)S(1)}, u32[]{:S(2)}, u32[]{:S(2)}) %collective-permute-start.10) | collective-permute-done | bytes 319520 | tf_op jit(solution)/shard_map/ppermute | solution.py:24
  110.0 2.6 %collective-permute-done.14 = bf16[416,384]{1,0:T(8,128)(2,1)S(1)} collective-permute-done((bf16[416,384]{1,0:T(8,128)(2,1)S(1)}, bf16[416,384]{1,0:T(8,128)(2,1)S(1)}, u32[]{:S(2)}, u32[]{:S(2)}) %collective-permute-start.14) | collective-permute-done | bytes 319520 | tf_op jit(solution)/shard_map/ppermute | solution.py:24
  112.8 3.5 %collective-permute-start.11 = (bf16[80,384]{1,0:T(8,128)(2,1)S(1)}, bf16[80,384]{1,0:T(8,128)(2,1)S(1)}, u32[]{:S(2)}, u32[]{:S(2)}) collective-permute-start(bf16[80,384]{1,0:T(8,128)(2,1)S(1)} %pad_maximum_fusion.27), channel_id=1, source_target_pairs={{0,8},{1,9},{2,10},{3,11},{4,12},{5,13},{6,14},{7,15},{8,0},{9,1},... | collective-permute-start | bytes 184328 | tf_op jit(solution)/shard_map/ppermute | solution.py:24
  116.4 0.6 pad_maximum_fusion.28
  117.1 0.8 squeeze.78
  117.9 0.7 squeeze.80
  118.9 1.0 mul.81
  120.1 1.0 mul.87
  121.1 1.4 %fusion.13 = bf16[2,128,384]{2,1,0:T(8,128)(2,1)S(1)} fusion(f32[2,128,384]{2,1,0:T(8,128)S(1)} %bitcast.231, f32[2,2,128,384]{3,2,1,0:T(8,128)S(1)} %fusion.3, f32[2,128,384]{2,1,0:T(8,128)} %mul.87, f32[2,128,384]{2,1,0:T(8,128)} %mul.81, f32[128,384]{1,0:T(8,128)} %mul.89, f32[128,384]{1,0:T(8,128)} %mul.83), kind=kLoop, calls=%fused_computation.38 | loop fusion | flops 589824 | bytes 2162688 | tf_op jit(solution)/shard_map/convert.13 | solution.py:315
  122.5 0.7 slice_bitcast_fusion.9
  123.1 0.8 slice.460
  124.2 0.2 mul.93
  124.4 0.7 slice.462
  125.3 0.2 mul.99
  125.6 0.6 copy-done.7
  126.4 0.8 copy-done.11
  127.1 0.7 pad_maximum_fusion.20
  127.8 0.7 pad_maximum_fusion.19
  (186 shorter events, 5.3 us)
Async XLA Ops:
  0.6 2.6 %copy-start.1 = (bf16[128,768]{1,0:T(8,128)(2,1)S(1)}, bf16[128,768]{1,0:T(8,128)(2,1)}, u32[]{:S(2)}) copy-start(bf16[128,768]{1,0:T(8,128)(2,1)} %param.7) | copy-start | bytes 589828
  0.6 3.3 %copy-start.17 = (s32[3,12]{1,0:T(4,128)S(1)}, s32[3,12]{1,0:T(4,128)}, u32[]{:S(2)}) copy-start(s32[3,12]{1,0:T(4,128)} %offsets_ref.3) | copy-start | bytes 436
  4.4 5.0 %copy-start.2 = (bf16[128,768]{1,0:T(8,128)(2,1)S(1)}, bf16[128,768]{1,0:T(8,128)(2,1)}, u32[]{:S(2)}) copy-start(bf16[128,768]{1,0:T(8,128)(2,1)} %param.6) | copy-start | bytes 589828
  5.2 7.0 %collective-permute-start.4 = (bf16[80,384]{1,0:T(8,128)(2,1)S(1)}, bf16[80,384]{1,0:T(8,128)(2,1)S(1)}, u32[]{:S(2)}, u32[]{:S(2)}) collective-permute-start(bf16[80,384]{1,0:T(8,128)(2,1)S(1)} %pad_maximum_fusion.26), channel_id=1, source_target_pairs={{0,8},{1,9},{2,10},{3,11},{4,12},{5,13},{6,14},{7,15},{8,0},{9,1},... | collective-permute-start | bytes 184328 | tf_op jit(solution)/shard_map/ppermute | solution.py:24
  9.3 5.6 %collective-permute-start = (bf16[80,384]{1,0:T(8,128)(2,1)S(1)}, bf16[80,384]{1,0:T(8,128)(2,1)S(1)}, u32[]{:S(2)}, u32[]{:S(2)}) collective-permute-start(bf16[80,384]{1,0:T(8,128)(2,1)S(1)} %pad_maximum_fusion.25), channel_id=1, source_target_pairs={{0,8},{1,9},{2,10},{3,11},{4,12},{5,13},{6,14},{7,15},{8,0},{9,1},... | collective-permute-start | bytes 184328 | tf_op jit(solution)/shard_map/ppermute | solution.py:24
  12.3 10.3 %collective-permute-start.5 = (bf16[416,384]{1,0:T(8,128)(2,1)S(1)}, bf16[416,384]{1,0:T(8,128)(2,1)S(1)}, u32[]{:S(2)}, u32[]{:S(2)}) collective-permute-start(bf16[416,384]{1,0:T(8,128)(2,1)S(1)} %pad_maximum_fusion.13), channel_id=1, source_target_pairs={{0,4},{1,5},{2,6},{3,7},{4,0},{5,1},{6,2},{7,3},{8,12},{9,13},{10,... | collective-permute-start | bytes 958472 | tf_op jit(solution)/shard_map/ppermute | solution.py:24
  15.1 9.4 %collective-permute-start.1 = (bf16[416,384]{1,0:T(8,128)(2,1)S(1)}, bf16[416,384]{1,0:T(8,128)(2,1)S(1)}, u32[]{:S(2)}, u32[]{:S(2)}) collective-permute-start(bf16[416,384]{1,0:T(8,128)(2,1)S(1)} %pad_maximum_fusion.12), channel_id=1, source_target_pairs={{0,2},{1,3},{2,0},{3,1},{4,6},{5,7},{6,4},{7,5},{8,10},{9,11},{10,... | collective-permute-start | bytes 958472 | tf_op jit(solution)/shard_map/ppermute | solution.py:24
  22.9 15.7 %collective-permute-start.6 = (bf16[832,384]{1,0:T(8,128)(2,1)S(1)}, bf16[832,384]{1,0:T(8,128)(2,1)S(1)}, u32[]{:S(2)}, u32[]{:S(2)}) collective-permute-start(bf16[832,384]{1,0:T(8,128)(2,1)S(1)} %pad_maximum_fusion.5), channel_id=1, source_target_pairs={{0,2},{1,3},{2,0},{3,1},{4,6},{5,7},{6,4},{7,5},{8,10},{9,11},{10,... | collective-permute-start | bytes 1916936 | tf_op jit(solution)/shard_map/ppermute | solution.py:24
  24.8 15.1 %collective-permute-start.2 = (bf16[832,384]{1,0:T(8,128)(2,1)S(1)}, bf16[832,384]{1,0:T(8,128)(2,1)S(1)}, u32[]{:S(2)}, u32[]{:S(2)}) collective-permute-start(bf16[832,384]{1,0:T(8,128)(2,1)S(1)} %pad_maximum_fusion.4), channel_id=1, source_target_pairs={{0,4},{1,5},{2,6},{3,7},{4,0},{5,1},{6,2},{7,3},{8,12},{9,13},{10,... | collective-permute-start | bytes 1916936 | tf_op jit(solution)/shard_map/ppermute | solution.py:24
  39.2 1.1 copy-start
  39.3 3.2 %collective-permute-start.7 = (bf16[1664,384]{1,0:T(8,128)(2,1)S(1)}, bf16[1664,384]{1,0:T(8,128)(2,1)S(1)}, u32[]{:S(2)}, u32[]{:S(2)}) collective-permute-start(bf16[1664,384]{1,0:T(8,128)(2,1)S(1)} %pad_maximum_fusion.1.mine_ref), channel_id=1, source_target_pairs={{0,1},{1,0},{2,3},{3,2},{4,5},{5,4},{6,7},{7,6},{8,9},{9,8},{10,11... | collective-permute-start | bytes 3833864 | tf_op jit(solution)/shard_map/ppermute | solution.py:24
  40.5 1.2 copy-start.13
  40.5 1.2 copy-start.14
  41.7 17.8 %collective-permute-start.3 = (bf16[1664,384]{1,0:T(8,128)(2,1)}, bf16[1664,384]{1,0:T(8,128)(2,1)}, u32[]{:S(2)}, u32[]{:S(2)}) collective-permute-start(bf16[1664,384]{1,0:T(8,128)(2,1)} %pad_maximum_fusion.mine_ref), channel_id=1, source_target_pairs={{0,1},{1,0},{2,3},{3,2},{4,5},{5,4},{6,7},{7,6},{8,9},{9,8},{10,11... | collective-permute-start | bytes 3833864 | tf_op jit(solution)/shard_map/ppermute | solution.py:24
  42.5 1.1 copy-start.5
  57.5 20.5 %collective-permute-start.8 = (bf16[1664,384]{1,0:T(8,128)(2,1)}, bf16[1664,384]{1,0:T(8,128)(2,1)}, u32[]{:S(2)}, u32[]{:S(2)}) collective-permute-start(bf16[1664,384]{1,0:T(8,128)(2,1)} %get-tuple-element.21), channel_id=1, source_target_pairs={{0,1},{1,0},{2,3},{3,2},{4,5},{5,4},{6,7},{7,6},{8,9},{9,8},{10,11... | collective-permute-start | bytes 3833864 | tf_op jit(solution)/shard_map/ppermute | solution.py:24
  73.5 1.7 %copy-start.18 = (s32[6]{0:T(128)S(1)}, s32[6]{0:T(128)}, u32[]{:S(2)}) copy-start(s32[6]{0:T(128)} %get-tuple-element.66) | copy-start | bytes 76
  73.5 1.7 %copy-start.19 = (s32[6]{0:T(128)S(1)}, s32[6]{0:T(128)}, u32[]{:S(2)}) copy-start(s32[6]{0:T(128)} %get-tuple-element.69) | copy-start | bytes 76
  73.5 9.9 %collective-permute-start.12 = (bf16[1664,384]{1,0:T(8,128)(2,1)}, bf16[1664,384]{1,0:T(8,128)(2,1)S(1)}, u32[]{:S(2)}, u32[]{:S(2)}) collective-permute-start(bf16[1664,384]{1,0:T(8,128)(2,1)} %get-tuple-element.25), channel_id=1, source_target_pairs={{0,1},{1,0},{2,3},{3,2},{4,5},{5,4},{6,7},{7,6},{8,9},{9,8},{10,11... | collective-permute-start | bytes 3833864 | tf_op jit(solution)/shard_map/ppermute | solution.py:24
  78.1 1.6 %copy-start.4 = (f32[2,512,384]{2,1,0:T(8,128)S(1)}, f32[2,512,384]{2,1,0:T(8,128)}, u32[]{:S(2)}) copy-start(f32[2,512,384]{2,1,0:T(8,128)} %get-tuple-element.20) | copy-start | bytes 4718596
  79.9 1.3 copy-start.10
  81.1 1.1 copy-start.16
  82.3 1.4 %copy-start.3 = (f32[2,512,384]{2,1,0:T(8,128)S(1)}, f32[2,512,384]{2,1,0:T(8,128)}, u32[]{:S(2)}) copy-start(f32[2,512,384]{2,1,0:T(8,128)} %get-tuple-element.24) | copy-start | bytes 4718596
  82.4 16.8 %collective-permute-start.9 = (bf16[832,384]{1,0:T(8,128)(2,1)S(1)}, bf16[832,384]{1,0:T(8,128)(2,1)S(1)}, u32[]{:S(2)}, u32[]{:S(2)}) collective-permute-start(bf16[832,384]{1,0:T(8,128)(2,1)S(1)} %pad_maximum_fusion.6), channel_id=1, source_target_pairs={{0,2},{1,3},{2,0},{3,1},{4,6},{5,7},{6,4},{7,5},{8,10},{9,11},{10,... | collective-permute-start | bytes 1916936 | tf_op jit(solution)/shard_map/ppermute | solution.py:24
  84.0 1.1 copy-start.9
  85.1 0.9 copy-start.15
  86.2 17.2 %collective-permute-start.13 = (bf16[832,384]{1,0:T(8,128)(2,1)S(1)}, bf16[832,384]{1,0:T(8,128)(2,1)S(1)}, u32[]{:S(2)}, u32[]{:S(2)}) collective-permute-start(bf16[832,384]{1,0:T(8,128)(2,1)S(1)} %pad_maximum_fusion.7), channel_id=1, source_target_pairs={{0,4},{1,5},{2,6},{3,7},{4,0},{5,1},{6,2},{7,3},{8,12},{9,13},{10,... | collective-permute-start | bytes 1916936 | tf_op jit(solution)/shard_map/ppermute | solution.py:24
  99.6 10.2 %collective-permute-start.10 = (bf16[416,384]{1,0:T(8,128)(2,1)S(1)}, bf16[416,384]{1,0:T(8,128)(2,1)S(1)}, u32[]{:S(2)}, u32[]{:S(2)}) collective-permute-start(bf16[416,384]{1,0:T(8,128)(2,1)S(1)} %pad_maximum_fusion.14), channel_id=1, source_target_pairs={{0,4},{1,5},{2,6},{3,7},{4,0},{5,1},{6,2},{7,3},{8,12},{9,13},{10,... | collective-permute-start | bytes 958472 | tf_op jit(solution)/shard_map/ppermute | solution.py:24
  103.8 8.8 %collective-permute-start.14 = (bf16[416,384]{1,0:T(8,128)(2,1)S(1)}, bf16[416,384]{1,0:T(8,128)(2,1)S(1)}, u32[]{:S(2)}, u32[]{:S(2)}) collective-permute-start(bf16[416,384]{1,0:T(8,128)(2,1)S(1)} %pad_maximum_fusion.15), channel_id=1, source_target_pairs={{0,2},{1,3},{2,0},{3,1},{4,6},{5,7},{6,4},{7,5},{8,10},{9,11},{10,... | collective-permute-start | bytes 958472 | tf_op jit(solution)/shard_map/ppermute | solution.py:24
  112.8 5.9 %collective-permute-start.11 = (bf16[80,384]{1,0:T(8,128)(2,1)S(1)}, bf16[80,384]{1,0:T(8,128)(2,1)S(1)}, u32[]{:S(2)}, u32[]{:S(2)}) collective-permute-start(bf16[80,384]{1,0:T(8,128)(2,1)S(1)} %pad_maximum_fusion.27), channel_id=1, source_target_pairs={{0,8},{1,9},{2,10},{3,11},{4,12},{5,13},{6,14},{7,15},{8,0},{9,1},... | collective-permute-start | bytes 184328 | tf_op jit(solution)/shard_map/ppermute | solution.py:24
  117.1 6.1 %collective-permute-start.15 = (bf16[80,384]{1,0:T(8,128)(2,1)}, bf16[80,384]{1,0:T(8,128)(2,1)}, u32[]{:S(2)}, u32[]{:S(2)}) collective-permute-start(bf16[80,384]{1,0:T(8,128)(2,1)} %pad_maximum_fusion.28), channel_id=1, source_target_pairs={{0,8},{1,9},{2,10},{3,11},{4,12},{5,13},{6,14},{7,15},{8,0},{9,1},... | collective-permute-start | bytes 184328 | tf_op jit(solution)/shard_map/ppermute | solution.py:24
  121.1 2.9 %copy-start.6 = (f32[2,32,6,64]{3,2,1,0:T(8,128)S(1)}, f32[2,32,6,64]{3,2,1,0:T(8,128)}, u32[]{:S(2)}) copy-start(f32[2,32,6,64]{3,2,1,0:T(8,128)} %squeeze.78) | copy-start | bytes 294916
  124.1 1.1 copy-start.12
  125.2 0.9 copy-start.7
  125.2 1.0 copy-start.8
  126.3 0.9 copy-start.11

commit v10 on v9

--- a/solution.py
+++ b/solution.py
@@ -111,7 +111,8 @@
             total = jnp.sum(expos[0], axis=1, keepdims=True)
             for branch in range(1, 3):
                 total = total + jnp.sum(expos[branch], axis=1, keepdims=True)
-            probs = [block / total for block in expos]
+            inverse = 1.0 / total
+            probs = [block * inverse for block in expos]
             weights = [block.astype(jnp.bfloat16) for block in probs]
             mixed = jnp.dot(weights[0], values[0], preferred_element_type=jnp.float32)
             for branch in range(1, 3):

time: 129 us -> 129 us (level)
  no operation moved by 1% of the time
where the time goes in v10:
time: 129 us
  waiting for transfers between devices  41.5 us (32%)
  Pallas kernels  28 us (22%)
  local copies, waits for them, and re-layouts  26.4 us (20%)
  starting transfers between devices  22.2 us (17%)
  other arithmetic  8.57 us (7%)
  between operations  1.81 us (1%)
    ppermute x16, waiting for transfers between devices, exchange(): return lax.ppermute(block, 'seq', route)  41.5 us
    pallas_call x2, Pallas kernels, per_device(): pl.pallas_call(attention_kernel(head_dim, score_scale, half * heads_per_h...  28 us
    ppermute x16, starting transfers between devices, exchange(): return lax.ppermute(block, 'seq', route)  22.2 us
    mul x16, local copies, waits for them, and re-layouts, spread_rows(): return (grouped * chosen).reshape(pair, count * stride, width)  6.5 us
    unnamed x40, local copies, waits for them, and re-layouts  5.08 us
    slice x6, local copies, waits for them, and re-layouts, per_device(): partial.append(kept + incoming[cursor:cursor + count].reshape(kept.shape))  3.55 us
    another operation x4, local copies, waits for them, and re-layouts, per_device(): kv_rows = jnp.stack([key_rows, value_rows])  3.2 us
  transfers between devices with their start and end apart: 16, of which 8 were waited for; matrix products, arithmetic and copies ran while one was open for 17% of the time, Pallas kernels for 22%

profile of v10, /device:TPU:0, one launch (start us, length us, event | category | flops | bytes accessed | tf_op | source)
XLA Modules:
  0.0 128.5 jit_solution(6587014117797990583)
XLA Ops:
  0.7 1.3 %stack.121 = bf16[1,32,4,12,64]{4,3,2,1,0:T(8,128)(2,1)S(1)} reshape(bf16[128,768]{1,0:T(8,128)(2,1)} %param.6) | data formatting | bytes 393216 | tf_op jit(solution)/shard_map/stack | solution.py:178
  2.0 1.3 stack.125
  3.2 0.3 stack.122
  3.6 0.3 stack.126
  3.9 0.5 fusion
  4.4 0.2 reshape.385
  4.6 0.4 fusion.1
  5.2 4.1 %collective-permute-start.4 = (bf16[80,384]{1,0:T(8,128)(2,1)S(1)}, bf16[80,384]{1,0:T(8,128)(2,1)S(1)}, u32[]{:S(2)}, u32[]{:S(2)}) collective-permute-start(bf16[80,384]{1,0:T(8,128)(2,1)S(1)} %pad_maximum_fusion.26), channel_id=1, source_target_pairs={{0,8},{1,9},{2,10},{3,11},{4,12},{5,13},{6,14},{7,15},{8,0},{9,1},... | collective-permute-start | bytes 184328 | tf_op jit(solution)/shard_map/ppermute | solution.py:24
  9.4 2.7 %collective-permute-done.4 = bf16[80,384]{1,0:T(8,128)(2,1)S(1)} collective-permute-done((bf16[80,384]{1,0:T(8,128)(2,1)S(1)}, bf16[80,384]{1,0:T(8,128)(2,1)S(1)}, u32[]{:S(2)}, u32[]{:S(2)}) %collective-permute-start.4) | collective-permute-done | bytes 61472 | tf_op jit(solution)/shard_map/ppermute | solution.py:24
  12.3 2.7 %collective-permute-start.5 = (bf16[416,384]{1,0:T(8,128)(2,1)S(1)}, bf16[416,384]{1,0:T(8,128)(2,1)S(1)}, u32[]{:S(2)}, u32[]{:S(2)}) collective-permute-start(bf16[416,384]{1,0:T(8,128)(2,1)S(1)} %pad_maximum_fusion.13), channel_id=1, source_target_pairs={{0,4},{1,5},{2,6},{3,7},{4,0},{5,1},{6,2},{7,3},{8,12},{9,13},{10,... | collective-permute-start | bytes 958472 | tf_op jit(solution)/shard_map/ppermute | solution.py:24
  15.1 2.3 %collective-permute-start.1 = (bf16[416,384]{1,0:T(8,128)(2,1)S(1)}, bf16[416,384]{1,0:T(8,128)(2,1)S(1)}, u32[]{:S(2)}, u32[]{:S(2)}) collective-permute-start(bf16[416,384]{1,0:T(8,128)(2,1)S(1)} %pad_maximum_fusion.12), channel_id=1, source_target_pairs={{0,2},{1,3},{2,0},{3,1},{4,6},{5,7},{6,4},{7,5},{8,10},{9,11},{10,... | collective-permute-start | bytes 958472 | tf_op jit(solution)/shard_map/ppermute | solution.py:24
  17.3 5.2 %collective-permute-done.5 = bf16[416,384]{1,0:T(8,128)(2,1)S(1)} collective-permute-done((bf16[416,384]{1,0:T(8,128)(2,1)S(1)}, bf16[416,384]{1,0:T(8,128)(2,1)S(1)}, u32[]{:S(2)}, u32[]{:S(2)}) %collective-permute-start.5) | collective-permute-done | bytes 319520 | tf_op jit(solution)/shard_map/ppermute | solution.py:24
  22.9 1.6 %collective-permute-start.6 = (bf16[832,384]{1,0:T(8,128)(2,1)S(1)}, bf16[832,384]{1,0:T(8,128)(2,1)S(1)}, u32[]{:S(2)}, u32[]{:S(2)}) collective-permute-start(bf16[832,384]{1,0:T(8,128)(2,1)S(1)} %pad_maximum_fusion.5), channel_id=1, source_target_pairs={{0,2},{1,3},{2,0},{3,1},{4,6},{5,7},{6,4},{7,5},{8,10},{9,11},{10,... | collective-permute-start | bytes 1916936 | tf_op jit(solution)/shard_map/ppermute | solution.py:24
  24.8 1.8 %collective-permute-start.2 = (bf16[832,384]{1,0:T(8,128)(2,1)S(1)}, bf16[832,384]{1,0:T(8,128)(2,1)S(1)}, u32[]{:S(2)}, u32[]{:S(2)}) collective-permute-start(bf16[832,384]{1,0:T(8,128)(2,1)S(1)} %pad_maximum_fusion.4), channel_id=1, source_target_pairs={{0,4},{1,5},{2,6},{3,7},{4,0},{5,1},{6,2},{7,3},{8,12},{9,13},{10,... | collective-permute-start | bytes 1916936 | tf_op jit(solution)/shard_map/ppermute | solution.py:24
  26.6 12.0 %collective-permute-done.6 = bf16[832,384]{1,0:T(8,128)(2,1)S(1)} collective-permute-done((bf16[832,384]{1,0:T(8,128)(2,1)S(1)}, bf16[832,384]{1,0:T(8,128)(2,1)S(1)}, u32[]{:S(2)}, u32[]{:S(2)}) %collective-permute-start.6) | collective-permute-done | bytes 639008 | tf_op jit(solution)/shard_map/ppermute | solution.py:24
  39.1 0.1 pad_maximum_fusion.1.mine_ref
  39.3 0.6 collective-permute-done.2
  40.2 0.2 copy-done
  40.6 1.2 pad_maximum_fusion.mine_ref
  41.7 0.7 fusion.37
  42.5 1.1 copy-done.5
  43.6 14.0 %shard_map.84 = (bf16[128,768]{1,0:T(8,128)(2,1)}, bf16[128,768]{1,0:T(8,128)(2,1)}, f32[2,512,384]{2,1,0:T(8,128)}, f32[2,256,384]{2,1,0:T(8,128)}, f32[2,64,384]{2,1,0:T(8,128)}, /*index=5*/bf16[1664,384]{1,0:T(8,128)(2,1)}) custom-call(s32[3,12]{1,0:T(4,128)} %offsets_ref.3, bf16[128,384]{1,0:T(8,128)(2,1)} %get-tuple-element.73.query_ref, ...), custom_call_target="tpu_custom_call" | custom-call | tf_op jit(solution)/shard_map/pallas_call | solution.py:226
  57.5 0.5 collective-permute-start.8
  58.0 1.5 %slice_bitcast_fusion.25 = (s32[6]{0:T(128)}, s32[6]{0:T(128)}, s32[6]{0:T(128)}, s32[6]{0:T(128)}) fusion(s32[3,12]{1,0:T(4,128)} %offsets_ref.3), kind=kLoop, calls=%fused_computation.117 | loop fusion | bytes 192 | tf_op jit(solution)/shard_map/eq | solution.py:46
  59.5 14.0 %shard_map.85 = (bf16[128,768]{1,0:T(8,128)(2,1)}, bf16[128,768]{1,0:T(8,128)(2,1)}, f32[2,512,384]{2,1,0:T(8,128)}, f32[2,256,384]{2,1,0:T(8,128)}, f32[2,64,384]{2,1,0:T(8,128)}, /*index=5*/bf16[1664,384]{1,0:T(8,128)(2,1)}) custom-call(s32[3,12]{1,0:T(4,128)} %offsets_ref.3, ...), custom_call_target="tpu_custom_call", output_to_operand_aliasing={{0}: (5, {}), {1}: (6, {})} | custom-call | tf_op jit(solution)/shard_map/pallas_call | solution.py:226
  73.6 0.7 fusion.23
  74.4 0.8 mul.89
  75.2 0.1 mul.82
  75.3 0.8 mul.83
  76.3 0.8 mul.101
  77.2 0.8 mul.95
  78.1 1.4 %slice.408 = f32[1024,384]{1,0:T(8,128)S(1)} slice(bf16[1664,384]{1,0:T(8,128)(2,1)} %collective-permute-done.8), slice={[0:1024], [0:384]} | slice | bytes 3145728 | tf_op jit(solution)/shard_map/slice | solution.py:270
  79.4 0.3 copy-done.4
  79.7 0.2 copy_add_fusion.1
  79.9 1.1 slice.411
  81.3 0.9 slice.413
  82.4 1.1 collective-permute-start.9
  83.5 0.2 copy-done.3
  83.8 0.2 copy_add_fusion
  84.1 1.0 copy-done.9
  85.3 0.7 copy-done.15
  86.2 1.8 %collective-permute-start.13 = (bf16[832,384]{1,0:T(8,128)(2,1)S(1)}, bf16[832,384]{1,0:T(8,128)(2,1)S(1)}, u32[]{:S(2)}, u32[]{:S(2)}) collective-permute-start(bf16[832,384]{1,0:T(8,128)(2,1)S(1)} %pad_maximum_fusion.7), channel_id=1, source_target_pairs={{0,4},{1,5},{2,6},{3,7},{4,0},{5,1},{6,2},{7,3},{8,12},{9,13},{10,... | collective-permute-start | bytes 1916936 | tf_op jit(solution)/shard_map/ppermute | solution.py:24
  88.0 11.2 %collective-permute-done.9 = bf16[832,384]{1,0:T(8,128)(2,1)S(1)} collective-permute-done((bf16[832,384]{1,0:T(8,128)(2,1)S(1)}, bf16[832,384]{1,0:T(8,128)(2,1)S(1)}, u32[]{:S(2)}, u32[]{:S(2)}) %collective-permute-start.9) | collective-permute-done | bytes 639008 | tf_op jit(solution)/shard_map/ppermute | solution.py:24
  99.6 1.7 %collective-permute-start.10 = (bf16[416,384]{1,0:T(8,128)(2,1)S(1)}, bf16[416,384]{1,0:T(8,128)(2,1)S(1)}, u32[]{:S(2)}, u32[]{:S(2)}) collective-permute-start(bf16[416,384]{1,0:T(8,128)(2,1)S(1)} %pad_maximum_fusion.14), channel_id=1, source_target_pairs={{0,4},{1,5},{2,6},{3,7},{4,0},{5,1},{6,2},{7,3},{8,12},{9,13},{10,... | collective-permute-start | bytes 958472 | tf_op jit(solution)/shard_map/ppermute | solution.py:24
  101.3 2.1 %collective-permute-done.13 = bf16[832,384]{1,0:T(8,128)(2,1)S(1)} collective-permute-done((bf16[832,384]{1,0:T(8,128)(2,1)S(1)}, bf16[832,384]{1,0:T(8,128)(2,1)S(1)}, u32[]{:S(2)}, u32[]{:S(2)}) %collective-permute-start.13) | collective-permute-done | bytes 639008 | tf_op jit(solution)/shard_map/ppermute | solution.py:24
  103.8 1.1 collective-permute-start.14
  105.0 4.9 %collective-permute-done.10 = bf16[416,384]{1,0:T(8,128)(2,1)S(1)} collective-permute-done((bf16[416,384]{1,0:T(8,128)(2,1)S(1)}, bf16[416,384]{1,0:T(8,128)(2,1)S(1)}, u32[]{:S(2)}, u32[]{:S(2)}) %collective-permute-start.10) | collective-permute-done | bytes 319520 | tf_op jit(solution)/shard_map/ppermute | solution.py:24
  110.0 2.6 %collective-permute-done.14 = bf16[416,384]{1,0:T(8,128)(2,1)S(1)} collective-permute-done((bf16[416,384]{1,0:T(8,128)(2,1)S(1)}, bf16[416,384]{1,0:T(8,128)(2,1)S(1)}, u32[]{:S(2)}, u32[]{:S(2)}) %collective-permute-start.14) | collective-permute-done | bytes 319520 | tf_op jit(solution)/shard_map/ppermute | solution.py:24
  112.8 3.5 %collective-permute-start.11 = (bf16[80,384]{1,0:T(8,128)(2,1)S(1)}, bf16[80,384]{1,0:T(8,128)(2,1)S(1)}, u32[]{:S(2)}, u32[]{:S(2)}) collective-permute-start(bf16[80,384]{1,0:T(8,128)(2,1)S(1)} %pad_maximum_fusion.27), channel_id=1, source_target_pairs={{0,8},{1,9},{2,10},{3,11},{4,12},{5,13},{6,14},{7,15},{8,0},{9,1},... | collective-permute-start | bytes 184328 | tf_op jit(solution)/shard_map/ppermute | solution.py:24
  116.4 0.6 pad_maximum_fusion.28
  117.1 0.8 squeeze.78
  117.9 0.7 squeeze.80
  118.9 1.0 mul.81
  120.1 1.0 mul.87
  121.1 1.4 %fusion.13 = bf16[2,128,384]{2,1,0:T(8,128)(2,1)S(1)} fusion(f32[2,128,384]{2,1,0:T(8,128)S(1)} %bitcast.231, f32[2,2,128,384]{3,2,1,0:T(8,128)S(1)} %fusion.3, f32[2,128,384]{2,1,0:T(8,128)} %mul.87, f32[2,128,384]{2,1,0:T(8,128)} %mul.81, f32[128,384]{1,0:T(8,128)} %mul.89, f32[128,384]{1,0:T(8,128)} %mul.83), kind=kLoop, calls=%fused_computation.38 | loop fusion | flops 589824 | bytes 2162688 | tf_op jit(solution)/shard_map/convert.13 | solution.py:316
  122.5 0.7 slice_bitcast_fusion.9
  123.1 0.8 slice.460
  124.2 0.2 mul.93
  124.4 0.7 slice.462
  125.3 0.2 mul.99
  125.6 0.6 copy-done.7
  126.4 0.8 copy-done.11
  127.1 0.7 pad_maximum_fusion.20
  127.8 0.7 pad_maximum_fusion.19
  (186 shorter events, 5.3 us)
Async XLA Ops:
  0.6 2.6 %copy-start.1 = (bf16[128,768]{1,0:T(8,128)(2,1)S(1)}, bf16[128,768]{1,0:T(8,128)(2,1)}, u32[]{:S(2)}) copy-start(bf16[128,768]{1,0:T(8,128)(2,1)} %param.7) | copy-start | bytes 589828
  0.6 3.3 %copy-start.17 = (s32[3,12]{1,0:T(4,128)S(1)}, s32[3,12]{1,0:T(4,128)}, u32[]{:S(2)}) copy-start(s32[3,12]{1,0:T(4,128)} %offsets_ref.3) | copy-start | bytes 436
  4.4 5.0 %copy-start.2 = (bf16[128,768]{1,0:T(8,128)(2,1)S(1)}, bf16[128,768]{1,0:T(8,128)(2,1)}, u32[]{:S(2)}) copy-start(bf16[128,768]{1,0:T(8,128)(2,1)} %param.6) | copy-start | bytes 589828
  5.2 7.0 %collective-permute-start.4 = (bf16[80,384]{1,0:T(8,128)(2,1)S(1)}, bf16[80,384]{1,0:T(8,128)(2,1)S(1)}, u32[]{:S(2)}, u32[]{:S(2)}) collective-permute-start(bf16[80,384]{1,0:T(8,128)(2,1)S(1)} %pad_maximum_fusion.26), channel_id=1, source_target_pairs={{0,8},{1,9},{2,10},{3,11},{4,12},{5,13},{6,14},{7,15},{8,0},{9,1},... | collective-permute-start | bytes 184328 | tf_op jit(solution)/shard_map/ppermute | solution.py:24
  9.3 5.6 %collective-permute-start = (bf16[80,384]{1,0:T(8,128)(2,1)S(1)}, bf16[80,384]{1,0:T(8,128)(2,1)S(1)}, u32[]{:S(2)}, u32[]{:S(2)}) collective-permute-start(bf16[80,384]{1,0:T(8,128)(2,1)S(1)} %pad_maximum_fusion.25), channel_id=1, source_target_pairs={{0,8},{1,9},{2,10},{3,11},{4,12},{5,13},{6,14},{7,15},{8,0},{9,1},... | collective-permute-start | bytes 184328 | tf_op jit(solution)/shard_map/ppermute | solution.py:24
  12.3 10.3 %collective-permute-start.5 = (bf16[416,384]{1,0:T(8,128)(2,1)S(1)}, bf16[416,384]{1,0:T(8,128)(2,1)S(1)}, u32[]{:S(2)}, u32[]{:S(2)}) collective-permute-start(bf16[416,384]{1,0:T(8,128)(2,1)S(1)} %pad_maximum_fusion.13), channel_id=1, source_target_pairs={{0,4},{1,5},{2,6},{3,7},{4,0},{5,1},{6,2},{7,3},{8,12},{9,13},{10,... | collective-permute-start | bytes 958472 | tf_op jit(solution)/shard_map/ppermute | solution.py:24
  15.1 9.4 %collective-permute-start.1 = (bf16[416,384]{1,0:T(8,128)(2,1)S(1)}, bf16[416,384]{1,0:T(8,128)(2,1)S(1)}, u32[]{:S(2)}, u32[]{:S(2)}) collective-permute-start(bf16[416,384]{1,0:T(8,128)(2,1)S(1)} %pad_maximum_fusion.12), channel_id=1, source_target_pairs={{0,2},{1,3},{2,0},{3,1},{4,6},{5,7},{6,4},{7,5},{8,10},{9,11},{10,... | collective-permute-start | bytes 958472 | tf_op jit(solution)/shard_map/ppermute | solution.py:24
  22.9 15.7 %collective-permute-start.6 = (bf16[832,384]{1,0:T(8,128)(2,1)S(1)}, bf16[832,384]{1,0:T(8,128)(2,1)S(1)}, u32[]{:S(2)}, u32[]{:S(2)}) collective-permute-start(bf16[832,384]{1,0:T(8,128)(2,1)S(1)} %pad_maximum_fusion.5), channel_id=1, source_target_pairs={{0,2},{1,3},{2,0},{3,1},{4,6},{5,7},{6,4},{7,5},{8,10},{9,11},{10,... | collective-permute-start | bytes 1916936 | tf_op jit(solution)/shard_map/ppermute | solution.py:24
  24.8 15.1 %collective-permute-start.2 = (bf16[832,384]{1,0:T(8,128)(2,1)S(1)}, bf16[832,384]{1,0:T(8,128)(2,1)S(1)}, u32[]{:S(2)}, u32[]{:S(2)}) collective-permute-start(bf16[832,384]{1,0:T(8,128)(2,1)S(1)} %pad_maximum_fusion.4), channel_id=1, source_target_pairs={{0,4},{1,5},{2,6},{3,7},{4,0},{5,1},{6,2},{7,3},{8,12},{9,13},{10,... | collective-permute-start | bytes 1916936 | tf_op jit(solution)/shard_map/ppermute | solution.py:24
  39.2 1.1 copy-start
  39.3 3.2 %collective-permute-start.7 = (bf16[1664,384]{1,0:T(8,128)(2,1)S(1)}, bf16[1664,384]{1,0:T(8,128)(2,1)S(1)}, u32[]{:S(2)}, u32[]{:S(2)}) collective-permute-start(bf16[1664,384]{1,0:T(8,128)(2,1)S(1)} %pad_maximum_fusion.1.mine_ref), channel_id=1, source_target_pairs={{0,1},{1,0},{2,3},{3,2},{4,5},{5,4},{6,7},{7,6},{8,9},{9,8},{10,11... | collective-permute-start | bytes 3833864 | tf_op jit(solution)/shard_map/ppermute | solution.py:24
  40.5 1.2 copy-start.13
  40.5 1.2 copy-start.14
  41.7 17.8 %collective-permute-start.3 = (bf16[1664,384]{1,0:T(8,128)(2,1)}, bf16[1664,384]{1,0:T(8,128)(2,1)}, u32[]{:S(2)}, u32[]{:S(2)}) collective-permute-start(bf16[1664,384]{1,0:T(8,128)(2,1)} %pad_maximum_fusion.mine_ref), channel_id=1, source_target_pairs={{0,1},{1,0},{2,3},{3,2},{4,5},{5,4},{6,7},{7,6},{8,9},{9,8},{10,11... | collective-permute-start | bytes 3833864 | tf_op jit(solution)/shard_map/ppermute | solution.py:24
  42.5 1.1 copy-start.5
  57.5 20.5 %collective-permute-start.8 = (bf16[1664,384]{1,0:T(8,128)(2,1)}, bf16[1664,384]{1,0:T(8,128)(2,1)}, u32[]{:S(2)}, u32[]{:S(2)}) collective-permute-start(bf16[1664,384]{1,0:T(8,128)(2,1)} %get-tuple-element.21), channel_id=1, source_target_pairs={{0,1},{1,0},{2,3},{3,2},{4,5},{5,4},{6,7},{7,6},{8,9},{9,8},{10,11... | collective-permute-start | bytes 3833864 | tf_op jit(solution)/shard_map/ppermute | solution.py:24
  73.5 1.7 %copy-start.18 = (s32[6]{0:T(128)S(1)}, s32[6]{0:T(128)}, u32[]{:S(2)}) copy-start(s32[6]{0:T(128)} %get-tuple-element.66) | copy-start | bytes 76
  73.5 1.7 %copy-start.19 = (s32[6]{0:T(128)S(1)}, s32[6]{0:T(128)}, u32[]{:S(2)}) copy-start(s32[6]{0:T(128)} %get-tuple-element.69) | copy-start | bytes 76
  73.5 9.9 %collective-permute-start.12 = (bf16[1664,384]{1,0:T(8,128)(2,1)}, bf16[1664,384]{1,0:T(8,128)(2,1)S(1)}, u32[]{:S(2)}, u32[]{:S(2)}) collective-permute-start(bf16[1664,384]{1,0:T(8,128)(2,1)} %get-tuple-element.25), channel_id=1, source_target_pairs={{0,1},{1,0},{2,3},{3,2},{4,5},{5,4},{6,7},{7,6},{8,9},{9,8},{10,11... | collective-permute-start | bytes 3833864 | tf_op jit(solution)/shard_map/ppermute | solution.py:24
  78.1 1.6 %copy-start.4 = (f32[2,512,384]{2,1,0:T(8,128)S(1)}, f32[2,512,384]{2,1,0:T(8,128)}, u32[]{:S(2)}) copy-start(f32[2,512,384]{2,1,0:T(8,128)} %get-tuple-element.20) | copy-start | bytes 4718596
  79.9 1.3 copy-start.10
  81.1 1.1 copy-start.16
  82.3 1.4 %copy-start.3 = (f32[2,512,384]{2,1,0:T(8,128)S(1)}, f32[2,512,384]{2,1,0:T(8,128)}, u32[]{:S(2)}) copy-start(f32[2,512,384]{2,1,0:T(8,128)} %get-tuple-element.24) | copy-start | bytes 4718596
  82.4 16.8 %collective-permute-start.9 = (bf16[832,384]{1,0:T(8,128)(2,1)S(1)}, bf16[832,384]{1,0:T(8,128)(2,1)S(1)}, u32[]{:S(2)}, u32[]{:S(2)}) collective-permute-start(bf16[832,384]{1,0:T(8,128)(2,1)S(1)} %pad_maximum_fusion.6), channel_id=1, source_target_pairs={{0,2},{1,3},{2,0},{3,1},{4,6},{5,7},{6,4},{7,5},{8,10},{9,11},{10,... | collective-permute-start | bytes 1916936 | tf_op jit(solution)/shard_map/ppermute | solution.py:24
  84.0 1.1 copy-start.9
  85.1 0.9 copy-start.15
  86.2 17.2 %collective-permute-start.13 = (bf16[832,384]{1,0:T(8,128)(2,1)S(1)}, bf16[832,384]{1,0:T(8,128)(2,1)S(1)}, u32[]{:S(2)}, u32[]{:S(2)}) collective-permute-start(bf16[832,384]{1,0:T(8,128)(2,1)S(1)} %pad_maximum_fusion.7), channel_id=1, source_target_pairs={{0,4},{1,5},{2,6},{3,7},{4,0},{5,1},{6,2},{7,3},{8,12},{9,13},{10,... | collective-permute-start | bytes 1916936 | tf_op jit(solution)/shard_map/ppermute | solution.py:24
  99.6 10.2 %collective-permute-start.10 = (bf16[416,384]{1,0:T(8,128)(2,1)S(1)}, bf16[416,384]{1,0:T(8,128)(2,1)S(1)}, u32[]{:S(2)}, u32[]{:S(2)}) collective-permute-start(bf16[416,384]{1,0:T(8,128)(2,1)S(1)} %pad_maximum_fusion.14), channel_id=1, source_target_pairs={{0,4},{1,5},{2,6},{3,7},{4,0},{5,1},{6,2},{7,3},{8,12},{9,13},{10,... | collective-permute-start | bytes 958472 | tf_op jit(solution)/shard_map/ppermute | solution.py:24
  103.8 8.8 %collective-permute-start.14 = (bf16[416,384]{1,0:T(8,128)(2,1)S(1)}, bf16[416,384]{1,0:T(8,128)(2,1)S(1)}, u32[]{:S(2)}, u32[]{:S(2)}) collective-permute-start(bf16[416,384]{1,0:T(8,128)(2,1)S(1)} %pad_maximum_fusion.15), channel_id=1, source_target_pairs={{0,2},{1,3},{2,0},{3,1},{4,6},{5,7},{6,4},{7,5},{8,10},{9,11},{10,... | collective-permute-start | bytes 958472 | tf_op jit(solution)/shard_map/ppermute | solution.py:24
  112.8 5.9 %collective-permute-start.11 = (bf16[80,384]{1,0:T(8,128)(2,1)S(1)}, bf16[80,384]{1,0:T(8,128)(2,1)S(1)}, u32[]{:S(2)}, u32[]{:S(2)}) collective-permute-start(bf16[80,384]{1,0:T(8,128)(2,1)S(1)} %pad_maximum_fusion.27), channel_id=1, source_target_pairs={{0,8},{1,9},{2,10},{3,11},{4,12},{5,13},{6,14},{7,15},{8,0},{9,1},... | collective-permute-start | bytes 184328 | tf_op jit(solution)/shard_map/ppermute | solution.py:24
  117.1 6.1 %collective-permute-start.15 = (bf16[80,384]{1,0:T(8,128)(2,1)}, bf16[80,384]{1,0:T(8,128)(2,1)}, u32[]{:S(2)}, u32[]{:S(2)}) collective-permute-start(bf16[80,384]{1,0:T(8,128)(2,1)} %pad_maximum_fusion.28), channel_id=1, source_target_pairs={{0,8},{1,9},{2,10},{3,11},{4,12},{5,13},{6,14},{7,15},{8,0},{9,1},... | collective-permute-start | bytes 184328 | tf_op jit(solution)/shard_map/ppermute | solution.py:24
  121.1 2.9 %copy-start.6 = (f32[2,32,6,64]{3,2,1,0:T(8,128)S(1)}, f32[2,32,6,64]{3,2,1,0:T(8,128)}, u32[]{:S(2)}) copy-start(f32[2,32,6,64]{3,2,1,0:T(8,128)} %squeeze.78) | copy-start | bytes 294916
  124.1 1.1 copy-start.12
  125.2 0.9 copy-start.7
  125.2 1.0 copy-start.8
  126.3 0.9 copy-start.11

commit v11 on v9

--- a/solution.py
+++ b/solution.py
@@ -185,12 +185,28 @@
 
         gathered_halves = []
         layouts = []
+        orders = [gather_order(top_bits, half == 1) for half in range(halves)]
+        shared = 1 if len(orders[0]) > 1 and all(o[0] == orders[0][0] for o in orders) else 0
+        shared_bits = [[] for _ in range(3)]
+        if shared:
+            bit = orders[0][0]
+            active = [branch for branch in range(3) if branch_bits[branch] > bit]
+            outgoing = jnp.concatenate([picked[branch].reshape(-1, model_width) for branch in active])
+            incoming = exchange(outgoing, bit)
+            cursor = 0
+            picked = list(picked)
+            for branch in active:
+                count = picked[branch].size // model_width
+                arrived = incoming[cursor : cursor + count].reshape(picked[branch].shape)
+                cursor += count
+                picked[branch] = jnp.stack([picked[branch], arrived], axis=1)
+                shared_bits[branch].insert(0, bit)
         for half in range(halves):
             cols = slice(half * half_width, (half + 1) * half_width)
-            buffers = [block[:, :, cols] for block in picked]
-            axis_bits = [[] for _ in range(3)]
-            order = gather_order(top_bits, half == 1)
-            for bit in order[:-1]:
+            buffers = [block[..., cols] for block in picked]
+            axis_bits = [list(bits) for bits in shared_bits]
+            order = orders[half]
+            for bit in order[shared:-1]:
                 active = [branch for branch in range(3) if branch_bits[branch] > bit]
                 outgoing = jnp.concatenate(
                     [buffers[branch].reshape(-1, half_width) for branch in active]
@@ -268,7 +284,7 @@
                 count = kept.size // half_width
                 partial.append(kept + incoming[cursor : cursor + count].reshape(kept.shape))
                 cursor += count
-            for bit in order[1:]:
+            for bit in order[1 : len(order) - shared]:
                 active = [branch for branch in range(3) if branch_bits[branch] > bit]
                 places = {branch: 1 + axis_bits[branch].index(bit) for branch in active}
                 outgoing = jnp.concatenate(
@@ -287,16 +303,39 @@
                     partial[branch] = kept + incoming[cursor : cursor + count].reshape(kept.shape)
                     cursor += count
                     axis_bits[branch].remove(bit)
-            offsets_half = head_offsets[:, half * heads_per_half : (half + 1) * heads_per_half]
-            total_grad = None
-            for branch in range(3):
-                spread = spread_rows(partial[branch], STRIDES[branch], offsets_half[branch])
-                total_grad = spread if total_grad is None else total_grad + spread
-            results.append((total_grad[0], total_grad[1]))
-
-        return full_outs + tuple(
-            jnp.concatenate([result[index] for result in results], axis=1).astype(jnp.bfloat16)
-            for index in range(2)
+            results.append((partial, axis_bits))
+
+        partial = [
+            jnp.concatenate([result[0][branch] for result in results], axis=-1)
+            for branch in range(3)
+        ]
+        axis_bits = results[0][1]
+        if shared:
+            bit = orders[0][0]
+            active = [branch for branch in range(3) if branch_bits[branch] > bit]
+            places = {branch: 1 + axis_bits[branch].index(bit) for branch in active}
+            outgoing = jnp.concatenate(
+                [
+                    lax.index_in_dim(partial[branch], 1, places[branch], keepdims=False)
+                    .reshape(-1, model_width)
+                    .astype(jnp.bfloat16)
+                    for branch in active
+                ]
+            )
+            incoming = exchange(outgoing, bit).astype(jnp.float32)
+            cursor = 0
+            for branch in active:
+                kept = lax.index_in_dim(partial[branch], 0, places[branch], keepdims=False)
+                count = kept.size // model_width
+                partial[branch] = kept + incoming[cursor : cursor + count].reshape(kept.shape)
+                cursor += count
+        total_grad = None
+        for branch in range(3):
+            spread = spread_rows(partial[branch], STRIDES[branch], head_offsets[branch])
+            total_grad = spread if total_grad is None else total_grad + spread
+        return full_outs + (
+            total_grad[0].astype(jnp.bfloat16),
+            total_grad[1].astype(jnp.bfloat16),
         )
 
     return per_device

time: 129 us -> 126 us (0.977)
  local copies, waits for them, and re-layouts: 26.4 us -> 22.8 us
  other arithmetic: 8.57 us -> 11.3 us
  starting transfers between devices: 22.2 us -> 19.9 us
    slice x16 -> x14, local copies, waits for them, and re-layouts: 1.81 us -> 5.41 us  [per_device(): partial[branch] = kept + incoming[cursor:cursor + count].reshape(kept.shape)]
    mul x16 -> x8, local copies, waits for them, and re-layouts: 6.5 us -> 3.92 us  [spread_rows(): return (grouped * chosen).reshape(pair, count * stride, width)]
    add x14, other arithmetic: 0.54 us -> 3.06 us  [per_device(): partial[branch] = kept + incoming[cursor:cursor + count].reshape(kept.shape)]
    ppermute x16 -> x14, starting transfers between devices: 22.2 us -> 19.9 us  [exchange(): return lax.ppermute(block, 'seq', route)]
    unnamed x40 -> x36, local copies, waits for them, and re-layouts: 5.08 us -> 3.35 us
    eq x1 -> x0, local copies, waits for them, and re-layouts: 1.48 us -> none  [spread_rows(): jnp.arange(stride, dtype=jnp.int32)[:, None] == offsets_row[None, :]]
    squeeze x4 -> x2, local copies, waits for them, and re-layouts: 1.67 us -> 0.2 us  [per_device(): kept = lax.index_in_dim(partial[branch], 0, places[branch], keepdims=False)]
    concatenate x2 -> x3, other arithmetic: 1.39 us -> 0.03 us  [the longest x2 0.02 us: per_device(): jnp.concatenate([result[0][branch] for result in results], axis=-1)]
  transfers between devices with their start and end apart: 16 -> 14, of which waited for: 8 -> 9; matrix products, arithmetic and copies ran while one was open for 17% -> 14% of each run, Pallas kernels for 22% -> 22%
where the time goes in v11:
time: 126 us; the launch traced here: 125 us
  waiting for transfers between devices  41.3 us (33%)
  Pallas kernels  27.9 us (22%)
  local copies, waits for them, and re-layouts  22.8 us (18%)
  starting transfers between devices  19.9 us (16%)
  other arithmetic  11.3 us (9%)
  between operations  1.64 us (1%)
    ppermute x14, waiting for transfers between devices, exchange(): return lax.ppermute(block, 'seq', route)  41.3 us
    pallas_call x2, Pallas kernels, per_device(): pl.pallas_call(attention_kernel(head_dim, score_scale, half * heads_per_h...  27.9 us
    ppermute x14, starting transfers between devices, exchange(): return lax.ppermute(block, 'seq', route)  19.9 us
    slice x14, local copies, waits for them, and re-layouts, per_device(): partial[branch] = kept + incoming[cursor:cursor + count].reshape(kept.shape)  5.41 us
    mul x8, local copies, waits for them, and re-layouts, spread_rows(): return (grouped * chosen).reshape(pair, count * stride, width)  3.92 us
    slice x6, local copies, waits for them, and re-layouts, per_device(): partial.append(kept + incoming[cursor:cursor + count].reshape(kept.shape))  3.53 us
    unnamed x36, local copies, waits for them, and re-layouts  3.35 us
    another operation x4, local copies, waits for them, and re-layouts, per_device(): kv_rows = jnp.stack([key_rows, value_rows])  3.2 us
  transfers between devices with their start and end apart: 14, of which 9 were waited for; matrix products, arithmetic and copies ran while one was open for 14% of the time, Pallas kernels for 22%

profile of v11, /device:TPU:0, one launch (start us, length us, event | category | flops | bytes accessed | tf_op | source)
XLA Modules:
  0.0 124.9 jit_solution(4111492182379229096)
XLA Ops:
  0.7 1.3 %stack.103 = bf16[1,32,4,12,64]{4,3,2,1,0:T(8,128)(2,1)S(1)} reshape(bf16[128,768]{1,0:T(8,128)(2,1)} %param.6) | data formatting | bytes 393216 | tf_op jit(solution)/shard_map/stack | solution.py:177
  2.0 1.3 %stack.106 = bf16[1,8,16,12,64]{4,3,2,1,0:T(8,128)(2,1)S(1)} reshape(bf16[128,768]{1,0:T(8,128)(2,1)} %param.6) | data formatting | bytes 393216 | tf_op jit(solution)/shard_map/stack | solution.py:177
  3.2 0.3 stack.104
  3.6 0.3 stack.107
  3.9 0.6 fusion.25
  4.5 0.5 fusion
  5.0 0.2 reshape_reshape.6
  5.2 0.6 fusion.24
  5.8 0.4 fusion.1
  6.3 4.1 %collective-permute-start = (bf16[80,768]{1,0:T(8,128)(2,1)S(1)}, bf16[80,768]{1,0:T(8,128)(2,1)S(1)}, u32[]{:S(2)}, u32[]{:S(2)}) collective-permute-start(bf16[80,768]{1,0:T(8,128)(2,1)S(1)} %pad_maximum_fusion.20), channel_id=1, source_target_pairs={{0,8},{1,9},{2,10},{3,11},{4,12},{5,13},{6,14},{7,15},{8,0},{9,1},... | collective-permute-start | bytes 368648 | tf_op jit(solution)/shard_map/ppermute | solution.py:24
  10.4 0.2 stack_reshape.48
  10.7 5.6 %collective-permute-done = bf16[80,768]{1,0:T(8,128)(2,1)S(1)} collective-permute-done((bf16[80,768]{1,0:T(8,128)(2,1)S(1)}, bf16[80,768]{1,0:T(8,128)(2,1)S(1)}, u32[]{:S(2)}, u32[]{:S(2)}) %collective-permute-start) | collective-permute-done | bytes 122912 | tf_op jit(solution)/shard_map/ppermute | solution.py:24
  16.5 0.8 collective-permute-start.4
  17.4 1.6 %collective-permute-start.1 = (bf16[416,384]{1,0:T(8,128)(2,1)S(1)}, bf16[416,384]{1,0:T(8,128)(2,1)S(1)}, u32[]{:S(2)}, u32[]{:S(2)}) collective-permute-start(bf16[416,384]{1,0:T(8,128)(2,1)S(1)} %pad_maximum_fusion.12), channel_id=1, source_target_pairs={{0,2},{1,3},{2,0},{3,1},{4,6},{5,7},{6,4},{7,5},{8,10},{9,11},{10,... | collective-permute-start | bytes 958472 | tf_op jit(solution)/shard_map/ppermute | solution.py:24
  18.9 6.4 %collective-permute-done.4 = bf16[416,384]{1,0:T(8,128)(2,1)S(1)} collective-permute-done((bf16[416,384]{1,0:T(8,128)(2,1)S(1)}, bf16[416,384]{1,0:T(8,128)(2,1)S(1)}, u32[]{:S(2)}, u32[]{:S(2)}) %collective-permute-start.4) | collective-permute-done | bytes 319520 | tf_op jit(solution)/shard_map/ppermute | solution.py:24
  25.7 1.3 %collective-permute-start.5 = (bf16[832,384]{1,0:T(8,128)(2,1)S(1)}, bf16[832,384]{1,0:T(8,128)(2,1)S(1)}, u32[]{:S(2)}, u32[]{:S(2)}) collective-permute-start(bf16[832,384]{1,0:T(8,128)(2,1)S(1)} %pad_maximum_fusion.5), channel_id=1, source_target_pairs={{0,2},{1,3},{2,0},{3,1},{4,6},{5,7},{6,4},{7,5},{8,10},{9,11},{10,... | collective-permute-start | bytes 1916936 | tf_op jit(solution)/shard_map/ppermute | solution.py:24
  27.3 1.8 %collective-permute-start.2 = (bf16[832,384]{1,0:T(8,128)(2,1)S(1)}, bf16[832,384]{1,0:T(8,128)(2,1)S(1)}, u32[]{:S(2)}, u32[]{:S(2)}) collective-permute-start(bf16[832,384]{1,0:T(8,128)(2,1)S(1)} %pad_maximum_fusion.4), channel_id=1, source_target_pairs={{0,4},{1,5},{2,6},{3,7},{4,0},{5,1},{6,2},{7,3},{8,12},{9,13},{10,... | collective-permute-start | bytes 1916936 | tf_op jit(solution)/shard_map/ppermute | solution.py:24
  29.1 11.3 %collective-permute-done.5 = bf16[832,384]{1,0:T(8,128)(2,1)S(1)} collective-permute-done((bf16[832,384]{1,0:T(8,128)(2,1)S(1)}, bf16[832,384]{1,0:T(8,128)(2,1)S(1)}, u32[]{:S(2)}, u32[]{:S(2)}) %collective-permute-start.5) | collective-permute-done | bytes 639008 | tf_op jit(solution)/shard_map/ppermute | solution.py:24
  41.0 1.5 %collective-permute-done.2 = bf16[832,384]{1,0:T(8,128)(2,1)S(1)} collective-permute-done((bf16[832,384]{1,0:T(8,128)(2,1)S(1)}, bf16[832,384]{1,0:T(8,128)(2,1)S(1)}, u32[]{:S(2)}, u32[]{:S(2)}) %collective-permute-start.2) | collective-permute-done | bytes 639008 | tf_op jit(solution)/shard_map/ppermute | solution.py:24
  43.0 1.2 pad_maximum_fusion.mine_ref
  44.2 0.8 fusion.32
  44.9 1.1 copy-done.5
  46.1 14.0 %shard_map.84 = (bf16[128,768]{1,0:T(8,128)(2,1)}, bf16[128,768]{1,0:T(8,128)(2,1)}, f32[2,512,384]{2,1,0:T(8,128)}, f32[2,256,384]{2,1,0:T(8,128)}, f32[2,64,384]{2,1,0:T(8,128)}, /*index=5*/bf16[1664,384]{1,0:T(8,128)(2,1)}) custom-call(s32[3,12]{1,0:T(4,128)} %offsets_ref.3, bf16[128,384]{1,0:T(8,128)(2,1)} %get-tuple-element.59.query_ref, ...), custom_call_target="tpu_custom_call" | custom-call | tf_op jit(solution)/shard_map/pallas_call | solution.py:241
  60.0 0.5 collective-permute-start.7
  60.5 14.0 %shard_map.85 = (bf16[128,768]{1,0:T(8,128)(2,1)}, bf16[128,768]{1,0:T(8,128)(2,1)}, f32[2,512,384]{2,1,0:T(8,128)}, f32[2,256,384]{2,1,0:T(8,128)}, f32[2,64,384]{2,1,0:T(8,128)}, /*index=5*/bf16[1664,384]{1,0:T(8,128)(2,1)}) custom-call(s32[3,12]{1,0:T(4,128)} %offsets_ref.3, ...), custom_call_target="tpu_custom_call", output_to_operand_aliasing={{0}: (5, {}), {1}: (6, {})} | custom-call | tf_op jit(solution)/shard_map/pallas_call | solution.py:241
  74.6 1.3 %slice.342 = f32[1024,384]{1,0:T(8,128)S(1)} slice(bf16[1664,384]{1,0:T(8,128)(2,1)} %collective-permute-done.7), slice={[0:1024], [0:384]} | slice | bytes 3145728 | tf_op jit(solution)/shard_map/slice | solution.py:285
  75.9 0.2 copy-done.4
  76.1 0.2 copy_add_fusion.1
  76.4 1.1 slice.345
  77.7 0.9 slice.347
  78.8 1.2 collective-permute-start.8
  80.2 0.2 copy_add_fusion
  80.5 1.0 copy-done.9
  81.7 0.7 copy-done.13
  82.6 1.9 %collective-permute-start.11 = (bf16[832,384]{1,0:T(8,128)(2,1)S(1)}, bf16[832,384]{1,0:T(8,128)(2,1)S(1)}, u32[]{:S(2)}, u32[]{:S(2)}) collective-permute-start(bf16[832,384]{1,0:T(8,128)(2,1)S(1)} %pad_maximum_fusion.7), channel_id=1, source_target_pairs={{0,4},{1,5},{2,6},{3,7},{4,0},{5,1},{6,2},{7,3},{8,12},{9,13},{10,... | collective-permute-start | bytes 1916936 | tf_op jit(solution)/shard_map/ppermute | solution.py:24
  84.4 10.9 %collective-permute-done.8 = bf16[832,384]{1,0:T(8,128)(2,1)S(1)} collective-permute-done((bf16[832,384]{1,0:T(8,128)(2,1)S(1)}, bf16[832,384]{1,0:T(8,128)(2,1)S(1)}, u32[]{:S(2)}, u32[]{:S(2)}) %collective-permute-start.8) | collective-permute-done | bytes 639008 | tf_op jit(solution)/shard_map/ppermute | solution.py:24
  95.7 0.8 pad_maximum_fusion.14
  96.5 1.7 %collective-permute-start.9 = (bf16[416,384]{1,0:T(8,128)(2,1)}, bf16[416,384]{1,0:T(8,128)(2,1)}, u32[]{:S(2)}, u32[]{:S(2)}) collective-permute-start(bf16[416,384]{1,0:T(8,128)(2,1)} %pad_maximum_fusion.14), channel_id=1, source_target_pairs={{0,4},{1,5},{2,6},{3,7},{4,0},{5,1},{6,2},{7,3},{8,12},{9,13},{10,... | collective-permute-start | bytes 958472 | tf_op jit(solution)/shard_map/ppermute | solution.py:24
  98.2 1.3 %collective-permute-done.11 = bf16[832,384]{1,0:T(8,128)(2,1)S(1)} collective-permute-done((bf16[832,384]{1,0:T(8,128)(2,1)S(1)}, bf16[832,384]{1,0:T(8,128)(2,1)S(1)}, u32[]{:S(2)}, u32[]{:S(2)}) %collective-permute-start.11) | collective-permute-done | bytes 639008 | tf_op jit(solution)/shard_map/ppermute | solution.py:24
  99.9 0.8 pad_maximum_fusion.15
  100.7 1.3 %collective-permute-start.12 = (bf16[416,384]{1,0:T(8,128)(2,1)}, bf16[416,384]{1,0:T(8,128)(2,1)}, u32[]{:S(2)}, u32[]{:S(2)}) collective-permute-start(bf16[416,384]{1,0:T(8,128)(2,1)} %pad_maximum_fusion.15), channel_id=1, source_target_pairs={{0,2},{1,3},{2,0},{3,1},{4,6},{5,7},{6,4},{7,5},{8,10},{9,11},{10,... | collective-permute-start | bytes 958472 | tf_op jit(solution)/shard_map/ppermute | solution.py:24
  101.9 0.2 mul.48
  102.1 0.3 mul.49
  102.4 0.2 mul.42
  102.6 1.0 mul.43
  103.6 2.4 %collective-permute-done.9 = bf16[416,384]{1,0:T(8,128)(2,1)} collective-permute-done((bf16[416,384]{1,0:T(8,128)(2,1)}, bf16[416,384]{1,0:T(8,128)(2,1)}, u32[]{:S(2)}, u32[]{:S(2)}) %collective-permute-start.9) | collective-permute-done | bytes 319520 | tf_op jit(solution)/shard_map/ppermute | solution.py:24
  106.1 0.9 slice.377
  107.0 1.0 fusion.14
  107.9 1.5 %collective-permute-done.12 = bf16[416,384]{1,0:T(8,128)(2,1)} collective-permute-done((bf16[416,384]{1,0:T(8,128)(2,1)}, bf16[416,384]{1,0:T(8,128)(2,1)}, u32[]{:S(2)}, u32[]{:S(2)}) %collective-permute-start.12) | collective-permute-done | bytes 319520 | tf_op jit(solution)/shard_map/ppermute | solution.py:24
  109.4 0.9 slice.379
  110.4 0.7 slice.383
  111.1 0.7 slice.385
  111.9 3.7 %collective-permute-start.13 = (bf16[80,768]{1,0:T(8,128)(2,1)S(1)}, bf16[80,768]{1,0:T(8,128)(2,1)S(1)}, u32[]{:S(2)}, u32[]{:S(2)}) collective-permute-start(bf16[80,768]{1,0:T(8,128)(2,1)S(1)} %pad_maximum_fusion.21), channel_id=1, source_target_pairs={{0,8},{1,9},{2,10},{3,11},{4,12},{5,13},{6,14},{7,15},{8,0},{9,1},... | collective-permute-start | bytes 368648 | tf_op jit(solution)/shard_map/ppermute | solution.py:24
  115.7 1.0 slice.358
  116.6 0.8 fusion.9
  117.4 1.0 slice.375
  118.4 0.8 fusion.7
  119.4 0.4 collective-permute-done.13
  120.1 0.2 mul.40
  120.2 0.5 mul.41
  120.9 0.2 mul.46
  121.0 1.4 %mul.47 = f32[2,128,768]{2,1,0:T(8,128)} reshape(f32[2,8,16,12,64]{4,3,2,1,0:T(8,128)S(1)} %mul.46) | data formatting | bytes 1572864 | tf_op jit(solution)/shard_map/mul | solution.py:49
  122.5 1.6 %fusion.5 = bf16[2,128,768]{2,1,0:T(8,128)(2,1)S(1)} fusion(f32[2,128,384]{2,1,0:T(8,128)} %fusion.7, f32[2,128,384]{2,1,0:T(8,128)} %fusion.9, f32[2,128,768]{2,1,0:T(8,128)} %mul.47, f32[2,128,768]{2,1,0:T(8,128)S(1)} %mul.41, f32[128,768]{1,0:T(8,128)S(1)} %mul.49, f32[128,768]{1,0:T(8,128)} %mul.43), kind=kLoop, calls=%fused_computation.18 | loop fusion | flops 1179648 | bytes 3538944 | tf_op jit(solution)/shard_map/convert.3 | solution.py:354
  124.1 0.8 slice_bitcast_fusion.6
  (145 shorter events, 4.2 us)
Async XLA Ops:
  0.6 2.6 %copy-start.1 = (bf16[128,768]{1,0:T(8,128)(2,1)S(1)}, bf16[128,768]{1,0:T(8,128)(2,1)}, u32[]{:S(2)}) copy-start(bf16[128,768]{1,0:T(8,128)(2,1)} %param.7) | copy-start | bytes 589828
  0.6 3.3 %copy-start.16 = (s32[3,12]{1,0:T(4,128)S(1)}, s32[3,12]{1,0:T(4,128)}, u32[]{:S(2)}) copy-start(s32[3,12]{1,0:T(4,128)} %offsets_ref.3) | copy-start | bytes 436
  5.0 5.7 %copy-start.2 = (bf16[128,768]{1,0:T(8,128)(2,1)S(1)}, bf16[128,768]{1,0:T(8,128)(2,1)}, u32[]{:S(2)}) copy-start(bf16[128,768]{1,0:T(8,128)(2,1)} %param.6) | copy-start | bytes 589828
  6.3 10.1 %collective-permute-start = (bf16[80,768]{1,0:T(8,128)(2,1)S(1)}, bf16[80,768]{1,0:T(8,128)(2,1)S(1)}, u32[]{:S(2)}, u32[]{:S(2)}) collective-permute-start(bf16[80,768]{1,0:T(8,128)(2,1)S(1)} %pad_maximum_fusion.20), channel_id=1, source_target_pairs={{0,8},{1,9},{2,10},{3,11},{4,12},{5,13},{6,14},{7,15},{8,0},{9,1},... | collective-permute-start | bytes 368648 | tf_op jit(solution)/shard_map/ppermute | solution.py:24
  16.5 8.8 %collective-permute-start.4 = (bf16[416,384]{1,0:T(8,128)(2,1)S(1)}, bf16[416,384]{1,0:T(8,128)(2,1)S(1)}, u32[]{:S(2)}, u32[]{:S(2)}) collective-permute-start(bf16[416,384]{1,0:T(8,128)(2,1)S(1)} %pad_maximum_fusion.13), channel_id=1, source_target_pairs={{0,4},{1,5},{2,6},{3,7},{4,0},{5,1},{6,2},{7,3},{8,12},{9,13},{10,... | collective-permute-start | bytes 958472 | tf_op jit(solution)/shard_map/ppermute | solution.py:24
  17.4 9.6 %collective-permute-start.1 = (bf16[416,384]{1,0:T(8,128)(2,1)S(1)}, bf16[416,384]{1,0:T(8,128)(2,1)S(1)}, u32[]{:S(2)}, u32[]{:S(2)}) collective-permute-start(bf16[416,384]{1,0:T(8,128)(2,1)S(1)} %pad_maximum_fusion.12), channel_id=1, source_target_pairs={{0,2},{1,3},{2,0},{3,1},{4,6},{5,7},{6,4},{7,5},{8,10},{9,11},{10,... | collective-permute-start | bytes 958472 | tf_op jit(solution)/shard_map/ppermute | solution.py:24
  25.7 14.7 %collective-permute-start.5 = (bf16[832,384]{1,0:T(8,128)(2,1)S(1)}, bf16[832,384]{1,0:T(8,128)(2,1)S(1)}, u32[]{:S(2)}, u32[]{:S(2)}) collective-permute-start(bf16[832,384]{1,0:T(8,128)(2,1)S(1)} %pad_maximum_fusion.5), channel_id=1, source_target_pairs={{0,2},{1,3},{2,0},{3,1},{4,6},{5,7},{6,4},{7,5},{8,10},{9,11},{10,... | collective-permute-start | bytes 1916936 | tf_op jit(solution)/shard_map/ppermute | solution.py:24
  27.3 15.2 %collective-permute-start.2 = (bf16[832,384]{1,0:T(8,128)(2,1)S(1)}, bf16[832,384]{1,0:T(8,128)(2,1)S(1)}, u32[]{:S(2)}, u32[]{:S(2)}) collective-permute-start(bf16[832,384]{1,0:T(8,128)(2,1)S(1)} %pad_maximum_fusion.4), channel_id=1, source_target_pairs={{0,4},{1,5},{2,6},{3,7},{4,0},{5,1},{6,2},{7,3},{8,12},{9,13},{10,... | collective-permute-start | bytes 1916936 | tf_op jit(solution)/shard_map/ppermute | solution.py:24
  40.9 1.8 %copy-start = (bf16[1664,384]{1,0:T(8,128)(2,1)}, bf16[1664,384]{1,0:T(8,128)(2,1)S(1)}, u32[]{:S(2)}) copy-start(bf16[1664,384]{1,0:T(8,128)(2,1)S(1)} %pad_maximum_fusion.1.mine_ref) | copy-start | bytes 3833860
  40.9 4.0 %collective-permute-start.6 = (bf16[1664,384]{1,0:T(8,128)(2,1)S(1)}, bf16[1664,384]{1,0:T(8,128)(2,1)S(1)}, u32[]{:S(2)}, u32[]{:S(2)}) collective-permute-start(bf16[1664,384]{1,0:T(8,128)(2,1)S(1)} %pad_maximum_fusion.1.mine_ref), channel_id=1, source_target_pairs={{0,1},{1,0},{2,3},{3,2},{4,5},{5,4},{6,7},{7,6},{8,9},{9,8},{10,11... | collective-permute-start | bytes 3833864 | tf_op jit(solution)/shard_map/ppermute | solution.py:24
  42.9 1.2 copy-start.11
  42.9 1.2 copy-start.12
  44.2 16.4 %collective-permute-start.3 = (bf16[1664,384]{1,0:T(8,128)(2,1)}, bf16[1664,384]{1,0:T(8,128)(2,1)}, u32[]{:S(2)}, u32[]{:S(2)}) collective-permute-start(bf16[1664,384]{1,0:T(8,128)(2,1)} %pad_maximum_fusion.mine_ref), channel_id=1, source_target_pairs={{0,1},{1,0},{2,3},{3,2},{4,5},{5,4},{6,7},{7,6},{8,9},{9,8},{10,11... | collective-permute-start | bytes 3833864 | tf_op jit(solution)/shard_map/ppermute | solution.py:24
  44.9 1.2 copy-start.5
  60.0 14.6 %collective-permute-start.7 = (bf16[1664,384]{1,0:T(8,128)(2,1)}, bf16[1664,384]{1,0:T(8,128)(2,1)}, u32[]{:S(2)}, u32[]{:S(2)}) collective-permute-start(bf16[1664,384]{1,0:T(8,128)(2,1)} %get-tuple-element.21), channel_id=1, source_target_pairs={{0,1},{1,0},{2,3},{3,2},{4,5},{5,4},{6,7},{7,6},{8,9},{9,8},{10,11... | collective-permute-start | bytes 3833864 | tf_op jit(solution)/shard_map/ppermute | solution.py:24
  74.5 1.6 %copy-start.4 = (f32[2,512,384]{2,1,0:T(8,128)S(1)}, f32[2,512,384]{2,1,0:T(8,128)}, u32[]{:S(2)}) copy-start(f32[2,512,384]{2,1,0:T(8,128)} %get-tuple-element.20) | copy-start | bytes 4718596
  74.5 5.4 %collective-permute-start.10 = (bf16[1664,384]{1,0:T(8,128)(2,1)}, bf16[1664,384]{1,0:T(8,128)(2,1)S(1)}, u32[]{:S(2)}, u32[]{:S(2)}) collective-permute-start(bf16[1664,384]{1,0:T(8,128)(2,1)} %get-tuple-element.25), channel_id=1, source_target_pairs={{0,1},{1,0},{2,3},{3,2},{4,5},{5,4},{6,7},{7,6},{8,9},{9,8},{10,11... | collective-permute-start | bytes 3833864 | tf_op jit(solution)/shard_map/ppermute | solution.py:24
  76.3 1.3 %copy-start.10 = (f32[2,256,384]{2,1,0:T(8,128)S(1)}, f32[2,256,384]{2,1,0:T(8,128)}, u32[]{:S(2)}) copy-start(f32[2,256,384]{2,1,0:T(8,128)} %get-tuple-element.22) | copy-start | bytes 2359300
  77.5 1.1 copy-start.14
  78.7 1.4 %copy-start.3 = (f32[2,512,384]{2,1,0:T(8,128)S(1)}, f32[2,512,384]{2,1,0:T(8,128)}, u32[]{:S(2)}) copy-start(f32[2,512,384]{2,1,0:T(8,128)} %get-tuple-element.24) | copy-start | bytes 4718596
  78.8 16.5 %collective-permute-start.8 = (bf16[832,384]{1,0:T(8,128)(2,1)S(1)}, bf16[832,384]{1,0:T(8,128)(2,1)S(1)}, u32[]{:S(2)}, u32[]{:S(2)}) collective-permute-start(bf16[832,384]{1,0:T(8,128)(2,1)S(1)} %pad_maximum_fusion.6), channel_id=1, source_target_pairs={{0,2},{1,3},{2,0},{3,1},{4,6},{5,7},{6,4},{7,5},{8,10},{9,11},{10,... | collective-permute-start | bytes 1916936 | tf_op jit(solution)/shard_map/ppermute | solution.py:24
  80.4 1.1 copy-start.9
  81.5 0.9 copy-start.13
  82.6 16.9 %collective-permute-start.11 = (bf16[832,384]{1,0:T(8,128)(2,1)S(1)}, bf16[832,384]{1,0:T(8,128)(2,1)S(1)}, u32[]{:S(2)}, u32[]{:S(2)}) collective-permute-start(bf16[832,384]{1,0:T(8,128)(2,1)S(1)} %pad_maximum_fusion.7), channel_id=1, source_target_pairs={{0,4},{1,5},{2,6},{3,7},{4,0},{5,1},{6,2},{7,3},{8,12},{9,13},{10,... | collective-permute-start | bytes 1916936 | tf_op jit(solution)/shard_map/ppermute | solution.py:24
  95.6 4.0 %copy-start.6 = (f32[2,2,2,32,384]{4,3,2,1,0:T(8,128)}, f32[2,2,2,32,384]{4,3,2,1,0:T(8,128)S(1)}, u32[]{:S(2)}) copy-start(f32[2,2,2,32,384]{4,3,2,1,0:T(8,128)S(1)} %fusion.8) | copy-start | bytes 1179652
  96.5 9.6 %collective-permute-start.9 = (bf16[416,384]{1,0:T(8,128)(2,1)}, bf16[416,384]{1,0:T(8,128)(2,1)}, u32[]{:S(2)}, u32[]{:S(2)}) collective-permute-start(bf16[416,384]{1,0:T(8,128)(2,1)} %pad_maximum_fusion.14), channel_id=1, source_target_pairs={{0,4},{1,5},{2,6},{3,7},{4,0},{5,1},{6,2},{7,3},{8,12},{9,13},{10,... | collective-permute-start | bytes 958472 | tf_op jit(solution)/shard_map/ppermute | solution.py:24
  99.8 2.2 %copy-start.15 = (f32[16,12]{1,0:T(8,128)S(1)}, f32[16,12]{1,0:T(8,128)}, u32[]{:S(2)}) copy-start(f32[16,12]{1,0:T(8,128)} %get-tuple-element.56) | copy-start | bytes 2308
  99.8 2.1 %copy-start.7 = (f32[2,2,2,32,384]{4,3,2,0,1:T(8,128)}, f32[2,2,2,32,384]{4,3,2,0,1:T(8,128)S(1)}, u32[]{:S(2)}) copy-start(f32[2,2,2,32,384]{4,3,2,0,1:T(8,128)S(1)} %fusion.6) | copy-start | bytes 1179652
  100.7 1.7 %copy-start.17 = (f32[4,12]{1,0:T(4,128)S(1)}, f32[4,12]{1,0:T(4,128)}, u32[]{:S(2)}) copy-start(f32[4,12]{1,0:T(4,128)} %get-tuple-element.54) | copy-start | bytes 580
  100.7 8.7 %collective-permute-start.12 = (bf16[416,384]{1,0:T(8,128)(2,1)}, bf16[416,384]{1,0:T(8,128)(2,1)}, u32[]{:S(2)}, u32[]{:S(2)}) collective-permute-start(bf16[416,384]{1,0:T(8,128)(2,1)} %pad_maximum_fusion.15), channel_id=1, source_target_pairs={{0,2},{1,3},{2,0},{3,1},{4,6},{5,7},{6,4},{7,5},{8,10},{9,11},{10,... | collective-permute-start | bytes 958472 | tf_op jit(solution)/shard_map/ppermute | solution.py:24
  103.6 6.7 %copy-start.8 = (f32[2,2,2,32,384]{4,3,2,0,1:T(8,128)S(1)}, f32[2,2,2,32,384]{4,3,2,0,1:T(8,128)}, u32[]{:S(2)}) copy-start(f32[2,2,2,32,384]{4,3,2,0,1:T(8,128)} %copy-done.7) | copy-start | bytes 1179652
  111.9 7.9 %collective-permute-start.13 = (bf16[80,768]{1,0:T(8,128)(2,1)S(1)}, bf16[80,768]{1,0:T(8,128)(2,1)S(1)}, u32[]{:S(2)}, u32[]{:S(2)}) collective-permute-start(bf16[80,768]{1,0:T(8,128)(2,1)S(1)} %pad_maximum_fusion.21), channel_id=1, source_target_pairs={{0,8},{1,9},{2,10},{3,11},{4,12},{5,13},{6,14},{7,15},{8,0},{9,1},... | collective-permute-start | bytes 368648 | tf_op jit(solution)/shard_map/ppermute | solution.py:24

commit v12 on v11

--- a/solution.py
+++ b/solution.py
@@ -203,7 +203,12 @@
                 shared_bits[branch].insert(0, bit)
         for half in range(halves):
             cols = slice(half * half_width, (half + 1) * half_width)
-            buffers = [block[..., cols] for block in picked]
+            buffers = [
+                jnp.stack([key_rows[:, cols], value_rows[:, cols]])
+                if STRIDES[branch] == 1 and not shared_bits[branch]
+                else picked[branch][..., cols]
+                for branch in range(3)
+            ]
             axis_bits = [list(bits) for bits in shared_bits]
             order = orders[half]
             for bit in order[shared:-1]:

time: 126 us -> 126 us (level)
  no operation moved by 1% of the time
where the time goes in v12:
time: 126 us; the launch traced here: 125 us
  waiting for transfers between devices  41.2 us (33%)
  Pallas kernels  27.9 us (22%)
  local copies, waits for them, and re-layouts  22.8 us (18%)
  starting transfers between devices  20 us (16%)
  other arithmetic  11.2 us (9%)
  between operations  1.63 us (1%)
    ppermute x14, waiting for transfers between devices, exchange(): return lax.ppermute(block, 'seq', route)  41.2 us
    pallas_call x2, Pallas kernels, per_device(): pl.pallas_call(attention_kernel(head_dim, score_scale, half * heads_per_h...  27.9 us
    ppermute x14, starting transfers between devices, exchange(): return lax.ppermute(block, 'seq', route)  20 us
    slice x14, local copies, waits for them, and re-layouts, per_device(): partial[branch] = kept + incoming[cursor:cursor + count].reshape(kept.shape)  5.41 us
    mul x8, local copies, waits for them, and re-layouts, spread_rows(): return (grouped * chosen).reshape(pair, count * stride, width)  3.91 us
    slice x6, local copies, waits for them, and re-layouts, per_device(): partial.append(kept + incoming[cursor:cursor + count].reshape(kept.shape))  3.53 us
    unnamed x36, local copies, waits for them, and re-layouts  3.32 us
    another operation x4, local copies, waits for them, and re-layouts, per_device(): kv_rows = jnp.stack([key_rows, value_rows])  3.2 us
  transfers between devices with their start and end apart: 14, of which 9 were waited for; matrix products, arithmetic and copies ran while one was open for 14% of the time, Pallas kernels for 22%

profile of v12, /device:TPU:0, one launch (start us, length us, event | category | flops | bytes accessed | tf_op | source)
XLA Modules:
  0.0 124.8 jit_solution(12174271923889545148)
XLA Ops:
  0.7 1.3 %stack.115 = bf16[1,32,4,12,64]{4,3,2,1,0:T(8,128)(2,1)S(1)} reshape(bf16[128,768]{1,0:T(8,128)(2,1)} %param.6) | data formatting | bytes 393216 | tf_op jit(solution)/shard_map/stack | solution.py:177
  2.0 1.3 %stack.118 = bf16[1,8,16,12,64]{4,3,2,1,0:T(8,128)(2,1)S(1)} reshape(bf16[128,768]{1,0:T(8,128)(2,1)} %param.6) | data formatting | bytes 393216 | tf_op jit(solution)/shard_map/stack | solution.py:177
  3.2 0.3 stack.116
  3.6 0.3 stack.119
  3.9 0.6 fusion.24
  4.5 0.5 fusion
  5.0 0.2 reshape_reshape.6
  5.1 0.6 fusion.23
  5.7 0.4 fusion.1
  6.3 4.1 %collective-permute-start = (bf16[80,768]{1,0:T(8,128)(2,1)S(1)}, bf16[80,768]{1,0:T(8,128)(2,1)S(1)}, u32[]{:S(2)}, u32[]{:S(2)}) collective-permute-start(bf16[80,768]{1,0:T(8,128)(2,1)S(1)} %pad_maximum_fusion.21), channel_id=1, source_target_pairs={{0,8},{1,9},{2,10},{3,11},{4,12},{5,13},{6,14},{7,15},{8,0},{9,1},... | collective-permute-start | bytes 368648 | tf_op jit(solution)/shard_map/ppermute | solution.py:24
  10.4 0.2 stack_reshape.48
  10.8 5.5 %collective-permute-done = bf16[80,768]{1,0:T(8,128)(2,1)S(1)} collective-permute-done((bf16[80,768]{1,0:T(8,128)(2,1)S(1)}, bf16[80,768]{1,0:T(8,128)(2,1)S(1)}, u32[]{:S(2)}, u32[]{:S(2)}) %collective-permute-start) | collective-permute-done | bytes 122912 | tf_op jit(solution)/shard_map/ppermute | solution.py:24
  16.5 0.8 collective-permute-start.4
  17.3 1.6 %collective-permute-start.1 = (bf16[416,384]{1,0:T(8,128)(2,1)S(1)}, bf16[416,384]{1,0:T(8,128)(2,1)S(1)}, u32[]{:S(2)}, u32[]{:S(2)}) collective-permute-start(bf16[416,384]{1,0:T(8,128)(2,1)S(1)} %pad_maximum_fusion.12), channel_id=1, source_target_pairs={{0,2},{1,3},{2,0},{3,1},{4,6},{5,7},{6,4},{7,5},{8,10},{9,11},{10,... | collective-permute-start | bytes 958472 | tf_op jit(solution)/shard_map/ppermute | solution.py:24
  18.9 6.4 %collective-permute-done.4 = bf16[416,384]{1,0:T(8,128)(2,1)S(1)} collective-permute-done((bf16[416,384]{1,0:T(8,128)(2,1)S(1)}, bf16[416,384]{1,0:T(8,128)(2,1)S(1)}, u32[]{:S(2)}, u32[]{:S(2)}) %collective-permute-start.4) | collective-permute-done | bytes 319520 | tf_op jit(solution)/shard_map/ppermute | solution.py:24
  25.6 1.3 %collective-permute-start.5 = (bf16[832,384]{1,0:T(8,128)(2,1)S(1)}, bf16[832,384]{1,0:T(8,128)(2,1)S(1)}, u32[]{:S(2)}, u32[]{:S(2)}) collective-permute-start(bf16[832,384]{1,0:T(8,128)(2,1)S(1)} %pad_maximum_fusion.5), channel_id=1, source_target_pairs={{0,2},{1,3},{2,0},{3,1},{4,6},{5,7},{6,4},{7,5},{8,10},{9,11},{10,... | collective-permute-start | bytes 1916936 | tf_op jit(solution)/shard_map/ppermute | solution.py:24
  27.2 1.8 %collective-permute-start.2 = (bf16[832,384]{1,0:T(8,128)(2,1)S(1)}, bf16[832,384]{1,0:T(8,128)(2,1)S(1)}, u32[]{:S(2)}, u32[]{:S(2)}) collective-permute-start(bf16[832,384]{1,0:T(8,128)(2,1)S(1)} %pad_maximum_fusion.4), channel_id=1, source_target_pairs={{0,4},{1,5},{2,6},{3,7},{4,0},{5,1},{6,2},{7,3},{8,12},{9,13},{10,... | collective-permute-start | bytes 1916936 | tf_op jit(solution)/shard_map/ppermute | solution.py:24
  29.0 11.3 %collective-permute-done.5 = bf16[832,384]{1,0:T(8,128)(2,1)S(1)} collective-permute-done((bf16[832,384]{1,0:T(8,128)(2,1)S(1)}, bf16[832,384]{1,0:T(8,128)(2,1)S(1)}, u32[]{:S(2)}, u32[]{:S(2)}) %collective-permute-start.5) | collective-permute-done | bytes 639008 | tf_op jit(solution)/shard_map/ppermute | solution.py:24
  41.0 1.5 %collective-permute-done.2 = bf16[832,384]{1,0:T(8,128)(2,1)S(1)} collective-permute-done((bf16[832,384]{1,0:T(8,128)(2,1)S(1)}, bf16[832,384]{1,0:T(8,128)(2,1)S(1)}, u32[]{:S(2)}, u32[]{:S(2)}) %collective-permute-start.2) | collective-permute-done | bytes 639008 | tf_op jit(solution)/shard_map/ppermute | solution.py:24
  42.9 1.2 pad_maximum_fusion.mine_ref
  44.1 0.7 fusion.33
  44.8 1.2 copy-done.5
  46.0 13.9 %shard_map.84 = (bf16[128,768]{1,0:T(8,128)(2,1)}, bf16[128,768]{1,0:T(8,128)(2,1)}, f32[2,512,384]{2,1,0:T(8,128)}, f32[2,256,384]{2,1,0:T(8,128)}, f32[2,64,384]{2,1,0:T(8,128)}, /*index=5*/bf16[1664,384]{1,0:T(8,128)(2,1)}) custom-call(s32[3,12]{1,0:T(4,128)} %offsets_ref.3, bf16[128,384]{1,0:T(8,128)(2,1)} %get-tuple-element.67.query_ref, ...), custom_call_target="tpu_custom_call" | custom-call | tf_op jit(solution)/shard_map/pallas_call | solution.py:246
  59.9 0.5 collective-permute-start.7
  60.5 14.0 %shard_map.85 = (bf16[128,768]{1,0:T(8,128)(2,1)}, bf16[128,768]{1,0:T(8,128)(2,1)}, f32[2,512,384]{2,1,0:T(8,128)}, f32[2,256,384]{2,1,0:T(8,128)}, f32[2,64,384]{2,1,0:T(8,128)}, /*index=5*/bf16[1664,384]{1,0:T(8,128)(2,1)}) custom-call(s32[3,12]{1,0:T(4,128)} %offsets_ref.3, ...), custom_call_target="tpu_custom_call", output_to_operand_aliasing={{0}: (5, {}), {1}: (6, {})} | custom-call | tf_op jit(solution)/shard_map/pallas_call | solution.py:246
  74.5 1.3 %slice.348 = f32[1024,384]{1,0:T(8,128)S(1)} slice(bf16[1664,384]{1,0:T(8,128)(2,1)} %collective-permute-done.7), slice={[0:1024], [0:384]} | slice | bytes 3145728 | tf_op jit(solution)/shard_map/slice | solution.py:290
  75.9 0.2 copy-done.4
  76.1 0.2 copy_add_fusion.1
  76.3 1.1 slice.351
  77.7 0.9 slice.353
  78.7 1.2 collective-permute-start.8
  80.1 0.2 copy_add_fusion
  80.4 1.0 copy-done.9
  81.6 0.7 copy-done.13
  82.5 1.8 %collective-permute-start.11 = (bf16[832,384]{1,0:T(8,128)(2,1)S(1)}, bf16[832,384]{1,0:T(8,128)(2,1)S(1)}, u32[]{:S(2)}, u32[]{:S(2)}) collective-permute-start(bf16[832,384]{1,0:T(8,128)(2,1)S(1)} %pad_maximum_fusion.7), channel_id=1, source_target_pairs={{0,4},{1,5},{2,6},{3,7},{4,0},{5,1},{6,2},{7,3},{8,12},{9,13},{10,... | collective-permute-start | bytes 1916936 | tf_op jit(solution)/shard_map/ppermute | solution.py:24
  84.4 10.9 %collective-permute-done.8 = bf16[832,384]{1,0:T(8,128)(2,1)S(1)} collective-permute-done((bf16[832,384]{1,0:T(8,128)(2,1)S(1)}, bf16[832,384]{1,0:T(8,128)(2,1)S(1)}, u32[]{:S(2)}, u32[]{:S(2)}) %collective-permute-start.8) | collective-permute-done | bytes 639008 | tf_op jit(solution)/shard_map/ppermute | solution.py:24
  95.6 0.8 pad_maximum_fusion.14
  96.4 1.7 %collective-permute-start.9 = (bf16[416,384]{1,0:T(8,128)(2,1)}, bf16[416,384]{1,0:T(8,128)(2,1)}, u32[]{:S(2)}, u32[]{:S(2)}) collective-permute-start(bf16[416,384]{1,0:T(8,128)(2,1)} %pad_maximum_fusion.14), channel_id=1, source_target_pairs={{0,4},{1,5},{2,6},{3,7},{4,0},{5,1},{6,2},{7,3},{8,12},{9,13},{10,... | collective-permute-start | bytes 958472 | tf_op jit(solution)/shard_map/ppermute | solution.py:24
  98.1 1.3 %collective-permute-done.11 = bf16[832,384]{1,0:T(8,128)(2,1)S(1)} collective-permute-done((bf16[832,384]{1,0:T(8,128)(2,1)S(1)}, bf16[832,384]{1,0:T(8,128)(2,1)S(1)}, u32[]{:S(2)}, u32[]{:S(2)}) %collective-permute-start.11) | collective-permute-done | bytes 639008 | tf_op jit(solution)/shard_map/ppermute | solution.py:24
  99.9 0.8 pad_maximum_fusion.15
  100.6 1.3 %collective-permute-start.12 = (bf16[416,384]{1,0:T(8,128)(2,1)}, bf16[416,384]{1,0:T(8,128)(2,1)}, u32[]{:S(2)}, u32[]{:S(2)}) collective-permute-start(bf16[416,384]{1,0:T(8,128)(2,1)} %pad_maximum_fusion.15), channel_id=1, source_target_pairs={{0,2},{1,3},{2,0},{3,1},{4,6},{5,7},{6,4},{7,5},{8,10},{9,11},{10,... | collective-permute-start | bytes 958472 | tf_op jit(solution)/shard_map/ppermute | solution.py:24
  101.9 0.2 mul.48
  102.1 0.3 mul.49
  102.4 0.2 mul.42
  102.6 1.0 mul.43
  103.6 2.4 %collective-permute-done.9 = bf16[416,384]{1,0:T(8,128)(2,1)} collective-permute-done((bf16[416,384]{1,0:T(8,128)(2,1)}, bf16[416,384]{1,0:T(8,128)(2,1)}, u32[]{:S(2)}, u32[]{:S(2)}) %collective-permute-start.9) | collective-permute-done | bytes 319520 | tf_op jit(solution)/shard_map/ppermute | solution.py:24
  106.0 0.9 slice.383
  106.9 1.0 fusion.13
  107.9 1.5 %collective-permute-done.12 = bf16[416,384]{1,0:T(8,128)(2,1)} collective-permute-done((bf16[416,384]{1,0:T(8,128)(2,1)}, bf16[416,384]{1,0:T(8,128)(2,1)}, u32[]{:S(2)}, u32[]{:S(2)}) %collective-permute-start.12) | collective-permute-done | bytes 319520 | tf_op jit(solution)/shard_map/ppermute | solution.py:24
  109.4 0.9 slice.385
  110.3 0.7 slice.389
  111.1 0.7 slice.391
  111.9 3.7 %collective-permute-start.13 = (bf16[80,768]{1,0:T(8,128)(2,1)S(1)}, bf16[80,768]{1,0:T(8,128)(2,1)S(1)}, u32[]{:S(2)}, u32[]{:S(2)}) collective-permute-start(bf16[80,768]{1,0:T(8,128)(2,1)S(1)} %pad_maximum_fusion.22), channel_id=1, source_target_pairs={{0,8},{1,9},{2,10},{3,11},{4,12},{5,13},{6,14},{7,15},{8,0},{9,1},... | collective-permute-start | bytes 368648 | tf_op jit(solution)/shard_map/ppermute | solution.py:24
  115.6 1.0 slice.364
  116.6 0.8 fusion.9
  117.4 1.0 slice.381
  118.3 0.8 fusion.7
  119.4 0.4 collective-permute-done.13
  120.0 0.2 mul.40
  120.2 0.5 mul.41
  120.8 0.2 mul.46
  121.0 1.4 %mul.47 = f32[2,128,768]{2,1,0:T(8,128)} reshape(f32[2,8,16,12,64]{4,3,2,1,0:T(8,128)S(1)} %mul.46) | data formatting | bytes 1572864 | tf_op jit(solution)/shard_map/mul | solution.py:49
  122.4 1.6 %fusion.5 = bf16[2,128,768]{2,1,0:T(8,128)(2,1)S(1)} fusion(f32[2,128,384]{2,1,0:T(8,128)} %fusion.7, f32[2,128,384]{2,1,0:T(8,128)} %fusion.9, f32[2,128,768]{2,1,0:T(8,128)} %mul.47, f32[2,128,768]{2,1,0:T(8,128)S(1)} %mul.41, f32[128,768]{1,0:T(8,128)S(1)} %mul.49, f32[128,768]{1,0:T(8,128)} %mul.43), kind=kLoop, calls=%fused_computation.18 | loop fusion | flops 1179648 | bytes 3538944 | tf_op jit(solution)/shard_map/convert.3 | solution.py:359
  124.0 0.8 slice_bitcast_fusion.6
  (146 shorter events, 4.2 us)
Async XLA Ops:
  0.6 2.6 %copy-start.2 = (bf16[128,768]{1,0:T(8,128)(2,1)S(1)}, bf16[128,768]{1,0:T(8,128)(2,1)}, u32[]{:S(2)}) copy-start(bf16[128,768]{1,0:T(8,128)(2,1)} %param.7) | copy-start | bytes 589828
  0.6 3.3 %copy-start.16 = (s32[3,12]{1,0:T(4,128)S(1)}, s32[3,12]{1,0:T(4,128)}, u32[]{:S(2)}) copy-start(s32[3,12]{1,0:T(4,128)} %offsets_ref.3) | copy-start | bytes 436
  4.5 5.9 %copy-start.1 = (bf16[128,768]{1,0:T(8,128)(2,1)S(1)}, bf16[128,768]{1,0:T(8,128)(2,1)}, u32[]{:S(2)}) copy-start(bf16[128,768]{1,0:T(8,128)(2,1)} %param.6) | copy-start | bytes 589828
  6.3 10.1 %collective-permute-start = (bf16[80,768]{1,0:T(8,128)(2,1)S(1)}, bf16[80,768]{1,0:T(8,128)(2,1)S(1)}, u32[]{:S(2)}, u32[]{:S(2)}) collective-permute-start(bf16[80,768]{1,0:T(8,128)(2,1)S(1)} %pad_maximum_fusion.21), channel_id=1, source_target_pairs={{0,8},{1,9},{2,10},{3,11},{4,12},{5,13},{6,14},{7,15},{8,0},{9,1},... | collective-permute-start | bytes 368648 | tf_op jit(solution)/shard_map/ppermute | solution.py:24
  16.5 8.8 %collective-permute-start.4 = (bf16[416,384]{1,0:T(8,128)(2,1)S(1)}, bf16[416,384]{1,0:T(8,128)(2,1)S(1)}, u32[]{:S(2)}, u32[]{:S(2)}) collective-permute-start(bf16[416,384]{1,0:T(8,128)(2,1)S(1)} %pad_maximum_fusion.13), channel_id=1, source_target_pairs={{0,4},{1,5},{2,6},{3,7},{4,0},{5,1},{6,2},{7,3},{8,12},{9,13},{10,... | collective-permute-start | bytes 958472 | tf_op jit(solution)/shard_map/ppermute | solution.py:24
  17.3 9.6 %collective-permute-start.1 = (bf16[416,384]{1,0:T(8,128)(2,1)S(1)}, bf16[416,384]{1,0:T(8,128)(2,1)S(1)}, u32[]{:S(2)}, u32[]{:S(2)}) collective-permute-start(bf16[416,384]{1,0:T(8,128)(2,1)S(1)} %pad_maximum_fusion.12), channel_id=1, source_target_pairs={{0,2},{1,3},{2,0},{3,1},{4,6},{5,7},{6,4},{7,5},{8,10},{9,11},{10,... | collective-permute-start | bytes 958472 | tf_op jit(solution)/shard_map/ppermute | solution.py:24
  25.6 14.7 %collective-permute-start.5 = (bf16[832,384]{1,0:T(8,128)(2,1)S(1)}, bf16[832,384]{1,0:T(8,128)(2,1)S(1)}, u32[]{:S(2)}, u32[]{:S(2)}) collective-permute-start(bf16[832,384]{1,0:T(8,128)(2,1)S(1)} %pad_maximum_fusion.5), channel_id=1, source_target_pairs={{0,2},{1,3},{2,0},{3,1},{4,6},{5,7},{6,4},{7,5},{8,10},{9,11},{10,... | collective-permute-start | bytes 1916936 | tf_op jit(solution)/shard_map/ppermute | solution.py:24
  27.2 15.2 %collective-permute-start.2 = (bf16[832,384]{1,0:T(8,128)(2,1)S(1)}, bf16[832,384]{1,0:T(8,128)(2,1)S(1)}, u32[]{:S(2)}, u32[]{:S(2)}) collective-permute-start(bf16[832,384]{1,0:T(8,128)(2,1)S(1)} %pad_maximum_fusion.4), channel_id=1, source_target_pairs={{0,4},{1,5},{2,6},{3,7},{4,0},{5,1},{6,2},{7,3},{8,12},{9,13},{10,... | collective-permute-start | bytes 1916936 | tf_op jit(solution)/shard_map/ppermute | solution.py:24
  40.9 1.8 %copy-start = (bf16[1664,384]{1,0:T(8,128)(2,1)}, bf16[1664,384]{1,0:T(8,128)(2,1)S(1)}, u32[]{:S(2)}) copy-start(bf16[1664,384]{1,0:T(8,128)(2,1)S(1)} %pad_maximum_fusion.1.mine_ref) | copy-start | bytes 3833860
  40.9 4.0 %collective-permute-start.6 = (bf16[1664,384]{1,0:T(8,128)(2,1)S(1)}, bf16[1664,384]{1,0:T(8,128)(2,1)S(1)}, u32[]{:S(2)}, u32[]{:S(2)}) collective-permute-start(bf16[1664,384]{1,0:T(8,128)(2,1)S(1)} %pad_maximum_fusion.1.mine_ref), channel_id=1, source_target_pairs={{0,1},{1,0},{2,3},{3,2},{4,5},{5,4},{6,7},{7,6},{8,9},{9,8},{10,11... | collective-permute-start | bytes 3833864 | tf_op jit(solution)/shard_map/ppermute | solution.py:24
  42.9 1.2 copy-start.11
  42.9 1.2 copy-start.12
  44.1 16.4 %collective-permute-start.3 = (bf16[1664,384]{1,0:T(8,128)(2,1)}, bf16[1664,384]{1,0:T(8,128)(2,1)}, u32[]{:S(2)}, u32[]{:S(2)}) collective-permute-start(bf16[1664,384]{1,0:T(8,128)(2,1)} %pad_maximum_fusion.mine_ref), channel_id=1, source_target_pairs={{0,1},{1,0},{2,3},{3,2},{4,5},{5,4},{6,7},{7,6},{8,9},{9,8},{10,11... | collective-permute-start | bytes 3833864 | tf_op jit(solution)/shard_map/ppermute | solution.py:24
  44.8 1.2 copy-start.5
  59.9 14.6 %collective-permute-start.7 = (bf16[1664,384]{1,0:T(8,128)(2,1)}, bf16[1664,384]{1,0:T(8,128)(2,1)}, u32[]{:S(2)}, u32[]{:S(2)}) collective-permute-start(bf16[1664,384]{1,0:T(8,128)(2,1)} %get-tuple-element.21), channel_id=1, source_target_pairs={{0,1},{1,0},{2,3},{3,2},{4,5},{5,4},{6,7},{7,6},{8,9},{9,8},{10,11... | collective-permute-start | bytes 3833864 | tf_op jit(solution)/shard_map/ppermute | solution.py:24
  74.4 1.6 %copy-start.4 = (f32[2,512,384]{2,1,0:T(8,128)S(1)}, f32[2,512,384]{2,1,0:T(8,128)}, u32[]{:S(2)}) copy-start(f32[2,512,384]{2,1,0:T(8,128)} %get-tuple-element.20) | copy-start | bytes 4718596
  74.4 5.5 %collective-permute-start.10 = (bf16[1664,384]{1,0:T(8,128)(2,1)}, bf16[1664,384]{1,0:T(8,128)(2,1)S(1)}, u32[]{:S(2)}, u32[]{:S(2)}) collective-permute-start(bf16[1664,384]{1,0:T(8,128)(2,1)} %get-tuple-element.25), channel_id=1, source_target_pairs={{0,1},{1,0},{2,3},{3,2},{4,5},{5,4},{6,7},{7,6},{8,9},{9,8},{10,11... | collective-permute-start | bytes 3833864 | tf_op jit(solution)/shard_map/ppermute | solution.py:24
  76.2 1.3 %copy-start.10 = (f32[2,256,384]{2,1,0:T(8,128)S(1)}, f32[2,256,384]{2,1,0:T(8,128)}, u32[]{:S(2)}) copy-start(f32[2,256,384]{2,1,0:T(8,128)} %get-tuple-element.22) | copy-start | bytes 2359300
  77.5 1.1 copy-start.14
  78.7 1.4 %copy-start.3 = (f32[2,512,384]{2,1,0:T(8,128)S(1)}, f32[2,512,384]{2,1,0:T(8,128)}, u32[]{:S(2)}) copy-start(f32[2,512,384]{2,1,0:T(8,128)} %get-tuple-element.24) | copy-start | bytes 4718596
  78.7 16.5 %collective-permute-start.8 = (bf16[832,384]{1,0:T(8,128)(2,1)S(1)}, bf16[832,384]{1,0:T(8,128)(2,1)S(1)}, u32[]{:S(2)}, u32[]{:S(2)}) collective-permute-start(bf16[832,384]{1,0:T(8,128)(2,1)S(1)} %pad_maximum_fusion.6), channel_id=1, source_target_pairs={{0,2},{1,3},{2,0},{3,1},{4,6},{5,7},{6,4},{7,5},{8,10},{9,11},{10,... | collective-permute-start | bytes 1916936 | tf_op jit(solution)/shard_map/ppermute | solution.py:24
  80.3 1.1 copy-start.9
  81.5 0.9 copy-start.13
  82.5 17.0 %collective-permute-start.11 = (bf16[832,384]{1,0:T(8,128)(2,1)S(1)}, bf16[832,384]{1,0:T(8,128)(2,1)S(1)}, u32[]{:S(2)}, u32[]{:S(2)}) collective-permute-start(bf16[832,384]{1,0:T(8,128)(2,1)S(1)} %pad_maximum_fusion.7), channel_id=1, source_target_pairs={{0,4},{1,5},{2,6},{3,7},{4,0},{5,1},{6,2},{7,3},{8,12},{9,13},{10,... | collective-permute-start | bytes 1916936 | tf_op jit(solution)/shard_map/ppermute | solution.py:24
  95.5 4.0 %copy-start.6 = (f32[2,2,2,32,384]{4,3,2,1,0:T(8,128)}, f32[2,2,2,32,384]{4,3,2,1,0:T(8,128)S(1)}, u32[]{:S(2)}) copy-start(f32[2,2,2,32,384]{4,3,2,1,0:T(8,128)S(1)} %fusion.8) | copy-start | bytes 1179652
  96.4 9.6 %collective-permute-start.9 = (bf16[416,384]{1,0:T(8,128)(2,1)}, bf16[416,384]{1,0:T(8,128)(2,1)}, u32[]{:S(2)}, u32[]{:S(2)}) collective-permute-start(bf16[416,384]{1,0:T(8,128)(2,1)} %pad_maximum_fusion.14), channel_id=1, source_target_pairs={{0,4},{1,5},{2,6},{3,7},{4,0},{5,1},{6,2},{7,3},{8,12},{9,13},{10,... | collective-permute-start | bytes 958472 | tf_op jit(solution)/shard_map/ppermute | solution.py:24
  99.7 2.2 %copy-start.15 = (f32[16,12]{1,0:T(8,128)S(1)}, f32[16,12]{1,0:T(8,128)}, u32[]{:S(2)}) copy-start(f32[16,12]{1,0:T(8,128)} %get-tuple-element.62) | copy-start | bytes 2308
  99.8 2.1 %copy-start.7 = (f32[2,2,2,32,384]{4,3,2,0,1:T(8,128)}, f32[2,2,2,32,384]{4,3,2,0,1:T(8,128)S(1)}, u32[]{:S(2)}) copy-start(f32[2,2,2,32,384]{4,3,2,0,1:T(8,128)S(1)} %fusion.6) | copy-start | bytes 1179652
  100.6 1.7 %copy-start.17 = (f32[4,12]{1,0:T(4,128)S(1)}, f32[4,12]{1,0:T(4,128)}, u32[]{:S(2)}) copy-start(f32[4,12]{1,0:T(4,128)} %get-tuple-element.60) | copy-start | bytes 580
  100.6 8.7 %collective-permute-start.12 = (bf16[416,384]{1,0:T(8,128)(2,1)}, bf16[416,384]{1,0:T(8,128)(2,1)}, u32[]{:S(2)}, u32[]{:S(2)}) collective-permute-start(bf16[416,384]{1,0:T(8,128)(2,1)} %pad_maximum_fusion.15), channel_id=1, source_target_pairs={{0,2},{1,3},{2,0},{3,1},{4,6},{5,7},{6,4},{7,5},{8,10},{9,11},{10,... | collective-permute-start | bytes 958472 | tf_op jit(solution)/shard_map/ppermute | solution.py:24
  103.6 6.7 %copy-start.8 = (f32[2,2,2,32,384]{4,3,2,0,1:T(8,128)S(1)}, f32[2,2,2,32,384]{4,3,2,0,1:T(8,128)}, u32[]{:S(2)}) copy-start(f32[2,2,2,32,384]{4,3,2,0,1:T(8,128)} %copy-done.7) | copy-start | bytes 1179652
  111.9 7.9 %collective-permute-start.13 = (bf16[80,768]{1,0:T(8,128)(2,1)S(1)}, bf16[80,768]{1,0:T(8,128)(2,1)S(1)}, u32[]{:S(2)}, u32[]{:S(2)}) collective-permute-start(bf16[80,768]{1,0:T(8,128)(2,1)S(1)} %pad_maximum_fusion.22), channel_id=1, source_target_pairs={{0,8},{1,9},{2,10},{3,11},{4,12},{5,13},{6,14},{7,15},{8,0},{9,1},... | collective-permute-start | bytes 368648 | tf_op jit(solution)/shard_map/ppermute | solution.py:24

commit v13 on v11

--- a/solution.py
+++ b/solution.py
@@ -104,10 +104,7 @@
                 peak = jnp.maximum(peak, jnp.max(scores[branch], axis=1, keepdims=True))
             expos = []
             for branch in range(3):
-                block = jnp.exp(scores[branch] - peak)
-                if members[branch] is not None:
-                    block = jnp.where(members[branch], block, 0.0)
-                expos.append(block)
+                expos.append(jnp.exp(scores[branch] - peak))
             total = jnp.sum(expos[0], axis=1, keepdims=True)
             for branch in range(1, 3):
                 total = total + jnp.sum(expos[branch], axis=1, keepdims=True)

time: 126 us -> 126 us (level)
  no operation moved by 1% of the time
where the time goes in v13:
time: 126 us; the launch traced here: 125 us
  waiting for transfers between devices  41.3 us (33%)
  Pallas kernels  27.9 us (22%)
  local copies, waits for them, and re-layouts  22.8 us (18%)
  starting transfers between devices  19.9 us (16%)
  other arithmetic  11.3 us (9%)
  between operations  1.64 us (1%)
    ppermute x14, waiting for transfers between devices, exchange(): return lax.ppermute(block, 'seq', route)  41.3 us
    pallas_call x2, Pallas kernels, per_device(): pl.pallas_call(attention_kernel(head_dim, score_scale, half * heads_per_h...  27.9 us
    ppermute x14, starting transfers between devices, exchange(): return lax.ppermute(block, 'seq', route)  19.9 us
    slice x14, local copies, waits for them, and re-layouts, per_device(): partial[branch] = kept + incoming[cursor:cursor + count].reshape(kept.shape)  5.41 us
    mul x8, local copies, waits for them, and re-layouts, spread_rows(): return (grouped * chosen).reshape(pair, count * stride, width)  3.92 us
    slice x6, local copies, waits for them, and re-layouts, per_device(): partial.append(kept + incoming[cursor:cursor + count].reshape(kept.shape))  3.52 us
    unnamed x36, local copies, waits for them, and re-layouts  3.34 us
    another operation x4, local copies, waits for them, and re-layouts, per_device(): kv_rows = jnp.stack([key_rows, value_rows])  3.2 us
  transfers between devices with their start and end apart: 14, of which 9 were waited for; matrix products, arithmetic and copies ran while one was open for 14% of the time, Pallas kernels for 22%

profile of v13, /device:TPU:0, one launch (start us, length us, event | category | flops | bytes accessed | tf_op | source)
XLA Modules:
  0.0 124.8 jit_solution(4499294916176899589)
XLA Ops:
  0.7 1.3 %stack.103 = bf16[1,32,4,12,64]{4,3,2,1,0:T(8,128)(2,1)S(1)} reshape(bf16[128,768]{1,0:T(8,128)(2,1)} %param.6) | data formatting | bytes 393216 | tf_op jit(solution)/shard_map/stack | solution.py:174
  2.0 1.3 %stack.106 = bf16[1,8,16,12,64]{4,3,2,1,0:T(8,128)(2,1)S(1)} reshape(bf16[128,768]{1,0:T(8,128)(2,1)} %param.6) | data formatting | bytes 393216 | tf_op jit(solution)/shard_map/stack | solution.py:174
  3.2 0.3 stack.104
  3.6 0.3 stack.107
  3.9 0.6 fusion.25
  4.5 0.5 fusion
  5.0 0.2 reshape_reshape.6
  5.2 0.6 fusion.24
  5.8 0.4 fusion.1
  6.3 4.1 %collective-permute-start = (bf16[80,768]{1,0:T(8,128)(2,1)S(1)}, bf16[80,768]{1,0:T(8,128)(2,1)S(1)}, u32[]{:S(2)}, u32[]{:S(2)}) collective-permute-start(bf16[80,768]{1,0:T(8,128)(2,1)S(1)} %pad_maximum_fusion.20), channel_id=1, source_target_pairs={{0,8},{1,9},{2,10},{3,11},{4,12},{5,13},{6,14},{7,15},{8,0},{9,1},... | collective-permute-start | bytes 368648 | tf_op jit(solution)/shard_map/ppermute | solution.py:24
  10.4 0.2 stack_reshape.48
  10.7 5.6 %collective-permute-done = bf16[80,768]{1,0:T(8,128)(2,1)S(1)} collective-permute-done((bf16[80,768]{1,0:T(8,128)(2,1)S(1)}, bf16[80,768]{1,0:T(8,128)(2,1)S(1)}, u32[]{:S(2)}, u32[]{:S(2)}) %collective-permute-start) | collective-permute-done | bytes 122912 | tf_op jit(solution)/shard_map/ppermute | solution.py:24
  16.5 0.8 collective-permute-start.4
  17.4 1.6 %collective-permute-start.1 = (bf16[416,384]{1,0:T(8,128)(2,1)S(1)}, bf16[416,384]{1,0:T(8,128)(2,1)S(1)}, u32[]{:S(2)}, u32[]{:S(2)}) collective-permute-start(bf16[416,384]{1,0:T(8,128)(2,1)S(1)} %pad_maximum_fusion.12), channel_id=1, source_target_pairs={{0,2},{1,3},{2,0},{3,1},{4,6},{5,7},{6,4},{7,5},{8,10},{9,11},{10,... | collective-permute-start | bytes 958472 | tf_op jit(solution)/shard_map/ppermute | solution.py:24
  18.9 6.4 %collective-permute-done.4 = bf16[416,384]{1,0:T(8,128)(2,1)S(1)} collective-permute-done((bf16[416,384]{1,0:T(8,128)(2,1)S(1)}, bf16[416,384]{1,0:T(8,128)(2,1)S(1)}, u32[]{:S(2)}, u32[]{:S(2)}) %collective-permute-start.4) | collective-permute-done | bytes 319520 | tf_op jit(solution)/shard_map/ppermute | solution.py:24
  25.7 1.3 %collective-permute-start.5 = (bf16[832,384]{1,0:T(8,128)(2,1)S(1)}, bf16[832,384]{1,0:T(8,128)(2,1)S(1)}, u32[]{:S(2)}, u32[]{:S(2)}) collective-permute-start(bf16[832,384]{1,0:T(8,128)(2,1)S(1)} %pad_maximum_fusion.5), channel_id=1, source_target_pairs={{0,2},{1,3},{2,0},{3,1},{4,6},{5,7},{6,4},{7,5},{8,10},{9,11},{10,... | collective-permute-start | bytes 1916936 | tf_op jit(solution)/shard_map/ppermute | solution.py:24
  27.3 1.8 %collective-permute-start.2 = (bf16[832,384]{1,0:T(8,128)(2,1)S(1)}, bf16[832,384]{1,0:T(8,128)(2,1)S(1)}, u32[]{:S(2)}, u32[]{:S(2)}) collective-permute-start(bf16[832,384]{1,0:T(8,128)(2,1)S(1)} %pad_maximum_fusion.4), channel_id=1, source_target_pairs={{0,4},{1,5},{2,6},{3,7},{4,0},{5,1},{6,2},{7,3},{8,12},{9,13},{10,... | collective-permute-start | bytes 1916936 | tf_op jit(solution)/shard_map/ppermute | solution.py:24
  29.1 11.3 %collective-permute-done.5 = bf16[832,384]{1,0:T(8,128)(2,1)S(1)} collective-permute-done((bf16[832,384]{1,0:T(8,128)(2,1)S(1)}, bf16[832,384]{1,0:T(8,128)(2,1)S(1)}, u32[]{:S(2)}, u32[]{:S(2)}) %collective-permute-start.5) | collective-permute-done | bytes 639008 | tf_op jit(solution)/shard_map/ppermute | solution.py:24
  41.0 1.5 %collective-permute-done.2 = bf16[832,384]{1,0:T(8,128)(2,1)S(1)} collective-permute-done((bf16[832,384]{1,0:T(8,128)(2,1)S(1)}, bf16[832,384]{1,0:T(8,128)(2,1)S(1)}, u32[]{:S(2)}, u32[]{:S(2)}) %collective-permute-start.2) | collective-permute-done | bytes 639008 | tf_op jit(solution)/shard_map/ppermute | solution.py:24
  43.0 1.2 pad_maximum_fusion.mine_ref
  44.2 0.8 fusion.32
  44.9 1.1 copy-done.5
  46.1 13.9 %shard_map.84 = (bf16[128,768]{1,0:T(8,128)(2,1)}, bf16[128,768]{1,0:T(8,128)(2,1)}, f32[2,512,384]{2,1,0:T(8,128)}, f32[2,256,384]{2,1,0:T(8,128)}, f32[2,64,384]{2,1,0:T(8,128)}, /*index=5*/bf16[1664,384]{1,0:T(8,128)(2,1)}) custom-call(s32[3,12]{1,0:T(4,128)} %offsets_ref.3, bf16[128,384]{1,0:T(8,128)(2,1)} %get-tuple-element.59.query_ref, ...), custom_call_target="tpu_custom_call" | custom-call | tf_op jit(solution)/shard_map/pallas_call | solution.py:238
  60.0 0.5 collective-permute-start.7
  60.5 13.9 %shard_map.85 = (bf16[128,768]{1,0:T(8,128)(2,1)}, bf16[128,768]{1,0:T(8,128)(2,1)}, f32[2,512,384]{2,1,0:T(8,128)}, f32[2,256,384]{2,1,0:T(8,128)}, f32[2,64,384]{2,1,0:T(8,128)}, /*index=5*/bf16[1664,384]{1,0:T(8,128)(2,1)}) custom-call(s32[3,12]{1,0:T(4,128)} %offsets_ref.3, ...), custom_call_target="tpu_custom_call", output_to_operand_aliasing={{0}: (5, {}), {1}: (6, {})} | custom-call | tf_op jit(solution)/shard_map/pallas_call | solution.py:238
  74.6 1.3 %slice.342 = f32[1024,384]{1,0:T(8,128)S(1)} slice(bf16[1664,384]{1,0:T(8,128)(2,1)} %collective-permute-done.7), slice={[0:1024], [0:384]} | slice | bytes 3145728 | tf_op jit(solution)/shard_map/slice | solution.py:282
  75.9 0.2 copy-done.4
  76.1 0.2 copy_add_fusion.1
  76.3 1.1 slice.345
  77.7 0.9 slice.347
  78.7 1.2 collective-permute-start.8
  80.1 0.2 copy_add_fusion
  80.5 1.0 copy-done.9
  81.7 0.7 copy-done.13
  82.5 1.8 %collective-permute-start.11 = (bf16[832,384]{1,0:T(8,128)(2,1)S(1)}, bf16[832,384]{1,0:T(8,128)(2,1)S(1)}, u32[]{:S(2)}, u32[]{:S(2)}) collective-permute-start(bf16[832,384]{1,0:T(8,128)(2,1)S(1)} %pad_maximum_fusion.7), channel_id=1, source_target_pairs={{0,4},{1,5},{2,6},{3,7},{4,0},{5,1},{6,2},{7,3},{8,12},{9,13},{10,... | collective-permute-start | bytes 1916936 | tf_op jit(solution)/shard_map/ppermute | solution.py:24
  84.4 10.9 %collective-permute-done.8 = bf16[832,384]{1,0:T(8,128)(2,1)S(1)} collective-permute-done((bf16[832,384]{1,0:T(8,128)(2,1)S(1)}, bf16[832,384]{1,0:T(8,128)(2,1)S(1)}, u32[]{:S(2)}, u32[]{:S(2)}) %collective-permute-start.8) | collective-permute-done | bytes 639008 | tf_op jit(solution)/shard_map/ppermute | solution.py:24
  95.7 0.8 pad_maximum_fusion.14
  96.5 1.7 %collective-permute-start.9 = (bf16[416,384]{1,0:T(8,128)(2,1)}, bf16[416,384]{1,0:T(8,128)(2,1)}, u32[]{:S(2)}, u32[]{:S(2)}) collective-permute-start(bf16[416,384]{1,0:T(8,128)(2,1)} %pad_maximum_fusion.14), channel_id=1, source_target_pairs={{0,4},{1,5},{2,6},{3,7},{4,0},{5,1},{6,2},{7,3},{8,12},{9,13},{10,... | collective-permute-start | bytes 958472 | tf_op jit(solution)/shard_map/ppermute | solution.py:24
  98.2 1.3 %collective-permute-done.11 = bf16[832,384]{1,0:T(8,128)(2,1)S(1)} collective-permute-done((bf16[832,384]{1,0:T(8,128)(2,1)S(1)}, bf16[832,384]{1,0:T(8,128)(2,1)S(1)}, u32[]{:S(2)}, u32[]{:S(2)}) %collective-permute-start.11) | collective-permute-done | bytes 639008 | tf_op jit(solution)/shard_map/ppermute | solution.py:24
  99.9 0.8 pad_maximum_fusion.15
  100.6 1.2 collective-permute-start.12
  101.9 0.2 mul.48
  102.0 0.3 mul.49
  102.3 0.2 mul.42
  102.5 1.0 mul.43
  103.6 2.5 %collective-permute-done.9 = bf16[416,384]{1,0:T(8,128)(2,1)} collective-permute-done((bf16[416,384]{1,0:T(8,128)(2,1)}, bf16[416,384]{1,0:T(8,128)(2,1)}, u32[]{:S(2)}, u32[]{:S(2)}) %collective-permute-start.9) | collective-permute-done | bytes 319520 | tf_op jit(solution)/shard_map/ppermute | solution.py:24
  106.0 0.9 slice.377
  106.9 1.0 fusion.14
  107.9 1.5 %collective-permute-done.12 = bf16[416,384]{1,0:T(8,128)(2,1)} collective-permute-done((bf16[416,384]{1,0:T(8,128)(2,1)}, bf16[416,384]{1,0:T(8,128)(2,1)}, u32[]{:S(2)}, u32[]{:S(2)}) %collective-permute-start.12) | collective-permute-done | bytes 319520 | tf_op jit(solution)/shard_map/ppermute | solution.py:24
  109.4 0.9 slice.379
  110.3 0.7 slice.383
  111.1 0.7 slice.385
  111.9 3.7 %collective-permute-start.13 = (bf16[80,768]{1,0:T(8,128)(2,1)S(1)}, bf16[80,768]{1,0:T(8,128)(2,1)S(1)}, u32[]{:S(2)}, u32[]{:S(2)}) collective-permute-start(bf16[80,768]{1,0:T(8,128)(2,1)S(1)} %pad_maximum_fusion.21), channel_id=1, source_target_pairs={{0,8},{1,9},{2,10},{3,11},{4,12},{5,13},{6,14},{7,15},{8,0},{9,1},... | collective-permute-start | bytes 368648 | tf_op jit(solution)/shard_map/ppermute | solution.py:24
  115.6 1.0 slice.358
  116.5 0.8 fusion.9
  117.4 1.0 slice.375
  118.3 0.8 fusion.7
  119.4 0.4 collective-permute-done.13
  120.0 0.2 mul.40
  120.2 0.5 mul.41
  120.8 0.2 mul.46
  121.0 1.4 %mul.47 = f32[2,128,768]{2,1,0:T(8,128)} reshape(f32[2,8,16,12,64]{4,3,2,1,0:T(8,128)S(1)} %mul.46) | data formatting | bytes 1572864 | tf_op jit(solution)/shard_map/mul | solution.py:49
  122.4 1.6 %fusion.5 = bf16[2,128,768]{2,1,0:T(8,128)(2,1)S(1)} fusion(f32[2,128,384]{2,1,0:T(8,128)} %fusion.7, f32[2,128,384]{2,1,0:T(8,128)} %fusion.9, f32[2,128,768]{2,1,0:T(8,128)} %mul.47, f32[2,128,768]{2,1,0:T(8,128)S(1)} %mul.41, f32[128,768]{1,0:T(8,128)S(1)} %mul.49, f32[128,768]{1,0:T(8,128)} %mul.43), kind=kLoop, calls=%fused_computation.18 | loop fusion | flops 1179648 | bytes 3538944 | tf_op jit(solution)/shard_map/convert.3 | solution.py:351
  124.0 0.8 slice_bitcast_fusion.6
  (145 shorter events, 4.3 us)
Async XLA Ops:
  0.6 2.6 %copy-start.1 = (bf16[128,768]{1,0:T(8,128)(2,1)S(1)}, bf16[128,768]{1,0:T(8,128)(2,1)}, u32[]{:S(2)}) copy-start(bf16[128,768]{1,0:T(8,128)(2,1)} %param.7) | copy-start | bytes 589828
  0.6 3.3 %copy-start.16 = (s32[3,12]{1,0:T(4,128)S(1)}, s32[3,12]{1,0:T(4,128)}, u32[]{:S(2)}) copy-start(s32[3,12]{1,0:T(4,128)} %offsets_ref.3) | copy-start | bytes 436
  5.0 5.7 %copy-start.2 = (bf16[128,768]{1,0:T(8,128)(2,1)S(1)}, bf16[128,768]{1,0:T(8,128)(2,1)}, u32[]{:S(2)}) copy-start(bf16[128,768]{1,0:T(8,128)(2,1)} %param.6) | copy-start | bytes 589828
  6.3 10.1 %collective-permute-start = (bf16[80,768]{1,0:T(8,128)(2,1)S(1)}, bf16[80,768]{1,0:T(8,128)(2,1)S(1)}, u32[]{:S(2)}, u32[]{:S(2)}) collective-permute-start(bf16[80,768]{1,0:T(8,128)(2,1)S(1)} %pad_maximum_fusion.20), channel_id=1, source_target_pairs={{0,8},{1,9},{2,10},{3,11},{4,12},{5,13},{6,14},{7,15},{8,0},{9,1},... | collective-permute-start | bytes 368648 | tf_op jit(solution)/shard_map/ppermute | solution.py:24
  16.5 8.8 %collective-permute-start.4 = (bf16[416,384]{1,0:T(8,128)(2,1)S(1)}, bf16[416,384]{1,0:T(8,128)(2,1)S(1)}, u32[]{:S(2)}, u32[]{:S(2)}) collective-permute-start(bf16[416,384]{1,0:T(8,128)(2,1)S(1)} %pad_maximum_fusion.13), channel_id=1, source_target_pairs={{0,4},{1,5},{2,6},{3,7},{4,0},{5,1},{6,2},{7,3},{8,12},{9,13},{10,... | collective-permute-start | bytes 958472 | tf_op jit(solution)/shard_map/ppermute | solution.py:24
  17.4 9.6 %collective-permute-start.1 = (bf16[416,384]{1,0:T(8,128)(2,1)S(1)}, bf16[416,384]{1,0:T(8,128)(2,1)S(1)}, u32[]{:S(2)}, u32[]{:S(2)}) collective-permute-start(bf16[416,384]{1,0:T(8,128)(2,1)S(1)} %pad_maximum_fusion.12), channel_id=1, source_target_pairs={{0,2},{1,3},{2,0},{3,1},{4,6},{5,7},{6,4},{7,5},{8,10},{9,11},{10,... | collective-permute-start | bytes 958472 | tf_op jit(solution)/shard_map/ppermute | solution.py:24
  25.7 14.7 %collective-permute-start.5 = (bf16[832,384]{1,0:T(8,128)(2,1)S(1)}, bf16[832,384]{1,0:T(8,128)(2,1)S(1)}, u32[]{:S(2)}, u32[]{:S(2)}) collective-permute-start(bf16[832,384]{1,0:T(8,128)(2,1)S(1)} %pad_maximum_fusion.5), channel_id=1, source_target_pairs={{0,2},{1,3},{2,0},{3,1},{4,6},{5,7},{6,4},{7,5},{8,10},{9,11},{10,... | collective-permute-start | bytes 1916936 | tf_op jit(solution)/shard_map/ppermute | solution.py:24
  27.3 15.2 %collective-permute-start.2 = (bf16[832,384]{1,0:T(8,128)(2,1)S(1)}, bf16[832,384]{1,0:T(8,128)(2,1)S(1)}, u32[]{:S(2)}, u32[]{:S(2)}) collective-permute-start(bf16[832,384]{1,0:T(8,128)(2,1)S(1)} %pad_maximum_fusion.4), channel_id=1, source_target_pairs={{0,4},{1,5},{2,6},{3,7},{4,0},{5,1},{6,2},{7,3},{8,12},{9,13},{10,... | collective-permute-start | bytes 1916936 | tf_op jit(solution)/shard_map/ppermute | solution.py:24
  40.9 1.8 %copy-start = (bf16[1664,384]{1,0:T(8,128)(2,1)}, bf16[1664,384]{1,0:T(8,128)(2,1)S(1)}, u32[]{:S(2)}) copy-start(bf16[1664,384]{1,0:T(8,128)(2,1)S(1)} %pad_maximum_fusion.1.mine_ref) | copy-start | bytes 3833860
  40.9 4.0 %collective-permute-start.6 = (bf16[1664,384]{1,0:T(8,128)(2,1)S(1)}, bf16[1664,384]{1,0:T(8,128)(2,1)S(1)}, u32[]{:S(2)}, u32[]{:S(2)}) collective-permute-start(bf16[1664,384]{1,0:T(8,128)(2,1)S(1)} %pad_maximum_fusion.1.mine_ref), channel_id=1, source_target_pairs={{0,1},{1,0},{2,3},{3,2},{4,5},{5,4},{6,7},{7,6},{8,9},{9,8},{10,11... | collective-permute-start | bytes 3833864 | tf_op jit(solution)/shard_map/ppermute | solution.py:24
  42.9 1.2 copy-start.11
  42.9 1.2 copy-start.12
  44.2 16.4 %collective-permute-start.3 = (bf16[1664,384]{1,0:T(8,128)(2,1)}, bf16[1664,384]{1,0:T(8,128)(2,1)}, u32[]{:S(2)}, u32[]{:S(2)}) collective-permute-start(bf16[1664,384]{1,0:T(8,128)(2,1)} %pad_maximum_fusion.mine_ref), channel_id=1, source_target_pairs={{0,1},{1,0},{2,3},{3,2},{4,5},{5,4},{6,7},{7,6},{8,9},{9,8},{10,11... | collective-permute-start | bytes 3833864 | tf_op jit(solution)/shard_map/ppermute | solution.py:24
  44.9 1.2 copy-start.5
  60.0 14.6 %collective-permute-start.7 = (bf16[1664,384]{1,0:T(8,128)(2,1)}, bf16[1664,384]{1,0:T(8,128)(2,1)}, u32[]{:S(2)}, u32[]{:S(2)}) collective-permute-start(bf16[1664,384]{1,0:T(8,128)(2,1)} %get-tuple-element.21), channel_id=1, source_target_pairs={{0,1},{1,0},{2,3},{3,2},{4,5},{5,4},{6,7},{7,6},{8,9},{9,8},{10,11... | collective-permute-start | bytes 3833864 | tf_op jit(solution)/shard_map/ppermute | solution.py:24
  74.5 1.6 %copy-start.4 = (f32[2,512,384]{2,1,0:T(8,128)S(1)}, f32[2,512,384]{2,1,0:T(8,128)}, u32[]{:S(2)}) copy-start(f32[2,512,384]{2,1,0:T(8,128)} %get-tuple-element.20) | copy-start | bytes 4718596
  74.5 5.4 %collective-permute-start.10 = (bf16[1664,384]{1,0:T(8,128)(2,1)}, bf16[1664,384]{1,0:T(8,128)(2,1)S(1)}, u32[]{:S(2)}, u32[]{:S(2)}) collective-permute-start(bf16[1664,384]{1,0:T(8,128)(2,1)} %get-tuple-element.25), channel_id=1, source_target_pairs={{0,1},{1,0},{2,3},{3,2},{4,5},{5,4},{6,7},{7,6},{8,9},{9,8},{10,11... | collective-permute-start | bytes 3833864 | tf_op jit(solution)/shard_map/ppermute | solution.py:24
  76.3 1.3 %copy-start.10 = (f32[2,256,384]{2,1,0:T(8,128)S(1)}, f32[2,256,384]{2,1,0:T(8,128)}, u32[]{:S(2)}) copy-start(f32[2,256,384]{2,1,0:T(8,128)} %get-tuple-element.22) | copy-start | bytes 2359300
  77.5 1.1 copy-start.14
  78.7 1.4 %copy-start.3 = (f32[2,512,384]{2,1,0:T(8,128)S(1)}, f32[2,512,384]{2,1,0:T(8,128)}, u32[]{:S(2)}) copy-start(f32[2,512,384]{2,1,0:T(8,128)} %get-tuple-element.24) | copy-start | bytes 4718596
  78.7 16.5 %collective-permute-start.8 = (bf16[832,384]{1,0:T(8,128)(2,1)S(1)}, bf16[832,384]{1,0:T(8,128)(2,1)S(1)}, u32[]{:S(2)}, u32[]{:S(2)}) collective-permute-start(bf16[832,384]{1,0:T(8,128)(2,1)S(1)} %pad_maximum_fusion.6), channel_id=1, source_target_pairs={{0,2},{1,3},{2,0},{3,1},{4,6},{5,7},{6,4},{7,5},{8,10},{9,11},{10,... | collective-permute-start | bytes 1916936 | tf_op jit(solution)/shard_map/ppermute | solution.py:24
  80.3 1.1 copy-start.9
  81.5 0.9 copy-start.13
  82.5 16.9 %collective-permute-start.11 = (bf16[832,384]{1,0:T(8,128)(2,1)S(1)}, bf16[832,384]{1,0:T(8,128)(2,1)S(1)}, u32[]{:S(2)}, u32[]{:S(2)}) collective-permute-start(bf16[832,384]{1,0:T(8,128)(2,1)S(1)} %pad_maximum_fusion.7), channel_id=1, source_target_pairs={{0,4},{1,5},{2,6},{3,7},{4,0},{5,1},{6,2},{7,3},{8,12},{9,13},{10,... | collective-permute-start | bytes 1916936 | tf_op jit(solution)/shard_map/ppermute | solution.py:24
  95.6 3.9 %copy-start.6 = (f32[2,2,2,32,384]{4,3,2,1,0:T(8,128)}, f32[2,2,2,32,384]{4,3,2,1,0:T(8,128)S(1)}, u32[]{:S(2)}) copy-start(f32[2,2,2,32,384]{4,3,2,1,0:T(8,128)S(1)} %fusion.8) | copy-start | bytes 1179652
  96.5 9.6 %collective-permute-start.9 = (bf16[416,384]{1,0:T(8,128)(2,1)}, bf16[416,384]{1,0:T(8,128)(2,1)}, u32[]{:S(2)}, u32[]{:S(2)}) collective-permute-start(bf16[416,384]{1,0:T(8,128)(2,1)} %pad_maximum_fusion.14), channel_id=1, source_target_pairs={{0,4},{1,5},{2,6},{3,7},{4,0},{5,1},{6,2},{7,3},{8,12},{9,13},{10,... | collective-permute-start | bytes 958472 | tf_op jit(solution)/shard_map/ppermute | solution.py:24
  99.7 2.2 %copy-start.15 = (f32[16,12]{1,0:T(8,128)S(1)}, f32[16,12]{1,0:T(8,128)}, u32[]{:S(2)}) copy-start(f32[16,12]{1,0:T(8,128)} %get-tuple-element.56) | copy-start | bytes 2308
  99.8 2.1 %copy-start.7 = (f32[2,2,2,32,384]{4,3,2,0,1:T(8,128)}, f32[2,2,2,32,384]{4,3,2,0,1:T(8,128)S(1)}, u32[]{:S(2)}) copy-start(f32[2,2,2,32,384]{4,3,2,0,1:T(8,128)S(1)} %fusion.6) | copy-start | bytes 1179652
  100.6 1.7 %copy-start.17 = (f32[4,12]{1,0:T(4,128)S(1)}, f32[4,12]{1,0:T(4,128)}, u32[]{:S(2)}) copy-start(f32[4,12]{1,0:T(4,128)} %get-tuple-element.54) | copy-start | bytes 580
  100.6 8.7 %collective-permute-start.12 = (bf16[416,384]{1,0:T(8,128)(2,1)}, bf16[416,384]{1,0:T(8,128)(2,1)}, u32[]{:S(2)}, u32[]{:S(2)}) collective-permute-start(bf16[416,384]{1,0:T(8,128)(2,1)} %pad_maximum_fusion.15), channel_id=1, source_target_pairs={{0,2},{1,3},{2,0},{3,1},{4,6},{5,7},{6,4},{7,5},{8,10},{9,11},{10,... | collective-permute-start | bytes 958472 | tf_op jit(solution)/shard_map/ppermute | solution.py:24
  103.6 6.7 %copy-start.8 = (f32[2,2,2,32,384]{4,3,2,0,1:T(8,128)S(1)}, f32[2,2,2,32,384]{4,3,2,0,1:T(8,128)}, u32[]{:S(2)}) copy-start(f32[2,2,2,32,384]{4,3,2,0,1:T(8,128)} %copy-done.7) | copy-start | bytes 1179652
  111.9 7.9 %collective-permute-start.13 = (bf16[80,768]{1,0:T(8,128)(2,1)S(1)}, bf16[80,768]{1,0:T(8,128)(2,1)S(1)}, u32[]{:S(2)}, u32[]{:S(2)}) collective-permute-start(bf16[80,768]{1,0:T(8,128)(2,1)S(1)} %pad_maximum_fusion.21), channel_id=1, source_target_pairs={{0,8},{1,9},{2,10},{3,11},{4,12},{5,13},{6,14},{7,15},{8,0},{9,1},... | collective-permute-start | bytes 368648 | tf_op jit(solution)/shard_map/ppermute | solution.py:24

commit v14 on v13

--- a/solution.py
+++ b/solution.py
@@ -279,14 +279,18 @@
                     (2,) + (2,) * len(axis_bits[branch]) + (-1, half_width)
                 )
                 count = kept.size // half_width
-                partial.append(kept + incoming[cursor : cursor + count].reshape(kept.shape))
+                partial.append((kept, incoming[cursor : cursor + count].reshape(kept.shape)))
                 cursor += count
+
+            def take(pair, index, place):
+                return tuple(lax.index_in_dim(part, index, place, keepdims=False) for part in pair)
+
             for bit in order[1 : len(order) - shared]:
                 active = [branch for branch in range(3) if branch_bits[branch] > bit]
                 places = {branch: 1 + axis_bits[branch].index(bit) for branch in active}
                 outgoing = jnp.concatenate(
                     [
-                        lax.index_in_dim(partial[branch], 1, places[branch], keepdims=False)
+                        sum(take(partial[branch], 1, places[branch]))
                         .reshape(-1, half_width)
                         .astype(jnp.bfloat16)
                         for branch in active
@@ -295,12 +299,12 @@
                 incoming = exchange(outgoing, bit).astype(jnp.float32)
                 cursor = 0
                 for branch in active:
-                    kept = lax.index_in_dim(partial[branch], 0, places[branch], keepdims=False)
+                    kept = sum(take(partial[branch], 0, places[branch]))
                     count = kept.size // half_width
-                    partial[branch] = kept + incoming[cursor : cursor + count].reshape(kept.shape)
+                    partial[branch] = (kept, incoming[cursor : cursor + count].reshape(kept.shape))
                     cursor += count
                     axis_bits[branch].remove(bit)
-            results.append((partial, axis_bits))
+            results.append(([pair[0] + pair[1] for pair in partial], axis_bits))
 
         partial = [
             jnp.concatenate([result[0][branch] for result in results], axis=-1)

time: 126 us -> 127 us (level)
  local copies, waits for them, and re-layouts: 22.8 us -> 26 us
    slice x14 -> x2, local copies, waits for them, and re-layouts: 5.41 us -> 0.02 us  [per_device(): partial[branch] = kept + incoming[cursor:cursor + count].reshape(kept.shape)]
    slice x21 -> x18, local copies, waits for them, and re-layouts: 3.85 us -> 9.03 us  [the longest x12 5.46 us: per_device(): incoming[cursor:cursor + count].reshape(kept.shape)]
    add x14 -> x2, other arithmetic: 3.06 us -> 0.09 us  [per_device(): partial[branch] = kept + incoming[cursor:cursor + count].reshape(kept.shape)]
    unnamed x36 -> x60, local copies, waits for them, and re-layouts: 3.34 us -> 5.93 us
    add x6 -> x12, other arithmetic: 0.57 us -> 3.09 us  [the longest x6 2.8 us: per_device(): results.append(([pair[0] + pair[1] for pair in partial], axis_bits))]
    concatenate x5 -> x1, other arithmetic: 1.72 us -> 0.01 us  [per_device(): jnp.concatenate([lax.index_in_dim(partial[branch], 1, places[branch], kee...]
    concatenate x0 -> x4, other arithmetic: none -> 1.65 us  [per_device(): jnp.concatenate([sum(take(partial[branch], 1, places[branch])).reshape(-1...]
where the time goes in v14:
time: 127 us
  waiting for transfers between devices  40.5 us (32%)
  Pallas kernels  27.9 us (22%)
  local copies, waits for them, and re-layouts  26 us (20%)
  starting transfers between devices  19.1 us (15%)
  other arithmetic  11.4 us (9%)
  between operations  1.71 us (1%)
    ppermute x14, waiting for transfers between devices, exchange(): return lax.ppermute(block, 'seq', route)  40.5 us
    pallas_call x2, Pallas kernels, per_device(): pl.pallas_call(attention_kernel(head_dim, score_scale, half * heads_per_h...  27.9 us
    ppermute x14, starting transfers between devices, exchange(): return lax.ppermute(block, 'seq', route)  19.1 us
    unnamed x60, local copies, waits for them, and re-layouts  5.93 us
    slice x12, local copies, waits for them, and re-layouts, per_device(): incoming[cursor:cursor + count].reshape(kept.shape)  5.46 us
    mul x8, local copies, waits for them, and re-layouts, spread_rows(): return (grouped * chosen).reshape(pair, count * stride, width)  4.68 us
    slice x6, local copies, waits for them, and re-layouts, per_device(): partial.append((kept, incoming[cursor:cursor + count].reshape(kept.shape)))  3.57 us
    another operation x4, local copies, waits for them, and re-layouts, per_device(): kv_rows = jnp.stack([key_rows, value_rows])  3.2 us
  transfers between devices with their start and end apart: 14, of which 9 were waited for; matrix products, arithmetic and copies ran while one was open for 14% of the time, Pallas kernels for 22%

profile of v14, /device:TPU:0, one launch (start us, length us, event | category | flops | bytes accessed | tf_op | source)
XLA Modules:
  0.0 126.6 jit_solution(14843701061732998463)
XLA Ops:
  0.7 1.3 %stack.103 = bf16[1,32,4,12,64]{4,3,2,1,0:T(8,128)(2,1)S(1)} reshape(bf16[128,768]{1,0:T(8,128)(2,1)} %param.6) | data formatting | bytes 393216 | tf_op jit(solution)/shard_map/stack | solution.py:174
  2.0 1.3 stack.106
  3.2 0.3 stack.104
  3.6 0.3 stack.107
  3.9 0.6 fusion.52
  4.5 0.5 fusion
  5.0 0.2 reshape_reshape.6
  5.1 0.6 fusion.51
  5.7 0.4 fusion.1
  6.3 4.1 %collective-permute-start = (bf16[80,768]{1,0:T(8,128)(2,1)S(1)}, bf16[80,768]{1,0:T(8,128)(2,1)S(1)}, u32[]{:S(2)}, u32[]{:S(2)}) collective-permute-start(bf16[80,768]{1,0:T(8,128)(2,1)S(1)} %pad_maximum_fusion.20), channel_id=1, source_target_pairs={{0,8},{1,9},{2,10},{3,11},{4,12},{5,13},{6,14},{7,15},{8,0},{9,1},... | collective-permute-start | bytes 368648 | tf_op jit(solution)/shard_map/ppermute | solution.py:24
  10.4 0.2 stack_reshape.48
  10.7 5.6 %collective-permute-done = bf16[80,768]{1,0:T(8,128)(2,1)S(1)} collective-permute-done((bf16[80,768]{1,0:T(8,128)(2,1)S(1)}, bf16[80,768]{1,0:T(8,128)(2,1)S(1)}, u32[]{:S(2)}, u32[]{:S(2)}) %collective-permute-start) | collective-permute-done | bytes 122912 | tf_op jit(solution)/shard_map/ppermute | solution.py:24
  16.5 0.8 collective-permute-start.4
  17.4 1.6 %collective-permute-start.1 = (bf16[416,384]{1,0:T(8,128)(2,1)S(1)}, bf16[416,384]{1,0:T(8,128)(2,1)S(1)}, u32[]{:S(2)}, u32[]{:S(2)}) collective-permute-start(bf16[416,384]{1,0:T(8,128)(2,1)S(1)} %pad_maximum_fusion.12), channel_id=1, source_target_pairs={{0,2},{1,3},{2,0},{3,1},{4,6},{5,7},{6,4},{7,5},{8,10},{9,11},{10,... | collective-permute-start | bytes 958472 | tf_op jit(solution)/shard_map/ppermute | solution.py:24
  18.9 6.4 %collective-permute-done.4 = bf16[416,384]{1,0:T(8,128)(2,1)S(1)} collective-permute-done((bf16[416,384]{1,0:T(8,128)(2,1)S(1)}, bf16[416,384]{1,0:T(8,128)(2,1)S(1)}, u32[]{:S(2)}, u32[]{:S(2)}) %collective-permute-start.4) | collective-permute-done | bytes 319520 | tf_op jit(solution)/shard_map/ppermute | solution.py:24
  25.7 1.3 %collective-permute-start.5 = (bf16[832,384]{1,0:T(8,128)(2,1)S(1)}, bf16[832,384]{1,0:T(8,128)(2,1)S(1)}, u32[]{:S(2)}, u32[]{:S(2)}) collective-permute-start(bf16[832,384]{1,0:T(8,128)(2,1)S(1)} %pad_maximum_fusion.5), channel_id=1, source_target_pairs={{0,2},{1,3},{2,0},{3,1},{4,6},{5,7},{6,4},{7,5},{8,10},{9,11},{10,... | collective-permute-start | bytes 1916936 | tf_op jit(solution)/shard_map/ppermute | solution.py:24
  27.3 1.8 %collective-permute-start.2 = (bf16[832,384]{1,0:T(8,128)(2,1)S(1)}, bf16[832,384]{1,0:T(8,128)(2,1)S(1)}, u32[]{:S(2)}, u32[]{:S(2)}) collective-permute-start(bf16[832,384]{1,0:T(8,128)(2,1)S(1)} %pad_maximum_fusion.4), channel_id=1, source_target_pairs={{0,4},{1,5},{2,6},{3,7},{4,0},{5,1},{6,2},{7,3},{8,12},{9,13},{10,... | collective-permute-start | bytes 1916936 | tf_op jit(solution)/shard_map/ppermute | solution.py:24
  29.1 11.3 %collective-permute-done.5 = bf16[832,384]{1,0:T(8,128)(2,1)S(1)} collective-permute-done((bf16[832,384]{1,0:T(8,128)(2,1)S(1)}, bf16[832,384]{1,0:T(8,128)(2,1)S(1)}, u32[]{:S(2)}, u32[]{:S(2)}) %collective-permute-start.5) | collective-permute-done | bytes 639008 | tf_op jit(solution)/shard_map/ppermute | solution.py:24
  41.0 1.5 %collective-permute-done.2 = bf16[832,384]{1,0:T(8,128)(2,1)S(1)} collective-permute-done((bf16[832,384]{1,0:T(8,128)(2,1)S(1)}, bf16[832,384]{1,0:T(8,128)(2,1)S(1)}, u32[]{:S(2)}, u32[]{:S(2)}) %collective-permute-start.2) | collective-permute-done | bytes 639008 | tf_op jit(solution)/shard_map/ppermute | solution.py:24
  42.9 1.2 pad_maximum_fusion.mine_ref
  44.1 0.7 fusion.62
  44.9 1.1 copy-done.14
  46.0 14.0 %shard_map.84 = (bf16[128,768]{1,0:T(8,128)(2,1)}, bf16[128,768]{1,0:T(8,128)(2,1)}, f32[2,512,384]{2,1,0:T(8,128)}, f32[2,256,384]{2,1,0:T(8,128)}, f32[2,64,384]{2,1,0:T(8,128)}, /*index=5*/bf16[1664,384]{1,0:T(8,128)(2,1)}) custom-call(s32[3,12]{1,0:T(4,128)} %offsets_ref.3, bf16[128,384]{1,0:T(8,128)(2,1)} %get-tuple-element.68.query_ref, ...), custom_call_target="tpu_custom_call" | custom-call | tf_op jit(solution)/shard_map/pallas_call | solution.py:238
  60.0 0.5 collective-permute-start.7
  60.5 14.0 %shard_map.85 = (bf16[128,768]{1,0:T(8,128)(2,1)}, bf16[128,768]{1,0:T(8,128)(2,1)}, f32[2,512,384]{2,1,0:T(8,128)}, f32[2,256,384]{2,1,0:T(8,128)}, f32[2,64,384]{2,1,0:T(8,128)}, /*index=5*/bf16[1664,384]{1,0:T(8,128)(2,1)}) custom-call(s32[3,12]{1,0:T(4,128)} %offsets_ref.3, ...), custom_call_target="tpu_custom_call", output_to_operand_aliasing={{0}: (5, {}), {1}: (6, {})} | custom-call | tf_op jit(solution)/shard_map/pallas_call | solution.py:238
  74.5 1.3 %slice.427 = f32[1024,384]{1,0:T(8,128)S(1)} slice(bf16[1664,384]{1,0:T(8,128)(2,1)} %collective-permute-done.7), slice={[0:1024], [0:384]} | slice | bytes 3145728 | tf_op jit(solution)/shard_map/slice | solution.py:282
  75.9 1.2 slice.433
  77.1 0.9 slice.436
  78.2 1.2 collective-permute-start.8
  79.6 1.4 %copy-done.10 = f32[2,512,384]{2,1,0:T(8,128)S(1)} copy-done((f32[2,512,384]{2,1,0:T(8,128)S(1)}, f32[2,512,384]{2,1,0:T(8,128)}, u32[]{:S(2)}) %copy-start.10) | copy-done | bytes 1572888
  81.1 0.2 fusion.59
  81.3 1.1 copy-done.15
  82.6 0.8 copy-done.25
  83.4 1.9 %collective-permute-start.11 = (bf16[832,384]{1,0:T(8,128)(2,1)S(1)}, bf16[832,384]{1,0:T(8,128)(2,1)S(1)}, u32[]{:S(2)}, u32[]{:S(2)}) collective-permute-start(bf16[832,384]{1,0:T(8,128)(2,1)S(1)} %pad_maximum_fusion.7), channel_id=1, source_target_pairs={{0,4},{1,5},{2,6},{3,7},{4,0},{5,1},{6,2},{7,3},{8,12},{9,13},{10,... | collective-permute-start | bytes 1916936 | tf_op jit(solution)/shard_map/ppermute | solution.py:24
  85.7 9.4 %collective-permute-done.8 = bf16[832,384]{1,0:T(8,128)(2,1)S(1)} collective-permute-done((bf16[832,384]{1,0:T(8,128)(2,1)S(1)}, bf16[832,384]{1,0:T(8,128)(2,1)S(1)}, u32[]{:S(2)}, u32[]{:S(2)}) %collective-permute-start.8) | collective-permute-done | bytes 639008 | tf_op jit(solution)/shard_map/ppermute | solution.py:24
  95.2 0.7 copy-done.6
  96.0 0.7 pad_maximum_fusion.14
  96.8 1.7 %collective-permute-start.9 = (bf16[416,384]{1,0:T(8,128)(2,1)}, bf16[416,384]{1,0:T(8,128)(2,1)}, u32[]{:S(2)}, u32[]{:S(2)}) collective-permute-start(bf16[416,384]{1,0:T(8,128)(2,1)} %pad_maximum_fusion.14), channel_id=1, source_target_pairs={{0,4},{1,5},{2,6},{3,7},{4,0},{5,1},{6,2},{7,3},{8,12},{9,13},{10,... | collective-permute-start | bytes 958472 | tf_op jit(solution)/shard_map/ppermute | solution.py:24
  98.5 2.2 %collective-permute-done.11 = bf16[832,384]{1,0:T(8,128)(2,1)S(1)} collective-permute-done((bf16[832,384]{1,0:T(8,128)(2,1)S(1)}, bf16[832,384]{1,0:T(8,128)(2,1)S(1)}, u32[]{:S(2)}, u32[]{:S(2)}) %collective-permute-start.11) | collective-permute-done | bytes 639008 | tf_op jit(solution)/shard_map/ppermute | solution.py:24
  100.9 0.7 copy-done.7
  101.6 0.8 pad_maximum_fusion.15
  102.4 0.5 collective-permute-start.12
  103.1 1.0 mul.49
  104.1 0.2 mul.42
  104.3 1.1 mul.43
  105.4 1.7 %collective-permute-done.9 = bf16[416,384]{1,0:T(8,128)(2,1)} collective-permute-done((bf16[416,384]{1,0:T(8,128)(2,1)}, bf16[416,384]{1,0:T(8,128)(2,1)}, u32[]{:S(2)}, u32[]{:S(2)}) %collective-permute-start.9) | collective-permute-done | bytes 319520 | tf_op jit(solution)/shard_map/ppermute | solution.py:24
  107.1 0.9 slice.482
  108.0 1.1 fusion.29
  109.1 2.0 %collective-permute-done.12 = bf16[416,384]{1,0:T(8,128)(2,1)} collective-permute-done((bf16[416,384]{1,0:T(8,128)(2,1)}, bf16[416,384]{1,0:T(8,128)(2,1)}, u32[]{:S(2)}, u32[]{:S(2)}) %collective-permute-start.12) | collective-permute-done | bytes 319520 | tf_op jit(solution)/shard_map/ppermute | solution.py:24
  111.1 0.9 slice.485
  112.1 0.8 slice.490
  112.9 0.7 slice.493
  113.7 3.6 %collective-permute-start.13 = (bf16[80,768]{1,0:T(8,128)(2,1)S(1)}, bf16[80,768]{1,0:T(8,128)(2,1)S(1)}, u32[]{:S(2)}, u32[]{:S(2)}) collective-permute-start(bf16[80,768]{1,0:T(8,128)(2,1)S(1)} %pad_maximum_fusion.21), channel_id=1, source_target_pairs={{0,8},{1,9},{2,10},{3,11},{4,12},{5,13},{6,14},{7,15},{8,0},{9,1},... | collective-permute-start | bytes 368648 | tf_op jit(solution)/shard_map/ppermute | solution.py:24
  117.3 1.0 slice.452
  118.3 0.8 fusion.19
  119.1 1.0 slice.479
  120.1 0.8 fusion.13
  121.2 0.4 collective-permute-done.13
  121.7 0.2 mul.40
  121.9 0.5 mul.41
  122.6 0.2 mul.46
  122.7 1.4 %mul.47 = f32[2,128,768]{2,1,0:T(8,128)} reshape(f32[2,8,16,12,64]{4,3,2,1,0:T(8,128)S(1)} %mul.46) | data formatting | bytes 1572864 | tf_op jit(solution)/shard_map/mul | solution.py:49
  124.2 1.6 %fusion.7 = bf16[2,128,768]{2,1,0:T(8,128)(2,1)S(1)} fusion(f32[2,128,384]{2,1,0:T(8,128)} %fusion.13, f32[2,128,384]{2,1,0:T(8,128)} %fusion.19, f32[2,128,768]{2,1,0:T(8,128)} %mul.47, f32[2,128,768]{2,1,0:T(8,128)S(1)} %mul.41, f32[128,768]{1,0:T(8,128)S(1)} %copy-done.5, f32[128,768]{1,0:T(8,128)} %mul.43), kind=kLoop, calls=%fused_computation.18 | loop fusion | flops 1179648 | bytes 3538944 | tf_op jit(solution)/shard_map/convert.3 | solution.py:355
  125.8 0.8 slice_bitcast_fusion.6
  (160 shorter events, 4.1 us)
Async XLA Ops:
  0.6 2.6 %copy-start.3 = (bf16[128,768]{1,0:T(8,128)(2,1)S(1)}, bf16[128,768]{1,0:T(8,128)(2,1)}, u32[]{:S(2)}) copy-start(bf16[128,768]{1,0:T(8,128)(2,1)} %param.7) | copy-start | bytes 589828
  0.6 3.3 %copy-start.28 = (s32[3,12]{1,0:T(4,128)S(1)}, s32[3,12]{1,0:T(4,128)}, u32[]{:S(2)}) copy-start(s32[3,12]{1,0:T(4,128)} %offsets_ref.3) | copy-start | bytes 436
  5.0 5.7 %copy-start.4 = (bf16[128,768]{1,0:T(8,128)(2,1)S(1)}, bf16[128,768]{1,0:T(8,128)(2,1)}, u32[]{:S(2)}) copy-start(bf16[128,768]{1,0:T(8,128)(2,1)} %param.6) | copy-start | bytes 589828
  6.3 10.1 %collective-permute-start = (bf16[80,768]{1,0:T(8,128)(2,1)S(1)}, bf16[80,768]{1,0:T(8,128)(2,1)S(1)}, u32[]{:S(2)}, u32[]{:S(2)}) collective-permute-start(bf16[80,768]{1,0:T(8,128)(2,1)S(1)} %pad_maximum_fusion.20), channel_id=1, source_target_pairs={{0,8},{1,9},{2,10},{3,11},{4,12},{5,13},{6,14},{7,15},{8,0},{9,1},... | collective-permute-start | bytes 368648 | tf_op jit(solution)/shard_map/ppermute | solution.py:24
  16.5 8.8 %collective-permute-start.4 = (bf16[416,384]{1,0:T(8,128)(2,1)S(1)}, bf16[416,384]{1,0:T(8,128)(2,1)S(1)}, u32[]{:S(2)}, u32[]{:S(2)}) collective-permute-start(bf16[416,384]{1,0:T(8,128)(2,1)S(1)} %pad_maximum_fusion.13), channel_id=1, source_target_pairs={{0,4},{1,5},{2,6},{3,7},{4,0},{5,1},{6,2},{7,3},{8,12},{9,13},{10,... | collective-permute-start | bytes 958472 | tf_op jit(solution)/shard_map/ppermute | solution.py:24
  17.4 9.6 %collective-permute-start.1 = (bf16[416,384]{1,0:T(8,128)(2,1)S(1)}, bf16[416,384]{1,0:T(8,128)(2,1)S(1)}, u32[]{:S(2)}, u32[]{:S(2)}) collective-permute-start(bf16[416,384]{1,0:T(8,128)(2,1)S(1)} %pad_maximum_fusion.12), channel_id=1, source_target_pairs={{0,2},{1,3},{2,0},{3,1},{4,6},{5,7},{6,4},{7,5},{8,10},{9,11},{10,... | collective-permute-start | bytes 958472 | tf_op jit(solution)/shard_map/ppermute | solution.py:24
  25.7 14.7 %collective-permute-start.5 = (bf16[832,384]{1,0:T(8,128)(2,1)S(1)}, bf16[832,384]{1,0:T(8,128)(2,1)S(1)}, u32[]{:S(2)}, u32[]{:S(2)}) collective-permute-start(bf16[832,384]{1,0:T(8,128)(2,1)S(1)} %pad_maximum_fusion.5), channel_id=1, source_target_pairs={{0,2},{1,3},{2,0},{3,1},{4,6},{5,7},{6,4},{7,5},{8,10},{9,11},{10,... | collective-permute-start | bytes 1916936 | tf_op jit(solution)/shard_map/ppermute | solution.py:24
  27.3 15.2 %collective-permute-start.2 = (bf16[832,384]{1,0:T(8,128)(2,1)S(1)}, bf16[832,384]{1,0:T(8,128)(2,1)S(1)}, u32[]{:S(2)}, u32[]{:S(2)}) collective-permute-start(bf16[832,384]{1,0:T(8,128)(2,1)S(1)} %pad_maximum_fusion.4), channel_id=1, source_target_pairs={{0,4},{1,5},{2,6},{3,7},{4,0},{5,1},{6,2},{7,3},{8,12},{9,13},{10,... | collective-permute-start | bytes 1916936 | tf_op jit(solution)/shard_map/ppermute | solution.py:24
  40.9 1.8 %copy-start = (bf16[1664,384]{1,0:T(8,128)(2,1)}, bf16[1664,384]{1,0:T(8,128)(2,1)S(1)}, u32[]{:S(2)}) copy-start(bf16[1664,384]{1,0:T(8,128)(2,1)S(1)} %pad_maximum_fusion.1.mine_ref) | copy-start | bytes 3833860
  40.9 3.9 %collective-permute-start.6 = (bf16[1664,384]{1,0:T(8,128)(2,1)S(1)}, bf16[1664,384]{1,0:T(8,128)(2,1)S(1)}, u32[]{:S(2)}, u32[]{:S(2)}) collective-permute-start(bf16[1664,384]{1,0:T(8,128)(2,1)S(1)} %pad_maximum_fusion.1.mine_ref), channel_id=1, source_target_pairs={{0,1},{1,0},{2,3},{3,2},{4,5},{5,4},{6,7},{7,6},{8,9},{9,8},{10,11... | collective-permute-start | bytes 3833864 | tf_op jit(solution)/shard_map/ppermute | solution.py:24
  42.9 1.2 copy-start.23
  42.9 1.2 copy-start.24
  44.1 16.4 %collective-permute-start.3 = (bf16[1664,384]{1,0:T(8,128)(2,1)}, bf16[1664,384]{1,0:T(8,128)(2,1)}, u32[]{:S(2)}, u32[]{:S(2)}) collective-permute-start(bf16[1664,384]{1,0:T(8,128)(2,1)} %pad_maximum_fusion.mine_ref), channel_id=1, source_target_pairs={{0,1},{1,0},{2,3},{3,2},{4,5},{5,4},{6,7},{7,6},{8,9},{9,8},{10,11... | collective-permute-start | bytes 3833864 | tf_op jit(solution)/shard_map/ppermute | solution.py:24
  44.9 1.1 copy-start.14
  60.0 14.6 %collective-permute-start.7 = (bf16[1664,384]{1,0:T(8,128)(2,1)}, bf16[1664,384]{1,0:T(8,128)(2,1)}, u32[]{:S(2)}, u32[]{:S(2)}) collective-permute-start(bf16[1664,384]{1,0:T(8,128)(2,1)} %get-tuple-element.21), channel_id=1, source_target_pairs={{0,1},{1,0},{2,3},{3,2},{4,5},{5,4},{6,7},{7,6},{8,9},{9,8},{10,11... | collective-permute-start | bytes 3833864 | tf_op jit(solution)/shard_map/ppermute | solution.py:24
  74.5 5.1 %collective-permute-start.10 = (bf16[1664,384]{1,0:T(8,128)(2,1)}, bf16[1664,384]{1,0:T(8,128)(2,1)S(1)}, u32[]{:S(2)}, u32[]{:S(2)}) collective-permute-start(bf16[1664,384]{1,0:T(8,128)(2,1)} %get-tuple-element.25), channel_id=1, source_target_pairs={{0,1},{1,0},{2,3},{3,2},{4,5},{5,4},{6,7},{7,6},{8,9},{9,8},{10,11... | collective-permute-start | bytes 3833864 | tf_op jit(solution)/shard_map/ppermute | solution.py:24
  74.5 3.5 %copy-start.16 = (f32[2,256,384]{2,1,0:T(8,128)S(1)}, f32[2,256,384]{2,1,0:T(8,128)}, u32[]{:S(2)}) copy-start(f32[2,256,384]{2,1,0:T(8,128)} %get-tuple-element.22) | copy-start | bytes 2359300
  75.9 2.1 %copy-start.26 = (f32[2,64,384]{2,1,0:T(8,128)S(1)}, f32[2,64,384]{2,1,0:T(8,128)}, u32[]{:S(2)}) copy-start(f32[2,64,384]{2,1,0:T(8,128)} %get-tuple-element.23) | copy-start | bytes 589828
  75.9 2.2 %copy-start.9 = (f32[2,512,384]{2,1,0:T(8,128)S(1)}, f32[2,512,384]{2,1,0:T(8,128)}, u32[]{:S(2)}) copy-start(f32[2,512,384]{2,1,0:T(8,128)} %get-tuple-element.20) | copy-start | bytes 4718596
  78.2 16.8 %collective-permute-start.8 = (bf16[832,384]{1,0:T(8,128)(2,1)S(1)}, bf16[832,384]{1,0:T(8,128)(2,1)S(1)}, u32[]{:S(2)}, u32[]{:S(2)}) collective-permute-start(bf16[832,384]{1,0:T(8,128)(2,1)S(1)} %pad_maximum_fusion.6), channel_id=1, source_target_pairs={{0,2},{1,3},{2,0},{3,1},{4,6},{5,7},{6,4},{7,5},{8,10},{9,11},{10,... | collective-permute-start | bytes 1916936 | tf_op jit(solution)/shard_map/ppermute | solution.py:24
  79.4 15.7 %copy-start.19 = (f32[2,2,2,8,384]{4,3,2,1,0:T(8,128)}, f32[2,2,2,8,384]{4,3,2,1,0:T(8,128)S(1)}, u32[]{:S(2)}) copy-start(f32[2,2,2,8,384]{4,3,2,1,0:T(8,128)S(1)} %fusion.36) | copy-start | bytes 294916
  79.5 15.7 %copy-start.11 = (f32[2,2,2,32,384]{4,3,2,1,0:T(8,128)}, f32[2,2,2,32,384]{4,3,2,1,0:T(8,128)S(1)}, u32[]{:S(2)}) copy-start(f32[2,2,2,32,384]{4,3,2,1,0:T(8,128)S(1)} %fusion.16) | copy-start | bytes 1179652
  79.5 1.6 %copy-start.10 = (f32[2,512,384]{2,1,0:T(8,128)S(1)}, f32[2,512,384]{2,1,0:T(8,128)}, u32[]{:S(2)}) copy-start(f32[2,512,384]{2,1,0:T(8,128)} %get-tuple-element.24) | copy-start | bytes 4718596
  81.3 1.1 copy-start.15
  82.4 0.9 copy-start.25
  83.4 17.3 %collective-permute-start.11 = (bf16[832,384]{1,0:T(8,128)(2,1)S(1)}, bf16[832,384]{1,0:T(8,128)(2,1)S(1)}, u32[]{:S(2)}, u32[]{:S(2)}) collective-permute-start(bf16[832,384]{1,0:T(8,128)(2,1)S(1)} %pad_maximum_fusion.7), channel_id=1, source_target_pairs={{0,4},{1,5},{2,6},{3,7},{4,0},{5,1},{6,2},{7,3},{8,12},{9,13},{10,... | collective-permute-start | bytes 1916936 | tf_op jit(solution)/shard_map/ppermute | solution.py:24
  85.4 15.4 %copy-start.12 = (f32[2,2,2,32,384]{4,3,2,0,1:T(8,128)}, f32[2,2,2,32,384]{4,3,2,0,1:T(8,128)S(1)}, u32[]{:S(2)}) copy-start(f32[2,2,2,32,384]{4,3,2,0,1:T(8,128)S(1)} %fusion.21) | copy-start | bytes 1179652
  85.5 16.1 %copy-start.21 = (f32[2,2,2,8,384]{4,3,2,0,1:T(8,128)}, f32[2,2,2,8,384]{4,3,2,0,1:T(8,128)S(1)}, u32[]{:S(2)}) copy-start(f32[2,2,2,8,384]{4,3,2,0,1:T(8,128)S(1)} %fusion.38) | copy-start | bytes 294916
  85.6 10.4 %copy-start.1 = (f32[2,2,128,384]{3,2,1,0:T(8,128)}, f32[2,2,128,384]{3,2,1,0:T(8,128)S(1)}, u32[]{:S(2)}) copy-start(f32[2,2,128,384]{3,2,1,0:T(8,128)S(1)} %fusion.5) | copy-start | bytes 2359300
  95.2 0.7 copy-start.6
  96.8 10.3 %collective-permute-start.9 = (bf16[416,384]{1,0:T(8,128)(2,1)}, bf16[416,384]{1,0:T(8,128)(2,1)}, u32[]{:S(2)}, u32[]{:S(2)}) collective-permute-start(bf16[416,384]{1,0:T(8,128)(2,1)} %pad_maximum_fusion.14), channel_id=1, source_target_pairs={{0,4},{1,5},{2,6},{3,7},{4,0},{5,1},{6,2},{7,3},{8,12},{9,13},{10,... | collective-permute-start | bytes 958472 | tf_op jit(solution)/shard_map/ppermute | solution.py:24
  100.8 2.1 %copy-start.27 = (f32[16,12]{1,0:T(8,128)S(1)}, f32[16,12]{1,0:T(8,128)}, u32[]{:S(2)}) copy-start(f32[16,12]{1,0:T(8,128)} %get-tuple-element.65) | copy-start | bytes 2308
  100.8 0.7 copy-start.7
  101.6 1.3 %copy-start.17 = (f32[64,384]{1,0:T(8,128)}, f32[64,384]{1,0:T(8,128)S(1)}, u32[]{:S(2)}) copy-start(f32[64,384]{1,0:T(8,128)S(1)} %slice.477) | copy-start | bytes 294916
  102.4 1.7 %copy-start.29 = (f32[4,12]{1,0:T(4,128)S(1)}, f32[4,12]{1,0:T(4,128)}, u32[]{:S(2)}) copy-start(f32[4,12]{1,0:T(4,128)} %get-tuple-element.63) | copy-start | bytes 580
  102.4 8.7 %collective-permute-start.12 = (bf16[416,384]{1,0:T(8,128)(2,1)}, bf16[416,384]{1,0:T(8,128)(2,1)}, u32[]{:S(2)}, u32[]{:S(2)}) collective-permute-start(bf16[416,384]{1,0:T(8,128)(2,1)} %pad_maximum_fusion.15), channel_id=1, source_target_pairs={{0,2},{1,3},{2,0},{3,1},{4,6},{5,7},{6,4},{7,5},{8,10},{9,11},{10,... | collective-permute-start | bytes 958472 | tf_op jit(solution)/shard_map/ppermute | solution.py:24
  105.3 6.7 %copy-start.8 = (f32[256,384]{1,0:T(8,128)S(1)}, f32[256,384]{1,0:T(8,128)}, u32[]{:S(2)}) copy-start(f32[256,384]{1,0:T(8,128)} %copy-done.7) | copy-start | bytes 1179652
  105.3 6.7 %copy-start.13 = (f32[2,2,2,32,384]{4,3,2,0,1:T(8,128)S(1)}, f32[2,2,2,32,384]{4,3,2,0,1:T(8,128)}, u32[]{:S(2)}) copy-start(f32[2,2,2,32,384]{4,3,2,0,1:T(8,128)} %copy-done.12) | copy-start | bytes 1179652
  105.4 7.5 %copy-start.20 = (f32[2,2,2,8,384]{4,3,2,1,0:T(8,128)S(1)}, f32[2,2,2,8,384]{4,3,2,1,0:T(8,128)}, u32[]{:S(2)}) copy-start(f32[2,2,2,8,384]{4,3,2,1,0:T(8,128)} %copy-done.19) | copy-start | bytes 294916
  108.0 5.7 %copy-start.18 = (f32[64,384]{1,0:T(8,128)S(1)}, f32[64,384]{1,0:T(8,128)}, u32[]{:S(2)}) copy-start(f32[64,384]{1,0:T(8,128)} %copy-done.17) | copy-start | bytes 294916
  108.0 5.7 %copy-start.22 = (f32[2,2,2,8,384]{4,3,2,0,1:T(8,128)S(1)}, f32[2,2,2,8,384]{4,3,2,0,1:T(8,128)}, u32[]{:S(2)}) copy-start(f32[2,2,2,8,384]{4,3,2,0,1:T(8,128)} %copy-done.21) | copy-start | bytes 294916
  112.1 6.2 %copy-start.2 = (f32[2,2,128,384]{3,2,1,0:T(8,128)S(1)}, f32[2,2,128,384]{3,2,1,0:T(8,128)}, u32[]{:S(2)}) copy-start(f32[2,2,128,384]{3,2,1,0:T(8,128)} %copy-done.1) | copy-start | bytes 2359300
  113.7 7.8 %collective-permute-start.13 = (bf16[80,768]{1,0:T(8,128)(2,1)S(1)}, bf16[80,768]{1,0:T(8,128)(2,1)S(1)}, u32[]{:S(2)}, u32[]{:S(2)}) collective-permute-start(bf16[80,768]{1,0:T(8,128)(2,1)S(1)} %pad_maximum_fusion.21), channel_id=1, source_target_pairs={{0,8},{1,9},{2,10},{3,11},{4,12},{5,13},{6,14},{7,15},{8,0},{9,1},... | collective-permute-start | bytes 368648 | tf_op jit(solution)/shard_map/ppermute | solution.py:24
  122.7 1.4 %copy-start.5 = (f32[128,768]{1,0:T(8,128)S(1)}, f32[128,768]{1,0:T(8,128)}, u32[]{:S(2)}) copy-start(f32[128,768]{1,0:T(8,128)} %mul.49) | copy-start | bytes 1179652
